TPU v7x, 32 devices: a whole 2x2x4 slice. The times are simulated.
32 devices in a mesh: groups: 2 (over x), ctx: 16 (over z, y, core).
Axes of the slice: x: 2, y: 2, z: 4, core: 2. Of those that a mesh axis runs over, the one named last changes fastest.
Arguments:
- query_proj: bfloat16 [4096, 4096], P(('groups', 'ctx')), parts along dimension 0, may hold values from -6 to 6
- key_proj: bfloat16 [4096, 4096], P(('groups', 'ctx')), parts along dimension 0, may hold values from -6 to 6
- value_proj: bfloat16 [4096, 4096], P(('groups', 'ctx')), parts along dimension 0, may hold values from -6 to 6
- out_grad: bfloat16 [4096, 4096], P(('groups', 'ctx')), parts along dimension 0, may hold values from -6 to 6
- decay_rate: float32 [256, 16], replicated, may hold values from 0 to 0.034, as said below
- residue: float32 [256, 16], replicated, may hold values from -0.3 to 0.3
- group_of: int32 [4096], replicated, may hold values from 0 to 255, as said below
Outputs:
- hyena_out: bfloat16 [4096, 4096], P(('groups', 'ctx')), parts along dimension 0
- query_grad: bfloat16 [4096, 4096], P(('groups', 'ctx')), parts along dimension 0
- key_grad: bfloat16 [4096, 4096], P(('groups', 'ctx')), parts along dimension 0
- value_grad: bfloat16 [4096, 4096], P(('groups', 'ctx')), parts along dimension 0
- filter_update: float32 [512, 16], P('groups'), parts along dimension 0
There are 2 independent parts, one for each index of `groups`. A program takes and returns all parts, laid end to end along the dimension named above; an argument that names none is the same for every part. Nothing has to cross between parts.
Inputs may be any that keep to these rules, and one draw needn't show every extreme that they name: `group_of`: each of the 256 filter groups holds exactly 16 channels. `decay_rate`: positive rates.
All inputs are finite; a program needn't handle non-finite values.
Results may differ from a plain program's by a relative error of at most 0.005.
Values sent between devices are 32-bit elements; how exact they have to be, the bound alone decides.
No kernel may reach another device: no remote copies, remote signals or barrier semaphores. Data moves between devices by JAX's collectives and lax.ppermute only.
A program may use at most 192 MiB of HBM per device.

v0:
```python
import jax
import jax.numpy as jnp
from jax import lax
from jax.sharding import PartitionSpec as P


def carried_in(part, axis, combine, identity, reverse):
    count = lax.axis_size(axis)
    place = lax.axis_index(axis)
    ahead = count - 1 - place if reverse else place
    gathered = jax.tree.map(lambda a: lax.all_gather(a, axis), part)
    state = jax.tree.map(lambda a, e: jnp.zeros_like(a) + jnp.asarray(e, a.dtype), part, identity)

    def one(lap, state):
        source = count - 1 - lap if reverse else lap
        return combine(
            state, jax.tree.map(lambda a: lax.dynamic_index_in_dim(a, source, 0, False), gathered)
        )

    return lax.fori_loop(0, ahead, one, state)


def on_device(query_proj, key_proj, value_proj, out_grad, decay_rate, residue, group_of):
    high = lax.Precision.HIGHEST
    row_count, channel_count = query_proj.shape
    group_count, mode_count = decay_rate.shape
    per_group = channel_count // group_count
    order = jnp.argsort(group_of, stable=True)
    inverse = jnp.argsort(order, stable=True)
    query_f = query_proj.astype(jnp.float32)
    key_f = key_proj.astype(jnp.float32)
    value_f = value_proj.astype(jnp.float32)
    grad_f = out_grad.astype(jnp.float32)
    mixed = lax.optimization_barrier((key_f * value_f).astype(jnp.bfloat16))
    mixed_sorted = (
        jnp.take(mixed.T, order, axis=0)
        .astype(jnp.float32)
        .reshape(group_count, per_group, row_count)
    )
    upstream = grad_f * query_f
    upstream_sorted = jnp.take(upstream.T, order, axis=0).reshape(group_count, per_group, row_count)
    positions = jnp.arange(row_count, dtype=jnp.float32)
    powers = jnp.exp(-decay_rate[:, :, None] * positions[None, None, :])
    inverse_powers = jnp.exp(decay_rate[:, :, None] * positions[None, None, :])
    later_powers = powers * jnp.exp(-decay_rate)[:, :, None]
    reversed_powers = powers[:, :, ::-1]
    weighted = later_powers * residue[:, :, None]
    weighted_back = reversed_powers * residue[:, :, None]
    causal = (
        jnp.arange(row_count, dtype=jnp.int32)[:, None]
        >= jnp.arange(row_count, dtype=jnp.int32)[None, :]
    )
    toeplitz = jnp.einsum(
        "gmt,gms->gts", powers * residue[:, :, None], inverse_powers, precision=high
    )
    toeplitz = jnp.where(causal[None], toeplitz, 0.0)
    local_out = jnp.einsum("gts,gcs->gct", toeplitz, mixed_sorted, precision=high)
    local_back = jnp.einsum("gts,gct->gcs", toeplitz, upstream_sorted, precision=high)
    end_state = jnp.einsum("gms,gcs->mgc", reversed_powers, mixed_sorted, precision=high).reshape(
        mode_count, channel_count
    )
    head_term = jnp.einsum("gmt,gct->mgc", later_powers, upstream_sorted, precision=high).reshape(
        mode_count, channel_count
    )
    empty_state = jnp.zeros((mode_count, channel_count), jnp.float32)
    group_decay = jnp.exp(-decay_rate * row_count).T
    unit_decay = jnp.ones_like(group_decay)

    def chain_decays(earlier, later):
        widened = jnp.repeat(later[0], per_group, axis=1)
        return (earlier[0] * later[0], widened * earlier[1] + later[1])

    carry_pair = carried_in(
        (group_decay, end_state), "ctx", chain_decays, (unit_decay, empty_state), False
    )
    back_pair = carried_in(
        (group_decay, head_term), "ctx", chain_decays, (unit_decay, empty_state), True
    )
    carry_in = carry_pair[1]
    carry_back = back_pair[1]
    carry_grouped = carry_in.reshape(mode_count, group_count, per_group)
    back_grouped = carry_back.reshape(mode_count, group_count, per_group)
    out_sorted = local_out + jnp.einsum("gmt,mgc->gct", weighted, carry_grouped, precision=high)
    back_sorted = local_back + jnp.einsum(
        "gms,mgc->gcs", weighted_back, back_grouped, precision=high
    )
    cross = jnp.einsum("gct,gcs->gts", upstream_sorted, mixed_sorted, precision=high)
    cross = jnp.where(causal[None], cross, 0.0)
    inner = jnp.einsum("gts,gms->gmt", cross, inverse_powers, precision=high)
    local_grad = jnp.sum(inner * powers, axis=2)
    local_grad = (
        local_grad
        + jnp.sum((carry_in * head_term).reshape(mode_count, group_count, per_group), axis=2).T
    )
    filter_grad = lax.psum(local_grad, "ctx")
    filter_update = filter_grad / jnp.sqrt(jnp.mean(filter_grad * filter_grad) + 1e-06)
    filtered = jnp.take(out_sorted.reshape(channel_count, row_count), inverse, axis=0).T
    mixed_grad = jnp.take(back_sorted.reshape(channel_count, row_count), inverse, axis=0).T
    hyena_out = (query_f * filtered).astype(jnp.bfloat16)
    query_grad = (grad_f * filtered).astype(jnp.bfloat16)
    key_grad = (mixed_grad * value_f).astype(jnp.bfloat16)
    value_grad = (mixed_grad * key_f).astype(jnp.bfloat16)
    return (hyena_out, query_grad, key_grad, value_grad, filter_update)


def solution(mesh):
    placed = (
        P(("groups", "ctx"), None),
        P(("groups", "ctx"), None),
        P(("groups", "ctx"), None),
        P(("groups", "ctx"), None),
        P(),
        P(),
        P(),
    )
    return jax.shard_map(
        on_device,
        mesh=mesh,
        in_specs=placed,
        out_specs=(
            P(("groups", "ctx"), None),
            P(("groups", "ctx"), None),
            P(("groups", "ctx"), None),
            P(("groups", "ctx"), None),
            P("groups", None),
        ),
        check_vma=False,
    )
```

profile of v0, /device:TPU:0, one launch (start us, length us, event | category | flops | bytes accessed | tf_op | source)
XLA Modules:
  0.0 484.5 jit_solution(5520543099957598316)
XLA Ops:
  7.2 6.6 %sort.31 = (s32[4096]{0:T(1024)}, s32[4096]{0:T(1024)S(1)}) sort(s32[4096]{0:T(1024)} %param.19, s32[4096]{0:T(1024)S(1)} %iota.26), dimensions={0}, to_apply=%region_0.0 | sort | flops 49152 | bytes 65536 | tf_op jit(solution)/shard_map/jit(argsort)/sort | solution.py:28
  14.8 1.6 copy.65
  18.2 1.7 multiply_exponential_fusion.3
  19.9 2.7 rev.3
  22.7 15.0 %gather_fusion = bf16[4096,128]{1,0:T(8,128)(2,1)} fusion(bf16[4096,128]{1,0:T(8,128)(2,1)S(1)} %bitcast.52, s32[4096]{0:T(1024)S(1)} %fusion.51), kind=kCustom, calls=%fused_computation.3 | custom fusion | bytes 2113536 | tf_op jit(solution)/shard_map/jit(_take)/gather | solution.py:36
  37.7 4.5 fusion.47
  42.2 3.0 copy.70
  45.4 5.8 %sort.32 = (s32[4096]{0:T(1024)}, s32[4096]{0:T(1024)S(1)}) sort(s32[4096]{0:T(1024)S(1)} %get-tuple-element.136, s32[4096]{0:T(1024)S(1)} %iota.27), dimensions={0}, to_apply=%region_3.4 | sort | flops 49152 | bytes 65536 | tf_op jit(solution)/shard_map/jit(argsort)/sort | solution.py:29
  52.0 1.3 copy.64
  53.4 1.3 copy.73
  54.7 25.9 %all-gather = f32[256,256]{1,0:T(8,128)} all-gather(f32[16,256]{1,0:T(8,128)S(1)} %get-tuple-element.186), channel_id=2, replica_groups=mesh['groups'=2,'ctx'=16] {'ctx'}, dimensions={0}, use_global_device_ids=true | all-gather | bytes 278528 | tf_op jit(solution)/shard_map/all_gather | solution.py:11
  81.8 28.7 %fusion.22 = f32[256,128,128]{2,1,0:T(8,128)S(1)} fusion(f32[256,16]{1,0:T(8,128)S(1)} %copy.69, f32[256,16]{1,0:T(8,128)S(1)} %copy.68, f32[256,16]{1,0:T(8,128)S(1)} %copy.67), kind=kOutput, calls=%fused_computation.38 | convolution fusion | flops 806879232 | bytes 16826368 | tf_op jit(solution)/shard_map/gmt,gms->gts/dot_general | solution.py:53
  110.5 5.7 %copy-done = f32[256,128,128]{2,1,0:T(8,128)} copy-done((f32[256,128,128]{2,1,0:T(8,128)}, f32[256,128,128]{2,1,0:T(8,128)S(1)}, u32[]{:S(2)}) %copy-start) | copy-done | bytes 16777240
  116.3 14.5 %fusion.4 = f32[256,16,128]{2,1,0:T(8,128)} fusion(f32[256,128,128]{2,1,0:T(8,128)S(1)} %fusion.22, pred[128,128]{1,0:T(8,128)(4,1)S(1)} %iota_compare_fusion, bf16[256,16,128]{2,1,0:T(8,128)(2,1)S(1)} %bitcast.59, pred[256,16]{1,0:T(8,128)(4,1)S(1)} %copy-done.17), kind=kOutput, calls=%fused_computation.12 | convolution fusion | flops 810024960 | bytes 19943424 | tf_op jit(solution)/shard_map/gts,gcs->gct/dot_general | solution.py:57
  131.9 2.9 copy.83
  134.8 5.0 %fusion.28 = f32[256,16,128]{2,1,0:T(8,128)S(1)} fusion(f32[256,16,128]{2,1,0:T(8,128)} %fusion.4, f32[16,256,16]{0,2,1:T(8,128)} %bitcast.61, f32[256,16]{1,0:T(8,128)S(1)} %copy-done.12, f32[256,16]{1,0:T(8,128)S(1)} %copy-done.10, f32[256,16]{1,0:T(8,128)S(1)} %copy.67), kind=kOutput, calls=%fused_computation.43 | convolution fusion | flops 102760448 | bytes 4505600 | tf_op jit(solution)/shard_map/gmt,mgc->gct/dot_general | solution.py:83
  139.8 15.5 %gather_fusion.1 = f32[4096,128]{1,0:T(8,128)} fusion(f32[4096,128]{1,0:T(8,128)S(1)} %bitcast.50, s32[4096]{0:T(1024)} %fusion.52), kind=kCustom, calls=%fused_computation.clone | custom fusion | bytes 4210688 | tf_op jit(solution)/shard_map/jit(_take)/gather | solution.py:97
  155.3 5.1 %fusion.16 = (bf16[128,4096]{0,1:T(8,128)(2,1)}, bf16[128,4096]{0,1:T(8,128)(2,1)}, f32[4096,128]{1,0:T(8,128)S(1)}) fusion(bf16[128,4096]{0,1:T(8,128)(2,1)} %copy.73, f32[4096,128]{1,0:T(8,128)} %gather_fusion.1, pred[4096]{0:T(1024)(128)(4,1)S(1)} %copy-done.26, bf16[128,4096]{0,1:T(8,128)(2,1)} %copy.64), kind=kLoop, calls=%fused_computation.30 | loop fusion | flops 4194304 | bytes 8392704 | tf_op jit(solution)/shard_map/convert_element_type | solution.py:100
  160.4 14.2 %gather_fusion.2 = f32[4096,128]{1,0:T(8,128)} fusion(f32[4096,128]{1,0:T(8,128)S(1)} %get-tuple-element.184, s32[4096]{0:T(1024)S(1)} %copy-done.21), kind=kCustom, calls=%fused_computation.1.clone | custom fusion | bytes 4210688 | tf_op jit(solution)/shard_map/jit(_take)/gather | solution.py:41
  174.6 3.6 broadcast_select_fusion
  178.2 5.4 %fusion.25 = f32[256,16,16]{2,1,0:T(8,128)} fusion(f32[256,16,128]{2,1,0:T(8,128)S(1)} %bitcast.53, f32[256,16]{1,0:T(8,128)S(1)} %copy-done.12, f32[256,16]{1,0:T(8,128)S(1)} %copy.67), kind=kOutput, calls=%fused_computation.42 | convolution fusion | flops 101711872 | bytes 2392064 | tf_op jit(solution)/shard_map/gmt,gct->mgc/dot_general | solution.py:62
  183.5 2.9 copy.74
  186.4 2.3 copy.79
  188.7 2.5 copy.78
  191.2 2.9 copy.76
  194.0 1.7 mul.121
  195.7 3.0 reshape.82
  198.7 2.2 reduce_sum.28
  201.7 14.0 %fusion.46 = f32[256,128,128]{2,1,0:T(8,128)S(1)} fusion(f32[256,16,128]{2,1,0:T(8,128)S(1)} %bitcast.54, bf16[256,16,128]{2,1,0:T(8,128)(2,1)S(1)} %bitcast.60, pred[256,16]{1,0:T(8,128)(4,1)S(1)} %copy-done.18), kind=kOutput, calls=%fused_computation.57 | convolution fusion | flops 805830656 | bytes 19927040 | tf_op jit(solution)/shard_map/gct,gcs->gts/dot_general | solution.py:87
  215.7 26.9 %multiply_reduce_fusion = f32[256,16]{1,0:T(8,128)S(1)} fusion(f32[256,16]{1,0:T(8,128)S(1)} %copy.67, f32[256,128,128]{2,1,0:T(8,128)S(1)} %fusion.46, pred[128,128]{1,0:T(8,128)(4,1)S(1)} %iota_compare_fusion, f32[256,16]{1,0:T(8,128)S(1)} %copy-done.8), kind=kOutput, calls=%fused_computation.32 | convolution fusion | flops 811593728 | bytes 16842752 | tf_op jit(solution)/shard_map/gts,gms->gmt/dot_general | solution.py:89
  242.6 127.4 %psum.7 = f32[256,16]{1,0:T(8,128)S(1)} all-reduce(f32[256,16]{1,0:T(8,128)S(1)} %bitcast_add_fusion.2), channel_id=1, replica_groups=mesh['groups'=2,'ctx'=16] {'ctx'}, use_global_device_ids=true, to_apply=%region_8.10 | all-reduce | flops 4096 | bytes 32768 | tf_op jit(solution)/shard_map/psum | solution.py:95
  372.1 17.6 %fusion.2 = f32[256,16,128]{2,1,0:T(8,128)} fusion(f32[256,16,128]{2,1,0:T(8,128)S(1)} %bitcast.55, f32[256,128,128]{2,1,0:T(8,128)} %copy-done, pred[128,128]{1,0:T(8,128)(4,1)S(1)} %iota_compare_fusion), kind=kOutput, calls=%fused_computation.10 | convolution fusion | flops 809500672 | bytes 20987904 | tf_op jit(solution)/shard_map/gts,gct->gcs/dot_general | solution.py:58
  389.7 59.8 %while.27 = (s32[]{:T(128)}, f32[16,4096]{1,0:T(8,128)S(1)}, s32[]{:T(128)}, f32[16,16,256]{2,1,0:T(8,128)}, f32[16,16,4096]{2,1,0:T(8,128)}, /*index=5*/s32[]{:T(128)}, s32[]{:T(128)}, s32[]{:T(128)}, s32[]{:T(128)}) while((s32[]{:T(128)}, f32[16,4096]{1,0:T(8,128)S(1)}, s32[]{:T(128)}, f32[16,16,256]{2,1,0:T(8,128)}, ...), condition=%wide.region_5.7_spmd, body=%wide.region_4.6_spmd.sunk | while | flops 131078 | bytes 1884315 | solution.py:20
  391.0 1.6 reshape.129
  392.6 1.1 bitcast_add_fusion.6
  395.0 1.6 reshape.129
  396.6 1.1 bitcast_add_fusion.6
  399.0 1.6 reshape.129
  400.5 1.1 bitcast_add_fusion.6
  403.0 1.6 reshape.129
  404.5 1.1 bitcast_add_fusion.6
  407.0 1.6 reshape.129
  408.5 1.1 bitcast_add_fusion.6
  411.0 1.6 reshape.129
  414.9 1.6 reshape.129
  418.9 1.6 reshape.129
  420.5 1.1 bitcast_add_fusion.6
  422.9 1.6 reshape.129
  424.5 1.1 bitcast_add_fusion.6
  426.9 1.6 reshape.129
  430.9 1.6 reshape.129
  434.9 1.6 reshape.129
  436.4 1.1 bitcast_add_fusion.6
  438.9 1.6 reshape.129
  440.4 1.1 bitcast_add_fusion.6
  442.9 1.6 reshape.129
  446.8 1.6 reshape.129
  448.4 1.1 bitcast_add_fusion.6
  449.5 1.9 copy.84
  451.4 5.1 %fusion.31 = f32[256,16,128]{2,1,0:T(8,128)S(1)} fusion(f32[256,16,128]{2,1,0:T(8,128)} %fusion.2, f32[16,256,16]{0,2,1:T(8,128)} %bitcast.63, f32[256,16,128]{2,1,0:T(8,128)} %copy-done.1, f32[256,16]{1,0:T(8,128)S(1)} %copy-done.11), kind=kOutput, calls=%fused_computation.44 | convolution fusion | flops 101711872 | bytes 6569984 | tf_op jit(solution)/shard_map/gms,mgc->gcs/dot_general | solution.py:84
  456.6 14.2 %gather_fusion.3 = f32[4096,128]{1,0:T(8,128)} fusion(f32[4096,128]{1,0:T(8,128)S(1)} %bitcast.51, s32[4096]{0:T(1024)S(1)} %copy-done.22), kind=kCustom, calls=%fused_computation.2.clone | custom fusion | bytes 4210688 | tf_op jit(solution)/shard_map/jit(_take)/gather | solution.py:98
  470.8 3.8 fusion.13
  474.6 1.3 copy.81
  475.9 1.3 copy.80
  (121 shorter events, 33.5 us)
Async XLA Ops:
  7.2 9.3 %copy-start.13 = (bf16[128,4096]{1,0:T(8,128)(2,1)S(1)}, bf16[128,4096]{1,0:T(8,128)(2,1)}, u32[]{:S(2)}) copy-start(bf16[128,4096]{1,0:T(8,128)(2,1)} %param.15) | copy-start | bytes 3145732
  7.2 123.6 %all-gather.4.cloned.1.call-start = ((), (), s32[]{:S(2)}) async-start(), calls=%async_computation | async-start | bytes 4456448 | tf_op jit(solution)/shard_map/all_gather | solution.py:11
  13.8 0.9 copy-start.24
  13.8 8.8 %copy-start.20 = (s32[4096]{0:T(1024)}, s32[4096]{0:T(1024)S(1)}, u32[]{:S(2)}) copy-start(s32[4096]{0:T(1024)S(1)} %fusion.51) | copy-start | bytes 49156
  14.0 23.7 %copy-start.16 = (pred[256,16]{1,0:T(8,128)(4,1)}, pred[256,16]{1,0:T(8,128)(4,1)S(1)}, u32[]{:S(2)}) copy-start(pred[256,16]{1,0:T(8,128)(4,1)S(1)} %broadcast_in_dim.68) | copy-start | bytes 12292
  16.5 1.0 copy-start.4
  17.1 1.1 copy-start.6
  22.6 15.1 %copy-start.1 = (f32[256,16,128]{2,1,0:T(8,128)}, f32[256,16,128]{2,1,0:T(8,128)S(1)}, u32[]{:S(2)}) copy-start(f32[256,16,128]{2,1,0:T(8,128)S(1)} %rev.3) | copy-start | bytes 6291460
  42.2 3.1 copy-start.23
  42.2 9.8 %copy-start.28 = (f32[256,16]{0,1:T(8,128)S(1)}, f32[256,16]{0,1:T(8,128)}, u32[]{:S(2)}) copy-start(f32[256,16]{0,1:T(8,128)} %param.18) | copy-start | bytes 49156
  42.2 9.9 %copy-start.14 = (bf16[128,4096]{1,0:T(8,128)(2,1)S(1)}, bf16[128,4096]{1,0:T(8,128)(2,1)}, u32[]{:S(2)}) copy-start(bf16[128,4096]{1,0:T(8,128)(2,1)} %param.13) | copy-start | bytes 3145732
  42.2 11.2 %copy-start.15 = (bf16[128,4096]{1,0:T(8,128)(2,1)S(1)}, bf16[128,4096]{1,0:T(8,128)(2,1)}, u32[]{:S(2)}) copy-start(bf16[128,4096]{1,0:T(8,128)(2,1)} %param.16) | copy-start | bytes 3145732
  45.2 344.4 %all-gather.6.cloned.1.call-start = ((), (), s32[]{:S(2)}) async-start(), calls=%async_computation.1 | async-start | bytes 4456448 | tf_op jit(solution)/shard_map/all_gather | solution.py:11
  45.4 36.4 %copy-start.7 = (f32[256,16]{1,0:T(8,128)}, f32[256,16]{1,0:T(8,128)S(1)}, u32[]{:S(2)}) copy-start(f32[256,16]{1,0:T(8,128)S(1)} %copy.69) | copy-start | bytes 49156
  52.0 29.8 %copy-start.9 = (f32[256,16]{1,0:T(8,128)}, f32[256,16]{1,0:T(8,128)S(1)}, u32[]{:S(2)}) copy-start(f32[256,16]{1,0:T(8,128)S(1)} %copy.68) | copy-start | bytes 49156
  81.8 34.5 %copy-start.2 = (bf16[4096,128]{1,0:T(8,128)(2,1)S(1)}, bf16[4096,128]{1,0:T(8,128)(2,1)}, u32[]{:S(2)}) copy-start(bf16[4096,128]{1,0:T(8,128)(2,1)} %gather_fusion) | copy-start | bytes 3145732
  81.8 34.5 %copy-start.17 = (pred[256,16]{1,0:T(8,128)(4,1)S(1)}, pred[256,16]{1,0:T(8,128)(4,1)}, u32[]{:S(2)}) copy-start(pred[256,16]{1,0:T(8,128)(4,1)} %copy-done.16) | copy-start | bytes 12292
  110.5 5.7 %copy-start = (f32[256,128,128]{2,1,0:T(8,128)}, f32[256,128,128]{2,1,0:T(8,128)S(1)}, u32[]{:S(2)}) copy-start(f32[256,128,128]{2,1,0:T(8,128)S(1)} %fusion.22) | copy-start | bytes 50331652
  131.8 3.0 copy-start.10
  131.9 2.9 copy-start.12
  139.8 15.5 %copy-start.26 = (pred[4096]{0:T(1024)(128)(4,1)S(1)}, pred[4096]{0:T(1024)(128)(4,1)}, u32[]{:S(2)}) copy-start(pred[4096]{0:T(1024)(128)(4,1)} %compare_and_fusion) | copy-start | bytes 12292
  155.3 5.1 %copy-start.21 = (s32[4096]{0:T(1024)S(1)}, s32[4096]{0:T(1024)}, u32[]{:S(2)}) copy-start(s32[4096]{0:T(1024)} %copy-done.20) | copy-start | bytes 49156
  160.4 14.2 %copy-start.25 = (pred[4096]{0:T(1024)(128)(4,1)S(1)}, pred[4096]{0:T(1024)(128)(4,1)}, u32[]{:S(2)}) copy-start(pred[4096]{0:T(1024)(128)(4,1)} %copy-done.24) | copy-start | bytes 12292
  188.7 5.3 %copy-start.3 = (f32[16,4096]{1,0:T(8,128)S(1)}, f32[16,4096]{1,0:T(8,128)}, u32[]{:S(2)}) copy-start(f32[16,4096]{1,0:T(8,128)} %get-tuple-element.137) | copy-start | bytes 786436
  195.7 6.0 %copy-start.18 = (pred[256,16]{1,0:T(8,128)(4,1)S(1)}, pred[256,16]{1,0:T(8,128)(4,1)}, u32[]{:S(2)}) copy-start(pred[256,16]{1,0:T(8,128)(4,1)} %copy-done.16) | copy-start | bytes 12292
  201.7 14.0 %copy-start.8 = (f32[256,16]{1,0:T(8,128)S(1)}, f32[256,16]{1,0:T(8,128)}, u32[]{:S(2)}) copy-start(f32[256,16]{1,0:T(8,128)} %copy-done.7) | copy-start | bytes 49156
  215.7 26.9 %copy-start.19 = (f32[16,256]{0,1:T(8,128)S(1)}, f32[16,256]{0,1:T(8,128)}, u32[]{:S(2)}) copy-start(f32[16,256]{0,1:T(8,128)} %copy.77) | copy-start | bytes 49156
  449.5 2.0 copy-start.11
  451.4 5.1 %copy-start.22 = (s32[4096]{0:T(1024)S(1)}, s32[4096]{0:T(1024)}, u32[]{:S(2)}) copy-start(s32[4096]{0:T(1024)} %fusion.52) | copy-start | bytes 49156
  456.6 14.2 %copy-start.5 = (bf16[128,4096]{0,1:T(8,128)(2,1)S(1)}, bf16[128,4096]{0,1:T(8,128)(2,1)}, u32[]{:S(2)}) copy-start(bf16[128,4096]{0,1:T(8,128)(2,1)} %copy-done.4) | copy-start | bytes 3145732
  456.6 14.2 %copy-start.27 = (pred[4096]{0:T(1024)(128)(4,1)S(1)}, pred[4096]{0:T(1024)(128)(4,1)}, u32[]{:S(2)}) copy-start(pred[4096]{0:T(1024)(128)(4,1)} %compare_and_fusion) | copy-start | bytes 12292
Sparse Core Ops, SparseCore 0:
  45.3 53.8 all-gather.3
  186.6 116.4 all-gather.5
where the time goes:
time: 493 us; the launch traced here: 484 us
  blocking collectives  153 us (31%)
  local copies, waits for them, and re-layouts  144 us (29%)
  matrix products  121 us (25%)
  other arithmetic  49.6 us (10%)
  between operations  15.6 us (3%)
    psum x1, blocking collectives, on_device(): filter_grad = lax.psum(local_grad, 'ctx')  127 us
    dot_general x1, matrix products, on_device(): jnp.einsum('gmt,gms->gts', powers * residue[:, :, None], inverse_powers,...  28.7 us
    dot_general x1, matrix products, on_device(): inner = jnp.einsum('gts,gms->gmt', cross, inverse_powers, precision=high)  26.9 us
    all_gather x1, blocking collectives, carried_in(): gathered = jax.tree.map(lambda a: lax.all_gather(a, axis), part)  25.9 us
    reshape x15, local copies, waits for them, and re-layouts, chain_decays(): widened = jnp.repeat(later[0], per_group, axis=1)  23.4 us
    unnamed x69, local copies, waits for them, and re-layouts  19.7 us
    dot_general x1, matrix products, on_device(): jnp.einsum('gts,gct->gcs', toeplitz, upstream_sorted, precision=high)  17.6 us
    add x15, other arithmetic, chain_decays(): return (earlier[0] * later[0], widened * earlier[1] + later[1])  16.3 us
  transfers between devices with their start and end apart: 2, of which 0 were waited for; matrix products, arithmetic and copies ran while one was open for 27% of the time, Pallas kernels for 0%

commit v1 on v0

v1 whole, which is shorter than its diff:
```python
import jax
import jax.numpy as jnp
from jax import lax
from jax.experimental import pallas as pl
from jax.experimental.pallas import tpu as pltpu
from jax.sharding import PartitionSpec as P

BLOCK = 1024
SUB = 256
ROWS = 8


def carry_kernel(q_ref, k_ref, v_ref, g_ref, p_ref, xend_ref, head_ref, mix_ref, up_ref):
    f32 = jnp.float32
    mix_ref[...] = (k_ref[...].astype(f32) * v_ref[...].astype(f32)).astype(jnp.bfloat16).astype(f32)
    up_ref[...] = g_ref[...].astype(f32) * q_ref[...].astype(f32)
    rows, width = mix_ref.shape
    chunks = rows // ROWS
    for h in range(width // SUB):
        cols = pl.ds(h * SUB, SUB)
        p = p_ref[:, cols]

        def body(c, carry):
            x, a = carry
            fb = pl.multiple_of(c * ROWS, ROWS)
            bb = pl.multiple_of((chunks - 1 - c) * ROWS, ROWS)
            mt = mix_ref[pl.ds(fb, ROWS), cols]
            ub = up_ref[pl.ds(bb, ROWS), cols]
            for j in range(ROWS):
                x = p * x + mt[j : j + 1, :]
                jb = ROWS - 1 - j
                a = p * a + ub[jb : jb + 1, :]
            return x, a

        zero = jnp.zeros(p.shape, f32)
        x, a = lax.fori_loop(0, chunks, body, (zero, zero))
        xend_ref[:, cols] = x
        head_ref[:, cols] = a


def main_kernel(
    q_ref, k_ref, v_ref, g_ref, p_ref, r_ref, s_ref, b_ref,
    ho_ref, qg_ref, kg_ref, vg_ref, tot_ref,
    mix_ref, up_ref, filt_ref, mg_ref,
):
    f32 = jnp.float32
    mix_ref[...] = (k_ref[...].astype(f32) * v_ref[...].astype(f32)).astype(jnp.bfloat16).astype(f32)
    up_ref[...] = g_ref[...].astype(f32) * q_ref[...].astype(f32)
    rows, width = mix_ref.shape
    chunks = rows // ROWS
    for h in range(width // SUB):
        cols = pl.ds(h * SUB, SUB)
        p = p_ref[:, cols]
        r = r_ref[:, cols]

        def body(c, carry):
            x, tot, a = carry
            fb = pl.multiple_of(c * ROWS, ROWS)
            bb = pl.multiple_of((chunks - 1 - c) * ROWS, ROWS)
            mt = mix_ref[pl.ds(fb, ROWS), cols]
            ut = up_ref[pl.ds(fb, ROWS), cols]
            ub = up_ref[pl.ds(bb, ROWS), cols]
            for j in range(ROWS):
                x = p * x + mt[j : j + 1, :]
                tot = tot + ut[j : j + 1, :] * x
                filt_ref[pl.ds(fb + j, 1), cols] = jnp.sum(r * x, axis=0, keepdims=True)
                jb = ROWS - 1 - j
                a = p * a + ub[jb : jb + 1, :]
                mg_ref[pl.ds(bb + jb, 1), cols] = jnp.sum(r * a, axis=0, keepdims=True)
            return x, tot, a

        zero = jnp.zeros(p.shape, f32)
        _, tot, _ = lax.fori_loop(0, chunks, body, (s_ref[:, cols], zero, b_ref[:, cols]))
        tot_ref[:, cols] = tot
    filt = filt_ref[...]
    mg = mg_ref[...]
    ho_ref[...] = (q_ref[...].astype(f32) * filt).astype(jnp.bfloat16)
    qg_ref[...] = (g_ref[...].astype(f32) * filt).astype(jnp.bfloat16)
    kg_ref[...] = (mg * v_ref[...].astype(f32)).astype(jnp.bfloat16)
    vg_ref[...] = (mg * k_ref[...].astype(f32)).astype(jnp.bfloat16)


def local_carries(query_proj, key_proj, value_proj, out_grad, factor):
    rows, width = query_proj.shape
    modes = factor.shape[0]
    big = pl.BlockSpec((rows, BLOCK), lambda i: (0, i))
    small = pl.BlockSpec((modes, BLOCK), lambda i: (0, i))
    return pl.pallas_call(
        carry_kernel,
        grid=(width // BLOCK,),
        in_specs=[big, big, big, big, small],
        out_specs=[small, small],
        out_shape=[jax.ShapeDtypeStruct((modes, width), jnp.float32)] * 2,
        scratch_shapes=[pltpu.VMEM((rows, BLOCK), jnp.float32)] * 2,
    )(query_proj, key_proj, value_proj, out_grad, factor)


def full_scans(query_proj, key_proj, value_proj, out_grad, factor, weight, state_in, adjoint_in):
    rows, width = query_proj.shape
    modes = factor.shape[0]
    big = pl.BlockSpec((rows, BLOCK), lambda i: (0, i))
    small = pl.BlockSpec((modes, BLOCK), lambda i: (0, i))
    out_big = jax.ShapeDtypeStruct((rows, width), jnp.bfloat16)
    return pl.pallas_call(
        main_kernel,
        grid=(width // BLOCK,),
        in_specs=[big, big, big, big, small, small, small, small],
        out_specs=[big, big, big, big, small],
        out_shape=[out_big] * 4 + [jax.ShapeDtypeStruct((modes, width), jnp.float32)],
        scratch_shapes=[pltpu.VMEM((rows, BLOCK), jnp.float32)] * 4,
    )(query_proj, key_proj, value_proj, out_grad, factor, weight, state_in, adjoint_in)


def make_on_device(count):
    def on_device(query_proj, key_proj, value_proj, out_grad, decay_rate, residue, group_of):
        high = lax.Precision.HIGHEST
        rows = query_proj.shape[0]
        group_count = decay_rate.shape[0]
        rate = jnp.take(decay_rate, group_of, axis=0).T
        weight = jnp.take(residue, group_of, axis=0).T
        factor = jnp.exp(-rate)
        end_state, head_adjoint = local_carries(query_proj, key_proj, value_proj, out_grad, factor)

        def span(blocks):
            return jnp.exp(-rate * float(rows * blocks))

        fwd_all = end_state
        bwd_all = head_adjoint
        state_in = jnp.zeros_like(end_state)
        adjoint_in = jnp.zeros_like(head_adjoint)
        shift = 1
        while shift < count:
            ahead = [(i, i + shift) for i in range(count - shift)]
            behind = [(i + shift, i) for i in range(count - shift)]
            got_fwd = lax.ppermute(fwd_all, "ctx", ahead)
            got_bwd = lax.ppermute(bwd_all, "ctx", behind)
            inner = span(shift - 1)
            outer = span(shift)
            state_in = state_in + inner * got_fwd
            adjoint_in = adjoint_in + inner * got_bwd
            fwd_all = fwd_all + outer * got_fwd
            bwd_all = bwd_all + outer * got_bwd
            shift *= 2

        hyena_out, query_grad, key_grad, value_grad, total = full_scans(
            query_proj, key_proj, value_proj, out_grad, factor, weight, state_in, adjoint_in
        )
        member = (group_of[:, None] == jnp.arange(group_count, dtype=jnp.int32)[None, :]).astype(
            jnp.float32
        )
        local_grad = jnp.dot(total, member, precision=high)
        filter_grad = lax.psum(local_grad, "ctx").T
        filter_update = filter_grad / jnp.sqrt(jnp.mean(filter_grad * filter_grad) + 1e-06)
        return (hyena_out, query_grad, key_grad, value_grad, filter_update)

    return on_device


def solution(mesh):
    placed = (
        P(("groups", "ctx"), None),
        P(("groups", "ctx"), None),
        P(("groups", "ctx"), None),
        P(("groups", "ctx"), None),
        P(),
        P(),
        P(),
    )
    return jax.shard_map(
        make_on_device(mesh.shape["ctx"]),
        mesh=mesh,
        in_specs=placed,
        out_specs=(
            P(("groups", "ctx"), None),
            P(("groups", "ctx"), None),
            P(("groups", "ctx"), None),
            P(("groups", "ctx"), None),
            P("groups", None),
        ),
        check_vma=False,
    )
```

time: 493 us -> 190 us (0.39); the launches traced: 484 us -> 189 us
  local copies, waits for them, and re-layouts: 144 us -> 24.3 us
  matrix products: 121 us -> 2.38 us
  blocking collectives: 153 us -> 62.8 us
  other arithmetic: 49.6 us -> 5.92 us
  waiting for transfers between devices: 0.04 us -> 34.3 us
  Pallas kernels: 0 us -> 31 us
  starting transfers between devices: 0.08 us -> 26.7 us
  between operations: 15.6 us -> 1.46 us
    dot_general x9 -> x1, matrix products: 121 us -> 2.38 us  [on_device(): local_grad = jnp.dot(total, member, precision=high)]
    psum x1, blocking collectives: 127 us -> 62.8 us  [on_device(): filter_grad = lax.psum(local_grad, 'ctx').T]
    gather x4, local copies, waits for them, and re-layouts: 58.9 us -> 22.7 us  [the longest x2 11.3 us: on_device(): rate = jnp.take(decay_rate, group_of, axis=0).T]
    ppermute x0 -> x8, waiting for transfers between devices: none -> 34.3 us  [the longest x4 25.7 us: on_device(): got_bwd = lax.ppermute(bwd_all, 'ctx', behind)]
    reshape x19 -> x0, local copies, waits for them, and re-layouts: 34.1 us -> none  [the longest x15 23.4 us: chain_decays(): widened = jnp.repeat(later[0], per_group, axis=1)]
    pallas_call x0 -> x2, Pallas kernels: none -> 31 us  [the longest x1 23.5 us: full_scans(): pl.pallas_call(main_kernel, grid=(width // BLOCK,), in_specs=[big, big, b...]
    ppermute x0 -> x8, starting transfers between devices: none -> 26.7 us  [the longest x4 21.4 us: on_device(): got_fwd = lax.ppermute(fwd_all, 'ctx', ahead)]
    all_gather x1 -> x0, blocking collectives: 25.9 us -> none  [carried_in(): gathered = jax.tree.map(lambda a: lax.all_gather(a, axis), part)]
  transfers between devices with their start and end apart: 2 -> 8, of which waited for: 0 -> 6; matrix products, arithmetic and copies ran while one was open for 27% -> 0% of each run, Pallas kernels for 0% -> 0%
where the time goes in v1:
time: 190 us; the launch traced here: 189 us
  blocking collectives  62.8 us (33%)
  waiting for transfers between devices  34.3 us (18%)
  Pallas kernels  31 us (16%)
  starting transfers between devices  26.7 us (14%)
  local copies, waits for them, and re-layouts  24.3 us (13%)
  other arithmetic  5.92 us (3%)
  matrix products  2.38 us (1%)
    psum x1, blocking collectives, on_device(): filter_grad = lax.psum(local_grad, 'ctx').T  62.8 us
    ppermute x4, waiting for transfers between devices, on_device(): got_bwd = lax.ppermute(bwd_all, 'ctx', behind)  25.7 us
    pallas_call x1, Pallas kernels, full_scans(): pl.pallas_call(main_kernel, grid=(width // BLOCK,), in_specs=[big, big, b...  23.5 us
    ppermute x4, starting transfers between devices, on_device(): got_fwd = lax.ppermute(fwd_all, 'ctx', ahead)  21.4 us
    gather x2, local copies, waits for them, and re-layouts, on_device(): rate = jnp.take(decay_rate, group_of, axis=0).T  11.3 us
    gather x2, local copies, waits for them, and re-layouts, on_device(): weight = jnp.take(residue, group_of, axis=0).T  11.3 us
    ppermute x4, waiting for transfers between devices, on_device(): got_fwd = lax.ppermute(fwd_all, 'ctx', ahead)  8.6 us
    pallas_call x1, Pallas kernels, local_carries(): pl.pallas_call(carry_kernel, grid=(width // BLOCK,), in_specs=[big, big,...  7.56 us
  transfers between devices with their start and end apart: 8, of which 6 were waited for; matrix products, arithmetic and copies ran while one was open for 0% of the time, Pallas kernels for 0%

profile of v1, /device:TPU:0, one launch (start us, length us, event | category | flops | bytes accessed | tf_op | source)
XLA Modules:
  0.0 188.9 jit_solution(16960345641018554348)
XLA Ops:
  0.6 0.7 compare_and_fusion
  1.4 0.7 fusion.14
  2.1 0.8 copy.12
  2.9 0.8 copy.14
  3.7 10.8 %gather_fusion.1 = f32[4096,16]{1,0:T(8,128)S(1)} fusion(f32[256,16]{1,0:T(8,128)S(1)} %copy.14, s32[4096]{0:T(1024)S(1)} %fusion.14), kind=kCustom, calls=%fused_computation.1.clone | custom fusion | bytes 540672 | tf_op jit(solution)/shard_map/jit(_take)/gather | solution.py:120
  14.5 0.6 copy.15
  15.1 10.8 %gather_fusion = f32[4096,16]{1,0:T(8,128)S(1)} fusion(f32[256,16]{1,0:T(8,128)S(1)} %copy.12, s32[4096]{0:T(1024)S(1)} %fusion.14), kind=kCustom, calls=%fused_computation.clone | custom fusion | bytes 540672 | tf_op jit(solution)/shard_map/jit(_take)/gather | solution.py:119
  25.8 0.6 copy.13
  26.4 0.9 select_bitcast_fusion
  27.3 7.6 %shard_map.110 = (f32[16,4096]{1,0:T(8,128)}, f32[16,4096]{1,0:T(8,128)}) custom-call(bf16[128,4096]{1,0:T(8,128)(2,1)} %q_ref.3, bf16[128,4096]{1,0:T(8,128)(2,1)} %k_ref.3, bf16[128,4096]{1,0:T(8,128)(2,1)} %v_ref.3, bf16[128,4096]{1,0:T(8,128)(2,1)} %g_ref.3, f32[16,4096]{1,0:T(8,128)} %get-tuple-element.25.p_ref), custom_call_target="tpu_custom_call" | custom-call | tf_op jit(solution)/shard_map/pallas_call | solution.py:88
  34.8 0.0 copy-start
  34.8 1.4 collective-permute-start.4
  36.3 2.3 %collective-permute-done.4 = f32[16,4096]{1,0:T(8,128)S(1)} collective-permute-done((f32[16,4096]{1,0:T(8,128)}, f32[16,4096]{1,0:T(8,128)S(1)}, u32[]{:S(2)}, u32[]{:S(2)}) %collective-permute-start.4) | collective-permute-done | bytes 262176 | tf_op jit(solution)/shard_map/ppermute | solution.py:136
  38.6 1.0 fusion.12
  39.6 1.3 collective-permute-start.5
  40.9 7.5 %collective-permute-start = (f32[16,4096]{1,0:T(8,128)}, f32[16,4096]{1,0:T(8,128)S(1)}, u32[]{:S(2)}, u32[]{:S(2)}) collective-permute-start(f32[16,4096]{1,0:T(8,128)} %get-tuple-element.13), channel_id=1, source_target_pairs={{0,1},{1,2},{2,3},{3,4},{4,5},{5,6},{6,7},{7,8},{8,9},{9,10},{10,1... | collective-permute-start | bytes 786440 | tf_op jit(solution)/shard_map/ppermute | solution.py:135
  48.5 3.8 %collective-permute-done.5 = f32[16,4096]{1,0:T(8,128)S(1)} collective-permute-done((f32[16,4096]{1,0:T(8,128)S(1)}, f32[16,4096]{1,0:T(8,128)S(1)}, u32[]{:S(2)}, u32[]{:S(2)}) %collective-permute-start.5) | collective-permute-done | bytes 262176 | tf_op jit(solution)/shard_map/ppermute | solution.py:136
  52.2 0.1 fusion.7
  52.3 1.3 collective-permute-start.6
  53.6 0.0 collective-permute-done
  53.6 14.5 %collective-permute-done.6 = f32[16,4096]{1,0:T(8,128)S(1)} collective-permute-done((f32[16,4096]{1,0:T(8,128)S(1)}, f32[16,4096]{1,0:T(8,128)S(1)}, u32[]{:S(2)}, u32[]{:S(2)}) %collective-permute-start.6) | collective-permute-done | bytes 262176 | tf_op jit(solution)/shard_map/ppermute | solution.py:136
  68.1 0.0 copy-done
  68.1 0.1 fusion.3
  68.2 1.8 collective-permute-start.1
  70.0 5.7 %collective-permute-done.1 = f32[16,4096]{1,0:T(8,128)S(1)} collective-permute-done((f32[16,4096]{1,0:T(8,128)S(1)}, f32[16,4096]{1,0:T(8,128)S(1)}, u32[]{:S(2)}, u32[]{:S(2)}) %collective-permute-start.1) | collective-permute-done | bytes 262176 | tf_op jit(solution)/shard_map/ppermute | solution.py:135
  75.7 0.1 fusion.6
  75.7 6.7 %collective-permute-start.2 = (f32[16,4096]{1,0:T(8,128)S(1)}, f32[16,4096]{1,0:T(8,128)S(1)}, u32[]{:S(2)}, u32[]{:S(2)}) collective-permute-start(f32[16,4096]{1,0:T(8,128)S(1)} %fusion.6), channel_id=1, source_target_pairs={{0,4},{1,5},{2,6},{3,7},{4,8},{5,9},{6,10},{7,11},{8,12},{9,13},{1... | collective-permute-start | bytes 786440 | tf_op jit(solution)/shard_map/ppermute | solution.py:135
  82.4 1.3 collective-permute-start.7
  83.7 2.9 %collective-permute-done.2 = f32[16,4096]{1,0:T(8,128)S(1)} collective-permute-done((f32[16,4096]{1,0:T(8,128)S(1)}, f32[16,4096]{1,0:T(8,128)S(1)}, u32[]{:S(2)}, u32[]{:S(2)}) %collective-permute-start.2) | collective-permute-done | bytes 262176 | tf_op jit(solution)/shard_map/ppermute | solution.py:135
  86.6 0.1 fusion.2
  86.7 5.4 %collective-permute-start.3 = (f32[16,4096]{1,0:T(8,128)S(1)}, f32[16,4096]{1,0:T(8,128)S(1)}, u32[]{:S(2)}, u32[]{:S(2)}) collective-permute-start(f32[16,4096]{1,0:T(8,128)S(1)} %fusion.2), channel_id=1, source_target_pairs={{0,8},{1,9},{2,10},{3,11},{4,12},{5,13},{6,14},{7,15},{16,24},{17,... | collective-permute-start | bytes 786440 | tf_op jit(solution)/shard_map/ppermute | solution.py:135
  92.1 5.1 %collective-permute-done.7 = f32[16,4096]{1,0:T(8,128)S(1)} collective-permute-done((f32[16,4096]{1,0:T(8,128)S(1)}, f32[16,4096]{1,0:T(8,128)S(1)}, u32[]{:S(2)}, u32[]{:S(2)}) %collective-permute-start.7) | collective-permute-done | bytes 262176 | tf_op jit(solution)/shard_map/ppermute | solution.py:136
  97.3 0.0 collective-permute-done.3
  97.3 1.0 fusion.5
  98.3 0.0 copy-start.1
  98.3 23.5 %shard_map.111 = (bf16[128,4096]{1,0:T(8,128)(2,1)}, bf16[128,4096]{1,0:T(8,128)(2,1)}, bf16[128,4096]{1,0:T(8,128)(2,1)}, bf16[128,4096]{1,0:T(8,128)(2,1)}, f32[16,4096]{1,0:T(8,128)}) custom-call(bf16[128,4096]{1,0:T(8,128)(2,1)} %q_ref.3, bf16[128,4096]{1,0:T(8,128)(2,1)} %k_ref.3, bf16[128,4096]{1,0:T(8,128)(2,1)} %v_ref.3, bf16[128,4096]{1,0:T(8,128)(2,1)} %g_ref.3, ...), custom_call_target="tpu_custom_call" | custom-call | tf_op jit(solution)/shard_map/pallas_call | solution.py:104
  121.8 0.0 copy-done.1
  121.8 2.4 %fusion = f32[16,256]{1,0:T(8,128)S(1)} fusion(f32[16,4096]{1,0:T(8,128)} %get-tuple-element.19, s32[4096]{0:T(1024)S(1)} %copy-done.1), kind=kOutput, calls=%fused_computation.3 | convolution fusion | flops 202375168 | bytes 294912 | tf_op jit(solution)/shard_map/dot_general | solution.py:151
  124.2 62.8 %psum.7 = f32[16,256]{1,0:T(8,128)S(1)} all-reduce(f32[16,256]{1,0:T(8,128)S(1)} %fusion), channel_id=1, replica_groups=mesh['groups'=2,'ctx'=16] {'ctx'}, use_global_device_ids=true, to_apply=%region_0.0 | all-reduce | flops 4096 | bytes 32768 | tf_op jit(solution)/shard_map/psum | solution.py:152
  187.0 0.6 multiply_reduce_fusion
  188.3 0.6 divide_bitcast_fusion
Async XLA Ops:
  34.8 33.3 %copy-start = (f32[16,4096]{1,0:T(8,128)S(1)}, f32[16,4096]{1,0:T(8,128)}, u32[]{:S(2)}) copy-start(f32[16,4096]{1,0:T(8,128)} %get-tuple-element.13) | copy-start | bytes 786436
  34.8 3.8 %collective-permute-start.4 = (f32[16,4096]{1,0:T(8,128)}, f32[16,4096]{1,0:T(8,128)S(1)}, u32[]{:S(2)}, u32[]{:S(2)}) collective-permute-start(f32[16,4096]{1,0:T(8,128)} %get-tuple-element.14), channel_id=1, source_target_pairs={{1,0},{2,1},{3,2},{4,3},{5,4},{6,5},{7,6},{8,7},{9,8},{10,9},{11,1... | collective-permute-start | bytes 786440 | tf_op jit(solution)/shard_map/ppermute | solution.py:136
  39.6 12.6 %collective-permute-start.5 = (f32[16,4096]{1,0:T(8,128)S(1)}, f32[16,4096]{1,0:T(8,128)S(1)}, u32[]{:S(2)}, u32[]{:S(2)}) collective-permute-start(f32[16,4096]{1,0:T(8,128)S(1)} %fusion.12), channel_id=1, source_target_pairs={{2,0},{3,1},{4,2},{5,3},{6,4},{7,5},{8,6},{9,7},{10,8},{11,9},{12,... | collective-permute-start | bytes 786440 | tf_op jit(solution)/shard_map/ppermute | solution.py:136
  40.9 12.7 %collective-permute-start = (f32[16,4096]{1,0:T(8,128)}, f32[16,4096]{1,0:T(8,128)S(1)}, u32[]{:S(2)}, u32[]{:S(2)}) collective-permute-start(f32[16,4096]{1,0:T(8,128)} %get-tuple-element.13), channel_id=1, source_target_pairs={{0,1},{1,2},{2,3},{3,4},{4,5},{5,6},{6,7},{7,8},{8,9},{9,10},{10,1... | collective-permute-start | bytes 786440 | tf_op jit(solution)/shard_map/ppermute | solution.py:135
  52.3 15.8 %collective-permute-start.6 = (f32[16,4096]{1,0:T(8,128)S(1)}, f32[16,4096]{1,0:T(8,128)S(1)}, u32[]{:S(2)}, u32[]{:S(2)}) collective-permute-start(f32[16,4096]{1,0:T(8,128)S(1)} %fusion.7), channel_id=1, source_target_pairs={{4,0},{5,1},{6,2},{7,3},{8,4},{9,5},{10,6},{11,7},{12,8},{13,9},{1... | collective-permute-start | bytes 786440 | tf_op jit(solution)/shard_map/ppermute | solution.py:136
  68.2 7.4 %collective-permute-start.1 = (f32[16,4096]{1,0:T(8,128)S(1)}, f32[16,4096]{1,0:T(8,128)S(1)}, u32[]{:S(2)}, u32[]{:S(2)}) collective-permute-start(f32[16,4096]{1,0:T(8,128)S(1)} %get-tuple-element.23), channel_id=1, source_target_pairs={{0,2},{1,3},{2,4},{3,5},{4,6},{5,7},{6,8},{7,9},{8,10},{9,11},{10,... | collective-permute-start | bytes 786440 | tf_op jit(solution)/shard_map/ppermute | solution.py:135
  75.7 10.9 %collective-permute-start.2 = (f32[16,4096]{1,0:T(8,128)S(1)}, f32[16,4096]{1,0:T(8,128)S(1)}, u32[]{:S(2)}, u32[]{:S(2)}) collective-permute-start(f32[16,4096]{1,0:T(8,128)S(1)} %fusion.6), channel_id=1, source_target_pairs={{0,4},{1,5},{2,6},{3,7},{4,8},{5,9},{6,10},{7,11},{8,12},{9,13},{1... | collective-permute-start | bytes 786440 | tf_op jit(solution)/shard_map/ppermute | solution.py:135
  82.4 14.9 %collective-permute-start.7 = (f32[16,4096]{1,0:T(8,128)S(1)}, f32[16,4096]{1,0:T(8,128)S(1)}, u32[]{:S(2)}, u32[]{:S(2)}) collective-permute-start(f32[16,4096]{1,0:T(8,128)S(1)} %get-tuple-element.22), channel_id=1, source_target_pairs={{8,0},{9,1},{10,2},{11,3},{12,4},{13,5},{14,6},{15,7},{24,16},{25,... | collective-permute-start | bytes 786440 | tf_op jit(solution)/shard_map/ppermute | solution.py:136
  86.7 10.6 %collective-permute-start.3 = (f32[16,4096]{1,0:T(8,128)S(1)}, f32[16,4096]{1,0:T(8,128)S(1)}, u32[]{:S(2)}, u32[]{:S(2)}) collective-permute-start(f32[16,4096]{1,0:T(8,128)S(1)} %fusion.2), channel_id=1, source_target_pairs={{0,8},{1,9},{2,10},{3,11},{4,12},{5,13},{6,14},{7,15},{16,24},{17,... | collective-permute-start | bytes 786440 | tf_op jit(solution)/shard_map/ppermute | solution.py:135
  98.3 23.5 %copy-start.1 = (s32[4096]{0:T(1024)S(1)}, s32[4096]{0:T(1024)}, u32[]{:S(2)}) copy-start(s32[4096]{0:T(1024)} %param.15) | copy-start | bytes 49156

commit v2 on v1

--- a/solution.py
+++ b/solution.py
@@ -10,7 +10,7 @@
 ROWS = 8
 
 
-def carry_kernel(q_ref, k_ref, v_ref, g_ref, p_ref, xend_ref, head_ref, mix_ref, up_ref):
+def carry_kernel(q_ref, k_ref, v_ref, g_ref, p_ref, xend_ref, head_ref, tot_ref, mix_ref, up_ref):
     f32 = jnp.float32
     mix_ref[...] = (k_ref[...].astype(f32) * v_ref[...].astype(f32)).astype(jnp.bfloat16).astype(f32)
     up_ref[...] = g_ref[...].astype(f32) * q_ref[...].astype(f32)
@@ -21,26 +21,29 @@
         p = p_ref[:, cols]
 
         def body(c, carry):
-            x, a = carry
+            x, tot, a = carry
             fb = pl.multiple_of(c * ROWS, ROWS)
             bb = pl.multiple_of((chunks - 1 - c) * ROWS, ROWS)
             mt = mix_ref[pl.ds(fb, ROWS), cols]
+            ut = up_ref[pl.ds(fb, ROWS), cols]
             ub = up_ref[pl.ds(bb, ROWS), cols]
             for j in range(ROWS):
                 x = p * x + mt[j : j + 1, :]
+                tot = tot + ut[j : j + 1, :] * x
                 jb = ROWS - 1 - j
                 a = p * a + ub[jb : jb + 1, :]
-            return x, a
+            return x, tot, a
 
         zero = jnp.zeros(p.shape, f32)
-        x, a = lax.fori_loop(0, chunks, body, (zero, zero))
+        x, tot, a = lax.fori_loop(0, chunks, body, (zero, zero, zero))
         xend_ref[:, cols] = x
         head_ref[:, cols] = a
+        tot_ref[:, cols] = tot
 
 
 def main_kernel(
     q_ref, k_ref, v_ref, g_ref, p_ref, r_ref, s_ref, b_ref,
-    ho_ref, qg_ref, kg_ref, vg_ref, tot_ref,
+    ho_ref, qg_ref, kg_ref, vg_ref,
     mix_ref, up_ref, filt_ref, mg_ref,
 ):
     f32 = jnp.float32
@@ -54,24 +57,20 @@
         r = r_ref[:, cols]
 
         def body(c, carry):
-            x, tot, a = carry
+            x, a = carry
             fb = pl.multiple_of(c * ROWS, ROWS)
             bb = pl.multiple_of((chunks - 1 - c) * ROWS, ROWS)
             mt = mix_ref[pl.ds(fb, ROWS), cols]
-            ut = up_ref[pl.ds(fb, ROWS), cols]
             ub = up_ref[pl.ds(bb, ROWS), cols]
             for j in range(ROWS):
                 x = p * x + mt[j : j + 1, :]
-                tot = tot + ut[j : j + 1, :] * x
                 filt_ref[pl.ds(fb + j, 1), cols] = jnp.sum(r * x, axis=0, keepdims=True)
                 jb = ROWS - 1 - j
                 a = p * a + ub[jb : jb + 1, :]
                 mg_ref[pl.ds(bb + jb, 1), cols] = jnp.sum(r * a, axis=0, keepdims=True)
-            return x, tot, a
+            return x, a
 
-        zero = jnp.zeros(p.shape, f32)
-        _, tot, _ = lax.fori_loop(0, chunks, body, (s_ref[:, cols], zero, b_ref[:, cols]))
-        tot_ref[:, cols] = tot
+        lax.fori_loop(0, chunks, body, (s_ref[:, cols], b_ref[:, cols]))
     filt = filt_ref[...]
     mg = mg_ref[...]
     ho_ref[...] = (q_ref[...].astype(f32) * filt).astype(jnp.bfloat16)
@@ -89,8 +88,8 @@
         carry_kernel,
         grid=(width // BLOCK,),
         in_specs=[big, big, big, big, small],
-        out_specs=[small, small],
-        out_shape=[jax.ShapeDtypeStruct((modes, width), jnp.float32)] * 2,
+        out_specs=[small, small, small],
+        out_shape=[jax.ShapeDtypeStruct((modes, width), jnp.float32)] * 3,
         scratch_shapes=[pltpu.VMEM((rows, BLOCK), jnp.float32)] * 2,
     )(query_proj, key_proj, value_proj, out_grad, factor)
 
@@ -105,8 +104,8 @@
         main_kernel,
         grid=(width // BLOCK,),
         in_specs=[big, big, big, big, small, small, small, small],
-        out_specs=[big, big, big, big, small],
-        out_shape=[out_big] * 4 + [jax.ShapeDtypeStruct((modes, width), jnp.float32)],
+        out_specs=[big, big, big, big],
+        out_shape=[out_big] * 4,
         scratch_shapes=[pltpu.VMEM((rows, BLOCK), jnp.float32)] * 4,
     )(query_proj, key_proj, value_proj, out_grad, factor, weight, state_in, adjoint_in)
 
@@ -116,10 +115,15 @@
         high = lax.Precision.HIGHEST
         rows = query_proj.shape[0]
         group_count = decay_rate.shape[0]
-        rate = jnp.take(decay_rate, group_of, axis=0).T
-        weight = jnp.take(residue, group_of, axis=0).T
+        member = (group_of[None, :] == jnp.arange(group_count, dtype=jnp.int32)[:, None]).astype(
+            jnp.float32
+        )
+        rate = jnp.dot(decay_rate.T, member, precision=high)
+        weight = jnp.dot(residue.T, member, precision=high)
         factor = jnp.exp(-rate)
-        end_state, head_adjoint = local_carries(query_proj, key_proj, value_proj, out_grad, factor)
+        end_state, head_adjoint, local_total = local_carries(
+            query_proj, key_proj, value_proj, out_grad, factor
+        )
 
         def span(blocks):
             return jnp.exp(-rate * float(rows * blocks))
@@ -134,6 +138,7 @@
             behind = [(i + shift, i) for i in range(count - shift)]
             got_fwd = lax.ppermute(fwd_all, "ctx", ahead)
             got_bwd = lax.ppermute(bwd_all, "ctx", behind)
+            got_fwd, got_bwd = lax.optimization_barrier((got_fwd, got_bwd))
             inner = span(shift - 1)
             outer = span(shift)
             state_in = state_in + inner * got_fwd
@@ -142,14 +147,13 @@
             bwd_all = bwd_all + outer * got_bwd
             shift *= 2
 
-        hyena_out, query_grad, key_grad, value_grad, total = full_scans(
+        total = local_total + state_in * factor * head_adjoint
+        local_grad = jnp.dot(total, member.T, precision=high)
+        gathered = lax.all_gather(local_grad, "ctx")
+        hyena_out, query_grad, key_grad, value_grad = full_scans(
             query_proj, key_proj, value_proj, out_grad, factor, weight, state_in, adjoint_in
         )
-        member = (group_of[:, None] == jnp.arange(group_count, dtype=jnp.int32)[None, :]).astype(
-            jnp.float32
-        )
-        local_grad = jnp.dot(total, member, precision=high)
-        filter_grad = lax.psum(local_grad, "ctx").T
+        filter_grad = jnp.sum(gathered, axis=0).T
         filter_update = filter_grad / jnp.sqrt(jnp.mean(filter_grad * filter_grad) + 1e-06)
         return (hyena_out, query_grad, key_grad, value_grad, filter_update)
 

time: 190 us -> 122 us (0.64)
  blocking collectives: 62.8 us -> 24.3 us
  local copies, waits for them, and re-layouts: 24.3 us -> 1.49 us
  waiting for transfers between devices: 34.3 us -> 28.7 us
  matrix products: 2.38 us -> 6.22 us
  other arithmetic: 5.92 us -> 3.43 us
    psum x1 -> x0, blocking collectives: 62.8 us -> none  [on_device(): filter_grad = lax.psum(local_grad, 'ctx').T]
    all_gather x0 -> x1, blocking collectives: none -> 24.3 us  [on_device(): gathered = lax.all_gather(local_grad, 'ctx')]
    gather x4 -> x0, local copies, waits for them, and re-layouts: 22.7 us -> none  [the longest x2 11.3 us: on_device(): rate = jnp.take(decay_rate, group_of, axis=0).T]
    ppermute x4, waiting for transfers between devices: 25.7 us -> 19.5 us  [on_device(): got_bwd = lax.ppermute(bwd_all, 'ctx', behind)]
    dot_general x1 -> x3, matrix products: 2.38 us -> 6.22 us  [the longest x1 2.12 us: on_device(): rate = jnp.dot(decay_rate.T, member, precision=high)]
    pallas_call x1, Pallas kernels: 23.5 us -> 21.1 us  [full_scans(): pl.pallas_call(main_kernel, grid=(width // BLOCK,), in_specs=[big, big, b...]
    pallas_call x1, Pallas kernels: 7.56 us -> 9.95 us  [local_carries(): pl.pallas_call(carry_kernel, grid=(width // BLOCK,), in_specs=[big, big,...]
  transfers between devices with their start and end apart: 8 -> 8, of which waited for: 6 -> 6; matrix products, arithmetic and copies ran while one was open for 0% -> 2% of each run, Pallas kernels for 0% -> 0%
where the time goes in v2:
time: 122 us
  Pallas kernels  31 us (25%)
  waiting for transfers between devices  28.7 us (24%)
  starting transfers between devices  25 us (20%)
  blocking collectives  24.3 us (20%)
  matrix products  6.22 us (5%)
  other arithmetic  3.43 us (3%)
  local copies, waits for them, and re-layouts  1.49 us (1%)
  between operations  1.45 us (1%)
    all_gather x1, blocking collectives, on_device(): gathered = lax.all_gather(local_grad, 'ctx')  24.3 us
    pallas_call x1, Pallas kernels, full_scans(): pl.pallas_call(main_kernel, grid=(width // BLOCK,), in_specs=[big, big, b...  21.1 us
    ppermute x4, starting transfers between devices, on_device(): got_fwd = lax.ppermute(fwd_all, 'ctx', ahead)  19.8 us
    ppermute x4, waiting for transfers between devices, on_device(): got_bwd = lax.ppermute(bwd_all, 'ctx', behind)  19.5 us
    pallas_call x1, Pallas kernels, local_carries(): pl.pallas_call(carry_kernel, grid=(width // BLOCK,), in_specs=[big, big,...  9.95 us
    ppermute x4, waiting for transfers between devices, on_device(): got_fwd = lax.ppermute(fwd_all, 'ctx', ahead)  9.14 us
    ppermute x4, starting transfers between devices, on_device(): got_bwd = lax.ppermute(bwd_all, 'ctx', behind)  5.17 us
  transfers between devices with their start and end apart: 8, of which 6 were waited for; matrix products, arithmetic and copies ran while one was open for 2% of the time, Pallas kernels for 0%

profile of v2, /device:TPU:0, one launch (start us, length us, event | category | flops | bytes accessed | tf_op | source)
XLA Modules:
  0.0 121.6 jit_solution(7235719885890807965)
XLA Ops:
  0.6 0.0 copy-start
  0.6 0.7 copy-done
  1.4 2.1 %convolution_negate_fusion = f32[4096,16]{0,1:T(8,128)S(1)} fusion(f32[256,16]{0,1:T(8,128)S(1)} %copy-done, s32[4096]{0:T(1024)} %param.13), kind=kOutput, calls=%fused_computation.1 | convolution fusion | flops 202440704 | bytes 294912 | tf_op jit(solution)/shard_map/dot_general | solution.py:121
  3.5 0.7 exponential_bitcast_fusion.p_ref
  4.2 9.9 %shard_map.110 = (f32[16,4096]{1,0:T(8,128)}, f32[16,4096]{1,0:T(8,128)}, f32[16,4096]{1,0:T(8,128)}) custom-call(bf16[128,4096]{1,0:T(8,128)(2,1)} %q_ref.3, bf16[128,4096]{1,0:T(8,128)(2,1)} %k_ref.3, bf16[128,4096]{1,0:T(8,128)(2,1)} %v_ref.3, bf16[128,4096]{1,0:T(8,128)(2,1)} %g_ref.3, f32[16,4096]{1,0:T(8,128)} %exponential_bitcast_fusion.p_ref), custom_call_target="tpu_custom_call" | custom-call | tf_op jit(solution)/shard_map/pallas_call | solution.py:87
  14.2 2.4 %collective-permute-start = (f32[16,4096]{1,0:T(8,128)}, f32[16,4096]{1,0:T(8,128)S(1)}, u32[]{:S(2)}, u32[]{:S(2)}) collective-permute-start(f32[16,4096]{1,0:T(8,128)} %get-tuple-element.20), channel_id=1, source_target_pairs={{0,1},{1,2},{2,3},{3,4},{4,5},{5,6},{6,7},{7,8},{8,9},{9,10},{10,1... | collective-permute-start | bytes 786440 | tf_op jit(solution)/shard_map/ppermute | solution.py:139
  16.5 1.3 %collective-permute-start.1 = (f32[16,4096]{1,0:T(8,128)}, f32[16,4096]{1,0:T(8,128)S(1)}, u32[]{:S(2)}, u32[]{:S(2)}) collective-permute-start(f32[16,4096]{1,0:T(8,128)} %get-tuple-element.21), channel_id=1, source_target_pairs={{1,0},{2,1},{3,2},{4,3},{5,4},{6,5},{7,6},{8,7},{9,8},{10,9},{11,1... | collective-permute-start | bytes 786440 | tf_op jit(solution)/shard_map/ppermute | solution.py:140
  17.8 0.0 collective-permute-done
  17.9 4.4 %collective-permute-done.1 = f32[16,4096]{1,0:T(8,128)S(1)} collective-permute-done((f32[16,4096]{1,0:T(8,128)}, f32[16,4096]{1,0:T(8,128)S(1)}, u32[]{:S(2)}, u32[]{:S(2)}) %collective-permute-start.1) | collective-permute-done | bytes 262176 | tf_op jit(solution)/shard_map/ppermute | solution.py:140
  22.3 1.1 fusion.13
  23.4 1.3 %collective-permute-start.3 = (f32[16,4096]{1,0:T(8,128)S(1)}, f32[16,4096]{1,0:T(8,128)S(1)}, u32[]{:S(2)}, u32[]{:S(2)}) collective-permute-start(f32[16,4096]{1,0:T(8,128)S(1)} %get-tuple-element.41), channel_id=1, source_target_pairs={{2,0},{3,1},{4,2},{5,3},{6,4},{7,5},{8,6},{9,7},{10,8},{11,9},{12,... | collective-permute-start | bytes 786440 | tf_op jit(solution)/shard_map/ppermute | solution.py:140
  24.7 7.1 %collective-permute-start.2 = (f32[16,4096]{1,0:T(8,128)S(1)}, f32[16,4096]{1,0:T(8,128)S(1)}, u32[]{:S(2)}, u32[]{:S(2)}) collective-permute-start(f32[16,4096]{1,0:T(8,128)S(1)} %get-tuple-element.42), channel_id=1, source_target_pairs={{0,2},{1,3},{2,4},{3,5},{4,6},{5,7},{6,8},{7,9},{8,10},{9,11},{10,... | collective-permute-start | bytes 786440 | tf_op jit(solution)/shard_map/ppermute | solution.py:139
  31.8 3.2 %collective-permute-done.3 = f32[16,4096]{1,0:T(8,128)S(1)} collective-permute-done((f32[16,4096]{1,0:T(8,128)S(1)}, f32[16,4096]{1,0:T(8,128)S(1)}, u32[]{:S(2)}, u32[]{:S(2)}) %collective-permute-start.3) | collective-permute-done | bytes 262176 | tf_op jit(solution)/shard_map/ppermute | solution.py:140
  35.1 7.9 %collective-permute-done.2 = f32[16,4096]{1,0:T(8,128)S(1)} collective-permute-done((f32[16,4096]{1,0:T(8,128)S(1)}, f32[16,4096]{1,0:T(8,128)S(1)}, u32[]{:S(2)}, u32[]{:S(2)}) %collective-permute-start.2) | collective-permute-done | bytes 262176 | tf_op jit(solution)/shard_map/ppermute | solution.py:139
  43.0 0.1 fusion.9
  43.1 0.0 copy-start.4
  43.1 0.0 copy-start.5
  43.1 1.3 %collective-permute-start.5 = (f32[16,4096]{1,0:T(8,128)S(1)}, f32[16,4096]{1,0:T(8,128)S(1)}, u32[]{:S(2)}, u32[]{:S(2)}) collective-permute-start(f32[16,4096]{1,0:T(8,128)S(1)} %get-tuple-element.39), channel_id=1, source_target_pairs={{4,0},{5,1},{6,2},{7,3},{8,4},{9,5},{10,6},{11,7},{12,8},{13,9},{1... | collective-permute-start | bytes 786440 | tf_op jit(solution)/shard_map/ppermute | solution.py:140
  44.4 4.8 %collective-permute-start.4 = (f32[16,4096]{1,0:T(8,128)S(1)}, f32[16,4096]{1,0:T(8,128)S(1)}, u32[]{:S(2)}, u32[]{:S(2)}) collective-permute-start(f32[16,4096]{1,0:T(8,128)S(1)} %get-tuple-element.40), channel_id=1, source_target_pairs={{0,4},{1,5},{2,6},{3,7},{4,8},{5,9},{6,10},{7,11},{8,12},{9,13},{1... | collective-permute-start | bytes 786440 | tf_op jit(solution)/shard_map/ppermute | solution.py:139
  49.2 4.8 %collective-permute-done.5 = f32[16,4096]{1,0:T(8,128)S(1)} collective-permute-done((f32[16,4096]{1,0:T(8,128)S(1)}, f32[16,4096]{1,0:T(8,128)S(1)}, u32[]{:S(2)}, u32[]{:S(2)}) %collective-permute-start.5) | collective-permute-done | bytes 262176 | tf_op jit(solution)/shard_map/ppermute | solution.py:140
  53.9 1.2 collective-permute-done.4
  55.1 0.1 fusion.5
  55.2 1.3 %collective-permute-start.7 = (f32[16,4096]{1,0:T(8,128)S(1)}, f32[16,4096]{1,0:T(8,128)S(1)}, u32[]{:S(2)}, u32[]{:S(2)}) collective-permute-start(f32[16,4096]{1,0:T(8,128)S(1)} %get-tuple-element.37), channel_id=1, source_target_pairs={{8,0},{9,1},{10,2},{11,3},{12,4},{13,5},{14,6},{15,7},{24,16},{25,... | collective-permute-start | bytes 786440 | tf_op jit(solution)/shard_map/ppermute | solution.py:140
  56.5 5.6 %collective-permute-start.6 = (f32[16,4096]{1,0:T(8,128)S(1)}, f32[16,4096]{1,0:T(8,128)S(1)}, u32[]{:S(2)}, u32[]{:S(2)}) collective-permute-start(f32[16,4096]{1,0:T(8,128)S(1)} %get-tuple-element.38), channel_id=1, source_target_pairs={{0,8},{1,9},{2,10},{3,11},{4,12},{5,13},{6,14},{7,15},{16,24},{17,... | collective-permute-start | bytes 786440 | tf_op jit(solution)/shard_map/ppermute | solution.py:139
  62.1 0.0 copy-done.4
  62.1 0.0 copy-done.5
  62.1 2.1 %convolution_bitcast_fusion.r_ref = f32[16,4096]{1,0:T(8,128)} fusion(f32[256,16]{0,1:T(8,128)S(1)} %copy-done.4, s32[4096]{0:T(1024)S(1)} %copy-done.5), kind=kOutput, calls=%fused_computation | convolution fusion | flops 202375168 | bytes 294912 | tf_op jit(solution)/shard_map/dot_general | solution.py:122
  64.2 0.0 copy-start.2
  64.2 0.0 copy-start.3
  64.2 7.1 %collective-permute-done.7 = f32[16,4096]{1,0:T(8,128)S(1)} collective-permute-done((f32[16,4096]{1,0:T(8,128)S(1)}, f32[16,4096]{1,0:T(8,128)S(1)}, u32[]{:S(2)}, u32[]{:S(2)}) %collective-permute-start.7) | collective-permute-done | bytes 262176 | tf_op jit(solution)/shard_map/ppermute | solution.py:140
  71.3 0.0 collective-permute-done.6
  71.3 0.9 fusion.7
  72.3 0.0 copy-start.1
  72.3 0.0 copy-done.2
  72.3 0.0 copy-done.3
  72.3 2.0 %fusion = f32[16,256]{1,0:T(8,128)S(1)} fusion(s32[4096]{0:T(1024)S(1)} %copy-done.5, f32[16,4096]{1,0:T(8,128)S(1)} %copy-done.3, f32[16,4096]{1,0:T(8,128)S(1)} %copy-done.2, f32[16,4096]{1,0:T(8,128)S(1)} %get-tuple-element.36.s_ref, f32[4096,16]{0,1:T(8,128)S(1)} %convolution_negate_fusion), kind=kOutput, calls=%fused_computation.3 | convolution fusion | flops 202571776 | bytes 1081344 | tf_op jit(solution)/shard_map/dot_general | solution.py:151
  74.3 24.3 %all-gather = f32[256,256]{1,0:T(8,128)S(1)} all-gather(f32[16,256]{1,0:T(8,128)S(1)} %fusion), channel_id=2, replica_groups=mesh['groups'=2,'ctx'=16] {'ctx'}, dimensions={0}, use_global_device_ids=true | all-gather | bytes 278528 | tf_op jit(solution)/shard_map/all_gather | solution.py:152
  98.6 0.6 multiply_reduce_fusion
  99.9 0.6 divide_bitcast_fusion
  100.5 0.0 copy-done.1
  100.6 21.1 %shard_map.111 = (bf16[128,4096]{1,0:T(8,128)(2,1)}, bf16[128,4096]{1,0:T(8,128)(2,1)}, bf16[128,4096]{1,0:T(8,128)(2,1)}, bf16[128,4096]{1,0:T(8,128)(2,1)}) custom-call(bf16[128,4096]{1,0:T(8,128)(2,1)} %q_ref.3, bf16[128,4096]{1,0:T(8,128)(2,1)} %k_ref.3, bf16[128,4096]{1,0:T(8,128)(2,1)} %v_ref.3, bf16[128,4096]{1,0:T(8,128)(2,1)} %g_ref.3, ...), custom_call_target="tpu_custom_call" | custom-call | tf_op jit(solution)/shard_map/pallas_call | solution.py:103
  (1 shorter events, 0.0 us)
Async XLA Ops:
  0.6 0.7 copy-start
  14.2 3.7 %collective-permute-start = (f32[16,4096]{1,0:T(8,128)}, f32[16,4096]{1,0:T(8,128)S(1)}, u32[]{:S(2)}, u32[]{:S(2)}) collective-permute-start(f32[16,4096]{1,0:T(8,128)} %get-tuple-element.20), channel_id=1, source_target_pairs={{0,1},{1,2},{2,3},{3,4},{4,5},{5,6},{6,7},{7,8},{8,9},{9,10},{10,1... | collective-permute-start | bytes 786440 | tf_op jit(solution)/shard_map/ppermute | solution.py:139
  16.5 5.8 %collective-permute-start.1 = (f32[16,4096]{1,0:T(8,128)}, f32[16,4096]{1,0:T(8,128)S(1)}, u32[]{:S(2)}, u32[]{:S(2)}) collective-permute-start(f32[16,4096]{1,0:T(8,128)} %get-tuple-element.21), channel_id=1, source_target_pairs={{1,0},{2,1},{3,2},{4,3},{5,4},{6,5},{7,6},{8,7},{9,8},{10,9},{11,1... | collective-permute-start | bytes 786440 | tf_op jit(solution)/shard_map/ppermute | solution.py:140
  23.4 11.7 %collective-permute-start.3 = (f32[16,4096]{1,0:T(8,128)S(1)}, f32[16,4096]{1,0:T(8,128)S(1)}, u32[]{:S(2)}, u32[]{:S(2)}) collective-permute-start(f32[16,4096]{1,0:T(8,128)S(1)} %get-tuple-element.41), channel_id=1, source_target_pairs={{2,0},{3,1},{4,2},{5,3},{6,4},{7,5},{8,6},{9,7},{10,8},{11,9},{12,... | collective-permute-start | bytes 786440 | tf_op jit(solution)/shard_map/ppermute | solution.py:140
  24.7 18.3 %collective-permute-start.2 = (f32[16,4096]{1,0:T(8,128)S(1)}, f32[16,4096]{1,0:T(8,128)S(1)}, u32[]{:S(2)}, u32[]{:S(2)}) collective-permute-start(f32[16,4096]{1,0:T(8,128)S(1)} %get-tuple-element.42), channel_id=1, source_target_pairs={{0,2},{1,3},{2,4},{3,5},{4,6},{5,7},{6,8},{7,9},{8,10},{9,11},{10,... | collective-permute-start | bytes 786440 | tf_op jit(solution)/shard_map/ppermute | solution.py:139
  43.1 19.0 %copy-start.4 = (f32[256,16]{0,1:T(8,128)S(1)}, f32[256,16]{0,1:T(8,128)}, u32[]{:S(2)}) copy-start(f32[256,16]{0,1:T(8,128)} %param.12) | copy-start | bytes 49156
  43.1 19.0 %copy-start.5 = (s32[4096]{0:T(1024)S(1)}, s32[4096]{0:T(1024)}, u32[]{:S(2)}) copy-start(s32[4096]{0:T(1024)} %param.13) | copy-start | bytes 49156
  43.1 10.8 %collective-permute-start.5 = (f32[16,4096]{1,0:T(8,128)S(1)}, f32[16,4096]{1,0:T(8,128)S(1)}, u32[]{:S(2)}, u32[]{:S(2)}) collective-permute-start(f32[16,4096]{1,0:T(8,128)S(1)} %get-tuple-element.39), channel_id=1, source_target_pairs={{4,0},{5,1},{6,2},{7,3},{8,4},{9,5},{10,6},{11,7},{12,8},{13,9},{1... | collective-permute-start | bytes 786440 | tf_op jit(solution)/shard_map/ppermute | solution.py:140
  44.4 10.7 %collective-permute-start.4 = (f32[16,4096]{1,0:T(8,128)S(1)}, f32[16,4096]{1,0:T(8,128)S(1)}, u32[]{:S(2)}, u32[]{:S(2)}) collective-permute-start(f32[16,4096]{1,0:T(8,128)S(1)} %get-tuple-element.40), channel_id=1, source_target_pairs={{0,4},{1,5},{2,6},{3,7},{4,8},{5,9},{6,10},{7,11},{8,12},{9,13},{1... | collective-permute-start | bytes 786440 | tf_op jit(solution)/shard_map/ppermute | solution.py:139
  55.2 16.1 %collective-permute-start.7 = (f32[16,4096]{1,0:T(8,128)S(1)}, f32[16,4096]{1,0:T(8,128)S(1)}, u32[]{:S(2)}, u32[]{:S(2)}) collective-permute-start(f32[16,4096]{1,0:T(8,128)S(1)} %get-tuple-element.37), channel_id=1, source_target_pairs={{8,0},{9,1},{10,2},{11,3},{12,4},{13,5},{14,6},{15,7},{24,16},{25,... | collective-permute-start | bytes 786440 | tf_op jit(solution)/shard_map/ppermute | solution.py:140
  56.5 14.8 %collective-permute-start.6 = (f32[16,4096]{1,0:T(8,128)S(1)}, f32[16,4096]{1,0:T(8,128)S(1)}, u32[]{:S(2)}, u32[]{:S(2)}) collective-permute-start(f32[16,4096]{1,0:T(8,128)S(1)} %get-tuple-element.38), channel_id=1, source_target_pairs={{0,8},{1,9},{2,10},{3,11},{4,12},{5,13},{6,14},{7,15},{16,24},{17,... | collective-permute-start | bytes 786440 | tf_op jit(solution)/shard_map/ppermute | solution.py:139
  64.2 8.1 %copy-start.2 = (f32[16,4096]{1,0:T(8,128)S(1)}, f32[16,4096]{1,0:T(8,128)}, u32[]{:S(2)}) copy-start(f32[16,4096]{1,0:T(8,128)} %get-tuple-element.21) | copy-start | bytes 786436
  64.2 8.1 %copy-start.3 = (f32[16,4096]{1,0:T(8,128)S(1)}, f32[16,4096]{1,0:T(8,128)}, u32[]{:S(2)}) copy-start(f32[16,4096]{1,0:T(8,128)} %get-tuple-element.34) | copy-start | bytes 786436
  72.3 28.3 %copy-start.1 = (f32[16,4096]{1,0:T(8,128)}, f32[16,4096]{1,0:T(8,128)S(1)}, u32[]{:S(2)}) copy-start(f32[16,4096]{1,0:T(8,128)S(1)} %get-tuple-element.36.s_ref) | copy-start | bytes 786436

commit v3 on v2

--- a/solution.py
+++ b/solution.py
@@ -147,13 +147,11 @@
             bwd_all = bwd_all + outer * got_bwd
             shift *= 2
 
-        total = local_total + state_in * factor * head_adjoint
-        local_grad = jnp.dot(total, member.T, precision=high)
-        gathered = lax.all_gather(local_grad, "ctx")
+        total = lax.psum(local_total + state_in * factor * head_adjoint, "ctx")
         hyena_out, query_grad, key_grad, value_grad = full_scans(
             query_proj, key_proj, value_proj, out_grad, factor, weight, state_in, adjoint_in
         )
-        filter_grad = jnp.sum(gathered, axis=0).T
+        filter_grad = jnp.dot(total, member.T, precision=high).T
         filter_update = filter_grad / jnp.sqrt(jnp.mean(filter_grad * filter_grad) + 1e-06)
         return (hyena_out, query_grad, key_grad, value_grad, filter_update)
 

time: 122 us -> 184 us (1.51)
  waiting for transfers between devices: 28.7 us -> 99.8 us
  blocking collectives: 24.3 us -> 0 us
  between operations: 1.45 us -> 14.9 us
    psum x0 -> x1, waiting for transfers between devices: none -> 69 us  [on_device(): total = lax.psum(local_total + state_in * factor * head_adjoint, 'ctx')]
    all_gather x1 -> x0, blocking collectives: 24.3 us -> none  [on_device(): gathered = lax.all_gather(local_grad, 'ctx')]
    ppermute x4, waiting for transfers between devices: 19.5 us -> 21.7 us  [on_device(): got_bwd = lax.ppermute(bwd_all, 'ctx', behind)]
  transfers between devices with their start and end apart: 8 -> 9, of which waited for: 6 -> 7; matrix products, arithmetic and copies ran while one was open for 2% -> 1% of each run, Pallas kernels for 0% -> 12%
where the time goes in v3:
time: 184 us; the launch traced here: 183 us
  waiting for transfers between devices  99.8 us (54%)
  Pallas kernels  31 us (17%)
  starting transfers between devices  25.2 us (14%)
  between operations  14.9 us (8%)
  matrix products  7.74 us (4%)
  other arithmetic  3.08 us (2%)
    psum x1, waiting for transfers between devices, on_device(): total = lax.psum(local_total + state_in * factor * head_adjoint, 'ctx')  69 us
    ppermute x4, waiting for transfers between devices, on_device(): got_bwd = lax.ppermute(bwd_all, 'ctx', behind)  21.7 us
    pallas_call x1, Pallas kernels, full_scans(): pl.pallas_call(main_kernel, grid=(width // BLOCK,), in_specs=[big, big, b...  21.1 us
    ppermute x4, starting transfers between devices, on_device(): got_fwd = lax.ppermute(fwd_all, 'ctx', ahead)  19.8 us
    pallas_call x1, Pallas kernels, local_carries(): pl.pallas_call(carry_kernel, grid=(width // BLOCK,), in_specs=[big, big,...  9.95 us
    ppermute x4, waiting for transfers between devices, on_device(): got_fwd = lax.ppermute(fwd_all, 'ctx', ahead)  9.14 us
    ppermute x4, starting transfers between devices, on_device(): got_bwd = lax.ppermute(bwd_all, 'ctx', behind)  5.3 us
  transfers between devices with their start and end apart: 9, of which 7 were waited for; matrix products, arithmetic and copies ran while one was open for 1% of the time, Pallas kernels for 12%

profile of v3, /device:TPU:0, one launch (start us, length us, event | category | flops | bytes accessed | tf_op | source)
XLA Modules:
  0.0 183.1 jit_solution(18079220191203324231)
XLA Ops:
  7.2 0.0 copy-start
  7.2 0.0 all-reduce.2.cloned.1.call-start
  7.2 0.7 copy-done
  7.9 2.1 %convolution_negate_fusion = f32[4096,16]{0,1:T(8,128)S(1)} fusion(f32[256,16]{0,1:T(8,128)S(1)} %copy-done, s32[4096]{0:T(1024)} %param.13), kind=kOutput, calls=%fused_computation.1 | convolution fusion | flops 202440704 | bytes 294912 | tf_op jit(solution)/shard_map/dot_general | solution.py:121
  10.0 0.7 exponential_bitcast_fusion.p_ref
  10.8 9.9 %shard_map.110 = (f32[16,4096]{1,0:T(8,128)}, f32[16,4096]{1,0:T(8,128)}, f32[16,4096]{1,0:T(8,128)}) custom-call(bf16[128,4096]{1,0:T(8,128)(2,1)} %q_ref.3, bf16[128,4096]{1,0:T(8,128)(2,1)} %k_ref.3, bf16[128,4096]{1,0:T(8,128)(2,1)} %v_ref.3, bf16[128,4096]{1,0:T(8,128)(2,1)} %g_ref.3, f32[16,4096]{1,0:T(8,128)} %exponential_bitcast_fusion.p_ref), custom_call_target="tpu_custom_call" | custom-call | tf_op jit(solution)/shard_map/pallas_call | solution.py:87
  20.7 2.4 %collective-permute-start = (f32[16,4096]{1,0:T(8,128)}, f32[16,4096]{1,0:T(8,128)S(1)}, u32[]{:S(2)}, u32[]{:S(2)}) collective-permute-start(f32[16,4096]{1,0:T(8,128)} %get-tuple-element.20), channel_id=1, source_target_pairs={{0,1},{1,2},{2,3},{3,4},{4,5},{5,6},{6,7},{7,8},{8,9},{9,10},{10,1... | collective-permute-start | bytes 786440 | tf_op jit(solution)/shard_map/ppermute | solution.py:139
  23.1 1.3 collective-permute-start.1
  24.4 0.0 collective-permute-done
  24.4 4.4 %collective-permute-done.1 = f32[16,4096]{1,0:T(8,128)S(1)} collective-permute-done((f32[16,4096]{1,0:T(8,128)}, f32[16,4096]{1,0:T(8,128)S(1)}, u32[]{:S(2)}, u32[]{:S(2)}) %collective-permute-start.1) | collective-permute-done | bytes 262176 | tf_op jit(solution)/shard_map/ppermute | solution.py:140
  28.8 1.1 fusion.13
  30.0 1.3 collective-permute-start.3
  31.3 7.1 %collective-permute-start.2 = (f32[16,4096]{1,0:T(8,128)S(1)}, f32[16,4096]{1,0:T(8,128)S(1)}, u32[]{:S(2)}, u32[]{:S(2)}) collective-permute-start(f32[16,4096]{1,0:T(8,128)S(1)} %get-tuple-element.43), channel_id=1, source_target_pairs={{0,2},{1,3},{2,4},{3,5},{4,6},{5,7},{6,8},{7,9},{8,10},{9,11},{10,... | collective-permute-start | bytes 786440 | tf_op jit(solution)/shard_map/ppermute | solution.py:139
  38.4 3.2 %collective-permute-done.3 = f32[16,4096]{1,0:T(8,128)S(1)} collective-permute-done((f32[16,4096]{1,0:T(8,128)S(1)}, f32[16,4096]{1,0:T(8,128)S(1)}, u32[]{:S(2)}, u32[]{:S(2)}) %collective-permute-start.3) | collective-permute-done | bytes 262176 | tf_op jit(solution)/shard_map/ppermute | solution.py:140
  41.6 7.9 %collective-permute-done.2 = f32[16,4096]{1,0:T(8,128)S(1)} collective-permute-done((f32[16,4096]{1,0:T(8,128)S(1)}, f32[16,4096]{1,0:T(8,128)S(1)}, u32[]{:S(2)}, u32[]{:S(2)}) %collective-permute-start.2) | collective-permute-done | bytes 262176 | tf_op jit(solution)/shard_map/ppermute | solution.py:139
  49.6 0.1 fusion.9
  49.7 0.0 copy-start.1
  49.7 0.0 copy-start.2
  49.7 1.4 collective-permute-start.5
  51.1 4.8 %collective-permute-start.4 = (f32[16,4096]{1,0:T(8,128)S(1)}, f32[16,4096]{1,0:T(8,128)S(1)}, u32[]{:S(2)}, u32[]{:S(2)}) collective-permute-start(f32[16,4096]{1,0:T(8,128)S(1)} %get-tuple-element.41), channel_id=1, source_target_pairs={{0,4},{1,5},{2,6},{3,7},{4,8},{5,9},{6,10},{7,11},{8,12},{9,13},{1... | collective-permute-start | bytes 786440 | tf_op jit(solution)/shard_map/ppermute | solution.py:139
  55.9 4.8 %collective-permute-done.5 = f32[16,4096]{1,0:T(8,128)S(1)} collective-permute-done((f32[16,4096]{1,0:T(8,128)S(1)}, f32[16,4096]{1,0:T(8,128)S(1)}, u32[]{:S(2)}, u32[]{:S(2)}) %collective-permute-start.5) | collective-permute-done | bytes 262176 | tf_op jit(solution)/shard_map/ppermute | solution.py:140
  60.7 1.2 collective-permute-done.4
  61.8 0.1 fusion.5
  61.9 1.3 collective-permute-start.7
  63.2 5.6 %collective-permute-start.6 = (f32[16,4096]{1,0:T(8,128)S(1)}, f32[16,4096]{1,0:T(8,128)S(1)}, u32[]{:S(2)}, u32[]{:S(2)}) collective-permute-start(f32[16,4096]{1,0:T(8,128)S(1)} %get-tuple-element.39), channel_id=1, source_target_pairs={{0,8},{1,9},{2,10},{3,11},{4,12},{5,13},{6,14},{7,15},{16,24},{17,... | collective-permute-start | bytes 786440 | tf_op jit(solution)/shard_map/ppermute | solution.py:139
  68.8 9.2 %collective-permute-done.7 = f32[16,4096]{1,0:T(8,128)S(1)} collective-permute-done((f32[16,4096]{1,0:T(8,128)S(1)}, f32[16,4096]{1,0:T(8,128)S(1)}, u32[]{:S(2)}, u32[]{:S(2)}) %collective-permute-start.7) | collective-permute-done | bytes 262176 | tf_op jit(solution)/shard_map/ppermute | solution.py:140
  78.1 0.0 collective-permute-done.6
  78.1 0.0 copy-done.1
  78.1 0.0 copy-done.2
  78.1 0.0 copy-start.3
  78.1 0.0 copy-start.4
  78.1 1.1 multiply_add_fusion
  79.2 0.0 all-reduce.2.cloned.1.call-update
  79.3 0.0 copy-done.3
  79.3 0.0 copy-done.4
  79.3 2.1 %convolution_bitcast_fusion.r_ref = f32[16,4096]{1,0:T(8,128)} fusion(f32[256,16]{0,1:T(8,128)S(1)} %copy-done.3, s32[4096]{0:T(1024)S(1)} %copy-done.4), kind=kOutput, calls=%fused_computation | convolution fusion | flops 202375168 | bytes 294912 | tf_op jit(solution)/shard_map/dot_general | solution.py:122
  81.4 21.1 %shard_map.111 = (bf16[128,4096]{1,0:T(8,128)(2,1)}, bf16[128,4096]{1,0:T(8,128)(2,1)}, bf16[128,4096]{1,0:T(8,128)(2,1)}, bf16[128,4096]{1,0:T(8,128)(2,1)}) custom-call(bf16[128,4096]{1,0:T(8,128)(2,1)} %q_ref.3, bf16[128,4096]{1,0:T(8,128)(2,1)} %k_ref.3, bf16[128,4096]{1,0:T(8,128)(2,1)} %v_ref.3, bf16[128,4096]{1,0:T(8,128)(2,1)} %g_ref.3, ...), custom_call_target="tpu_custom_call" | custom-call | tf_op jit(solution)/shard_map/pallas_call | solution.py:103
  102.4 69.0 %all-reduce.2.cloned.1.call-done = f32[16,4096]{1,0:T(8,128)} async-done(((f32[16,4096]{1,0:T(8,128)}), f32[16,4096]{1,0:T(8,128)}) %all-reduce.2.cloned.1.call-update) | async-done | bytes 262160 | tf_op jit(solution)/shard_map/psum | solution.py:150
  171.4 3.5 %multiply_reduce_fusion = (f32[]{:T(128)}, f32[256,16]{0,1:T(8,128)S(1)}) fusion(f32[16,4096]{1,0:T(8,128)} %all-reduce.2.cloned.1.call-done, s32[4096]{0:T(1024)S(1)} %copy-done.4), kind=kOutput, calls=%fused_computation.41 | convolution fusion | flops 202383360 | bytes 294916 | tf_op jit(solution)/shard_map/dot_general | solution.py:154
  175.6 0.6 broadcast_divide_fusion
Async XLA Ops:
  7.2 0.7 copy-start
  7.2 164.2 %all-reduce.2.cloned.1.call-start = ((), (), s32[]{:S(2)}) async-start(), calls=%async_computation | async-start | bytes 524288 | tf_op jit(solution)/shard_map/psum | solution.py:150
  20.7 3.7 %collective-permute-start = (f32[16,4096]{1,0:T(8,128)}, f32[16,4096]{1,0:T(8,128)S(1)}, u32[]{:S(2)}, u32[]{:S(2)}) collective-permute-start(f32[16,4096]{1,0:T(8,128)} %get-tuple-element.20), channel_id=1, source_target_pairs={{0,1},{1,2},{2,3},{3,4},{4,5},{5,6},{6,7},{7,8},{8,9},{9,10},{10,1... | collective-permute-start | bytes 786440 | tf_op jit(solution)/shard_map/ppermute | solution.py:139
  23.1 5.8 %collective-permute-start.1 = (f32[16,4096]{1,0:T(8,128)}, f32[16,4096]{1,0:T(8,128)S(1)}, u32[]{:S(2)}, u32[]{:S(2)}) collective-permute-start(f32[16,4096]{1,0:T(8,128)} %get-tuple-element.21), channel_id=1, source_target_pairs={{1,0},{2,1},{3,2},{4,3},{5,4},{6,5},{7,6},{8,7},{9,8},{10,9},{11,1... | collective-permute-start | bytes 786440 | tf_op jit(solution)/shard_map/ppermute | solution.py:140
  30.0 11.7 %collective-permute-start.3 = (f32[16,4096]{1,0:T(8,128)S(1)}, f32[16,4096]{1,0:T(8,128)S(1)}, u32[]{:S(2)}, u32[]{:S(2)}) collective-permute-start(f32[16,4096]{1,0:T(8,128)S(1)} %get-tuple-element.42), channel_id=1, source_target_pairs={{2,0},{3,1},{4,2},{5,3},{6,4},{7,5},{8,6},{9,7},{10,8},{11,9},{12,... | collective-permute-start | bytes 786440 | tf_op jit(solution)/shard_map/ppermute | solution.py:140
  31.3 18.3 %collective-permute-start.2 = (f32[16,4096]{1,0:T(8,128)S(1)}, f32[16,4096]{1,0:T(8,128)S(1)}, u32[]{:S(2)}, u32[]{:S(2)}) collective-permute-start(f32[16,4096]{1,0:T(8,128)S(1)} %get-tuple-element.43), channel_id=1, source_target_pairs={{0,2},{1,3},{2,4},{3,5},{4,6},{5,7},{6,8},{7,9},{8,10},{9,11},{10,... | collective-permute-start | bytes 786440 | tf_op jit(solution)/shard_map/ppermute | solution.py:139
  49.7 28.4 %copy-start.1 = (f32[16,4096]{1,0:T(8,128)S(1)}, f32[16,4096]{1,0:T(8,128)}, u32[]{:S(2)}) copy-start(f32[16,4096]{1,0:T(8,128)} %get-tuple-element.21) | copy-start | bytes 786436
  49.7 28.4 %copy-start.2 = (f32[16,4096]{1,0:T(8,128)S(1)}, f32[16,4096]{1,0:T(8,128)}, u32[]{:S(2)}) copy-start(f32[16,4096]{1,0:T(8,128)} %get-tuple-element.34) | copy-start | bytes 786436
  49.7 11.0 %collective-permute-start.5 = (f32[16,4096]{1,0:T(8,128)S(1)}, f32[16,4096]{1,0:T(8,128)S(1)}, u32[]{:S(2)}, u32[]{:S(2)}) collective-permute-start(f32[16,4096]{1,0:T(8,128)S(1)} %get-tuple-element.40), channel_id=1, source_target_pairs={{4,0},{5,1},{6,2},{7,3},{8,4},{9,5},{10,6},{11,7},{12,8},{13,9},{1... | collective-permute-start | bytes 786440 | tf_op jit(solution)/shard_map/ppermute | solution.py:140
  51.1 10.7 %collective-permute-start.4 = (f32[16,4096]{1,0:T(8,128)S(1)}, f32[16,4096]{1,0:T(8,128)S(1)}, u32[]{:S(2)}, u32[]{:S(2)}) collective-permute-start(f32[16,4096]{1,0:T(8,128)S(1)} %get-tuple-element.41), channel_id=1, source_target_pairs={{0,4},{1,5},{2,6},{3,7},{4,8},{5,9},{6,10},{7,11},{8,12},{9,13},{1... | collective-permute-start | bytes 786440 | tf_op jit(solution)/shard_map/ppermute | solution.py:139
  61.9 16.1 %collective-permute-start.7 = (f32[16,4096]{1,0:T(8,128)S(1)}, f32[16,4096]{1,0:T(8,128)S(1)}, u32[]{:S(2)}, u32[]{:S(2)}) collective-permute-start(f32[16,4096]{1,0:T(8,128)S(1)} %get-tuple-element.38), channel_id=1, source_target_pairs={{8,0},{9,1},{10,2},{11,3},{12,4},{13,5},{14,6},{15,7},{24,16},{25,... | collective-permute-start | bytes 786440 | tf_op jit(solution)/shard_map/ppermute | solution.py:140
  63.2 14.8 %collective-permute-start.6 = (f32[16,4096]{1,0:T(8,128)S(1)}, f32[16,4096]{1,0:T(8,128)S(1)}, u32[]{:S(2)}, u32[]{:S(2)}) collective-permute-start(f32[16,4096]{1,0:T(8,128)S(1)} %get-tuple-element.39), channel_id=1, source_target_pairs={{0,8},{1,9},{2,10},{3,11},{4,12},{5,13},{6,14},{7,15},{16,24},{17,... | collective-permute-start | bytes 786440 | tf_op jit(solution)/shard_map/ppermute | solution.py:139
  78.1 1.2 copy-start.3
  78.1 1.2 copy-start.4
Sparse Core Ops, SparseCore 0:
  79.4 91.9 all-reduce.1

commit v4 on v3

--- a/solution.py
+++ b/solution.py
@@ -126,32 +126,46 @@
         )
 
         def span(blocks):
-            return jnp.exp(-rate * float(rows * blocks))
+            return jnp.exp(-rate * (blocks * float(rows)))
 
-        fwd_all = end_state
-        bwd_all = head_adjoint
+        def grouped(a):
+            return jnp.dot(a, member.T, precision=high)
+
+        place = lax.axis_index("ctx")
+        fwd_cube = end_state
+        bwd_cube = head_adjoint
+        grad_cube = grouped(local_total)
         state_in = jnp.zeros_like(end_state)
         adjoint_in = jnp.zeros_like(head_adjoint)
-        shift = 1
-        while shift < count:
-            ahead = [(i, i + shift) for i in range(count - shift)]
-            behind = [(i + shift, i) for i in range(count - shift)]
-            got_fwd = lax.ppermute(fwd_all, "ctx", ahead)
-            got_bwd = lax.ppermute(bwd_all, "ctx", behind)
-            got_fwd, got_bwd = lax.optimization_barrier((got_fwd, got_bwd))
-            inner = span(shift - 1)
-            outer = span(shift)
-            state_in = state_in + inner * got_fwd
-            adjoint_in = adjoint_in + inner * got_bwd
-            fwd_all = fwd_all + outer * got_fwd
-            bwd_all = bwd_all + outer * got_bwd
-            shift *= 2
+        bit = 1
+        while bit < count:
+            pairs = [(i, i ^ bit) for i in range(count)]
+            width = fwd_cube.shape[1]
+            packed = jnp.concatenate([fwd_cube, bwd_cube, grad_cube], axis=1)
+            got = lax.ppermute(packed, "ctx", pairs)
+            got_fwd = got[:, :width]
+            got_bwd = got[:, width : 2 * width]
+            got_grad = got[:, 2 * width :]
+            upper = (place & bit) != 0
+            offset = (place % bit).astype(jnp.float32)
+            low_fwd = jnp.where(upper, got_fwd, fwd_cube)
+            high_fwd = jnp.where(upper, fwd_cube, got_fwd)
+            low_bwd = jnp.where(upper, got_bwd, bwd_cube)
+            high_bwd = jnp.where(upper, bwd_cube, got_bwd)
+            low_grad = jnp.where(upper, got_grad, grad_cube)
+            high_grad = jnp.where(upper, grad_cube, got_grad)
+            state_in = state_in + jnp.where(upper, span(offset) * got_fwd, 0.0)
+            adjoint_in = adjoint_in + jnp.where(upper, 0.0, span(bit - 1 - offset) * got_bwd)
+            whole = span(bit)
+            grad_cube = (low_grad + high_grad) + grouped((factor * low_fwd) * high_bwd)
+            fwd_cube = high_fwd + whole * low_fwd
+            bwd_cube = low_bwd + whole * high_bwd
+            bit *= 2
 
-        total = lax.psum(local_total + state_in * factor * head_adjoint, "ctx")
         hyena_out, query_grad, key_grad, value_grad = full_scans(
             query_proj, key_proj, value_proj, out_grad, factor, weight, state_in, adjoint_in
         )
-        filter_grad = jnp.dot(total, member.T, precision=high).T
+        filter_grad = grad_cube.T
         filter_update = filter_grad / jnp.sqrt(jnp.mean(filter_grad * filter_grad) + 1e-06)
         return (hyena_out, query_grad, key_grad, value_grad, filter_update)
 

time: 184 us -> 109 us (0.59)
  waiting for transfers between devices: 99.8 us -> 47 us
  starting transfers between devices: 25.2 us -> 7.89 us
  between operations: 14.9 us -> 1.43 us
  matrix products: 7.74 us -> 16.9 us
    psum x1 -> x0, waiting for transfers between devices: 69 us -> none  [on_device(): total = lax.psum(local_total + state_in * factor * head_adjoint, 'ctx')]
    ppermute x8 -> x4, starting transfers between devices: 25.1 us -> 7.89 us  [on_device(): got = lax.ppermute(packed, 'ctx', pairs)]
    ppermute x8 -> x4, waiting for transfers between devices: 30.8 us -> 47 us  [on_device(): got = lax.ppermute(packed, 'ctx', pairs)]
    dot_general x1 -> x5, matrix products: 3.52 us -> 12.6 us  [grouped(): return jnp.dot(a, member.T, precision=high)]
  transfers between devices with their start and end apart: 9 -> 4, of which waited for: 7 -> 4; matrix products, arithmetic and copies ran while one was open for 1% -> 2% of each run, Pallas kernels for 12% -> 0%
where the time goes in v4:
time: 109 us
  waiting for transfers between devices  47 us (43%)
  Pallas kernels  31 us (28%)
  matrix products  16.9 us (16%)
  starting transfers between devices  7.89 us (7%)
  other arithmetic  3.33 us (3%)
  local copies, waits for them, and re-layouts  1.52 us (1%)
  between operations  1.43 us (1%)
    ppermute x4, waiting for transfers between devices, on_device(): got = lax.ppermute(packed, 'ctx', pairs)  47 us
    pallas_call x1, Pallas kernels, full_scans(): pl.pallas_call(main_kernel, grid=(width // BLOCK,), in_specs=[big, big, b...  21.1 us
    dot_general x5, matrix products, grouped(): return jnp.dot(a, member.T, precision=high)  12.6 us
    pallas_call x1, Pallas kernels, local_carries(): pl.pallas_call(carry_kernel, grid=(width // BLOCK,), in_specs=[big, big,...  9.96 us
    ppermute x4, starting transfers between devices, on_device(): got = lax.ppermute(packed, 'ctx', pairs)  7.89 us
    add x1, other arithmetic, on_device(): adjoint_in + jnp.where(upper, 0.0, span(bit - 1 - offset) * got_bwd)  2.23 us
  transfers between devices with their start and end apart: 4, of which 4 were waited for; matrix products, arithmetic and copies ran while one was open for 2% of the time, Pallas kernels for 0%

profile of v4, /device:TPU:0, one launch (start us, length us, event | category | flops | bytes accessed | tf_op | source)
XLA Modules:
  0.0 109.1 jit_solution(3773499010920391143)
XLA Ops:
  0.6 0.0 copy-start
  0.6 0.7 copy-done
  1.4 2.1 %convolution_negate_fusion = f32[4096,16]{0,1:T(8,128)S(1)} fusion(f32[256,16]{0,1:T(8,128)S(1)} %copy-done, s32[4096]{0:T(1024)} %param.13), kind=kOutput, calls=%fused_computation.1 | convolution fusion | flops 202440704 | bytes 294912 | tf_op jit(solution)/shard_map/dot_general | solution.py:121
  3.5 0.8 exponential_bitcast_fusion.p_ref
  4.2 0.0 copy-start.4
  4.2 10.0 %shard_map.110 = (f32[16,4096]{1,0:T(8,128)}, f32[16,4096]{1,0:T(8,128)}, f32[16,4096]{1,0:T(8,128)}) custom-call(bf16[128,4096]{1,0:T(8,128)(2,1)} %q_ref.3, bf16[128,4096]{1,0:T(8,128)(2,1)} %k_ref.3, bf16[128,4096]{1,0:T(8,128)(2,1)} %v_ref.3, bf16[128,4096]{1,0:T(8,128)(2,1)} %g_ref.3, f32[16,4096]{1,0:T(8,128)} %exponential_bitcast_fusion.p_ref), custom_call_target="tpu_custom_call" | custom-call | tf_op jit(solution)/shard_map/pallas_call | solution.py:87
  14.2 0.0 copy-start.1
  14.2 0.0 copy-start.2
  14.2 0.0 copy-done.4
  14.2 3.0 %fusion.4 = f32[16,256]{1,0:T(8,128)S(1)} fusion(f32[16,4096]{1,0:T(8,128)} %get-tuple-element.14, s32[4096]{0:T(1024)S(1)} %copy-done.4), kind=kOutput, calls=%fused_computation.7 | convolution fusion | flops 202375168 | bytes 294912 | tf_op jit(solution)/shard_map/dot_general | solution.py:132
  17.2 0.0 copy-done.1
  17.2 0.0 copy-done.2
  17.2 0.5 collective-permute-start
  17.8 1.6 %collective-permute-done = f32[16,8448]{1,0:T(8,128)S(1)} collective-permute-done((f32[16,8448]{1,0:T(8,128)S(1)}, f32[16,8448]{1,0:T(8,128)S(1)}, u32[]{:S(2)}, u32[]{:S(2)}) %collective-permute-start) | collective-permute-done | bytes 540704 | tf_op jit(solution)/shard_map/ppermute | solution.py:145
  19.3 2.0 %add_add_fusion.3 = f32[16,256]{1,0:T(8,128)S(1)} fusion(f32[16,256]{1,0:T(8,128)S(1)} %fusion.4, f32[16,8448]{1,0:T(8,128)S(1)} %collective-permute-done, pred[]{:T(512)S(6)} %ne.28, s32[4096]{0:T(1024)S(1)} %copy-done.4, f32[16,4096]{1,0:T(8,128)S(1)} %copy-done.2, f32[16,4096]{1,0:T(8,128)S(1)} %copy-done.1, f32[4096,16]{0,1:T(8,128)S(1)} %convolution_negate_fusion), kind=kOutput, calls=%fused_computation.85 | convolution fusion | flops 202653696 | bytes 1377280 | tf_op jit(solution)/shard_map/dot_general | solution.py:132
  21.3 0.1 fusion.26
  21.5 3.0 %collective-permute-start.1 = (f32[16,8448]{1,0:T(8,128)S(1)}, f32[16,8448]{1,0:T(8,128)S(1)}, u32[]{:S(2)}, u32[]{:S(2)}) collective-permute-start(f32[16,8448]{1,0:T(8,128)S(1)} %pad_maximum_fusion.1), channel_id=1, source_target_pairs={{0,2},{1,3},{2,0},{3,1},{4,6},{5,7},{6,4},{7,5},{8,10},{9,11},{10,... | collective-permute-start | bytes 1622024 | tf_op jit(solution)/shard_map/ppermute | solution.py:145
  24.5 12.6 %collective-permute-done.1 = f32[16,8448]{1,0:T(8,128)S(1)} collective-permute-done((f32[16,8448]{1,0:T(8,128)S(1)}, f32[16,8448]{1,0:T(8,128)S(1)}, u32[]{:S(2)}, u32[]{:S(2)}) %collective-permute-start.1) | collective-permute-done | bytes 540704 | tf_op jit(solution)/shard_map/ppermute | solution.py:145
  37.0 2.0 %add_add_fusion.2 = f32[16,256]{1,0:T(8,128)S(1)} fusion(f32[16,256]{1,0:T(8,128)S(1)} %add_add_fusion.3, f32[16,8448]{1,0:T(8,128)S(1)} %collective-permute-done.1, pred[]{:T(512)S(6)} %ne.29, s32[4096]{0:T(1024)S(1)} %copy-done.4, f32[16,4096]{1,0:T(8,128)S(1)} %get-tuple-element.26, f32[16,4096]{1,0:T(8,128)S(1)} %get-tuple-element.25, ...), kind=kOutput, calls=%fused_computation.84 | convolution fusion | flops 202653696 | bytes 1377280 | tf_op jit(solution)/shard_map/dot_general | solution.py:132
  39.0 0.1 fusion.22
  39.2 1.9 %collective-permute-start.2 = (f32[16,8448]{1,0:T(8,128)S(1)}, f32[16,8448]{1,0:T(8,128)S(1)}, u32[]{:S(2)}, u32[]{:S(2)}) collective-permute-start(f32[16,8448]{1,0:T(8,128)S(1)} %pad_maximum_fusion.2), channel_id=1, source_target_pairs={{0,4},{1,5},{2,6},{3,7},{4,0},{5,1},{6,2},{7,3},{8,12},{9,13},{10,... | collective-permute-start | bytes 1622024 | tf_op jit(solution)/shard_map/ppermute | solution.py:145
  41.1 12.0 %collective-permute-done.2 = f32[16,8448]{1,0:T(8,128)S(1)} collective-permute-done((f32[16,8448]{1,0:T(8,128)S(1)}, f32[16,8448]{1,0:T(8,128)S(1)}, u32[]{:S(2)}, u32[]{:S(2)}) %collective-permute-start.2) | collective-permute-done | bytes 540704 | tf_op jit(solution)/shard_map/ppermute | solution.py:145
  53.1 2.0 %add_add_fusion.1 = f32[16,256]{1,0:T(8,128)S(1)} fusion(f32[16,256]{1,0:T(8,128)S(1)} %add_add_fusion.2, f32[16,8448]{1,0:T(8,128)S(1)} %collective-permute-done.2, pred[]{:T(512)S(6)} %ne.31, s32[4096]{0:T(1024)S(1)} %copy-done.4, f32[16,4096]{1,0:T(8,128)S(1)} %get-tuple-element.24, f32[16,4096]{1,0:T(8,128)S(1)} %get-tuple-element.23, ...), kind=kOutput, calls=%fused_computation.83 | convolution fusion | flops 202653696 | bytes 1377280 | tf_op jit(solution)/shard_map/dot_general | solution.py:132
  55.1 0.0 copy-start.3
  55.1 0.1 fusion.18
  55.3 2.6 %collective-permute-start.3 = (f32[16,8448]{1,0:T(8,128)S(1)}, f32[16,8448]{1,0:T(8,128)}, u32[]{:S(2)}, u32[]{:S(2)}) collective-permute-start(f32[16,8448]{1,0:T(8,128)S(1)} %pad_maximum_fusion.3), channel_id=1, source_target_pairs={{0,8},{1,9},{2,10},{3,11},{4,12},{5,13},{6,14},{7,15},{8,0},{9,1},... | collective-permute-start | bytes 1622024 | tf_op jit(solution)/shard_map/ppermute | solution.py:145
  57.8 0.0 copy-done.3
  57.8 2.1 %convolution_bitcast_fusion.r_ref = f32[16,4096]{1,0:T(8,128)} fusion(f32[256,16]{0,1:T(8,128)S(1)} %copy-done.3, s32[4096]{0:T(1024)S(1)} %copy-done.4), kind=kOutput, calls=%fused_computation | convolution fusion | flops 202375168 | bytes 294912 | tf_op jit(solution)/shard_map/dot_general | solution.py:122
  59.9 20.9 %collective-permute-done.3 = f32[16,8448]{1,0:T(8,128)} collective-permute-done((f32[16,8448]{1,0:T(8,128)S(1)}, f32[16,8448]{1,0:T(8,128)}, u32[]{:S(2)}, u32[]{:S(2)}) %collective-permute-start.3) | collective-permute-done | bytes 540704 | tf_op jit(solution)/shard_map/ppermute | solution.py:145
  80.8 3.7 %multiply_reduce_fusion = (f32[]{:T(128)}, f32[16,256]{1,0:T(8,128)S(1)}) fusion(s32[4096]{0:T(1024)S(1)} %copy-done.4, f32[16,4096]{1,0:T(8,128)S(1)} %get-tuple-element.22, f32[16,4096]{1,0:T(8,128)S(1)} %get-tuple-element.21, f32[16,8448]{1,0:T(8,128)} %collective-permute-done.3, pred[]{:T(512)S(6)} %ne.33, f32[4096,16]{0,1:T(8,128)S(1)} %convolution_negate_fusion, ...), kind=kOutput, calls=%fused_computation.81 | convolution fusion | flops 202661888 | bytes 1377284 | tf_op jit(solution)/shard_map/dot_general | solution.py:132
  85.2 0.6 divide_bitcast_fusion
  85.8 2.2 %fusion.13 = (f32[16,4096]{1,0:T(8,128)}, f32[16,4096]{1,0:T(8,128)}) fusion(f32[4096,16]{0,1:T(8,128)S(1)} %convolution_negate_fusion, f32[16,8448]{1,0:T(8,128)} %collective-permute-done.3, f32[16,8448]{1,0:T(8,128)S(1)} %collective-permute-done.2, f32[16,8448]{1,0:T(8,128)S(1)} %collective-permute-done.1, f32[16,8448]{1,0:T(8,128)S(1)} %collective-permute-done, ...), kind=kLoop, calls=%fused_computation.21 | loop fusion | flops 1900544 | bytes 2883612 | tf_op jit(solution)/shard_map/add | solution.py:158
  88.0 21.1 %shard_map.111 = (bf16[128,4096]{1,0:T(8,128)(2,1)}, bf16[128,4096]{1,0:T(8,128)(2,1)}, bf16[128,4096]{1,0:T(8,128)(2,1)}, bf16[128,4096]{1,0:T(8,128)(2,1)}) custom-call(bf16[128,4096]{1,0:T(8,128)(2,1)} %q_ref.3, bf16[128,4096]{1,0:T(8,128)(2,1)} %k_ref.3, bf16[128,4096]{1,0:T(8,128)(2,1)} %v_ref.3, bf16[128,4096]{1,0:T(8,128)(2,1)} %g_ref.3, ...), custom_call_target="tpu_custom_call" | custom-call | tf_op jit(solution)/shard_map/pallas_call | solution.py:103
  (4 shorter events, 0.1 us)
Async XLA Ops:
  0.6 0.7 copy-start
  4.2 10.0 %copy-start.4 = (s32[4096]{0:T(1024)S(1)}, s32[4096]{0:T(1024)}, u32[]{:S(2)}) copy-start(s32[4096]{0:T(1024)} %param.13) | copy-start | bytes 49156
  14.2 3.0 %copy-start.1 = (f32[16,4096]{1,0:T(8,128)S(1)}, f32[16,4096]{1,0:T(8,128)}, u32[]{:S(2)}) copy-start(f32[16,4096]{1,0:T(8,128)} %get-tuple-element.12) | copy-start | bytes 786436
  14.2 3.0 %copy-start.2 = (f32[16,4096]{1,0:T(8,128)S(1)}, f32[16,4096]{1,0:T(8,128)}, u32[]{:S(2)}) copy-start(f32[16,4096]{1,0:T(8,128)} %get-tuple-element.13) | copy-start | bytes 786436
  17.2 2.1 %collective-permute-start = (f32[16,8448]{1,0:T(8,128)S(1)}, f32[16,8448]{1,0:T(8,128)S(1)}, u32[]{:S(2)}, u32[]{:S(2)}) collective-permute-start(f32[16,8448]{1,0:T(8,128)S(1)} %pad_maximum_fusion), channel_id=1, source_target_pairs={{0,1},{1,0},{2,3},{3,2},{4,5},{5,4},{6,7},{7,6},{8,9},{9,8},{10,11... | collective-permute-start | bytes 1622024 | tf_op jit(solution)/shard_map/ppermute | solution.py:145
  21.5 15.5 %collective-permute-start.1 = (f32[16,8448]{1,0:T(8,128)S(1)}, f32[16,8448]{1,0:T(8,128)S(1)}, u32[]{:S(2)}, u32[]{:S(2)}) collective-permute-start(f32[16,8448]{1,0:T(8,128)S(1)} %pad_maximum_fusion.1), channel_id=1, source_target_pairs={{0,2},{1,3},{2,0},{3,1},{4,6},{5,7},{6,4},{7,5},{8,10},{9,11},{10,... | collective-permute-start | bytes 1622024 | tf_op jit(solution)/shard_map/ppermute | solution.py:145
  39.2 13.9 %collective-permute-start.2 = (f32[16,8448]{1,0:T(8,128)S(1)}, f32[16,8448]{1,0:T(8,128)S(1)}, u32[]{:S(2)}, u32[]{:S(2)}) collective-permute-start(f32[16,8448]{1,0:T(8,128)S(1)} %pad_maximum_fusion.2), channel_id=1, source_target_pairs={{0,4},{1,5},{2,6},{3,7},{4,0},{5,1},{6,2},{7,3},{8,12},{9,13},{10,... | collective-permute-start | bytes 1622024 | tf_op jit(solution)/shard_map/ppermute | solution.py:145
  55.1 2.7 %copy-start.3 = (f32[256,16]{0,1:T(8,128)S(1)}, f32[256,16]{0,1:T(8,128)}, u32[]{:S(2)}) copy-start(f32[256,16]{0,1:T(8,128)} %param.12) | copy-start | bytes 49156
  55.3 25.6 %collective-permute-start.3 = (f32[16,8448]{1,0:T(8,128)S(1)}, f32[16,8448]{1,0:T(8,128)}, u32[]{:S(2)}, u32[]{:S(2)}) collective-permute-start(f32[16,8448]{1,0:T(8,128)S(1)} %pad_maximum_fusion.3), channel_id=1, source_target_pairs={{0,8},{1,9},{2,10},{3,11},{4,12},{5,13},{6,14},{7,15},{8,0},{9,1},... | collective-permute-start | bytes 1622024 | tf_op jit(solution)/shard_map/ppermute | solution.py:145

commit v5 on v4

--- a/solution.py
+++ b/solution.py
@@ -142,7 +142,17 @@
             pairs = [(i, i ^ bit) for i in range(count)]
             width = fwd_cube.shape[1]
             packed = jnp.concatenate([fwd_cube, bwd_cube, grad_cube], axis=1)
-            got = lax.ppermute(packed, "ctx", pairs)
+            if bit == 1:
+                got = lax.ppermute(packed, "ctx", pairs)
+            else:
+                half = packed.shape[1] // 2
+                core = place % 2
+                mine = lax.dynamic_slice_in_dim(packed, core * half, half, axis=1)
+                got_mine = lax.ppermute(mine, "ctx", pairs)
+                got_other = lax.ppermute(got_mine, "ctx", [(i, i ^ 1) for i in range(count)])
+                first = jnp.where(core == 0, got_mine, got_other)
+                second = jnp.where(core == 0, got_other, got_mine)
+                got = jnp.concatenate([first, second], axis=1)
             got_fwd = got[:, :width]
             got_bwd = got[:, width : 2 * width]
             got_grad = got[:, 2 * width :]

time: 109 us -> 93.5 us (0.86)
  waiting for transfers between devices: 47 us -> 30.8 us
  matrix products: 16.9 us -> 15.8 us
    ppermute x4 -> x1, waiting for transfers between devices: 47 us -> 1.56 us  [on_device(): got = lax.ppermute(packed, 'ctx', pairs)]
    ppermute x0 -> x6, waiting for transfers between devices: none -> 29.2 us  [the longest x3 26.1 us: on_device(): got_mine = lax.ppermute(mine, 'ctx', pairs)]
    ppermute x0 -> x6, starting transfers between devices: none -> 7.64 us  [the longest x3 7.63 us: on_device(): got_mine = lax.ppermute(mine, 'ctx', pairs)]
    ppermute x4 -> x1, starting transfers between devices: 7.89 us -> 0.52 us  [on_device(): got = lax.ppermute(packed, 'ctx', pairs)]
    add x1, other arithmetic: 2.23 us -> 0.92 us  [on_device(): adjoint_in + jnp.where(upper, 0.0, span(bit - 1 - offset) * got_bwd)]
  transfers between devices with their start and end apart: 4 -> 7, of which waited for: 4 -> 6; matrix products, arithmetic and copies ran while one was open for 2% -> 2% of each run, Pallas kernels for 0% -> 0%
where the time goes in v5:
time: 93.5 us; the launch traced here: 93.1 us
  Pallas kernels  31 us (33%)
  waiting for transfers between devices  30.8 us (33%)
  matrix products  15.8 us (17%)
  starting transfers between devices  8.16 us (9%)
  other arithmetic  4.34 us (5%)
  local copies, waits for them, and re-layouts  1.5 us (2%)
  between operations  1.44 us (2%)
    ppermute x3, waiting for transfers between devices, on_device(): got_mine = lax.ppermute(mine, 'ctx', pairs)  26.1 us
    pallas_call x1, Pallas kernels, full_scans(): pl.pallas_call(main_kernel, grid=(width // BLOCK,), in_specs=[big, big, b...  21.1 us
    dot_general x5, matrix products, grouped(): return jnp.dot(a, member.T, precision=high)  11.6 us
    pallas_call x1, Pallas kernels, local_carries(): pl.pallas_call(carry_kernel, grid=(width // BLOCK,), in_specs=[big, big,...  9.96 us
    ppermute x3, starting transfers between devices, on_device(): got_mine = lax.ppermute(mine, 'ctx', pairs)  7.63 us
    ppermute x3, waiting for transfers between devices, on_device(): lax.ppermute(got_mine, 'ctx', [(i, i ^ 1) for i in range(count)])  3.09 us
    dot_general x1, matrix products, on_device(): rate = jnp.dot(decay_rate.T, member, precision=high)  2.12 us
    dot_general x1, matrix products, on_device(): weight = jnp.dot(residue.T, member, precision=high)  2.09 us
  transfers between devices with their start and end apart: 7, of which 6 were waited for; matrix products, arithmetic and copies ran while one was open for 2% of the time, Pallas kernels for 0%

profile of v5, /device:TPU:0, one launch (start us, length us, event | category | flops | bytes accessed | tf_op | source)
XLA Modules:
  0.0 93.1 jit_solution(16829314066917444525)
XLA Ops:
  0.6 0.0 copy-start
  0.6 0.7 copy-done
  1.4 2.1 %convolution_negate_fusion = f32[4096,16]{0,1:T(8,128)S(1)} fusion(f32[256,16]{0,1:T(8,128)S(1)} %copy-done, s32[4096]{0:T(1024)} %param.13), kind=kOutput, calls=%fused_computation.1 | convolution fusion | flops 202440704 | bytes 294912 | tf_op jit(solution)/shard_map/dot_general | solution.py:121
  3.5 0.7 exponential_bitcast_fusion.p_ref
  4.2 0.0 copy-start.4
  4.2 10.0 %shard_map.110 = (f32[16,4096]{1,0:T(8,128)}, f32[16,4096]{1,0:T(8,128)}, f32[16,4096]{1,0:T(8,128)}) custom-call(bf16[128,4096]{1,0:T(8,128)(2,1)} %q_ref.3, bf16[128,4096]{1,0:T(8,128)(2,1)} %k_ref.3, bf16[128,4096]{1,0:T(8,128)(2,1)} %v_ref.3, bf16[128,4096]{1,0:T(8,128)(2,1)} %g_ref.3, f32[16,4096]{1,0:T(8,128)} %exponential_bitcast_fusion.p_ref), custom_call_target="tpu_custom_call" | custom-call | tf_op jit(solution)/shard_map/pallas_call | solution.py:87
  14.2 0.0 copy-start.1
  14.2 0.0 copy-start.2
  14.2 0.0 copy-done.4
  14.2 3.0 %fusion.4 = f32[16,256]{1,0:T(8,128)S(1)} fusion(f32[16,4096]{1,0:T(8,128)} %get-tuple-element.14, s32[4096]{0:T(1024)S(1)} %copy-done.4), kind=kOutput, calls=%fused_computation.7 | convolution fusion | flops 202375168 | bytes 294912 | tf_op jit(solution)/shard_map/dot_general | solution.py:132
  17.2 0.0 copy-done.1
  17.2 0.0 copy-done.2
  17.2 0.5 collective-permute-start
  17.8 1.6 %collective-permute-done = f32[16,8448]{1,0:T(8,128)S(1)} collective-permute-done((f32[16,8448]{1,0:T(8,128)S(1)}, f32[16,8448]{1,0:T(8,128)S(1)}, u32[]{:S(2)}, u32[]{:S(2)}) %collective-permute-start) | collective-permute-done | bytes 540704 | tf_op jit(solution)/shard_map/ppermute | solution.py:146
  19.3 2.0 %add_add_fusion.3 = f32[16,256]{1,0:T(8,128)S(1)} fusion(f32[16,256]{1,0:T(8,128)S(1)} %fusion.4, f32[16,8448]{1,0:T(8,128)S(1)} %collective-permute-done, pred[]{:T(512)S(6)} %ne.34, s32[4096]{0:T(1024)S(1)} %copy-done.4, f32[16,4096]{1,0:T(8,128)S(1)} %copy-done.2, f32[16,4096]{1,0:T(8,128)S(1)} %copy-done.1, f32[4096,16]{0,1:T(8,128)S(1)} %convolution_negate_fusion), kind=kOutput, calls=%fused_computation.105 | convolution fusion | flops 202653696 | bytes 1377280 | tf_op jit(solution)/shard_map/dot_general | solution.py:132
  21.3 0.1 fusion.33
  21.5 0.1 fusion.17
  21.6 3.0 %collective-permute-start.1 = (f32[16,4224]{1,0:T(8,128)S(1)}, f32[16,4224]{1,0:T(8,128)S(1)}, u32[]{:S(2)}, u32[]{:S(2)}) collective-permute-start(f32[16,4224]{1,0:T(8,128)S(1)} %fusion.17), channel_id=1, source_target_pairs={{0,2},{1,3},{2,0},{3,1},{4,6},{5,7},{6,4},{7,5},{8,10},{9,11},{10,... | collective-permute-start | bytes 811016 | tf_op jit(solution)/shard_map/ppermute | solution.py:151
  24.6 6.8 %collective-permute-done.1 = f32[16,4224]{1,0:T(8,128)S(1)} collective-permute-done((f32[16,4224]{1,0:T(8,128)S(1)}, f32[16,4224]{1,0:T(8,128)S(1)}, u32[]{:S(2)}, u32[]{:S(2)}) %collective-permute-start.1) | collective-permute-done | bytes 270368 | tf_op jit(solution)/shard_map/ppermute | solution.py:151
  31.4 0.0 collective-permute-start.2
  31.4 1.5 %collective-permute-done.2 = f32[16,4224]{1,0:T(8,128)S(1)} collective-permute-done((f32[16,4224]{1,0:T(8,128)S(1)}, f32[16,4224]{1,0:T(8,128)S(1)}, u32[]{:S(2)}, u32[]{:S(2)}) %collective-permute-start.2) | collective-permute-done | bytes 270368 | tf_op jit(solution)/shard_map/ppermute | solution.py:152
  32.9 0.1 fusion.29
  33.1 2.0 %add_add_fusion.2 = f32[16,256]{1,0:T(8,128)S(1)} fusion(f32[16,256]{1,0:T(8,128)S(1)} %add_add_fusion.3, f32[16,4224]{1,0:T(8,128)S(1)} %get-tuple-element.29, pred[]{:T(512)S(6)} %ne.35, s32[4096]{0:T(1024)S(1)} %copy-done.4, f32[16,4096]{1,0:T(8,128)S(1)} %get-tuple-element.24, f32[16,4224]{1,0:T(8,128)S(1)} %get-tuple-element.30, ...), kind=kOutput, calls=%fused_computation.104 | convolution fusion | flops 202653696 | bytes 1377280 | tf_op jit(solution)/shard_map/dot_general | solution.py:132
  35.1 0.1 fusion.15
  35.2 1.9 %collective-permute-start.3 = (f32[16,4224]{1,0:T(8,128)S(1)}, f32[16,4224]{1,0:T(8,128)S(1)}, u32[]{:S(2)}, u32[]{:S(2)}) collective-permute-start(f32[16,4224]{1,0:T(8,128)S(1)} %fusion.15), channel_id=1, source_target_pairs={{0,4},{1,5},{2,6},{3,7},{4,0},{5,1},{6,2},{7,3},{8,12},{9,13},{10,... | collective-permute-start | bytes 811016 | tf_op jit(solution)/shard_map/ppermute | solution.py:151
  37.1 6.8 %collective-permute-done.3 = f32[16,4224]{1,0:T(8,128)S(1)} collective-permute-done((f32[16,4224]{1,0:T(8,128)S(1)}, f32[16,4224]{1,0:T(8,128)S(1)}, u32[]{:S(2)}, u32[]{:S(2)}) %collective-permute-start.3) | collective-permute-done | bytes 270368 | tf_op jit(solution)/shard_map/ppermute | solution.py:151
  43.9 0.0 collective-permute-start.4
  43.9 1.5 %collective-permute-done.4 = f32[16,4224]{1,0:T(8,128)S(1)} collective-permute-done((f32[16,4224]{1,0:T(8,128)S(1)}, f32[16,4224]{1,0:T(8,128)S(1)}, u32[]{:S(2)}, u32[]{:S(2)}) %collective-permute-start.4) | collective-permute-done | bytes 270368 | tf_op jit(solution)/shard_map/ppermute | solution.py:152
  45.5 0.1 fusion.25
  45.6 0.0 copy-start.3
  45.6 2.0 %add_add_fusion.1 = f32[16,256]{1,0:T(8,128)S(1)} fusion(f32[16,256]{1,0:T(8,128)S(1)} %add_add_fusion.2, f32[16,4224]{1,0:T(8,128)S(1)} %get-tuple-element.27, pred[]{:T(512)S(6)} %ne.37, s32[4096]{0:T(1024)S(1)} %copy-done.4, f32[16,4096]{1,0:T(8,128)S(1)} %get-tuple-element.32, f32[16,4224]{1,0:T(8,128)S(1)} %get-tuple-element.28, ...), kind=kOutput, calls=%fused_computation.103 | convolution fusion | flops 202653696 | bytes 1377280 | tf_op jit(solution)/shard_map/dot_general | solution.py:132
  47.6 0.1 fusion.13
  47.8 2.8 %collective-permute-start.5 = (f32[16,4224]{1,0:T(8,128)S(1)}, f32[16,4224]{1,0:T(8,128)S(1)}, u32[]{:S(2)}, u32[]{:S(2)}) collective-permute-start(f32[16,4224]{1,0:T(8,128)S(1)} %fusion.13), channel_id=1, source_target_pairs={{0,8},{1,9},{2,10},{3,11},{4,12},{5,13},{6,14},{7,15},{8,0},{9,1},... | collective-permute-start | bytes 811016 | tf_op jit(solution)/shard_map/ppermute | solution.py:151
  50.6 12.6 %collective-permute-done.5 = f32[16,4224]{1,0:T(8,128)S(1)} collective-permute-done((f32[16,4224]{1,0:T(8,128)S(1)}, f32[16,4224]{1,0:T(8,128)S(1)}, u32[]{:S(2)}, u32[]{:S(2)}) %collective-permute-start.5) | collective-permute-done | bytes 270368 | tf_op jit(solution)/shard_map/ppermute | solution.py:151
  63.2 0.0 collective-permute-start.6
  63.2 0.0 copy-done.3
  63.2 2.1 %convolution_bitcast_fusion.r_ref = f32[16,4096]{1,0:T(8,128)} fusion(f32[256,16]{0,1:T(8,128)S(1)} %copy-done.3, s32[4096]{0:T(1024)S(1)} %copy-done.4), kind=kOutput, calls=%fused_computation | convolution fusion | flops 202375168 | bytes 294912 | tf_op jit(solution)/shard_map/dot_general | solution.py:122
  65.3 0.0 collective-permute-done.6
  65.3 1.0 %broadcast_select_fusion = (f32[16,4224]{1,0:T(8,128)S(1)}, f32[16,4224]{1,0:T(8,128)S(1)}) fusion(f32[16,4224]{1,0:T(8,128)} %collective-permute-done.6, f32[16,4224]{1,0:T(8,128)S(1)} %collective-permute-done.5, pred[]{:T(512)S(6)} %eq.32), kind=kLoop, calls=%fused_computation.88 | loop fusion | flops 135168 | bytes 1081345 | tf_op jit(solution)/shard_map/jit(_where)/select_n | solution.py:154
  66.3 2.6 %multiply_reduce_fusion = (f32[]{:T(128)}, f32[16,256]{1,0:T(8,128)S(1)}) fusion(s32[4096]{0:T(1024)S(1)} %copy-done.4, f32[16,4096]{1,0:T(8,128)S(1)} %get-tuple-element.19, f32[16,4096]{1,0:T(8,128)S(1)} %get-tuple-element.31, f32[16,4224]{1,0:T(8,128)S(1)} %get-tuple-element.26, pred[]{:T(512)S(6)} %ne.39, f32[16,4224]{1,0:T(8,128)S(1)} %get-tuple-element.25, ...), kind=kOutput, calls=%fused_computation.101 | convolution fusion | flops 202727424 | bytes 1655812 | tf_op jit(solution)/shard_map/dot_general | solution.py:132
  69.6 0.6 divide_bitcast_fusion
  70.2 0.9 fusion.27.s_ref
  71.1 0.9 fusion.19.b_ref
  72.0 21.1 %shard_map.111 = (bf16[128,4096]{1,0:T(8,128)(2,1)}, bf16[128,4096]{1,0:T(8,128)(2,1)}, bf16[128,4096]{1,0:T(8,128)(2,1)}, bf16[128,4096]{1,0:T(8,128)(2,1)}) custom-call(bf16[128,4096]{1,0:T(8,128)(2,1)} %q_ref.3, bf16[128,4096]{1,0:T(8,128)(2,1)} %k_ref.3, bf16[128,4096]{1,0:T(8,128)(2,1)} %v_ref.3, bf16[128,4096]{1,0:T(8,128)(2,1)} %g_ref.3, ...), custom_call_target="tpu_custom_call" | custom-call | tf_op jit(solution)/shard_map/pallas_call | solution.py:103
  (3 shorter events, 0.1 us)
Async XLA Ops:
  0.6 0.7 copy-start
  4.2 10.0 %copy-start.4 = (s32[4096]{0:T(1024)S(1)}, s32[4096]{0:T(1024)}, u32[]{:S(2)}) copy-start(s32[4096]{0:T(1024)} %param.13) | copy-start | bytes 49156
  14.2 3.0 %copy-start.1 = (f32[16,4096]{1,0:T(8,128)S(1)}, f32[16,4096]{1,0:T(8,128)}, u32[]{:S(2)}) copy-start(f32[16,4096]{1,0:T(8,128)} %get-tuple-element.12) | copy-start | bytes 786436
  14.2 3.0 %copy-start.2 = (f32[16,4096]{1,0:T(8,128)S(1)}, f32[16,4096]{1,0:T(8,128)}, u32[]{:S(2)}) copy-start(f32[16,4096]{1,0:T(8,128)} %get-tuple-element.13) | copy-start | bytes 786436
  17.2 2.1 %collective-permute-start = (f32[16,8448]{1,0:T(8,128)S(1)}, f32[16,8448]{1,0:T(8,128)S(1)}, u32[]{:S(2)}, u32[]{:S(2)}) collective-permute-start(f32[16,8448]{1,0:T(8,128)S(1)} %pad_maximum_fusion), channel_id=1, source_target_pairs={{0,1},{1,0},{2,3},{3,2},{4,5},{5,4},{6,7},{7,6},{8,9},{9,8},{10,11... | collective-permute-start | bytes 1622024 | tf_op jit(solution)/shard_map/ppermute | solution.py:146
  21.6 9.7 %collective-permute-start.1 = (f32[16,4224]{1,0:T(8,128)S(1)}, f32[16,4224]{1,0:T(8,128)S(1)}, u32[]{:S(2)}, u32[]{:S(2)}) collective-permute-start(f32[16,4224]{1,0:T(8,128)S(1)} %fusion.17), channel_id=1, source_target_pairs={{0,2},{1,3},{2,0},{3,1},{4,6},{5,7},{6,4},{7,5},{8,10},{9,11},{10,... | collective-permute-start | bytes 811016 | tf_op jit(solution)/shard_map/ppermute | solution.py:151
  31.4 1.5 %collective-permute-start.2 = (f32[16,4224]{1,0:T(8,128)S(1)}, f32[16,4224]{1,0:T(8,128)S(1)}, u32[]{:S(2)}, u32[]{:S(2)}) collective-permute-start(f32[16,4224]{1,0:T(8,128)S(1)} %collective-permute-done.1), channel_id=1, source_target_pairs={{0,1},{1,0},{2,3},{3,2},{4,5},{5,4},{6,7},{7,6},{8,9},{9,8},{10,11... | collective-permute-start | bytes 811016 | tf_op jit(solution)/shard_map/ppermute | solution.py:152
  35.2 8.6 %collective-permute-start.3 = (f32[16,4224]{1,0:T(8,128)S(1)}, f32[16,4224]{1,0:T(8,128)S(1)}, u32[]{:S(2)}, u32[]{:S(2)}) collective-permute-start(f32[16,4224]{1,0:T(8,128)S(1)} %fusion.15), channel_id=1, source_target_pairs={{0,4},{1,5},{2,6},{3,7},{4,0},{5,1},{6,2},{7,3},{8,12},{9,13},{10,... | collective-permute-start | bytes 811016 | tf_op jit(solution)/shard_map/ppermute | solution.py:151
  43.9 1.5 %collective-permute-start.4 = (f32[16,4224]{1,0:T(8,128)S(1)}, f32[16,4224]{1,0:T(8,128)S(1)}, u32[]{:S(2)}, u32[]{:S(2)}) collective-permute-start(f32[16,4224]{1,0:T(8,128)S(1)} %collective-permute-done.3), channel_id=1, source_target_pairs={{0,1},{1,0},{2,3},{3,2},{4,5},{5,4},{6,7},{7,6},{8,9},{9,8},{10,11... | collective-permute-start | bytes 811016 | tf_op jit(solution)/shard_map/ppermute | solution.py:152
  45.6 17.6 %copy-start.3 = (f32[256,16]{0,1:T(8,128)S(1)}, f32[256,16]{0,1:T(8,128)}, u32[]{:S(2)}) copy-start(f32[256,16]{0,1:T(8,128)} %param.12) | copy-start | bytes 49156
  47.8 15.4 %collective-permute-start.5 = (f32[16,4224]{1,0:T(8,128)S(1)}, f32[16,4224]{1,0:T(8,128)S(1)}, u32[]{:S(2)}, u32[]{:S(2)}) collective-permute-start(f32[16,4224]{1,0:T(8,128)S(1)} %fusion.13), channel_id=1, source_target_pairs={{0,8},{1,9},{2,10},{3,11},{4,12},{5,13},{6,14},{7,15},{8,0},{9,1},... | collective-permute-start | bytes 811016 | tf_op jit(solution)/shard_map/ppermute | solution.py:151
  63.2 2.1 %collective-permute-start.6 = (f32[16,4224]{1,0:T(8,128)S(1)}, f32[16,4224]{1,0:T(8,128)}, u32[]{:S(2)}, u32[]{:S(2)}) collective-permute-start(f32[16,4224]{1,0:T(8,128)S(1)} %collective-permute-done.5), channel_id=1, source_target_pairs={{0,1},{1,0},{2,3},{3,2},{4,5},{5,4},{6,7},{7,6},{8,9},{9,8},{10,11... | collective-permute-start | bytes 811016 | tf_op jit(solution)/shard_map/ppermute | solution.py:152

commit v6 on v5

--- a/solution.py
+++ b/solution.py
@@ -79,50 +79,58 @@
     vg_ref[...] = (mg * k_ref[...].astype(f32)).astype(jnp.bfloat16)
 
 
-def local_carries(query_proj, key_proj, value_proj, out_grad, factor):
+def local_carries(query_proj, key_proj, value_proj, out_grad, factor, first, blocks):
     rows, width = query_proj.shape
     modes = factor.shape[0]
-    big = pl.BlockSpec((rows, BLOCK), lambda i: (0, i))
+    big = pl.BlockSpec((rows, BLOCK), lambda i: (0, i + first))
     small = pl.BlockSpec((modes, BLOCK), lambda i: (0, i))
     return pl.pallas_call(
         carry_kernel,
-        grid=(width // BLOCK,),
+        grid=(blocks,),
         in_specs=[big, big, big, big, small],
         out_specs=[small, small, small],
-        out_shape=[jax.ShapeDtypeStruct((modes, width), jnp.float32)] * 3,
+        out_shape=[jax.ShapeDtypeStruct((modes, blocks * BLOCK), jnp.float32)] * 3,
         scratch_shapes=[pltpu.VMEM((rows, BLOCK), jnp.float32)] * 2,
     )(query_proj, key_proj, value_proj, out_grad, factor)
 
 
-def full_scans(query_proj, key_proj, value_proj, out_grad, factor, weight, state_in, adjoint_in):
+def full_scans(
+    query_proj, key_proj, value_proj, out_grad, factor, weight, state_in, adjoint_in,
+    first, blocks, previous,
+):
     rows, width = query_proj.shape
     modes = factor.shape[0]
-    big = pl.BlockSpec((rows, BLOCK), lambda i: (0, i))
+    big = pl.BlockSpec((rows, BLOCK), lambda i: (0, i + first))
     small = pl.BlockSpec((modes, BLOCK), lambda i: (0, i))
     out_big = jax.ShapeDtypeStruct((rows, width), jnp.bfloat16)
+    operands = [query_proj, key_proj, value_proj, out_grad, factor, weight, state_in, adjoint_in]
+    specs = [big, big, big, big, small, small, small, small]
+    aliases = {}
+    kernel = main_kernel
+    if previous is not None:
+        operands += list(previous)
+        specs += [pl.BlockSpec(memory_space=pl.ANY)] * 4
+        aliases = {8: 0, 9: 1, 10: 2, 11: 3}
+
+        def kernel(*refs):
+            main_kernel(*refs[:8], *refs[12:])
+
     return pl.pallas_call(
-        main_kernel,
-        grid=(width // BLOCK,),
-        in_specs=[big, big, big, big, small, small, small, small],
+        kernel,
+        grid=(blocks,),
+        in_specs=specs,
         out_specs=[big, big, big, big],
         out_shape=[out_big] * 4,
         scratch_shapes=[pltpu.VMEM((rows, BLOCK), jnp.float32)] * 4,
-    )(query_proj, key_proj, value_proj, out_grad, factor, weight, state_in, adjoint_in)
+        input_output_aliases=aliases,
+    )(*operands)
 
 
 def make_on_device(count):
-    def on_device(query_proj, key_proj, value_proj, out_grad, decay_rate, residue, group_of):
+    def exchange(query_proj, key_proj, value_proj, out_grad, rate, factor, member, first, blocks, rows, place):
         high = lax.Precision.HIGHEST
-        rows = query_proj.shape[0]
-        group_count = decay_rate.shape[0]
-        member = (group_of[None, :] == jnp.arange(group_count, dtype=jnp.int32)[:, None]).astype(
-            jnp.float32
-        )
-        rate = jnp.dot(decay_rate.T, member, precision=high)
-        weight = jnp.dot(residue.T, member, precision=high)
-        factor = jnp.exp(-rate)
         end_state, head_adjoint, local_total = local_carries(
-            query_proj, key_proj, value_proj, out_grad, factor
+            query_proj, key_proj, value_proj, out_grad, factor, first, blocks
         )
 
         def span(blocks):
@@ -131,7 +139,6 @@
         def grouped(a):
             return jnp.dot(a, member.T, precision=high)
 
-        place = lax.axis_index("ctx")
         fwd_cube = end_state
         bwd_cube = head_adjoint
         grad_cube = grouped(local_total)
@@ -150,9 +157,9 @@
                 mine = lax.dynamic_slice_in_dim(packed, core * half, half, axis=1)
                 got_mine = lax.ppermute(mine, "ctx", pairs)
                 got_other = lax.ppermute(got_mine, "ctx", [(i, i ^ 1) for i in range(count)])
-                first = jnp.where(core == 0, got_mine, got_other)
-                second = jnp.where(core == 0, got_other, got_mine)
-                got = jnp.concatenate([first, second], axis=1)
+                lead = jnp.where(core == 0, got_mine, got_other)
+                trail = jnp.where(core == 0, got_other, got_mine)
+                got = jnp.concatenate([lead, trail], axis=1)
             got_fwd = got[:, :width]
             got_bwd = got[:, width : 2 * width]
             got_grad = got[:, 2 * width :]
@@ -172,10 +179,37 @@
             bwd_cube = low_bwd + whole * high_bwd
             bit *= 2
 
-        hyena_out, query_grad, key_grad, value_grad = full_scans(
-            query_proj, key_proj, value_proj, out_grad, factor, weight, state_in, adjoint_in
+        return state_in, adjoint_in, grad_cube
+
+    def on_device(query_proj, key_proj, value_proj, out_grad, decay_rate, residue, group_of):
+        high = lax.Precision.HIGHEST
+        rows = query_proj.shape[0]
+        group_count = decay_rate.shape[0]
+        member = (group_of[None, :] == jnp.arange(group_count, dtype=jnp.int32)[:, None]).astype(
+            jnp.float32
         )
-        filter_grad = grad_cube.T
+        rate = jnp.dot(decay_rate.T, member, precision=high)
+        weight = jnp.dot(residue.T, member, precision=high)
+        factor = jnp.exp(-rate)
+        width = query_proj.shape[1]
+        pieces = 2 if width % (2 * BLOCK) == 0 else 1
+        blocks = width // BLOCK // pieces
+        place = lax.axis_index("ctx")
+        previous = None
+        grad_total = None
+        for piece in range(pieces):
+            lanes = slice(piece * blocks * BLOCK, (piece + 1) * blocks * BLOCK)
+            state_in, adjoint_in, grad_cube = exchange(
+                query_proj, key_proj, value_proj, out_grad, rate[:, lanes], factor[:, lanes],
+                member[:, lanes], piece * blocks, blocks, rows, place,
+            )
+            grad_total = grad_cube if grad_total is None else grad_total + grad_cube
+            previous = full_scans(
+                query_proj, key_proj, value_proj, out_grad, factor[:, lanes], weight[:, lanes],
+                state_in, adjoint_in, piece * blocks, blocks, previous,
+            )
+        hyena_out, query_grad, key_grad, value_grad = previous
+        filter_grad = grad_total.T
         filter_update = filter_grad / jnp.sqrt(jnp.mean(filter_grad * filter_grad) + 1e-06)
         return (hyena_out, query_grad, key_grad, value_grad, filter_update)
 

time: 93.5 us -> 110 us (1.18)
  starting transfers between devices: 8.16 us -> 13.5 us
  other arithmetic: 4.34 us -> 8.55 us
  Pallas kernels: 31 us -> 35 us
  waiting for transfers between devices: 30.8 us -> 33.4 us
    ppermute x7 -> x14, starting transfers between devices: 8.16 us -> 13.5 us  [the longest x6 12.5 us: exchange(): got_mine = lax.ppermute(mine, 'ctx', pairs)]
    pallas_call x2 -> x4, Pallas kernels: 31 us -> 35 us  [the longest x2 23.2 us: full_scans(): pl.pallas_call(kernel, grid=(blocks,), in_specs=specs, out_specs=[big, bi...]
    ppermute x7 -> x14, waiting for transfers between devices: 30.8 us -> 33.4 us  [the longest x6 30.3 us: exchange(): got_mine = lax.ppermute(mine, 'ctx', pairs)]
    slice x0 -> x2, local copies, waits for them, and re-layouts: none -> 1.48 us  [the longest x1 0.75 us: on_device(): factor[:, lanes]]
    eq x0 -> x1, other arithmetic: none -> 1.33 us  [on_device(): group_of[None, :] == jnp.arange(group_count, dtype=jnp.int32)[:, None]]
    add x5 -> x8, other arithmetic: 2.18 us -> 3.43 us  [the longest x6 1.9 us: exchange(): bwd_cube = low_bwd + whole * high_bwd]
    dot_general x5 -> x10, matrix products: 11.6 us -> 12.4 us  [grouped(): return jnp.dot(a, member.T, precision=high)]
  transfers between devices with their start and end apart: 7 -> 14, of which waited for: 6 -> 10; matrix products, arithmetic and copies ran while one was open for 2% -> 7% of each run, Pallas kernels for 0% -> 16%
where the time goes in v6:
time: 110 us; the launch traced here: 109 us
  Pallas kernels  35 us (32%)
  waiting for transfers between devices  33.4 us (30%)
  matrix products  15.2 us (14%)
  starting transfers between devices  13.5 us (12%)
  other arithmetic  8.55 us (8%)
  local copies, waits for them, and re-layouts  1.76 us (2%)
  between operations  1.64 us (1%)
    ppermute x6, waiting for transfers between devices, exchange(): got_mine = lax.ppermute(mine, 'ctx', pairs)  30.3 us
    pallas_call x2, Pallas kernels, full_scans(): pl.pallas_call(kernel, grid=(blocks,), in_specs=specs, out_specs=[big, bi...  23.2 us
    ppermute x6, starting transfers between devices, exchange(): got_mine = lax.ppermute(mine, 'ctx', pairs)  12.5 us
    dot_general x10, matrix products, grouped(): return jnp.dot(a, member.T, precision=high)  12.4 us
    pallas_call x2, Pallas kernels, local_carries(): pl.pallas_call(carry_kernel, grid=(blocks,), in_specs=[big, big, big, big...  11.8 us
  transfers between devices with their start and end apart: 14, of which 10 were waited for; matrix products, arithmetic and copies ran while one was open for 7% of the time, Pallas kernels for 16%

profile of v6, /device:TPU:0, one launch (start us, length us, event | category | flops | bytes accessed | tf_op | source)
XLA Modules:
  0.0 109.1 jit_solution(3150849724428745687)
XLA Ops:
  0.6 0.0 copy-start
  0.7 1.3 %iota_compare_fusion = pred[256,4096]{1,0:T(32,128)(4,1)S(1)} fusion(s32[4096]{0:T(1024)} %param.13), kind=kLoop, calls=%fused_computation.2 | loop fusion | flops 1048576 | bytes 1064960 | tf_op jit(solution)/shard_map/eq | solution.py:188
  2.0 1.4 %negate_exponential_fusion = (f32[16,4096]{1,0:T(8,128)S(1)}, f32[16,4096]{1,0:T(8,128)S(1)}) fusion(f32[256,16]{0,1:T(8,128)S(1)} %copy-done, s32[4096]{0:T(1024)S(1)} %copy-done.10), kind=kOutput, calls=%fused_computation.25 | convolution fusion | flops 202440704 | bytes 557056 | tf_op jit(solution)/shard_map/dot_general | solution.py:191
  3.4 0.8 fusion.103
  4.2 5.9 %shard_map.111 = (f32[16,2048]{1,0:T(8,128)}, f32[16,2048]{1,0:T(8,128)}, f32[16,2048]{1,0:T(8,128)}) custom-call(bf16[128,4096]{1,0:T(8,128)(2,1)} %refs_0_.1, bf16[128,4096]{1,0:T(8,128)(2,1)} %refs_1_.1, bf16[128,4096]{1,0:T(8,128)(2,1)} %refs_2_.1, bf16[128,4096]{1,0:T(8,128)(2,1)} %refs_3_.1, f32[16,2048]{1,0:T(8,128)} %get-tuple-element.65.p_ref), custom_call_target="tpu_custom_call" | custom-call | tf_op jit(solution)/shard_map/pallas_call | solution.py:87
  10.1 1.9 %fusion.48 = f32[16,256]{1,0:T(8,128)S(1)} fusion(f32[16,2048]{1,0:T(8,128)} %get-tuple-element.24, pred[256,4096]{1,0:T(32,128)(4,1)S(1)} %iota_compare_fusion), kind=kOutput, calls=%fused_computation.112 | convolution fusion | flops 100663296 | bytes 671744 | tf_op jit(solution)/shard_map/dot_general | solution.py:140
  11.9 0.0 copy-done.3
  12.0 0.5 collective-permute-start.7
  12.5 1.2 %collective-permute-done.7 = f32[16,4352]{1,0:T(8,128)S(1)} collective-permute-done((f32[16,4352]{1,0:T(8,128)S(1)}, f32[16,4352]{1,0:T(8,128)S(1)}, u32[]{:S(2)}, u32[]{:S(2)}) %collective-permute-start.7) | collective-permute-done | bytes 278560 | tf_op jit(solution)/shard_map/ppermute | solution.py:153
  13.7 1.0 add_add_fusion.3
  14.7 0.1 multiply_add_fusion.4
  14.8 0.1 fusion.7
  14.9 3.0 %collective-permute-start.8 = (f32[16,2176]{1,0:T(8,128)S(1)}, f32[16,2176]{1,0:T(8,128)S(1)}, u32[]{:S(2)}, u32[]{:S(2)}) collective-permute-start(f32[16,2176]{1,0:T(8,128)S(1)} %fusion.7), channel_id=1, source_target_pairs={{0,2},{1,3},{2,0},{3,1},{4,6},{5,7},{6,4},{7,5},{8,10},{9,11},{10,... | collective-permute-start | bytes 417800 | tf_op jit(solution)/shard_map/ppermute | solution.py:158
  17.8 4.0 %collective-permute-done.8 = f32[16,2176]{1,0:T(8,128)S(1)} collective-permute-done((f32[16,2176]{1,0:T(8,128)S(1)}, f32[16,2176]{1,0:T(8,128)S(1)}, u32[]{:S(2)}, u32[]{:S(2)}) %collective-permute-start.8) | collective-permute-done | bytes 139296 | tf_op jit(solution)/shard_map/ppermute | solution.py:158
  21.8 5.9 %shard_map.110 = (f32[16,2048]{1,0:T(8,128)}, f32[16,2048]{1,0:T(8,128)}, f32[16,2048]{1,0:T(8,128)}) custom-call(bf16[128,4096]{1,0:T(8,128)(2,1)} %refs_0_.1, bf16[128,4096]{1,0:T(8,128)(2,1)} %refs_1_.1, bf16[128,4096]{1,0:T(8,128)(2,1)} %refs_2_.1, bf16[128,4096]{1,0:T(8,128)(2,1)} %refs_3_.1, f32[16,2048]{1,0:T(8,128)} %get-tuple-element.66.p_ref.refs_4_), custom_call_target="tpu_custom_call" | custom-call | tf_op jit(solution)/shard_map/pallas_call | solution.py:87
  27.7 0.1 multiply_add_fusion.2
  27.8 1.0 add_add_fusion.2
  28.8 0.0 copy-start.13
  28.9 0.0 copy-start.2
  28.9 0.1 fusion.5
  29.0 1.9 %collective-permute-start.10 = (f32[16,2176]{1,0:T(8,128)S(1)}, f32[16,2176]{1,0:T(8,128)S(1)}, u32[]{:S(2)}, u32[]{:S(2)}) collective-permute-start(f32[16,2176]{1,0:T(8,128)S(1)} %fusion.5), channel_id=1, source_target_pairs={{0,4},{1,5},{2,6},{3,7},{4,0},{5,1},{6,2},{7,3},{8,12},{9,13},{10,... | collective-permute-start | bytes 417800 | tf_op jit(solution)/shard_map/ppermute | solution.py:158
  30.8 1.0 fusion.54
  31.8 0.0 copy-done.13
  31.9 3.3 %collective-permute-done.10 = f32[16,2176]{1,0:T(8,128)S(1)} collective-permute-done((f32[16,2176]{1,0:T(8,128)S(1)}, f32[16,2176]{1,0:T(8,128)S(1)}, u32[]{:S(2)}, u32[]{:S(2)}) %collective-permute-start.10) | collective-permute-done | bytes 139296 | tf_op jit(solution)/shard_map/ppermute | solution.py:158
  35.2 0.7 pad_maximum_fusion
  35.9 0.5 collective-permute-start
  36.4 0.1 collective-permute-done.11
  36.6 0.1 multiply_add_fusion
  36.6 0.0 copy-start.5
  36.6 1.8 %add_add_fusion.1 = f32[16,256]{1,0:T(8,128)S(1)} fusion(f32[16,256]{1,0:T(8,128)} %copy-done.13, f32[16,2176]{1,0:T(8,128)S(1)} %get-tuple-element.51, pred[]{:T(512)S(6)} %ne.55, pred[256,4096]{1,0:T(32,128)(4,1)S(1)} %iota_compare_fusion, f32[16,2048]{1,0:T(8,128)S(1)} %get-tuple-element.46, f32[16,2176]{1,0:T(8,128)S(1)} %get-tuple-element.52, ...), kind=kOutput, calls=%fused_computation.147 | convolution fusion | flops 100810752 | bytes 1229824 | tf_op jit(solution)/shard_map/dot_general | solution.py:140
  38.5 0.1 fusion.3
  38.6 2.8 %collective-permute-start.12 = (f32[16,2176]{1,0:T(8,128)S(1)}, f32[16,2176]{1,0:T(8,128)S(1)}, u32[]{:S(2)}, u32[]{:S(2)}) collective-permute-start(f32[16,2176]{1,0:T(8,128)S(1)} %fusion.3), channel_id=1, source_target_pairs={{0,8},{1,9},{2,10},{3,11},{4,12},{5,13},{6,14},{7,15},{8,0},{9,1},... | collective-permute-start | bytes 417800 | tf_op jit(solution)/shard_map/ppermute | solution.py:158
  41.4 7.0 %collective-permute-done.12 = f32[16,2176]{1,0:T(8,128)S(1)} collective-permute-done((f32[16,2176]{1,0:T(8,128)S(1)}, f32[16,2176]{1,0:T(8,128)S(1)}, u32[]{:S(2)}, u32[]{:S(2)}) %collective-permute-start.12) | collective-permute-done | bytes 139296 | tf_op jit(solution)/shard_map/ppermute | solution.py:158
  48.4 1.0 add_add_fusion.6
  49.4 0.0 copy-start.11
  49.4 0.3 collective-permute-done.13
  49.7 0.8 multiply_add_fusion.10
  50.6 0.1 fusion.13
  50.6 1.6 %collective-permute-start.1 = (f32[16,2176]{1,0:T(8,128)S(1)}, f32[16,2176]{1,0:T(8,128)S(1)}, u32[]{:S(2)}, u32[]{:S(2)}) collective-permute-start(f32[16,2176]{1,0:T(8,128)S(1)} %fusion.13), channel_id=1, source_target_pairs={{0,2},{1,3},{2,0},{3,1},{4,6},{5,7},{6,4},{7,5},{8,10},{9,11},{10,... | collective-permute-start | bytes 417800 | tf_op jit(solution)/shard_map/ppermute | solution.py:158
  52.3 4.2 %collective-permute-done.1 = f32[16,2176]{1,0:T(8,128)S(1)} collective-permute-done((f32[16,2176]{1,0:T(8,128)S(1)}, f32[16,2176]{1,0:T(8,128)S(1)}, u32[]{:S(2)}, u32[]{:S(2)}) %collective-permute-start.1) | collective-permute-done | bytes 139296 | tf_op jit(solution)/shard_map/ppermute | solution.py:158
  56.5 1.5 %collective-permute-done.2 = f32[16,2176]{1,0:T(8,128)} collective-permute-done((f32[16,2176]{1,0:T(8,128)S(1)}, f32[16,2176]{1,0:T(8,128)}, u32[]{:S(2)}, u32[]{:S(2)}) %collective-permute-start.2) | collective-permute-done | bytes 139296 | tf_op jit(solution)/shard_map/ppermute | solution.py:159
  58.0 0.9 broadcast_select_fusion.10
  59.0 0.8 multiply_add_fusion.8
  59.8 0.1 copy-done.8
  59.9 1.0 add_add_fusion.5
  60.9 0.1 fusion.11
  61.0 0.8 collective-permute-start.3
  61.8 5.0 %collective-permute-done.3 = f32[16,2176]{1,0:T(8,128)S(1)} collective-permute-done((f32[16,2176]{1,0:T(8,128)S(1)}, f32[16,2176]{1,0:T(8,128)S(1)}, u32[]{:S(2)}, u32[]{:S(2)}) %collective-permute-start.3) | collective-permute-done | bytes 139296 | tf_op jit(solution)/shard_map/ppermute | solution.py:158
  66.8 1.4 %convolution_bitcast_fusion = f32[16,4096]{1,0:T(8,128)S(1)} fusion(f32[256,16]{0,1:T(8,128)S(1)} %copy-done.15, s32[4096]{0:T(1024)S(1)} %copy-done.10), kind=kOutput, calls=%fused_computation | convolution fusion | flops 202375168 | bytes 294912 | tf_op jit(solution)/shard_map/dot_general | solution.py:192
  68.2 0.1 multiply_add_fusion.6
  68.3 1.0 add_add_fusion.4
  69.3 0.1 fusion.9
  69.4 2.4 %collective-permute-start.5 = (f32[16,2176]{1,0:T(8,128)S(1)}, f32[16,2176]{1,0:T(8,128)S(1)}, u32[]{:S(2)}, u32[]{:S(2)}) collective-permute-start(f32[16,2176]{1,0:T(8,128)S(1)} %fusion.9), channel_id=1, source_target_pairs={{0,8},{1,9},{2,10},{3,11},{4,12},{5,13},{6,14},{7,15},{8,0},{9,1},... | collective-permute-start | bytes 417800 | tf_op jit(solution)/shard_map/ppermute | solution.py:158
  71.8 0.7 fusion.102
  72.6 6.9 %collective-permute-done.5 = f32[16,2176]{1,0:T(8,128)S(1)} collective-permute-done((f32[16,2176]{1,0:T(8,128)S(1)}, f32[16,2176]{1,0:T(8,128)S(1)}, u32[]{:S(2)}, u32[]{:S(2)}) %collective-permute-start.5) | collective-permute-done | bytes 139296 | tf_op jit(solution)/shard_map/ppermute | solution.py:158
  79.4 1.0 fusion.19
  80.5 0.0 copy-start.9
  80.5 11.6 %shard_map.112 = (bf16[128,4096]{1,0:T(8,128)(2,1)}, bf16[128,4096]{1,0:T(8,128)(2,1)}, bf16[128,4096]{1,0:T(8,128)(2,1)}, bf16[128,4096]{1,0:T(8,128)(2,1)}) custom-call(bf16[128,4096]{1,0:T(8,128)(2,1)} %refs_0_.1, bf16[128,4096]{1,0:T(8,128)(2,1)} %refs_1_.1, bf16[128,4096]{1,0:T(8,128)(2,1)} %refs_2_.1, bf16[128,4096]{1,0:T(8,128)(2,1)} %refs_3_.1, ...), custom_call_target="tpu_custom_call" | custom-call | tf_op jit(solution)/shard_map/pallas_call | solution.py:118
  92.1 0.9 broadcast_select_fusion.6
  93.0 1.6 %multiply_reduce_fusion = (f32[]{:T(128)}, f32[16,256]{1,0:T(8,128)S(1)}) fusion(pred[256,4096]{1,0:T(32,128)(4,1)S(1)} %iota_compare_fusion, f32[16,2048]{1,0:T(8,128)S(1)} %get-tuple-element.37, f32[16,2048]{1,0:T(8,128)S(1)} %get-tuple-element.47, f32[16,2176]{1,0:T(8,128)S(1)} %get-tuple-element.56, pred[]{:T(512)S(6)} %ne.57, ...), kind=kOutput, calls=%fused_computation.145 | convolution fusion | flops 100872192 | bytes 1426436 | tf_op jit(solution)/shard_map/dot_general | solution.py:140
  95.4 0.6 divide_bitcast_fusion
  96.0 0.8 select_add_fusion.3.refs_6_
  96.8 0.8 select_add_fusion.2.refs_7_
  97.5 11.6 %shard_map.113 = (bf16[128,4096]{1,0:T(8,128)(2,1)}, bf16[128,4096]{1,0:T(8,128)(2,1)}, bf16[128,4096]{1,0:T(8,128)(2,1)}, bf16[128,4096]{1,0:T(8,128)(2,1)}) custom-call(bf16[128,4096]{1,0:T(8,128)(2,1)} %refs_0_.1, bf16[128,4096]{1,0:T(8,128)(2,1)} %refs_1_.1, ...), custom_call_target="tpu_custom_call", output_to_operand_aliasing={{0}: (8, {}), {1}: (9, {}), {2}: (10, {}), {3}: (11, {})} | custom-call | tf_op jit(solution)/shard_map/pallas_call | solution.py:118
  (38 shorter events, 0.2 us)
Async XLA Ops:
  0.6 1.4 %copy-start = (f32[256,16]{0,1:T(8,128)S(1)}, f32[256,16]{0,1:T(8,128)}, u32[]{:S(2)}) copy-start(f32[256,16]{0,1:T(8,128)} %param.11) | copy-start | bytes 49156
  0.6 1.4 %copy-start.10 = (s32[4096]{0:T(1024)S(1)}, s32[4096]{0:T(1024)}, u32[]{:S(2)}) copy-start(s32[4096]{0:T(1024)} %param.13) | copy-start | bytes 49156
  3.4 44.9 %copy-start.7 = (f32[16,4096]{1,0:T(8,128)}, f32[16,4096]{1,0:T(8,128)S(1)}, u32[]{:S(2)}) copy-start(f32[16,4096]{1,0:T(8,128)S(1)} %get-tuple-element.67) | copy-start | bytes 786436
  10.1 1.9 %copy-start.3 = (f32[16,2048]{1,0:T(8,128)S(1)}, f32[16,2048]{1,0:T(8,128)}, u32[]{:S(2)}) copy-start(f32[16,2048]{1,0:T(8,128)} %get-tuple-element.22) | copy-start | bytes 393220
  10.1 1.9 %copy-start.4 = (f32[16,2048]{1,0:T(8,128)S(1)}, f32[16,2048]{1,0:T(8,128)}, u32[]{:S(2)}) copy-start(f32[16,2048]{1,0:T(8,128)} %get-tuple-element.23) | copy-start | bytes 393220
  12.0 1.7 %collective-permute-start.7 = (f32[16,4352]{1,0:T(8,128)S(1)}, f32[16,4352]{1,0:T(8,128)S(1)}, u32[]{:S(2)}, u32[]{:S(2)}) collective-permute-start(f32[16,4352]{1,0:T(8,128)S(1)} %pad_maximum_fusion.1), channel_id=1, source_target_pairs={{0,1},{1,0},{2,3},{3,2},{4,5},{5,4},{6,7},{7,6},{8,9},{9,8},{10,11... | collective-permute-start | bytes 835592 | tf_op jit(solution)/shard_map/ppermute | solution.py:153
  14.9 6.9 %collective-permute-start.8 = (f32[16,2176]{1,0:T(8,128)S(1)}, f32[16,2176]{1,0:T(8,128)S(1)}, u32[]{:S(2)}, u32[]{:S(2)}) collective-permute-start(f32[16,2176]{1,0:T(8,128)S(1)} %fusion.7), channel_id=1, source_target_pairs={{0,2},{1,3},{2,0},{3,1},{4,6},{5,7},{6,4},{7,5},{8,10},{9,11},{10,... | collective-permute-start | bytes 417800 | tf_op jit(solution)/shard_map/ppermute | solution.py:158
  21.8 5.9 %collective-permute-start.9 = (f32[16,2176]{1,0:T(8,128)S(1)}, f32[16,2176]{1,0:T(8,128)S(1)}, u32[]{:S(2)}, u32[]{:S(2)}) collective-permute-start(f32[16,2176]{1,0:T(8,128)S(1)} %collective-permute-done.8), channel_id=1, source_target_pairs={{0,1},{1,0},{2,3},{3,2},{4,5},{5,4},{6,7},{7,6},{8,9},{9,8},{10,11... | collective-permute-start | bytes 417800 | tf_op jit(solution)/shard_map/ppermute | solution.py:159
  27.8 3.0 %copy-start.14 = (f32[16,2048]{1,0:T(8,128)S(1)}, f32[16,2048]{1,0:T(8,128)}, u32[]{:S(2)}) copy-start(f32[16,2048]{1,0:T(8,128)} %get-tuple-element.21) | copy-start | bytes 393220
  28.8 3.0 %copy-start.13 = (f32[16,256]{1,0:T(8,128)}, f32[16,256]{1,0:T(8,128)S(1)}, u32[]{:S(2)}) copy-start(f32[16,256]{1,0:T(8,128)S(1)} %add_add_fusion.2) | copy-start | bytes 49156
  28.9 6.3 %copy-start.1 = (f32[16,2048]{1,0:T(8,128)S(1)}, f32[16,2048]{1,0:T(8,128)}, u32[]{:S(2)}) copy-start(f32[16,2048]{1,0:T(8,128)} %get-tuple-element.19) | copy-start | bytes 393220
  28.9 6.3 %copy-start.2 = (f32[16,2048]{1,0:T(8,128)S(1)}, f32[16,2048]{1,0:T(8,128)}, u32[]{:S(2)}) copy-start(f32[16,2048]{1,0:T(8,128)} %get-tuple-element.20) | copy-start | bytes 393220
  29.0 6.2 %collective-permute-start.10 = (f32[16,2176]{1,0:T(8,128)S(1)}, f32[16,2176]{1,0:T(8,128)S(1)}, u32[]{:S(2)}, u32[]{:S(2)}) collective-permute-start(f32[16,2176]{1,0:T(8,128)S(1)} %fusion.5), channel_id=1, source_target_pairs={{0,4},{1,5},{2,6},{3,7},{4,0},{5,1},{6,2},{7,3},{8,12},{9,13},{10,... | collective-permute-start | bytes 417800 | tf_op jit(solution)/shard_map/ppermute | solution.py:158
  35.2 1.4 %collective-permute-start.11 = (f32[16,2176]{1,0:T(8,128)S(1)}, f32[16,2176]{1,0:T(8,128)S(1)}, u32[]{:S(2)}, u32[]{:S(2)}) collective-permute-start(f32[16,2176]{1,0:T(8,128)S(1)} %collective-permute-done.10), channel_id=1, source_target_pairs={{0,1},{1,0},{2,3},{3,2},{4,5},{5,4},{6,7},{7,6},{8,9},{9,8},{10,11... | collective-permute-start | bytes 417800 | tf_op jit(solution)/shard_map/ppermute | solution.py:159
  35.9 12.4 %collective-permute-start = (f32[16,4352]{1,0:T(8,128)}, f32[16,4352]{1,0:T(8,128)S(1)}, u32[]{:S(2)}, u32[]{:S(2)}) collective-permute-start(f32[16,4352]{1,0:T(8,128)} %pad_maximum_fusion), channel_id=1, source_target_pairs={{0,1},{1,0},{2,3},{3,2},{4,5},{5,4},{6,7},{7,6},{8,9},{9,8},{10,11... | collective-permute-start | bytes 835592 | tf_op jit(solution)/shard_map/ppermute | solution.py:153
  36.6 1.9 %copy-start.5 = (f32[16,2048]{1,0:T(8,128)}, f32[16,2048]{1,0:T(8,128)S(1)}, u32[]{:S(2)}) copy-start(f32[16,2048]{1,0:T(8,128)S(1)} %get-tuple-element.45) | copy-start | bytes 393220
  38.6 9.8 %collective-permute-start.12 = (f32[16,2176]{1,0:T(8,128)S(1)}, f32[16,2176]{1,0:T(8,128)S(1)}, u32[]{:S(2)}, u32[]{:S(2)}) collective-permute-start(f32[16,2176]{1,0:T(8,128)S(1)} %fusion.3), channel_id=1, source_target_pairs={{0,8},{1,9},{2,10},{3,11},{4,12},{5,13},{6,14},{7,15},{8,0},{9,1},... | collective-permute-start | bytes 417800 | tf_op jit(solution)/shard_map/ppermute | solution.py:158
  48.3 1.4 %collective-permute-start.13 = (f32[16,2176]{1,0:T(8,128)S(1)}, f32[16,2176]{1,0:T(8,128)S(1)}, u32[]{:S(2)}, u32[]{:S(2)}) collective-permute-start(f32[16,2176]{1,0:T(8,128)S(1)} %collective-permute-done.12), channel_id=1, source_target_pairs={{0,1},{1,0},{2,3},{3,2},{4,5},{5,4},{6,7},{7,6},{8,9},{9,8},{10,11... | collective-permute-start | bytes 417800 | tf_op jit(solution)/shard_map/ppermute | solution.py:159
  49.4 1.2 %copy-start.11 = (f32[16,256]{1,0:T(8,128)}, f32[16,256]{1,0:T(8,128)S(1)}, u32[]{:S(2)}) copy-start(f32[16,256]{1,0:T(8,128)S(1)} %add_add_fusion.6) | copy-start | bytes 49156
  50.6 5.9 %collective-permute-start.1 = (f32[16,2176]{1,0:T(8,128)S(1)}, f32[16,2176]{1,0:T(8,128)S(1)}, u32[]{:S(2)}, u32[]{:S(2)}) collective-permute-start(f32[16,2176]{1,0:T(8,128)S(1)} %fusion.13), channel_id=1, source_target_pairs={{0,2},{1,3},{2,0},{3,1},{4,6},{5,7},{6,4},{7,5},{8,10},{9,11},{10,... | collective-permute-start | bytes 417800 | tf_op jit(solution)/shard_map/ppermute | solution.py:158
  56.5 1.5 %collective-permute-start.2 = (f32[16,2176]{1,0:T(8,128)S(1)}, f32[16,2176]{1,0:T(8,128)}, u32[]{:S(2)}, u32[]{:S(2)}) collective-permute-start(f32[16,2176]{1,0:T(8,128)S(1)} %collective-permute-done.1), channel_id=1, source_target_pairs={{0,1},{1,0},{2,3},{3,2},{4,5},{5,4},{6,7},{7,6},{8,9},{9,8},{10,11... | collective-permute-start | bytes 417800 | tf_op jit(solution)/shard_map/ppermute | solution.py:159
  58.9 1.0 copy-start.8
  58.9 0.9 copy-start.12
  59.9 6.9 %copy-start.15 = (f32[256,16]{0,1:T(8,128)S(1)}, f32[256,16]{0,1:T(8,128)}, u32[]{:S(2)}) copy-start(f32[256,16]{0,1:T(8,128)} %param.12) | copy-start | bytes 49156
  61.0 5.8 %collective-permute-start.3 = (f32[16,2176]{1,0:T(8,128)S(1)}, f32[16,2176]{1,0:T(8,128)S(1)}, u32[]{:S(2)}, u32[]{:S(2)}) collective-permute-start(f32[16,2176]{1,0:T(8,128)S(1)} %fusion.11), channel_id=1, source_target_pairs={{0,4},{1,5},{2,6},{3,7},{4,0},{5,1},{6,2},{7,3},{8,12},{9,13},{10,... | collective-permute-start | bytes 417800 | tf_op jit(solution)/shard_map/ppermute | solution.py:158
  66.8 1.4 %collective-permute-start.4 = (f32[16,2176]{1,0:T(8,128)S(1)}, f32[16,2176]{1,0:T(8,128)S(1)}, u32[]{:S(2)}, u32[]{:S(2)}) collective-permute-start(f32[16,2176]{1,0:T(8,128)S(1)} %collective-permute-done.3), channel_id=1, source_target_pairs={{0,1},{1,0},{2,3},{3,2},{4,5},{5,4},{6,7},{7,6},{8,9},{9,8},{10,11... | collective-permute-start | bytes 417800 | tf_op jit(solution)/shard_map/ppermute | solution.py:159
  68.3 11.2 %copy-start.6 = (f32[16,2048]{1,0:T(8,128)S(1)}, f32[16,2048]{1,0:T(8,128)}, u32[]{:S(2)}) copy-start(f32[16,2048]{1,0:T(8,128)} %copy-done.5) | copy-start | bytes 393220
  69.4 10.0 %collective-permute-start.5 = (f32[16,2176]{1,0:T(8,128)S(1)}, f32[16,2176]{1,0:T(8,128)S(1)}, u32[]{:S(2)}, u32[]{:S(2)}) collective-permute-start(f32[16,2176]{1,0:T(8,128)S(1)} %fusion.9), channel_id=1, source_target_pairs={{0,8},{1,9},{2,10},{3,11},{4,12},{5,13},{6,14},{7,15},{8,0},{9,1},... | collective-permute-start | bytes 417800 | tf_op jit(solution)/shard_map/ppermute | solution.py:158
  79.4 12.7 %collective-permute-start.6 = (f32[16,2176]{1,0:T(8,128)S(1)}, f32[16,2176]{1,0:T(8,128)}, u32[]{:S(2)}, u32[]{:S(2)}) collective-permute-start(f32[16,2176]{1,0:T(8,128)S(1)} %collective-permute-done.5), channel_id=1, source_target_pairs={{0,1},{1,0},{2,3},{3,2},{4,5},{5,4},{6,7},{7,6},{8,9},{9,8},{10,11... | collective-permute-start | bytes 417800 | tf_op jit(solution)/shard_map/ppermute | solution.py:159
  80.5 12.6 %copy-start.9 = (f32[16,4096]{1,0:T(8,128)S(1)}, f32[16,4096]{1,0:T(8,128)}, u32[]{:S(2)}) copy-start(f32[16,4096]{1,0:T(8,128)} %copy-done.7) | copy-start | bytes 786436

commit v7 on v5

--- a/solution.py
+++ b/solution.py
@@ -8,6 +8,7 @@
 BLOCK = 1024
 SUB = 256
 ROWS = 8
+LANE = 128
 
 
 def carry_kernel(q_ref, k_ref, v_ref, g_ref, p_ref, xend_ref, head_ref, tot_ref, mix_ref, up_ref):
@@ -47,36 +48,37 @@
     mix_ref, up_ref, filt_ref, mg_ref,
 ):
     f32 = jnp.float32
-    mix_ref[...] = (k_ref[...].astype(f32) * v_ref[...].astype(f32)).astype(jnp.bfloat16).astype(f32)
-    up_ref[...] = g_ref[...].astype(f32) * q_ref[...].astype(f32)
-    rows, width = mix_ref.shape
-    chunks = rows // ROWS
-    for h in range(width // SUB):
-        cols = pl.ds(h * SUB, SUB)
-        p = p_ref[:, cols]
-        r = r_ref[:, cols]
-
-        def body(c, carry):
-            x, a = carry
-            fb = pl.multiple_of(c * ROWS, ROWS)
-            bb = pl.multiple_of((chunks - 1 - c) * ROWS, ROWS)
-            mt = mix_ref[pl.ds(fb, ROWS), cols]
-            ub = up_ref[pl.ds(bb, ROWS), cols]
-            for j in range(ROWS):
-                x = p * x + mt[j : j + 1, :]
-                filt_ref[pl.ds(fb + j, 1), cols] = jnp.sum(r * x, axis=0, keepdims=True)
-                jb = ROWS - 1 - j
-                a = p * a + ub[jb : jb + 1, :]
-                mg_ref[pl.ds(bb + jb, 1), cols] = jnp.sum(r * a, axis=0, keepdims=True)
-            return x, a
-
-        lax.fori_loop(0, chunks, body, (s_ref[:, cols], b_ref[:, cols]))
-    filt = filt_ref[...]
-    mg = mg_ref[...]
-    ho_ref[...] = (q_ref[...].astype(f32) * filt).astype(jnp.bfloat16)
-    qg_ref[...] = (g_ref[...].astype(f32) * filt).astype(jnp.bfloat16)
-    kg_ref[...] = (mg * v_ref[...].astype(f32)).astype(jnp.bfloat16)
-    vg_ref[...] = (mg * k_ref[...].astype(f32)).astype(jnp.bfloat16)
+    rows, width = q_ref.shape
+    lanes = width // LANE
+    for c in range(lanes):
+        cols = slice(c * LANE, (c + 1) * LANE)
+        band = slice(c * rows, (c + 1) * rows)
+        kf = k_ref[:, cols].astype(f32)
+        vf = v_ref[:, cols].astype(f32)
+        mix_ref[band, :] = (kf * vf).astype(jnp.bfloat16).astype(f32)
+        up_ref[band, :] = g_ref[:, cols].astype(f32) * q_ref[:, cols].astype(f32)
+
+    def body(t, carry):
+        x, a = carry
+        p = p_ref[...]
+        r = r_ref[...]
+        x = p * x + mix_ref[pl.ds(t, lanes, stride=rows), :][None]
+        filt_ref[pl.ds(t, lanes, stride=rows), :] = jnp.sum(r * x, axis=0)
+        tb = rows - 1 - t
+        a = p * a + up_ref[pl.ds(tb, lanes, stride=rows), :][None]
+        mg_ref[pl.ds(tb, lanes, stride=rows), :] = jnp.sum(r * a, axis=0)
+        return x, a
+
+    lax.fori_loop(0, rows, body, (s_ref[...], b_ref[...]), unroll=2)
+    for c in range(lanes):
+        cols = slice(c * LANE, (c + 1) * LANE)
+        band = slice(c * rows, (c + 1) * rows)
+        filt = filt_ref[band, :]
+        mg = mg_ref[band, :]
+        ho_ref[:, cols] = (q_ref[:, cols].astype(f32) * filt).astype(jnp.bfloat16)
+        qg_ref[:, cols] = (g_ref[:, cols].astype(f32) * filt).astype(jnp.bfloat16)
+        kg_ref[:, cols] = (mg * v_ref[:, cols].astype(f32)).astype(jnp.bfloat16)
+        vg_ref[:, cols] = (mg * k_ref[:, cols].astype(f32)).astype(jnp.bfloat16)
 
 
 def local_carries(query_proj, key_proj, value_proj, out_grad, factor):
@@ -97,17 +99,19 @@
 def full_scans(query_proj, key_proj, value_proj, out_grad, factor, weight, state_in, adjoint_in):
     rows, width = query_proj.shape
     modes = factor.shape[0]
+    lanes = BLOCK // LANE
     big = pl.BlockSpec((rows, BLOCK), lambda i: (0, i))
-    small = pl.BlockSpec((modes, BLOCK), lambda i: (0, i))
+    small = pl.BlockSpec((modes, lanes, LANE), lambda i: (0, i, 0))
     out_big = jax.ShapeDtypeStruct((rows, width), jnp.bfloat16)
+    tiles = [a.reshape(modes, width // LANE, LANE) for a in (factor, weight, state_in, adjoint_in)]
     return pl.pallas_call(
         main_kernel,
         grid=(width // BLOCK,),
         in_specs=[big, big, big, big, small, small, small, small],
         out_specs=[big, big, big, big],
         out_shape=[out_big] * 4,
-        scratch_shapes=[pltpu.VMEM((rows, BLOCK), jnp.float32)] * 4,
-    )(query_proj, key_proj, value_proj, out_grad, factor, weight, state_in, adjoint_in)
+        scratch_shapes=[pltpu.VMEM((lanes * rows, LANE), jnp.float32)] * 4,
+    )(query_proj, key_proj, value_proj, out_grad, *tiles)
 
 
 def make_on_device(count):

time: 93.5 us -> 92.1 us (0.985)
  local copies, waits for them, and re-layouts: 1.5 us -> 4.47 us
  Pallas kernels: 31 us -> 28.7 us
  other arithmetic: 4.34 us -> 2.94 us
    unnamed x10 -> x14, local copies, waits for them, and re-layouts: 0.75 us -> 3.73 us
    pallas_call x1, Pallas kernels: 21.1 us -> 18.8 us  [full_scans(): pl.pallas_call(main_kernel, grid=(width // BLOCK,), in_specs=[big, big, b...]
    add x2 -> x0, other arithmetic: 1.82 us -> none  [the longest x1 0.92 us: on_device(): adjoint_in + jnp.where(upper, 0.0, span(bit - 1 - offset) * got_bwd)]
  transfers between devices with their start and end apart: 7 -> 7, of which waited for: 6 -> 6; matrix products, arithmetic and copies ran while one was open for 2% -> 3% of each run, Pallas kernels for 0% -> 0%
where the time goes in v7:
time: 92.1 us; the launch traced here: 91.7 us
  waiting for transfers between devices  30.8 us (33%)
  Pallas kernels  28.7 us (31%)
  matrix products  15.2 us (17%)
  starting transfers between devices  8.16 us (9%)
  local copies, waits for them, and re-layouts  4.47 us (5%)
  other arithmetic  2.94 us (3%)
  between operations  1.44 us (2%)
    ppermute x3, waiting for transfers between devices, on_device(): got_mine = lax.ppermute(mine, 'ctx', pairs)  26.1 us
    pallas_call x1, Pallas kernels, full_scans(): pl.pallas_call(main_kernel, grid=(width // BLOCK,), in_specs=[big, big, b...  18.8 us
    dot_general x5, matrix products, grouped(): return jnp.dot(a, member.T, precision=high)  11.6 us
    pallas_call x1, Pallas kernels, local_carries(): pl.pallas_call(carry_kernel, grid=(width // BLOCK,), in_specs=[big, big,...  9.96 us
    ppermute x3, starting transfers between devices, on_device(): got_mine = lax.ppermute(mine, 'ctx', pairs)  7.63 us
    unnamed x14, local copies, waits for them, and re-layouts  3.73 us
    ppermute x3, waiting for transfers between devices, on_device(): lax.ppermute(got_mine, 'ctx', [(i, i ^ 1) for i in range(count)])  3.09 us
    dot_general x1, matrix products, on_device(): rate = jnp.dot(decay_rate.T, member, precision=high)  2.12 us
  transfers between devices with their start and end apart: 7, of which 6 were waited for; matrix products, arithmetic and copies ran while one was open for 3% of the time, Pallas kernels for 0%

profile of v7, /device:TPU:0, one launch (start us, length us, event | category | flops | bytes accessed | tf_op | source)
XLA Modules:
  0.0 91.7 jit_solution(7099388417484825676)
XLA Ops:
  0.6 0.0 copy-start
  0.6 0.7 copy-done
  1.4 2.1 %convolution_negate_fusion = f32[4096,16]{0,1:T(8,128)S(1)} fusion(f32[256,16]{0,1:T(8,128)S(1)} %copy-done, s32[4096]{0:T(1024)} %param.13), kind=kOutput, calls=%fused_computation | convolution fusion | flops 202440704 | bytes 294912 | tf_op jit(solution)/shard_map/dot_general | solution.py:125
  3.5 0.7 exponential_bitcast_fusion.1
  4.2 0.0 copy-start.4
  4.2 10.0 %shard_map.110 = (f32[16,4096]{1,0:T(8,128)}, f32[16,4096]{1,0:T(8,128)}, f32[16,4096]{1,0:T(8,128)}) custom-call(bf16[128,4096]{1,0:T(8,128)(2,1)} %q_ref.3, bf16[128,4096]{1,0:T(8,128)(2,1)} %k_ref.3, bf16[128,4096]{1,0:T(8,128)(2,1)} %v_ref.3, bf16[128,4096]{1,0:T(8,128)(2,1)} %g_ref.3, f32[16,4096]{1,0:T(8,128)} %get-tuple-element.33.p_ref), custom_call_target="tpu_custom_call" | custom-call | tf_op jit(solution)/shard_map/pallas_call | solution.py:89
  14.2 0.0 copy-start.1
  14.2 0.0 copy-start.2
  14.2 0.0 copy-done.4
  14.2 3.0 %fusion.4 = f32[16,256]{1,0:T(8,128)S(1)} fusion(f32[16,4096]{1,0:T(8,128)} %get-tuple-element.14, s32[4096]{0:T(1024)S(1)} %copy-done.4), kind=kOutput, calls=%fused_computation.6 | convolution fusion | flops 202375168 | bytes 294912 | tf_op jit(solution)/shard_map/dot_general | solution.py:136
  17.2 0.0 copy-done.1
  17.2 0.0 copy-done.2
  17.2 0.5 collective-permute-start
  17.8 1.6 %collective-permute-done = f32[16,8448]{1,0:T(8,128)S(1)} collective-permute-done((f32[16,8448]{1,0:T(8,128)S(1)}, f32[16,8448]{1,0:T(8,128)S(1)}, u32[]{:S(2)}, u32[]{:S(2)}) %collective-permute-start) | collective-permute-done | bytes 540704 | tf_op jit(solution)/shard_map/ppermute | solution.py:150
  19.3 2.0 %add_add_fusion.3 = f32[16,256]{1,0:T(8,128)S(1)} fusion(f32[16,256]{1,0:T(8,128)S(1)} %fusion.4, f32[16,8448]{1,0:T(8,128)S(1)} %collective-permute-done, pred[]{:T(512)S(6)} %ne.34, s32[4096]{0:T(1024)S(1)} %copy-done.4, f32[16,4096]{1,0:T(8,128)S(1)} %copy-done.2, f32[16,4096]{1,0:T(8,128)S(1)} %copy-done.1, f32[4096,16]{0,1:T(8,128)S(1)} %convolution_negate_fusion), kind=kOutput, calls=%fused_computation.109 | convolution fusion | flops 202653696 | bytes 1377280 | tf_op jit(solution)/shard_map/dot_general | solution.py:136
  21.3 0.1 fusion.37
  21.5 0.1 fusion.19
  21.6 3.0 %collective-permute-start.1 = (f32[16,4224]{1,0:T(8,128)S(1)}, f32[16,4224]{1,0:T(8,128)S(1)}, u32[]{:S(2)}, u32[]{:S(2)}) collective-permute-start(f32[16,4224]{1,0:T(8,128)S(1)} %fusion.19), channel_id=1, source_target_pairs={{0,2},{1,3},{2,0},{3,1},{4,6},{5,7},{6,4},{7,5},{8,10},{9,11},{10,... | collective-permute-start | bytes 811016 | tf_op jit(solution)/shard_map/ppermute | solution.py:155
  24.6 6.8 %collective-permute-done.1 = f32[16,4224]{1,0:T(8,128)S(1)} collective-permute-done((f32[16,4224]{1,0:T(8,128)S(1)}, f32[16,4224]{1,0:T(8,128)S(1)}, u32[]{:S(2)}, u32[]{:S(2)}) %collective-permute-start.1) | collective-permute-done | bytes 270368 | tf_op jit(solution)/shard_map/ppermute | solution.py:155
  31.4 0.0 collective-permute-start.2
  31.4 1.5 %collective-permute-done.2 = f32[16,4224]{1,0:T(8,128)S(1)} collective-permute-done((f32[16,4224]{1,0:T(8,128)S(1)}, f32[16,4224]{1,0:T(8,128)S(1)}, u32[]{:S(2)}, u32[]{:S(2)}) %collective-permute-start.2) | collective-permute-done | bytes 270368 | tf_op jit(solution)/shard_map/ppermute | solution.py:156
  32.9 0.1 fusion.33
  33.1 2.0 %add_add_fusion.2 = f32[16,256]{1,0:T(8,128)S(1)} fusion(f32[16,256]{1,0:T(8,128)S(1)} %add_add_fusion.3, f32[16,4224]{1,0:T(8,128)S(1)} %get-tuple-element.29, pred[]{:T(512)S(6)} %ne.35, s32[4096]{0:T(1024)S(1)} %copy-done.4, f32[16,4096]{1,0:T(8,128)S(1)} %get-tuple-element.24, f32[16,4224]{1,0:T(8,128)S(1)} %get-tuple-element.30, ...), kind=kOutput, calls=%fused_computation.108 | convolution fusion | flops 202653696 | bytes 1377280 | tf_op jit(solution)/shard_map/dot_general | solution.py:136
  35.1 0.1 fusion.17
  35.2 1.9 %collective-permute-start.3 = (f32[16,4224]{1,0:T(8,128)S(1)}, f32[16,4224]{1,0:T(8,128)S(1)}, u32[]{:S(2)}, u32[]{:S(2)}) collective-permute-start(f32[16,4224]{1,0:T(8,128)S(1)} %fusion.17), channel_id=1, source_target_pairs={{0,4},{1,5},{2,6},{3,7},{4,0},{5,1},{6,2},{7,3},{8,12},{9,13},{10,... | collective-permute-start | bytes 811016 | tf_op jit(solution)/shard_map/ppermute | solution.py:155
  37.1 6.8 %collective-permute-done.3 = f32[16,4224]{1,0:T(8,128)S(1)} collective-permute-done((f32[16,4224]{1,0:T(8,128)S(1)}, f32[16,4224]{1,0:T(8,128)S(1)}, u32[]{:S(2)}, u32[]{:S(2)}) %collective-permute-start.3) | collective-permute-done | bytes 270368 | tf_op jit(solution)/shard_map/ppermute | solution.py:155
  43.9 0.0 collective-permute-start.4
  43.9 1.5 %collective-permute-done.4 = f32[16,4224]{1,0:T(8,128)S(1)} collective-permute-done((f32[16,4224]{1,0:T(8,128)S(1)}, f32[16,4224]{1,0:T(8,128)S(1)}, u32[]{:S(2)}, u32[]{:S(2)}) %collective-permute-start.4) | collective-permute-done | bytes 270368 | tf_op jit(solution)/shard_map/ppermute | solution.py:156
  45.5 0.1 fusion.28
  45.6 0.0 copy-start.3
  45.6 2.0 %add_add_fusion.1 = f32[16,256]{1,0:T(8,128)S(1)} fusion(f32[16,256]{1,0:T(8,128)S(1)} %add_add_fusion.2, f32[16,4224]{1,0:T(8,128)S(1)} %get-tuple-element.27, pred[]{:T(512)S(6)} %ne.37, s32[4096]{0:T(1024)S(1)} %copy-done.4, f32[16,4096]{1,0:T(8,128)S(1)} %get-tuple-element.32, f32[16,4224]{1,0:T(8,128)S(1)} %get-tuple-element.28, ...), kind=kOutput, calls=%fused_computation.107 | convolution fusion | flops 202653696 | bytes 1377280 | tf_op jit(solution)/shard_map/dot_general | solution.py:136
  47.6 0.1 fusion.15
  47.8 2.8 %collective-permute-start.5 = (f32[16,4224]{1,0:T(8,128)S(1)}, f32[16,4224]{1,0:T(8,128)S(1)}, u32[]{:S(2)}, u32[]{:S(2)}) collective-permute-start(f32[16,4224]{1,0:T(8,128)S(1)} %fusion.15), channel_id=1, source_target_pairs={{0,8},{1,9},{2,10},{3,11},{4,12},{5,13},{6,14},{7,15},{8,0},{9,1},... | collective-permute-start | bytes 811016 | tf_op jit(solution)/shard_map/ppermute | solution.py:155
  50.6 12.6 %collective-permute-done.5 = f32[16,4224]{1,0:T(8,128)S(1)} collective-permute-done((f32[16,4224]{1,0:T(8,128)S(1)}, f32[16,4224]{1,0:T(8,128)S(1)}, u32[]{:S(2)}, u32[]{:S(2)}) %collective-permute-start.5) | collective-permute-done | bytes 270368 | tf_op jit(solution)/shard_map/ppermute | solution.py:155
  63.2 0.0 collective-permute-start.6
  63.2 0.0 copy-done.3
  63.2 1.4 %fusion.13 = f32[2,8,32,128]{3,1,2,0:T(8,128)S(1)} fusion(f32[256,16]{0,1:T(8,128)S(1)} %copy-done.3, s32[4096]{0:T(1024)S(1)} %copy-done.4), kind=kOutput, calls=%fused_computation.15 | convolution fusion | flops 202375168 | bytes 294912 | tf_op jit(solution)/shard_map/dot_general | solution.py:126
  64.6 0.7 copy.13
  65.3 0.7 copy.12
  66.1 0.0 collective-permute-done.6
  66.1 1.0 %broadcast_select_fusion = (f32[16,4224]{1,0:T(8,128)S(1)}, f32[16,4224]{1,0:T(8,128)S(1)}) fusion(f32[16,4224]{1,0:T(8,128)} %collective-permute-done.6, f32[16,4224]{1,0:T(8,128)S(1)} %collective-permute-done.5, pred[]{:T(512)S(6)} %eq.32), kind=kLoop, calls=%fused_computation.92 | loop fusion | flops 135168 | bytes 1081345 | tf_op jit(solution)/shard_map/jit(_where)/select_n | solution.py:158
  67.1 2.6 %multiply_reduce_fusion = (f32[]{:T(128)}, f32[16,256]{1,0:T(8,128)S(1)}) fusion(s32[4096]{0:T(1024)S(1)} %copy-done.4, f32[16,4096]{1,0:T(8,128)S(1)} %get-tuple-element.19, f32[16,4096]{1,0:T(8,128)S(1)} %get-tuple-element.31, f32[16,4224]{1,0:T(8,128)S(1)} %get-tuple-element.26, pred[]{:T(512)S(6)} %ne.39, f32[16,4224]{1,0:T(8,128)S(1)} %get-tuple-element.25, ...), kind=kOutput, calls=%fused_computation.105 | convolution fusion | flops 202727424 | bytes 1655812 | tf_op jit(solution)/shard_map/dot_general | solution.py:136
  70.4 0.2 fusion.22
  70.6 0.8 copy.15
  71.4 0.2 fusion.31
  71.6 0.7 copy.14
  72.3 0.6 divide_bitcast_fusion
  72.9 18.8 %shard_map.111 = (bf16[128,4096]{1,0:T(8,128)(2,1)}, bf16[128,4096]{1,0:T(8,128)(2,1)}, bf16[128,4096]{1,0:T(8,128)(2,1)}, bf16[128,4096]{1,0:T(8,128)(2,1)}) custom-call(bf16[128,4096]{1,0:T(8,128)(2,1)} %q_ref.3, bf16[128,4096]{1,0:T(8,128)(2,1)} %k_ref.3, bf16[128,4096]{1,0:T(8,128)(2,1)} %v_ref.3, bf16[128,4096]{1,0:T(8,128)(2,1)} %g_ref.3, ...), custom_call_target="tpu_custom_call" | custom-call | tf_op jit(solution)/shard_map/pallas_call | solution.py:107
  (3 shorter events, 0.1 us)
Async XLA Ops:
  0.6 0.7 copy-start
  4.2 10.0 %copy-start.4 = (s32[4096]{0:T(1024)S(1)}, s32[4096]{0:T(1024)}, u32[]{:S(2)}) copy-start(s32[4096]{0:T(1024)} %param.13) | copy-start | bytes 49156
  14.2 3.0 %copy-start.1 = (f32[16,4096]{1,0:T(8,128)S(1)}, f32[16,4096]{1,0:T(8,128)}, u32[]{:S(2)}) copy-start(f32[16,4096]{1,0:T(8,128)} %get-tuple-element.12) | copy-start | bytes 786436
  14.2 3.0 %copy-start.2 = (f32[16,4096]{1,0:T(8,128)S(1)}, f32[16,4096]{1,0:T(8,128)}, u32[]{:S(2)}) copy-start(f32[16,4096]{1,0:T(8,128)} %get-tuple-element.13) | copy-start | bytes 786436
  17.2 2.1 %collective-permute-start = (f32[16,8448]{1,0:T(8,128)S(1)}, f32[16,8448]{1,0:T(8,128)S(1)}, u32[]{:S(2)}, u32[]{:S(2)}) collective-permute-start(f32[16,8448]{1,0:T(8,128)S(1)} %pad_maximum_fusion), channel_id=1, source_target_pairs={{0,1},{1,0},{2,3},{3,2},{4,5},{5,4},{6,7},{7,6},{8,9},{9,8},{10,11... | collective-permute-start | bytes 1622024 | tf_op jit(solution)/shard_map/ppermute | solution.py:150
  21.6 9.7 %collective-permute-start.1 = (f32[16,4224]{1,0:T(8,128)S(1)}, f32[16,4224]{1,0:T(8,128)S(1)}, u32[]{:S(2)}, u32[]{:S(2)}) collective-permute-start(f32[16,4224]{1,0:T(8,128)S(1)} %fusion.19), channel_id=1, source_target_pairs={{0,2},{1,3},{2,0},{3,1},{4,6},{5,7},{6,4},{7,5},{8,10},{9,11},{10,... | collective-permute-start | bytes 811016 | tf_op jit(solution)/shard_map/ppermute | solution.py:155
  31.4 1.5 %collective-permute-start.2 = (f32[16,4224]{1,0:T(8,128)S(1)}, f32[16,4224]{1,0:T(8,128)S(1)}, u32[]{:S(2)}, u32[]{:S(2)}) collective-permute-start(f32[16,4224]{1,0:T(8,128)S(1)} %collective-permute-done.1), channel_id=1, source_target_pairs={{0,1},{1,0},{2,3},{3,2},{4,5},{5,4},{6,7},{7,6},{8,9},{9,8},{10,11... | collective-permute-start | bytes 811016 | tf_op jit(solution)/shard_map/ppermute | solution.py:156
  35.2 8.6 %collective-permute-start.3 = (f32[16,4224]{1,0:T(8,128)S(1)}, f32[16,4224]{1,0:T(8,128)S(1)}, u32[]{:S(2)}, u32[]{:S(2)}) collective-permute-start(f32[16,4224]{1,0:T(8,128)S(1)} %fusion.17), channel_id=1, source_target_pairs={{0,4},{1,5},{2,6},{3,7},{4,0},{5,1},{6,2},{7,3},{8,12},{9,13},{10,... | collective-permute-start | bytes 811016 | tf_op jit(solution)/shard_map/ppermute | solution.py:155
  43.9 1.5 %collective-permute-start.4 = (f32[16,4224]{1,0:T(8,128)S(1)}, f32[16,4224]{1,0:T(8,128)S(1)}, u32[]{:S(2)}, u32[]{:S(2)}) collective-permute-start(f32[16,4224]{1,0:T(8,128)S(1)} %collective-permute-done.3), channel_id=1, source_target_pairs={{0,1},{1,0},{2,3},{3,2},{4,5},{5,4},{6,7},{7,6},{8,9},{9,8},{10,11... | collective-permute-start | bytes 811016 | tf_op jit(solution)/shard_map/ppermute | solution.py:156
  45.6 17.6 %copy-start.3 = (f32[256,16]{0,1:T(8,128)S(1)}, f32[256,16]{0,1:T(8,128)}, u32[]{:S(2)}) copy-start(f32[256,16]{0,1:T(8,128)} %param.12) | copy-start | bytes 49156
  47.8 15.4 %collective-permute-start.5 = (f32[16,4224]{1,0:T(8,128)S(1)}, f32[16,4224]{1,0:T(8,128)S(1)}, u32[]{:S(2)}, u32[]{:S(2)}) collective-permute-start(f32[16,4224]{1,0:T(8,128)S(1)} %fusion.15), channel_id=1, source_target_pairs={{0,8},{1,9},{2,10},{3,11},{4,12},{5,13},{6,14},{7,15},{8,0},{9,1},... | collective-permute-start | bytes 811016 | tf_op jit(solution)/shard_map/ppermute | solution.py:155
  63.2 2.9 %collective-permute-start.6 = (f32[16,4224]{1,0:T(8,128)S(1)}, f32[16,4224]{1,0:T(8,128)}, u32[]{:S(2)}, u32[]{:S(2)}) collective-permute-start(f32[16,4224]{1,0:T(8,128)S(1)} %collective-permute-done.5), channel_id=1, source_target_pairs={{0,1},{1,0},{2,3},{3,2},{4,5},{5,4},{6,7},{7,6},{8,9},{9,8},{10,11... | collective-permute-start | bytes 811016 | tf_op jit(solution)/shard_map/ppermute | solution.py:156

commit v8 on v7

--- a/solution.py
+++ b/solution.py
@@ -42,12 +42,11 @@
         tot_ref[:, cols] = tot
 
 
-def main_kernel(
-    q_ref, k_ref, v_ref, g_ref, p_ref, r_ref, s_ref, b_ref,
-    ho_ref, qg_ref, kg_ref, vg_ref,
-    mix_ref, up_ref, filt_ref, mg_ref,
-):
+def local_kernel(q_ref, k_ref, v_ref, g_ref, p_ref, r_ref, *refs):
     f32 = jnp.float32
+    if len(refs) == 8:
+        refs = refs[2:]
+    filt_out, mg_out, mix_ref, up_ref, filt_ref, mg_ref = refs
     rows, width = q_ref.shape
     lanes = width // LANE
     for c in range(lanes):
@@ -69,12 +68,40 @@
         mg_ref[pl.ds(tb, lanes, stride=rows), :] = jnp.sum(r * a, axis=0)
         return x, a
 
-    lax.fori_loop(0, rows, body, (s_ref[...], b_ref[...]), unroll=2)
+    zero = jnp.zeros(p_ref.shape, f32)
+    lax.fori_loop(0, rows, body, (zero, zero), unroll=2)
     for c in range(lanes):
         cols = slice(c * LANE, (c + 1) * LANE)
         band = slice(c * rows, (c + 1) * rows)
-        filt = filt_ref[band, :]
-        mg = mg_ref[band, :]
+        filt_out[:, cols] = filt_ref[band, :]
+        mg_out[:, cols] = mg_ref[band, :]
+
+
+def correct_kernel(
+    q_ref, k_ref, v_ref, g_ref, fl_ref, ml_ref, p_ref, r_ref, s_ref, b_ref,
+    ho_ref, qg_ref, kg_ref, vg_ref,
+    filt_ref, mg_ref,
+):
+    f32 = jnp.float32
+    rows, width = q_ref.shape
+    lanes = width // LANE
+
+    def body(t, carry):
+        z, w = carry
+        p = p_ref[...]
+        filt_ref[pl.ds(t, lanes, stride=rows), :] = jnp.sum(z, axis=0)
+        tb = rows - 1 - t
+        mg_ref[pl.ds(tb, lanes, stride=rows), :] = jnp.sum(w, axis=0)
+        return z * p, w * p
+
+    p = p_ref[...]
+    r = r_ref[...]
+    lax.fori_loop(0, rows, body, ((r * p) * s_ref[...], (r * p) * b_ref[...]), unroll=2)
+    for c in range(lanes):
+        cols = slice(c * LANE, (c + 1) * LANE)
+        band = slice(c * rows, (c + 1) * rows)
+        filt = fl_ref[:, cols] + filt_ref[band, :]
+        mg = ml_ref[:, cols] + mg_ref[band, :]
         ho_ref[:, cols] = (q_ref[:, cols].astype(f32) * filt).astype(jnp.bfloat16)
         qg_ref[:, cols] = (g_ref[:, cols].astype(f32) * filt).astype(jnp.bfloat16)
         kg_ref[:, cols] = (mg * v_ref[:, cols].astype(f32)).astype(jnp.bfloat16)
@@ -96,22 +123,46 @@
     )(query_proj, key_proj, value_proj, out_grad, factor)
 
 
-def full_scans(query_proj, key_proj, value_proj, out_grad, factor, weight, state_in, adjoint_in):
+def local_scans(query_proj, key_proj, value_proj, out_grad, factor4, weight4, first, previous):
     rows, width = query_proj.shape
-    modes = factor.shape[0]
+    modes = factor4.shape[0]
+    lanes = BLOCK // LANE
+    big = pl.BlockSpec((rows, BLOCK), lambda i: (0, i + first))
+    small = pl.BlockSpec((modes, lanes, LANE), lambda i: (0, i + first, 0))
+    operands = [query_proj, key_proj, value_proj, out_grad, factor4, weight4]
+    specs = [big, big, big, big, small, small]
+    aliases = {}
+    if previous is not None:
+        operands += list(previous)
+        specs += [pl.BlockSpec(memory_space=pl.ANY)] * 2
+        aliases = {6: 0, 7: 1}
+    return pl.pallas_call(
+        local_kernel,
+        grid=(1,),
+        in_specs=specs,
+        out_specs=[big, big],
+        out_shape=[jax.ShapeDtypeStruct((rows, width), jnp.float32)] * 2,
+        scratch_shapes=[pltpu.VMEM((lanes * rows, LANE), jnp.float32)] * 4,
+        input_output_aliases=aliases,
+    )(*operands)
+
+
+def corrected(query_proj, key_proj, value_proj, out_grad, local, factor4, weight4, state_in, adjoint_in):
+    rows, width = query_proj.shape
+    modes = factor4.shape[0]
     lanes = BLOCK // LANE
     big = pl.BlockSpec((rows, BLOCK), lambda i: (0, i))
     small = pl.BlockSpec((modes, lanes, LANE), lambda i: (0, i, 0))
     out_big = jax.ShapeDtypeStruct((rows, width), jnp.bfloat16)
-    tiles = [a.reshape(modes, width // LANE, LANE) for a in (factor, weight, state_in, adjoint_in)]
+    tiles = [a.reshape(modes, width // LANE, LANE) for a in (state_in, adjoint_in)]
     return pl.pallas_call(
-        main_kernel,
+        correct_kernel,
         grid=(width // BLOCK,),
-        in_specs=[big, big, big, big, small, small, small, small],
+        in_specs=[big] * 6 + [small] * 4,
         out_specs=[big, big, big, big],
         out_shape=[out_big] * 4,
-        scratch_shapes=[pltpu.VMEM((lanes * rows, LANE), jnp.float32)] * 4,
-    )(query_proj, key_proj, value_proj, out_grad, *tiles)
+        scratch_shapes=[pltpu.VMEM((lanes * rows, LANE), jnp.float32)] * 2,
+    )(query_proj, key_proj, value_proj, out_grad, *local, factor4, weight4, *tiles)
 
 
 def make_on_device(count):
@@ -128,6 +179,13 @@
         end_state, head_adjoint, local_total = local_carries(
             query_proj, key_proj, value_proj, out_grad, factor
         )
+        width = query_proj.shape[1]
+        modes = factor.shape[0]
+        factor4 = factor.reshape(modes, width // LANE, LANE)
+        weight4 = weight.reshape(modes, width // LANE, LANE)
+        pieces = width // BLOCK
+        local = None
+        made = 0
 
         def span(blocks):
             return jnp.exp(-rate * (blocks * float(rows)))
@@ -142,10 +200,12 @@
         state_in = jnp.zeros_like(end_state)
         adjoint_in = jnp.zeros_like(head_adjoint)
         bit = 1
+        level = 0
         while bit < count:
             pairs = [(i, i ^ bit) for i in range(count)]
-            width = fwd_cube.shape[1]
             packed = jnp.concatenate([fwd_cube, bwd_cube, grad_cube], axis=1)
+            need = min(pieces, level)
+            level += 1
             if bit == 1:
                 got = lax.ppermute(packed, "ctx", pairs)
             else:
@@ -153,6 +213,14 @@
                 core = place % 2
                 mine = lax.dynamic_slice_in_dim(packed, core * half, half, axis=1)
                 got_mine = lax.ppermute(mine, "ctx", pairs)
+                if need > made:
+                    while made < need:
+                        local = local_scans(
+                            query_proj, key_proj, value_proj, out_grad, factor4, weight4, made,
+                            local,
+                        )
+                        made += 1
+                    got_mine, local = lax.optimization_barrier((got_mine, local))
                 got_other = lax.ppermute(got_mine, "ctx", [(i, i ^ 1) for i in range(count)])
                 first = jnp.where(core == 0, got_mine, got_other)
                 second = jnp.where(core == 0, got_other, got_mine)
@@ -176,8 +244,13 @@
             bwd_cube = low_bwd + whole * high_bwd
             bit *= 2
 
-        hyena_out, query_grad, key_grad, value_grad = full_scans(
-            query_proj, key_proj, value_proj, out_grad, factor, weight, state_in, adjoint_in
+        while made < pieces:
+            local = local_scans(
+                query_proj, key_proj, value_proj, out_grad, factor4, weight4, made, local
+            )
+            made += 1
+        hyena_out, query_grad, key_grad, value_grad = corrected(
+            query_proj, key_proj, value_proj, out_grad, local, factor4, weight4, state_in, adjoint_in
         )
         filter_grad = grad_cube.T
         filter_update = filter_grad / jnp.sqrt(jnp.mean(filter_grad * filter_grad) + 1e-06)

time: 92.1 us -> 92 us (level)
  waiting for transfers between devices: 30.8 us -> 12 us
  Pallas kernels: 28.7 us -> 46.5 us
  other arithmetic: 2.94 us -> 3.98 us
    ppermute x3, waiting for transfers between devices: 26.1 us -> 7.37 us  [on_device(): got_mine = lax.ppermute(mine, 'ctx', pairs)]
    pallas_call x1 -> x5, Pallas kernels: 18.8 us -> 36.6 us  [the longest x4 24.5 us: local_scans(): pl.pallas_call(local_kernel, grid=(1,), in_specs=specs, out_specs=[big, b...]
    concatenate x4, other arithmetic: 0.48 us -> 1.53 us  [on_device(): packed = jnp.concatenate([fwd_cube, bwd_cube, grad_cube], axis=1)]
  transfers between devices with their start and end apart: 7 -> 7, of which waited for: 6 -> 5; matrix products, arithmetic and copies ran while one was open for 3% -> 3% of each run, Pallas kernels for 0% -> 27%
where the time goes in v8:
time: 92 us; the launch traced here: 91.6 us
  Pallas kernels  46.5 us (51%)
  matrix products  15.1 us (16%)
  waiting for transfers between devices  12 us (13%)
  starting transfers between devices  7.77 us (8%)
  local copies, waits for them, and re-layouts  4.52 us (5%)
  other arithmetic  3.98 us (4%)
  between operations  1.59 us (2%)
    pallas_call x4, Pallas kernels, local_scans(): pl.pallas_call(local_kernel, grid=(1,), in_specs=specs, out_specs=[big, b...  24.5 us
    pallas_call x1, Pallas kernels, corrected(): pl.pallas_call(correct_kernel, grid=(width // BLOCK,), in_specs=[big] * 6...  12.1 us
    dot_general x5, matrix products, grouped(): return jnp.dot(a, member.T, precision=high)  11.6 us
    pallas_call x1, Pallas kernels, local_carries(): pl.pallas_call(carry_kernel, grid=(width // BLOCK,), in_specs=[big, big,...  9.96 us
    ppermute x3, waiting for transfers between devices, on_device(): got_mine = lax.ppermute(mine, 'ctx', pairs)  7.37 us
    ppermute x3, starting transfers between devices, on_device(): got_mine = lax.ppermute(mine, 'ctx', pairs)  7.25 us
    unnamed x14, local copies, waits for them, and re-layouts  3.77 us
    ppermute x3, waiting for transfers between devices, on_device(): lax.ppermute(got_mine, 'ctx', [(i, i ^ 1) for i in range(count)])  3.08 us
  transfers between devices with their start and end apart: 7, of which 5 were waited for; matrix products, arithmetic and copies ran while one was open for 3% of the time, Pallas kernels for 27%

profile of v8, /device:TPU:0, one launch (start us, length us, event | category | flops | bytes accessed | tf_op | source)
XLA Modules:
  0.0 91.6 jit_solution(6257410491150479310)
XLA Ops:
  0.6 0.0 copy-start
  0.6 0.7 copy-done
  1.4 2.1 %convolution_negate_fusion = f32[4096,16]{0,1:T(8,128)S(1)} fusion(f32[256,16]{0,1:T(8,128)S(1)} %copy-done, s32[4096]{0:T(1024)} %param.13), kind=kOutput, calls=%fused_computation | convolution fusion | flops 202440704 | bytes 294912 | tf_op jit(solution)/shard_map/dot_general | solution.py:176
  3.5 0.7 exponential_bitcast_fusion.1
  4.2 0.0 copy-start.4
  4.2 10.0 %shard_map.110 = (f32[16,4096]{1,0:T(8,128)}, f32[16,4096]{1,0:T(8,128)}, f32[16,4096]{1,0:T(8,128)}) custom-call(bf16[128,4096]{1,0:T(8,128)(2,1)} %q_ref.11, bf16[128,4096]{1,0:T(8,128)(2,1)} %k_ref.11, bf16[128,4096]{1,0:T(8,128)(2,1)} %v_ref.11, bf16[128,4096]{1,0:T(8,128)(2,1)} %g_ref.11, f32[16,4096]{1,0:T(8,128)} %get-tuple-element.67.p_ref), custom_call_target="tpu_custom_call" | custom-call | tf_op jit(solution)/shard_map/pallas_call | solution.py:116
  14.2 0.0 copy-start.1
  14.2 0.0 copy-start.2
  14.2 0.0 copy-done.4
  14.2 3.0 %fusion.4 = f32[16,256]{1,0:T(8,128)S(1)} fusion(f32[16,4096]{1,0:T(8,128)} %get-tuple-element.31, s32[4096]{0:T(1024)S(1)} %copy-done.4), kind=kOutput, calls=%fused_computation.6 | convolution fusion | flops 202375168 | bytes 294912 | tf_op jit(solution)/shard_map/dot_general | solution.py:194
  17.2 1.1 %pad_maximum_fusion = f32[16,8448]{1,0:T(8,128)S(1)} fusion(f32[16,256]{1,0:T(8,128)S(1)} %fusion.4, f32[16,4096]{1,0:T(8,128)} %get-tuple-element.30, f32[16,4096]{1,0:T(8,128)} %get-tuple-element.29), kind=kLoop, calls=%fused_computation.16 | loop fusion | flops 270336 | bytes 1081344 | tf_op jit(solution)/shard_map/concatenate | solution.py:206
  18.2 0.5 collective-permute-start
  18.8 0.0 copy-start.3
  18.8 1.6 %collective-permute-done = f32[16,8448]{1,0:T(8,128)S(1)} collective-permute-done((f32[16,8448]{1,0:T(8,128)S(1)}, f32[16,8448]{1,0:T(8,128)S(1)}, u32[]{:S(2)}, u32[]{:S(2)}) %collective-permute-start) | collective-permute-done | bytes 540704 | tf_op jit(solution)/shard_map/ppermute | solution.py:210
  20.3 0.0 copy-done.1
  20.3 0.0 copy-done.2
  20.3 2.0 %add_add_fusion.3 = f32[16,256]{1,0:T(8,128)S(1)} fusion(f32[16,256]{1,0:T(8,128)S(1)} %fusion.4, f32[16,8448]{1,0:T(8,128)S(1)} %collective-permute-done, pred[]{:T(512)S(6)} %ne.36, s32[4096]{0:T(1024)S(1)} %copy-done.4, f32[16,4096]{1,0:T(8,128)S(1)} %copy-done.2, f32[16,4096]{1,0:T(8,128)S(1)} %copy-done.1, f32[4096,16]{0,1:T(8,128)S(1)} %convolution_negate_fusion), kind=kOutput, calls=%fused_computation.109 | convolution fusion | flops 202653696 | bytes 1377280 | tf_op jit(solution)/shard_map/dot_general | solution.py:194
  22.3 0.1 fusion.41
  22.5 0.1 fusion.19
  22.6 3.0 %collective-permute-start.1 = (f32[16,4224]{1,0:T(8,128)S(1)}, f32[16,4224]{1,0:T(8,128)S(1)}, u32[]{:S(2)}, u32[]{:S(2)}) collective-permute-start(f32[16,4224]{1,0:T(8,128)S(1)} %fusion.19), channel_id=1, source_target_pairs={{0,2},{1,3},{2,0},{3,1},{4,6},{5,7},{6,4},{7,5},{8,10},{9,11},{10,... | collective-permute-start | bytes 811016 | tf_op jit(solution)/shard_map/ppermute | solution.py:215
  25.6 0.8 copy.18
  26.3 0.0 copy-done.3
  26.3 1.4 %fusion.13 = f32[2,8,32,128]{3,1,2,0:T(8,128)S(1)} fusion(f32[256,16]{0,1:T(8,128)S(1)} %copy-done.3, s32[4096]{0:T(1024)S(1)} %copy-done.4), kind=kOutput, calls=%fused_computation.15 | convolution fusion | flops 202375168 | bytes 294912 | tf_op jit(solution)/shard_map/dot_general | solution.py:177
  27.7 0.8 copy.19
  28.5 6.1 %shard_map.111 = (f32[128,4096]{1,0:T(8,128)}, f32[128,4096]{1,0:T(8,128)}) custom-call(bf16[128,4096]{1,0:T(8,128)(2,1)} %q_ref.11, bf16[128,4096]{1,0:T(8,128)(2,1)} %k_ref.11, bf16[128,4096]{1,0:T(8,128)(2,1)} %v_ref.11, bf16[128,4096]{1,0:T(8,128)(2,1)} %g_ref.11, f32[16,32,128]{2,1,0:T(8,128)} %bitcast.120, f32[16,32,128]{2,1,0:T(8,128)} %bitcast.125), custom_call_target="tpu_custom_call" | custom-call | tf_op jit(solution)/shard_map/pallas_call | solution.py:139
  34.6 0.0 collective-permute-done.1
  34.6 0.0 collective-permute-start.2
  34.6 1.5 %collective-permute-done.2 = f32[16,4224]{1,0:T(8,128)S(1)} collective-permute-done((f32[16,4224]{1,0:T(8,128)S(1)}, f32[16,4224]{1,0:T(8,128)S(1)}, u32[]{:S(2)}, u32[]{:S(2)}) %collective-permute-start.2) | collective-permute-done | bytes 270368 | tf_op jit(solution)/shard_map/ppermute | solution.py:224
  36.2 0.1 fusion.39
  36.3 2.0 %add_add_fusion.2 = f32[16,256]{1,0:T(8,128)S(1)} fusion(f32[16,256]{1,0:T(8,128)S(1)} %add_add_fusion.3, f32[16,4224]{1,0:T(8,128)S(1)} %get-tuple-element.63, pred[]{:T(512)S(6)} %ne.35, s32[4096]{0:T(1024)S(1)} %copy-done.4, f32[16,4096]{1,0:T(8,128)S(1)} %get-tuple-element.58, f32[16,4224]{1,0:T(8,128)S(1)} %get-tuple-element.64, ...), kind=kOutput, calls=%fused_computation.108 | convolution fusion | flops 202653696 | bytes 1377280 | tf_op jit(solution)/shard_map/dot_general | solution.py:194
  38.3 0.1 fusion.17
  38.5 1.6 %collective-permute-start.3 = (f32[16,4224]{1,0:T(8,128)S(1)}, f32[16,4224]{1,0:T(8,128)S(1)}, u32[]{:S(2)}, u32[]{:S(2)}) collective-permute-start(f32[16,4224]{1,0:T(8,128)S(1)} %fusion.17), channel_id=1, source_target_pairs={{0,4},{1,5},{2,6},{3,7},{4,0},{5,1},{6,2},{7,3},{8,12},{9,13},{10,... | collective-permute-start | bytes 811016 | tf_op jit(solution)/shard_map/ppermute | solution.py:215
  40.1 6.1 %shard_map.112 = (f32[128,4096]{1,0:T(8,128)}, f32[128,4096]{1,0:T(8,128)}) custom-call(bf16[128,4096]{1,0:T(8,128)(2,1)} %q_ref.11, bf16[128,4096]{1,0:T(8,128)(2,1)} %k_ref.11, bf16[128,4096]{1,0:T(8,128)(2,1)} %v_ref.11, bf16[128,4096]{1,0:T(8,128)(2,1)} %g_ref.11, f32[16,32,128]{2,1,0:T(8,128)} %bitcast.121, ...), custom_call_target="tpu_custom_call", output_to_operand_aliasing={{0}: (6, {}), {1}: (7, {})} | custom-call | tf_op jit(solution)/shard_map/pallas_call | solution.py:139
  46.2 0.9 collective-permute-done.3
  47.0 0.0 collective-permute-start.4
  47.0 1.5 %collective-permute-done.4 = f32[16,4224]{1,0:T(8,128)S(1)} collective-permute-done((f32[16,4224]{1,0:T(8,128)S(1)}, f32[16,4224]{1,0:T(8,128)S(1)}, u32[]{:S(2)}, u32[]{:S(2)}) %collective-permute-start.4) | collective-permute-done | bytes 270368 | tf_op jit(solution)/shard_map/ppermute | solution.py:224
  48.6 0.1 fusion.37
  48.8 2.0 %add_add_fusion.1 = f32[16,256]{1,0:T(8,128)S(1)} fusion(f32[16,256]{1,0:T(8,128)S(1)} %add_add_fusion.2, f32[16,4224]{1,0:T(8,128)S(1)} %get-tuple-element.61, pred[]{:T(512)S(6)} %ne.34, s32[4096]{0:T(1024)S(1)} %copy-done.4, f32[16,4096]{1,0:T(8,128)S(1)} %get-tuple-element.66, f32[16,4224]{1,0:T(8,128)S(1)} %get-tuple-element.62, ...), kind=kOutput, calls=%fused_computation.107 | convolution fusion | flops 202653696 | bytes 1377280 | tf_op jit(solution)/shard_map/dot_general | solution.py:194
  50.8 0.1 fusion.15
  50.9 2.7 %collective-permute-start.5 = (f32[16,4224]{1,0:T(8,128)S(1)}, f32[16,4224]{1,0:T(8,128)S(1)}, u32[]{:S(2)}, u32[]{:S(2)}) collective-permute-start(f32[16,4224]{1,0:T(8,128)S(1)} %fusion.15), channel_id=1, source_target_pairs={{0,8},{1,9},{2,10},{3,11},{4,12},{5,13},{6,14},{7,15},{8,0},{9,1},... | collective-permute-start | bytes 811016 | tf_op jit(solution)/shard_map/ppermute | solution.py:215
  53.6 6.1 %shard_map.113 = (f32[128,4096]{1,0:T(8,128)}, f32[128,4096]{1,0:T(8,128)}) custom-call(bf16[128,4096]{1,0:T(8,128)(2,1)} %q_ref.11, bf16[128,4096]{1,0:T(8,128)(2,1)} %k_ref.11, bf16[128,4096]{1,0:T(8,128)(2,1)} %v_ref.11, bf16[128,4096]{1,0:T(8,128)(2,1)} %g_ref.11, f32[16,32,128]{2,1,0:T(8,128)} %bitcast.122, ...), custom_call_target="tpu_custom_call", output_to_operand_aliasing={{0}: (6, {}), {1}: (7, {})} | custom-call | tf_op jit(solution)/shard_map/pallas_call | solution.py:139
  59.7 6.5 %collective-permute-done.5 = f32[16,4224]{1,0:T(8,128)S(1)} collective-permute-done((f32[16,4224]{1,0:T(8,128)S(1)}, f32[16,4224]{1,0:T(8,128)S(1)}, u32[]{:S(2)}, u32[]{:S(2)}) %collective-permute-start.5) | collective-permute-done | bytes 270368 | tf_op jit(solution)/shard_map/ppermute | solution.py:215
  66.2 0.0 collective-permute-start.6
  66.2 6.2 %shard_map.114 = (f32[128,4096]{1,0:T(8,128)}, f32[128,4096]{1,0:T(8,128)}) custom-call(bf16[128,4096]{1,0:T(8,128)(2,1)} %q_ref.11, bf16[128,4096]{1,0:T(8,128)(2,1)} %k_ref.11, bf16[128,4096]{1,0:T(8,128)(2,1)} %v_ref.11, bf16[128,4096]{1,0:T(8,128)(2,1)} %g_ref.11, f32[16,32,128]{2,1,0:T(8,128)} %bitcast.123, ...), custom_call_target="tpu_custom_call", output_to_operand_aliasing={{0}: (6, {}), {1}: (7, {})} | custom-call | tf_op jit(solution)/shard_map/pallas_call | solution.py:139
  72.5 0.0 collective-permute-done.6
  72.5 1.0 %broadcast_select_fusion = (f32[16,4224]{1,0:T(8,128)S(1)}, f32[16,4224]{1,0:T(8,128)S(1)}) fusion(f32[16,4224]{1,0:T(8,128)} %collective-permute-done.6, f32[16,4224]{1,0:T(8,128)S(1)} %collective-permute-done.5, pred[]{:T(512)S(6)} %eq.32), kind=kLoop, calls=%fused_computation.92 | loop fusion | flops 135168 | bytes 1081345 | tf_op jit(solution)/shard_map/jit(_where)/select_n | solution.py:226
  73.4 2.6 %multiply_reduce_fusion = (f32[]{:T(128)}, f32[16,256]{1,0:T(8,128)S(1)}) fusion(s32[4096]{0:T(1024)S(1)} %copy-done.4, f32[16,4096]{1,0:T(8,128)S(1)} %get-tuple-element.53, f32[16,4096]{1,0:T(8,128)S(1)} %get-tuple-element.65, f32[16,4224]{1,0:T(8,128)S(1)} %get-tuple-element.60, pred[]{:T(512)S(6)} %ne.39, f32[16,4224]{1,0:T(8,128)S(1)} %get-tuple-element.59, ...), kind=kOutput, calls=%fused_computation.105 | convolution fusion | flops 202727424 | bytes 1655812 | tf_op jit(solution)/shard_map/dot_general | solution.py:194
  76.8 0.2 fusion.22
  77.0 0.8 copy.21
  77.8 0.2 fusion.29
  78.0 0.8 copy.20
  78.7 0.6 divide_bitcast_fusion
  79.3 12.1 %shard_map.115 = (bf16[128,4096]{1,0:T(8,128)(2,1)}, bf16[128,4096]{1,0:T(8,128)(2,1)}, bf16[128,4096]{1,0:T(8,128)(2,1)}, bf16[128,4096]{1,0:T(8,128)(2,1)}) custom-call(bf16[128,4096]{1,0:T(8,128)(2,1)} %q_ref.11, bf16[128,4096]{1,0:T(8,128)(2,1)} %k_ref.11, bf16[128,4096]{1,0:T(8,128)(2,1)} %v_ref.11, bf16[128,4096]{1,0:T(8,128)(2,1)} %g_ref.11, ...), custom_call_target="tpu_custom_call" | custom-call | tf_op jit(solution)/shard_map/pallas_call | solution.py:158
  (2 shorter events, 0.1 us)
Async XLA Ops:
  0.6 0.7 copy-start
  4.2 10.0 %copy-start.4 = (s32[4096]{0:T(1024)S(1)}, s32[4096]{0:T(1024)}, u32[]{:S(2)}) copy-start(s32[4096]{0:T(1024)} %param.13) | copy-start | bytes 49156
  14.2 6.1 %copy-start.1 = (f32[16,4096]{1,0:T(8,128)S(1)}, f32[16,4096]{1,0:T(8,128)}, u32[]{:S(2)}) copy-start(f32[16,4096]{1,0:T(8,128)} %get-tuple-element.29) | copy-start | bytes 786436
  14.2 6.1 %copy-start.2 = (f32[16,4096]{1,0:T(8,128)S(1)}, f32[16,4096]{1,0:T(8,128)}, u32[]{:S(2)}) copy-start(f32[16,4096]{1,0:T(8,128)} %get-tuple-element.30) | copy-start | bytes 786436
  18.2 2.1 %collective-permute-start = (f32[16,8448]{1,0:T(8,128)S(1)}, f32[16,8448]{1,0:T(8,128)S(1)}, u32[]{:S(2)}, u32[]{:S(2)}) collective-permute-start(f32[16,8448]{1,0:T(8,128)S(1)} %pad_maximum_fusion), channel_id=1, source_target_pairs={{0,1},{1,0},{2,3},{3,2},{4,5},{5,4},{6,7},{7,6},{8,9},{9,8},{10,11... | collective-permute-start | bytes 1622024 | tf_op jit(solution)/shard_map/ppermute | solution.py:210
  18.8 7.6 %copy-start.3 = (f32[256,16]{0,1:T(8,128)S(1)}, f32[256,16]{0,1:T(8,128)}, u32[]{:S(2)}) copy-start(f32[256,16]{0,1:T(8,128)} %param.12) | copy-start | bytes 49156
  22.6 12.0 %collective-permute-start.1 = (f32[16,4224]{1,0:T(8,128)S(1)}, f32[16,4224]{1,0:T(8,128)S(1)}, u32[]{:S(2)}, u32[]{:S(2)}) collective-permute-start(f32[16,4224]{1,0:T(8,128)S(1)} %fusion.19), channel_id=1, source_target_pairs={{0,2},{1,3},{2,0},{3,1},{4,6},{5,7},{6,4},{7,5},{8,10},{9,11},{10,... | collective-permute-start | bytes 811016 | tf_op jit(solution)/shard_map/ppermute | solution.py:215
  34.6 1.5 %collective-permute-start.2 = (f32[16,4224]{1,0:T(8,128)S(1)}, f32[16,4224]{1,0:T(8,128)S(1)}, u32[]{:S(2)}, u32[]{:S(2)}) collective-permute-start(f32[16,4224]{1,0:T(8,128)S(1)} %collective-permute-done.1), channel_id=1, source_target_pairs={{0,1},{1,0},{2,3},{3,2},{4,5},{5,4},{6,7},{7,6},{8,9},{9,8},{10,11... | collective-permute-start | bytes 811016 | tf_op jit(solution)/shard_map/ppermute | solution.py:224
  38.5 8.6 %collective-permute-start.3 = (f32[16,4224]{1,0:T(8,128)S(1)}, f32[16,4224]{1,0:T(8,128)S(1)}, u32[]{:S(2)}, u32[]{:S(2)}) collective-permute-start(f32[16,4224]{1,0:T(8,128)S(1)} %fusion.17), channel_id=1, source_target_pairs={{0,4},{1,5},{2,6},{3,7},{4,0},{5,1},{6,2},{7,3},{8,12},{9,13},{10,... | collective-permute-start | bytes 811016 | tf_op jit(solution)/shard_map/ppermute | solution.py:215
  47.0 1.5 %collective-permute-start.4 = (f32[16,4224]{1,0:T(8,128)S(1)}, f32[16,4224]{1,0:T(8,128)S(1)}, u32[]{:S(2)}, u32[]{:S(2)}) collective-permute-start(f32[16,4224]{1,0:T(8,128)S(1)} %collective-permute-done.3), channel_id=1, source_target_pairs={{0,1},{1,0},{2,3},{3,2},{4,5},{5,4},{6,7},{7,6},{8,9},{9,8},{10,11... | collective-permute-start | bytes 811016 | tf_op jit(solution)/shard_map/ppermute | solution.py:224
  50.9 15.3 %collective-permute-start.5 = (f32[16,4224]{1,0:T(8,128)S(1)}, f32[16,4224]{1,0:T(8,128)S(1)}, u32[]{:S(2)}, u32[]{:S(2)}) collective-permute-start(f32[16,4224]{1,0:T(8,128)S(1)} %fusion.15), channel_id=1, source_target_pairs={{0,8},{1,9},{2,10},{3,11},{4,12},{5,13},{6,14},{7,15},{8,0},{9,1},... | collective-permute-start | bytes 811016 | tf_op jit(solution)/shard_map/ppermute | solution.py:215
  66.2 6.2 %collective-permute-start.6 = (f32[16,4224]{1,0:T(8,128)S(1)}, f32[16,4224]{1,0:T(8,128)}, u32[]{:S(2)}, u32[]{:S(2)}) collective-permute-start(f32[16,4224]{1,0:T(8,128)S(1)} %collective-permute-done.5), channel_id=1, source_target_pairs={{0,1},{1,0},{2,3},{3,2},{4,5},{5,4},{6,7},{7,6},{8,9},{9,8},{10,11... | collective-permute-start | bytes 811016 | tf_op jit(solution)/shard_map/ppermute | solution.py:224

commit v9 on v8

--- a/solution.py
+++ b/solution.py
@@ -204,7 +204,7 @@
         while bit < count:
             pairs = [(i, i ^ bit) for i in range(count)]
             packed = jnp.concatenate([fwd_cube, bwd_cube, grad_cube], axis=1)
-            need = min(pieces, level)
+            need = pieces if bit * 2 >= count else min(pieces, level)
             level += 1
             if bit == 1:
                 got = lax.ppermute(packed, "ctx", pairs)

time: 92 us -> 87.4 us (0.950)
  waiting for transfers between devices: 12 us -> 7.44 us
    ppermute x3, waiting for transfers between devices: 7.37 us -> 1.13 us  [on_device(): got_mine = lax.ppermute(mine, 'ctx', pairs)]
    ppermute x3, waiting for transfers between devices: 3.08 us -> 4.75 us  [on_device(): lax.ppermute(got_mine, 'ctx', [(i, i ^ 1) for i in range(count)])]
    unnamed x14 -> x15, local copies, waits for them, and re-layouts: 3.77 us -> 4.52 us
  transfers between devices with their start and end apart: 7 -> 7, of which waited for: 5 -> 6; matrix products, arithmetic and copies ran while one was open for 3% -> 3% of each run, Pallas kernels for 27% -> 28%
where the time goes in v9:
time: 87.4 us; the launch traced here: 87 us
  Pallas kernels  46.5 us (53%)
  matrix products  15.1 us (17%)
  starting transfers between devices  7.77 us (9%)
  waiting for transfers between devices  7.44 us (9%)
  local copies, waits for them, and re-layouts  4.52 us (5%)
  other arithmetic  3.98 us (5%)
  between operations  1.59 us (2%)
    pallas_call x4, Pallas kernels, local_scans(): pl.pallas_call(local_kernel, grid=(1,), in_specs=specs, out_specs=[big, b...  24.5 us
    pallas_call x1, Pallas kernels, corrected(): pl.pallas_call(correct_kernel, grid=(width // BLOCK,), in_specs=[big] * 6...  12.1 us
    dot_general x5, matrix products, grouped(): return jnp.dot(a, member.T, precision=high)  11.6 us
    pallas_call x1, Pallas kernels, local_carries(): pl.pallas_call(carry_kernel, grid=(width // BLOCK,), in_specs=[big, big,...  9.96 us
    ppermute x3, starting transfers between devices, on_device(): got_mine = lax.ppermute(mine, 'ctx', pairs)  7.25 us
    ppermute x3, waiting for transfers between devices, on_device(): lax.ppermute(got_mine, 'ctx', [(i, i ^ 1) for i in range(count)])  4.75 us
    unnamed x15, local copies, waits for them, and re-layouts  4.52 us
    dot_general x1, matrix products, on_device(): rate = jnp.dot(decay_rate.T, member, precision=high)  2.12 us
  transfers between devices with their start and end apart: 7, of which 6 were waited for; matrix products, arithmetic and copies ran while one was open for 3% of the time, Pallas kernels for 28%

profile of v9, /device:TPU:0, one launch (start us, length us, event | category | flops | bytes accessed | tf_op | source)
XLA Modules:
  0.0 87.0 jit_solution(13029970242407295038)
XLA Ops:
  0.6 0.0 copy-start
  0.6 0.7 copy-done
  1.4 2.1 %convolution_negate_fusion = f32[4096,16]{0,1:T(8,128)S(1)} fusion(f32[256,16]{0,1:T(8,128)S(1)} %copy-done, s32[4096]{0:T(1024)} %param.13), kind=kOutput, calls=%fused_computation | convolution fusion | flops 202440704 | bytes 294912 | tf_op jit(solution)/shard_map/dot_general | solution.py:176
  3.5 0.7 exponential_bitcast_fusion
  4.2 0.0 copy-start.4
  4.2 10.0 %shard_map.110 = (f32[16,4096]{1,0:T(8,128)}, f32[16,4096]{1,0:T(8,128)}, f32[16,4096]{1,0:T(8,128)}) custom-call(bf16[128,4096]{1,0:T(8,128)(2,1)} %q_ref.11, bf16[128,4096]{1,0:T(8,128)(2,1)} %k_ref.11, bf16[128,4096]{1,0:T(8,128)(2,1)} %v_ref.11, bf16[128,4096]{1,0:T(8,128)(2,1)} %g_ref.11, f32[16,4096]{1,0:T(8,128)} %get-tuple-element.68.p_ref), custom_call_target="tpu_custom_call" | custom-call | tf_op jit(solution)/shard_map/pallas_call | solution.py:116
  14.2 0.0 copy-start.1
  14.2 0.0 copy-start.2
  14.2 0.0 copy-done.4
  14.2 3.0 %fusion.5 = f32[16,256]{1,0:T(8,128)S(1)} fusion(f32[16,4096]{1,0:T(8,128)} %get-tuple-element.31, s32[4096]{0:T(1024)S(1)} %copy-done.4), kind=kOutput, calls=%fused_computation.7 | convolution fusion | flops 202375168 | bytes 294912 | tf_op jit(solution)/shard_map/dot_general | solution.py:194
  17.2 1.1 %pad_maximum_fusion = f32[16,8448]{1,0:T(8,128)S(1)} fusion(f32[16,256]{1,0:T(8,128)S(1)} %fusion.5, f32[16,4096]{1,0:T(8,128)} %get-tuple-element.30, f32[16,4096]{1,0:T(8,128)} %get-tuple-element.29), kind=kLoop, calls=%fused_computation.16 | loop fusion | flops 270336 | bytes 1081344 | tf_op jit(solution)/shard_map/concatenate | solution.py:206
  18.2 0.5 collective-permute-start
  18.8 0.0 copy-start.3
  18.8 1.6 %collective-permute-done = f32[16,8448]{1,0:T(8,128)S(1)} collective-permute-done((f32[16,8448]{1,0:T(8,128)S(1)}, f32[16,8448]{1,0:T(8,128)S(1)}, u32[]{:S(2)}, u32[]{:S(2)}) %collective-permute-start) | collective-permute-done | bytes 540704 | tf_op jit(solution)/shard_map/ppermute | solution.py:210
  20.3 0.0 copy-done.1
  20.3 0.0 copy-done.2
  20.3 2.0 %add_add_fusion.3 = f32[16,256]{1,0:T(8,128)S(1)} fusion(f32[16,256]{1,0:T(8,128)S(1)} %fusion.5, f32[16,8448]{1,0:T(8,128)S(1)} %collective-permute-done, pred[]{:T(512)S(6)} %ne.36, s32[4096]{0:T(1024)S(1)} %copy-done.4, f32[16,4096]{1,0:T(8,128)S(1)} %copy-done.2, f32[16,4096]{1,0:T(8,128)S(1)} %copy-done.1, f32[4096,16]{0,1:T(8,128)S(1)} %convolution_negate_fusion), kind=kOutput, calls=%fused_computation.109 | convolution fusion | flops 202653696 | bytes 1377280 | tf_op jit(solution)/shard_map/dot_general | solution.py:194
  22.3 0.1 fusion.41
  22.5 0.1 fusion.19
  22.6 3.0 %collective-permute-start.1 = (f32[16,4224]{1,0:T(8,128)S(1)}, f32[16,4224]{1,0:T(8,128)S(1)}, u32[]{:S(2)}, u32[]{:S(2)}) collective-permute-start(f32[16,4224]{1,0:T(8,128)S(1)} %fusion.19), channel_id=1, source_target_pairs={{0,2},{1,3},{2,0},{3,1},{4,6},{5,7},{6,4},{7,5},{8,10},{9,11},{10,... | collective-permute-start | bytes 811016 | tf_op jit(solution)/shard_map/ppermute | solution.py:215
  25.6 0.8 copy.18
  26.3 0.0 copy-done.3
  26.3 1.4 %fusion.13 = f32[2,8,32,128]{3,1,2,0:T(8,128)S(1)} fusion(f32[256,16]{0,1:T(8,128)S(1)} %copy-done.3, s32[4096]{0:T(1024)S(1)} %copy-done.4), kind=kOutput, calls=%fused_computation.15 | convolution fusion | flops 202375168 | bytes 294912 | tf_op jit(solution)/shard_map/dot_general | solution.py:177
  27.7 0.8 copy.19
  28.5 6.1 %shard_map.111 = (f32[128,4096]{1,0:T(8,128)}, f32[128,4096]{1,0:T(8,128)}) custom-call(bf16[128,4096]{1,0:T(8,128)(2,1)} %q_ref.11, bf16[128,4096]{1,0:T(8,128)(2,1)} %k_ref.11, bf16[128,4096]{1,0:T(8,128)(2,1)} %v_ref.11, bf16[128,4096]{1,0:T(8,128)(2,1)} %g_ref.11, f32[16,32,128]{2,1,0:T(8,128)} %bitcast.120, f32[16,32,128]{2,1,0:T(8,128)} %bitcast.125), custom_call_target="tpu_custom_call" | custom-call | tf_op jit(solution)/shard_map/pallas_call | solution.py:139
  34.6 0.0 collective-permute-done.1
  34.6 0.0 collective-permute-start.2
  34.6 1.5 %collective-permute-done.2 = f32[16,4224]{1,0:T(8,128)S(1)} collective-permute-done((f32[16,4224]{1,0:T(8,128)S(1)}, f32[16,4224]{1,0:T(8,128)S(1)}, u32[]{:S(2)}, u32[]{:S(2)}) %collective-permute-start.2) | collective-permute-done | bytes 270368 | tf_op jit(solution)/shard_map/ppermute | solution.py:224
  36.2 0.1 fusion.39
  36.3 2.0 %add_add_fusion.2 = f32[16,256]{1,0:T(8,128)S(1)} fusion(f32[16,256]{1,0:T(8,128)S(1)} %add_add_fusion.3, f32[16,4224]{1,0:T(8,128)S(1)} %get-tuple-element.63, pred[]{:T(512)S(6)} %ne.35, s32[4096]{0:T(1024)S(1)} %copy-done.4, f32[16,4096]{1,0:T(8,128)S(1)} %get-tuple-element.58, f32[16,4224]{1,0:T(8,128)S(1)} %get-tuple-element.64, ...), kind=kOutput, calls=%fused_computation.108 | convolution fusion | flops 202653696 | bytes 1377280 | tf_op jit(solution)/shard_map/dot_general | solution.py:194
  38.3 0.1 fusion.17
  38.5 1.6 %collective-permute-start.3 = (f32[16,4224]{1,0:T(8,128)S(1)}, f32[16,4224]{1,0:T(8,128)S(1)}, u32[]{:S(2)}, u32[]{:S(2)}) collective-permute-start(f32[16,4224]{1,0:T(8,128)S(1)} %fusion.17), channel_id=1, source_target_pairs={{0,4},{1,5},{2,6},{3,7},{4,0},{5,1},{6,2},{7,3},{8,12},{9,13},{10,... | collective-permute-start | bytes 811016 | tf_op jit(solution)/shard_map/ppermute | solution.py:215
  40.1 6.1 %shard_map.112 = (f32[128,4096]{1,0:T(8,128)}, f32[128,4096]{1,0:T(8,128)}) custom-call(bf16[128,4096]{1,0:T(8,128)(2,1)} %q_ref.11, bf16[128,4096]{1,0:T(8,128)(2,1)} %k_ref.11, bf16[128,4096]{1,0:T(8,128)(2,1)} %v_ref.11, bf16[128,4096]{1,0:T(8,128)(2,1)} %g_ref.11, f32[16,32,128]{2,1,0:T(8,128)} %bitcast.121, ...), custom_call_target="tpu_custom_call", output_to_operand_aliasing={{0}: (6, {}), {1}: (7, {})} | custom-call | tf_op jit(solution)/shard_map/pallas_call | solution.py:139
  46.2 0.9 %collective-permute-done.3 = f32[16,4224]{1,0:T(8,128)S(1)} collective-permute-done((f32[16,4224]{1,0:T(8,128)S(1)}, f32[16,4224]{1,0:T(8,128)S(1)}, u32[]{:S(2)}, u32[]{:S(2)}) %collective-permute-start.3) | collective-permute-done | bytes 270368 | tf_op jit(solution)/shard_map/ppermute | solution.py:215
  47.0 0.0 collective-permute-start.4
  47.0 1.5 %collective-permute-done.4 = f32[16,4224]{1,0:T(8,128)S(1)} collective-permute-done((f32[16,4224]{1,0:T(8,128)S(1)}, f32[16,4224]{1,0:T(8,128)S(1)}, u32[]{:S(2)}, u32[]{:S(2)}) %collective-permute-start.4) | collective-permute-done | bytes 270368 | tf_op jit(solution)/shard_map/ppermute | solution.py:224
  48.6 0.1 fusion.37
  48.8 2.0 %add_add_fusion.1 = f32[16,256]{1,0:T(8,128)S(1)} fusion(f32[16,256]{1,0:T(8,128)S(1)} %add_add_fusion.2, f32[16,4224]{1,0:T(8,128)S(1)} %get-tuple-element.61, pred[]{:T(512)S(6)} %ne.34, s32[4096]{0:T(1024)S(1)} %copy-done.4, f32[16,4096]{1,0:T(8,128)S(1)} %get-tuple-element.66, f32[16,4224]{1,0:T(8,128)S(1)} %get-tuple-element.62, ...), kind=kOutput, calls=%fused_computation.107 | convolution fusion | flops 202653696 | bytes 1377280 | tf_op jit(solution)/shard_map/dot_general | solution.py:194
  50.8 0.1 fusion.15
  50.9 2.7 %collective-permute-start.5 = (f32[16,4224]{1,0:T(8,128)S(1)}, f32[16,4224]{1,0:T(8,128)S(1)}, u32[]{:S(2)}, u32[]{:S(2)}) collective-permute-start(f32[16,4224]{1,0:T(8,128)S(1)} %fusion.15), channel_id=1, source_target_pairs={{0,8},{1,9},{2,10},{3,11},{4,12},{5,13},{6,14},{7,15},{8,0},{9,1},... | collective-permute-start | bytes 811016 | tf_op jit(solution)/shard_map/ppermute | solution.py:215
  53.6 6.1 %shard_map.113 = (f32[128,4096]{1,0:T(8,128)}, f32[128,4096]{1,0:T(8,128)}) custom-call(bf16[128,4096]{1,0:T(8,128)(2,1)} %q_ref.11, bf16[128,4096]{1,0:T(8,128)(2,1)} %k_ref.11, bf16[128,4096]{1,0:T(8,128)(2,1)} %v_ref.11, bf16[128,4096]{1,0:T(8,128)(2,1)} %g_ref.11, f32[16,32,128]{2,1,0:T(8,128)} %bitcast.122, ...), custom_call_target="tpu_custom_call", output_to_operand_aliasing={{0}: (6, {}), {1}: (7, {})} | custom-call | tf_op jit(solution)/shard_map/pallas_call | solution.py:139
  59.7 6.2 %shard_map.114 = (f32[128,4096]{1,0:T(8,128)}, f32[128,4096]{1,0:T(8,128)}) custom-call(bf16[128,4096]{1,0:T(8,128)(2,1)} %q_ref.11, bf16[128,4096]{1,0:T(8,128)(2,1)} %k_ref.11, bf16[128,4096]{1,0:T(8,128)(2,1)} %v_ref.11, bf16[128,4096]{1,0:T(8,128)(2,1)} %g_ref.11, f32[16,32,128]{2,1,0:T(8,128)} %bitcast.123, ...), custom_call_target="tpu_custom_call", output_to_operand_aliasing={{0}: (6, {}), {1}: (7, {})} | custom-call | tf_op jit(solution)/shard_map/pallas_call | solution.py:139
  66.0 0.3 collective-permute-done.5
  66.2 0.0 collective-permute-start.6
  66.2 1.7 %collective-permute-done.6 = f32[16,4224]{1,0:T(8,128)} collective-permute-done((f32[16,4224]{1,0:T(8,128)S(1)}, f32[16,4224]{1,0:T(8,128)}, u32[]{:S(2)}, u32[]{:S(2)}) %collective-permute-start.6) | collective-permute-done | bytes 270368 | tf_op jit(solution)/shard_map/ppermute | solution.py:224
  67.9 1.0 %broadcast_select_fusion = (f32[16,4224]{1,0:T(8,128)S(1)}, f32[16,4224]{1,0:T(8,128)S(1)}) fusion(f32[16,4224]{1,0:T(8,128)} %collective-permute-done.6, f32[16,4224]{1,0:T(8,128)S(1)} %collective-permute-done.5, pred[]{:T(512)S(6)} %eq.32), kind=kLoop, calls=%fused_computation.92 | loop fusion | flops 135168 | bytes 1081345 | tf_op jit(solution)/shard_map/jit(_where)/select_n | solution.py:226
  68.9 2.6 %multiply_reduce_fusion = (f32[]{:T(128)}, f32[16,256]{1,0:T(8,128)S(1)}) fusion(s32[4096]{0:T(1024)S(1)} %copy-done.4, f32[16,4096]{1,0:T(8,128)S(1)} %get-tuple-element.53, f32[16,4096]{1,0:T(8,128)S(1)} %get-tuple-element.65, f32[16,4224]{1,0:T(8,128)S(1)} %get-tuple-element.60, pred[]{:T(512)S(6)} %ne.39, f32[16,4224]{1,0:T(8,128)S(1)} %get-tuple-element.59, ...), kind=kOutput, calls=%fused_computation.105 | convolution fusion | flops 202727424 | bytes 1655812 | tf_op jit(solution)/shard_map/dot_general | solution.py:194
  72.2 0.2 fusion.22
  72.4 0.8 copy.21
  73.2 0.2 fusion.29
  73.4 0.8 copy.20
  74.1 0.6 divide_bitcast_fusion
  74.8 12.1 %shard_map.115 = (bf16[128,4096]{1,0:T(8,128)(2,1)}, bf16[128,4096]{1,0:T(8,128)(2,1)}, bf16[128,4096]{1,0:T(8,128)(2,1)}, bf16[128,4096]{1,0:T(8,128)(2,1)}) custom-call(bf16[128,4096]{1,0:T(8,128)(2,1)} %q_ref.11, bf16[128,4096]{1,0:T(8,128)(2,1)} %k_ref.11, bf16[128,4096]{1,0:T(8,128)(2,1)} %v_ref.11, bf16[128,4096]{1,0:T(8,128)(2,1)} %g_ref.11, ...), custom_call_target="tpu_custom_call" | custom-call | tf_op jit(solution)/shard_map/pallas_call | solution.py:158
  (2 shorter events, 0.1 us)
Async XLA Ops:
  0.6 0.7 copy-start
  4.2 10.0 %copy-start.4 = (s32[4096]{0:T(1024)S(1)}, s32[4096]{0:T(1024)}, u32[]{:S(2)}) copy-start(s32[4096]{0:T(1024)} %param.13) | copy-start | bytes 49156
  14.2 6.1 %copy-start.1 = (f32[16,4096]{1,0:T(8,128)S(1)}, f32[16,4096]{1,0:T(8,128)}, u32[]{:S(2)}) copy-start(f32[16,4096]{1,0:T(8,128)} %get-tuple-element.29) | copy-start | bytes 786436
  14.2 6.1 %copy-start.2 = (f32[16,4096]{1,0:T(8,128)S(1)}, f32[16,4096]{1,0:T(8,128)}, u32[]{:S(2)}) copy-start(f32[16,4096]{1,0:T(8,128)} %get-tuple-element.30) | copy-start | bytes 786436
  18.2 2.1 %collective-permute-start = (f32[16,8448]{1,0:T(8,128)S(1)}, f32[16,8448]{1,0:T(8,128)S(1)}, u32[]{:S(2)}, u32[]{:S(2)}) collective-permute-start(f32[16,8448]{1,0:T(8,128)S(1)} %pad_maximum_fusion), channel_id=1, source_target_pairs={{0,1},{1,0},{2,3},{3,2},{4,5},{5,4},{6,7},{7,6},{8,9},{9,8},{10,11... | collective-permute-start | bytes 1622024 | tf_op jit(solution)/shard_map/ppermute | solution.py:210
  18.8 7.6 %copy-start.3 = (f32[256,16]{0,1:T(8,128)S(1)}, f32[256,16]{0,1:T(8,128)}, u32[]{:S(2)}) copy-start(f32[256,16]{0,1:T(8,128)} %param.12) | copy-start | bytes 49156
  22.6 12.0 %collective-permute-start.1 = (f32[16,4224]{1,0:T(8,128)S(1)}, f32[16,4224]{1,0:T(8,128)S(1)}, u32[]{:S(2)}, u32[]{:S(2)}) collective-permute-start(f32[16,4224]{1,0:T(8,128)S(1)} %fusion.19), channel_id=1, source_target_pairs={{0,2},{1,3},{2,0},{3,1},{4,6},{5,7},{6,4},{7,5},{8,10},{9,11},{10,... | collective-permute-start | bytes 811016 | tf_op jit(solution)/shard_map/ppermute | solution.py:215
  34.6 1.5 %collective-permute-start.2 = (f32[16,4224]{1,0:T(8,128)S(1)}, f32[16,4224]{1,0:T(8,128)S(1)}, u32[]{:S(2)}, u32[]{:S(2)}) collective-permute-start(f32[16,4224]{1,0:T(8,128)S(1)} %collective-permute-done.1), channel_id=1, source_target_pairs={{0,1},{1,0},{2,3},{3,2},{4,5},{5,4},{6,7},{7,6},{8,9},{9,8},{10,11... | collective-permute-start | bytes 811016 | tf_op jit(solution)/shard_map/ppermute | solution.py:224
  38.5 8.6 %collective-permute-start.3 = (f32[16,4224]{1,0:T(8,128)S(1)}, f32[16,4224]{1,0:T(8,128)S(1)}, u32[]{:S(2)}, u32[]{:S(2)}) collective-permute-start(f32[16,4224]{1,0:T(8,128)S(1)} %fusion.17), channel_id=1, source_target_pairs={{0,4},{1,5},{2,6},{3,7},{4,0},{5,1},{6,2},{7,3},{8,12},{9,13},{10,... | collective-permute-start | bytes 811016 | tf_op jit(solution)/shard_map/ppermute | solution.py:215
  47.0 1.5 %collective-permute-start.4 = (f32[16,4224]{1,0:T(8,128)S(1)}, f32[16,4224]{1,0:T(8,128)S(1)}, u32[]{:S(2)}, u32[]{:S(2)}) collective-permute-start(f32[16,4224]{1,0:T(8,128)S(1)} %collective-permute-done.3), channel_id=1, source_target_pairs={{0,1},{1,0},{2,3},{3,2},{4,5},{5,4},{6,7},{7,6},{8,9},{9,8},{10,11... | collective-permute-start | bytes 811016 | tf_op jit(solution)/shard_map/ppermute | solution.py:224
  50.9 15.3 %collective-permute-start.5 = (f32[16,4224]{1,0:T(8,128)S(1)}, f32[16,4224]{1,0:T(8,128)S(1)}, u32[]{:S(2)}, u32[]{:S(2)}) collective-permute-start(f32[16,4224]{1,0:T(8,128)S(1)} %fusion.15), channel_id=1, source_target_pairs={{0,8},{1,9},{2,10},{3,11},{4,12},{5,13},{6,14},{7,15},{8,0},{9,1},... | collective-permute-start | bytes 811016 | tf_op jit(solution)/shard_map/ppermute | solution.py:215
  66.2 1.7 %collective-permute-start.6 = (f32[16,4224]{1,0:T(8,128)S(1)}, f32[16,4224]{1,0:T(8,128)}, u32[]{:S(2)}, u32[]{:S(2)}) collective-permute-start(f32[16,4224]{1,0:T(8,128)S(1)} %collective-permute-done.5), channel_id=1, source_target_pairs={{0,1},{1,0},{2,3},{3,2},{4,5},{5,4},{6,7},{7,6},{8,9},{9,8},{10,11... | collective-permute-start | bytes 811016 | tf_op jit(solution)/shard_map/ppermute | solution.py:224

commit v10 on v9

--- a/solution.py
+++ b/solution.py
@@ -165,16 +165,30 @@
     )(query_proj, key_proj, value_proj, out_grad, *local, factor4, weight4, *tiles)
 
 
+def split_dot(a, member):
+    bf16 = jnp.bfloat16
+    top = lax.reduce_precision(a, exponent_bits=8, mantissa_bits=7)
+    rest = a - top
+    middle = lax.reduce_precision(rest, exponent_bits=8, mantissa_bits=7)
+    hi = top.astype(bf16)
+    mid = middle.astype(bf16)
+    lo = (rest - middle).astype(bf16)
+    rows = a.shape[0]
+    out = jnp.dot(jnp.concatenate([hi, mid, lo], axis=0), member, preferred_element_type=jnp.float32)
+    return (out[:rows] + out[rows : 2 * rows]) + out[2 * rows :]
+
+
 def make_on_device(count):
     def on_device(query_proj, key_proj, value_proj, out_grad, decay_rate, residue, group_of):
-        high = lax.Precision.HIGHEST
         rows = query_proj.shape[0]
         group_count = decay_rate.shape[0]
         member = (group_of[None, :] == jnp.arange(group_count, dtype=jnp.int32)[:, None]).astype(
-            jnp.float32
+            jnp.bfloat16
         )
-        rate = jnp.dot(decay_rate.T, member, precision=high)
-        weight = jnp.dot(residue.T, member, precision=high)
+        modes = decay_rate.shape[1]
+        params = split_dot(jnp.concatenate([decay_rate.T, residue.T], axis=0), member)
+        rate = params[:modes]
+        weight = params[modes:]
         factor = jnp.exp(-rate)
         end_state, head_adjoint, local_total = local_carries(
             query_proj, key_proj, value_proj, out_grad, factor
@@ -190,8 +204,10 @@
         def span(blocks):
             return jnp.exp(-rate * (blocks * float(rows)))
 
+        member_t = member.T
+
         def grouped(a):
-            return jnp.dot(a, member.T, precision=high)
+            return split_dot(a, member_t)
 
         place = lax.axis_index("ctx")
         fwd_cube = end_state

time: 87.4 us -> 78.2 us (0.89)
  matrix products: 15.1 us -> 5.68 us
  other arithmetic: 3.98 us -> 5.76 us
  local copies, waits for them, and re-layouts: 4.52 us -> 3.04 us
    dot_general x7 -> x6, matrix products: 15.1 us -> 5.68 us  [split_dot(): jnp.dot(jnp.concatenate([hi, mid, lo], axis=0), member, preferred_element...]
    convert_element_type x0 -> x10, other arithmetic: none -> 2.8 us  [the longest x6 2.54 us: split_dot(): hi = top.astype(bf16)]
    unnamed x15 -> x10, local copies, waits for them, and re-layouts: 4.52 us -> 3.04 us
    concatenate x4, other arithmetic: 1.53 us -> 0.47 us  [on_device(): packed = jnp.concatenate([fwd_cube, bwd_cube, grad_cube], axis=1)]
    select_n x3, other arithmetic: 1.07 us -> 0.11 us  [on_device(): second = jnp.where(core == 0, got_other, got_mine)]
  transfers between devices with their start and end apart: 7 -> 7, of which waited for: 6 -> 6; matrix products, arithmetic and copies ran while one was open for 3% -> 2% of each run, Pallas kernels for 28% -> 31%
where the time goes in v10:
time: 78.2 us; the launch traced here: 77.7 us
  Pallas kernels  46.4 us (59%)
  starting transfers between devices  7.78 us (10%)
  waiting for transfers between devices  7.53 us (10%)
  other arithmetic  5.76 us (7%)
  matrix products  5.68 us (7%)
  local copies, waits for them, and re-layouts  3.04 us (4%)
  between operations  1.56 us (2%)
    pallas_call x4, Pallas kernels, local_scans(): pl.pallas_call(local_kernel, grid=(1,), in_specs=specs, out_specs=[big, b...  24.4 us
    pallas_call x1, Pallas kernels, corrected(): pl.pallas_call(correct_kernel, grid=(width // BLOCK,), in_specs=[big] * 6...  12.1 us
    pallas_call x1, Pallas kernels, local_carries(): pl.pallas_call(carry_kernel, grid=(width // BLOCK,), in_specs=[big, big,...  9.96 us
    ppermute x3, starting transfers between devices, on_device(): got_mine = lax.ppermute(mine, 'ctx', pairs)  7.25 us
    dot_general x6, matrix products, split_dot(): jnp.dot(jnp.concatenate([hi, mid, lo], axis=0), member, preferred_element...  5.68 us
    ppermute x3, waiting for transfers between devices, on_device(): lax.ppermute(got_mine, 'ctx', [(i, i ^ 1) for i in range(count)])  4.62 us
    unnamed x10, local copies, waits for them, and re-layouts  3.04 us
    convert_element_type x6, other arithmetic, split_dot(): hi = top.astype(bf16)  2.54 us
  transfers between devices with their start and end apart: 7, of which 6 were waited for; matrix products, arithmetic and copies ran while one was open for 2% of the time, Pallas kernels for 31%

profile of v10, /device:TPU:0, one launch (start us, length us, event | category | flops | bytes accessed | tf_op | source)
XLA Modules:
  0.0 77.7 jit_solution(8800613179225703526)
XLA Ops:
  0.6 0.7 reduce-precision_convert_fusion.11
  1.4 1.6 %fusion.5 = f32[96,4096]{1,0:T(8,128)S(1)} fusion(s32[4096]{0:T(1024)} %param.13, bf16[32,256]{1,0:T(8,128)(2,1)S(1)} %get-tuple-element.91, bf16[32,256]{1,0:T(8,128)(2,1)S(1)} %get-tuple-element.90, bf16[32,256]{1,0:T(8,128)(2,1)S(1)} %get-tuple-element.89), kind=kOutput, calls=%fused_computation.6 | convolution fusion | flops 202522624 | bytes 1638400 | tf_op jit(solution)/shard_map/dot_general | solution.py:177
  3.0 0.1 slice_add_fusion
  3.1 0.7 fusion.58.p_ref
  3.8 0.0 copy-start.2
  3.8 10.0 %shard_map.110 = (f32[16,4096]{1,0:T(8,128)}, f32[16,4096]{1,0:T(8,128)}, f32[16,4096]{1,0:T(8,128)}) custom-call(bf16[128,4096]{1,0:T(8,128)(2,1)} %q_ref.11, bf16[128,4096]{1,0:T(8,128)(2,1)} %k_ref.11, bf16[128,4096]{1,0:T(8,128)(2,1)} %v_ref.11, bf16[128,4096]{1,0:T(8,128)(2,1)} %g_ref.11, f32[16,4096]{1,0:T(8,128)} %fusion.58.p_ref), custom_call_target="tpu_custom_call" | custom-call | tf_op jit(solution)/shard_map/pallas_call | solution.py:116
  13.8 0.0 copy-start
  13.8 0.0 copy-start.1
  13.8 1.1 %reduce-precision_convert_fusion.9 = (bf16[16,4096]{1,0:T(8,128)(2,1)S(1)}, bf16[16,4096]{1,0:T(8,128)(2,1)S(1)}, bf16[16,4096]{1,0:T(8,128)(2,1)S(1)}) fusion(f32[16,4096]{1,0:T(8,128)} %get-tuple-element.31), kind=kLoop, calls=%fused_computation.69 | loop fusion | flops 458752 | bytes 655360 | tf_op jit(solution)/shard_map/convert_element_type | solution.py:173
  14.8 0.0 copy-done.2
  14.8 0.8 %fusion.4 = f32[48,256]{1,0:T(8,128)S(1)} fusion(s32[4096]{0:T(1024)S(1)} %copy-done.2, bf16[16,4096]{1,0:T(8,128)(2,1)S(1)} %get-tuple-element.87, bf16[16,4096]{1,0:T(8,128)(2,1)S(1)} %get-tuple-element.88, bf16[16,4096]{1,0:T(8,128)(2,1)S(1)} %get-tuple-element.86), kind=kOutput, calls=%fused_computation.5 | convolution fusion | flops 102891520 | bytes 458752 | tf_op jit(solution)/shard_map/dot_general | solution.py:177
  15.7 0.0 copy-done
  15.7 0.0 copy-done.1
  15.7 0.5 collective-permute-start
  16.3 1.6 %collective-permute-done = f32[16,8448]{1,0:T(8,128)S(1)} collective-permute-done((f32[16,8448]{1,0:T(8,128)S(1)}, f32[16,8448]{1,0:T(8,128)S(1)}, u32[]{:S(2)}, u32[]{:S(2)}) %collective-permute-start) | collective-permute-done | bytes 540704 | tf_op jit(solution)/shard_map/ppermute | solution.py:226
  17.8 0.2 reduce-precision_convert_fusion.7
  18.1 0.8 %fusion.3 = f32[48,256]{1,0:T(8,128)S(1)} fusion(s32[4096]{0:T(1024)S(1)} %copy-done.2, bf16[16,4096]{1,0:T(8,128)(2,1)S(1)} %get-tuple-element.85, bf16[16,4096]{1,0:T(8,128)(2,1)S(1)} %get-tuple-element.84, bf16[16,4096]{1,0:T(8,128)(2,1)S(1)} %get-tuple-element.63), kind=kOutput, calls=%fused_computation.4 | convolution fusion | flops 102891520 | bytes 458752 | tf_op jit(solution)/shard_map/dot_general | solution.py:177
  18.9 0.1 fusion.42
  19.1 3.0 %collective-permute-start.1 = (f32[16,4224]{1,0:T(8,128)S(1)}, f32[16,4224]{1,0:T(8,128)S(1)}, u32[]{:S(2)}, u32[]{:S(2)}) collective-permute-start(f32[16,4224]{1,0:T(8,128)S(1)} %fusion.42), channel_id=1, source_target_pairs={{0,2},{1,3},{2,0},{3,1},{4,6},{5,7},{6,4},{7,5},{8,10},{9,11},{10,... | collective-permute-start | bytes 811016 | tf_op jit(solution)/shard_map/ppermute | solution.py:231
  22.0 0.8 copy.18
  22.8 0.8 copy.19
  23.5 6.1 %shard_map.111 = (f32[128,4096]{1,0:T(8,128)}, f32[128,4096]{1,0:T(8,128)}) custom-call(bf16[128,4096]{1,0:T(8,128)(2,1)} %q_ref.11, bf16[128,4096]{1,0:T(8,128)(2,1)} %k_ref.11, bf16[128,4096]{1,0:T(8,128)(2,1)} %v_ref.11, bf16[128,4096]{1,0:T(8,128)(2,1)} %g_ref.11, f32[16,32,128]{2,1,0:T(8,128)} %bitcast.16, f32[16,32,128]{2,1,0:T(8,128)} %bitcast.21), custom_call_target="tpu_custom_call" | custom-call | tf_op jit(solution)/shard_map/pallas_call | solution.py:139
  29.7 0.0 collective-permute-done.1
  29.7 0.0 collective-permute-start.2
  29.7 1.5 %collective-permute-done.2 = f32[16,4224]{1,0:T(8,128)S(1)} collective-permute-done((f32[16,4224]{1,0:T(8,128)S(1)}, f32[16,4224]{1,0:T(8,128)S(1)}, u32[]{:S(2)}, u32[]{:S(2)}) %collective-permute-start.2) | collective-permute-done | bytes 270368 | tf_op jit(solution)/shard_map/ppermute | solution.py:240
  31.3 0.1 reduce-precision_convert_fusion.5
  31.4 0.1 reduce-precision_convert_fusion.4
  31.5 0.8 %fusion.2 = f32[48,256]{1,0:T(8,128)S(1)} fusion(s32[4096]{0:T(1024)S(1)} %copy-done.2, bf16[16,4096]{1,0:T(8,128)(2,1)S(1)} %get-tuple-element.83, bf16[16,4096]{1,0:T(8,128)(2,1)S(1)} %get-tuple-element.82, bf16[16,4096]{1,0:T(8,128)(2,1)S(1)} %get-tuple-element.60), kind=kOutput, calls=%fused_computation.3 | convolution fusion | flops 102891520 | bytes 458752 | tf_op jit(solution)/shard_map/dot_general | solution.py:177
  32.4 0.1 fusion.40
  32.5 1.6 %collective-permute-start.3 = (f32[16,4224]{1,0:T(8,128)S(1)}, f32[16,4224]{1,0:T(8,128)S(1)}, u32[]{:S(2)}, u32[]{:S(2)}) collective-permute-start(f32[16,4224]{1,0:T(8,128)S(1)} %fusion.40), channel_id=1, source_target_pairs={{0,4},{1,5},{2,6},{3,7},{4,0},{5,1},{6,2},{7,3},{8,12},{9,13},{10,... | collective-permute-start | bytes 811016 | tf_op jit(solution)/shard_map/ppermute | solution.py:231
  34.2 6.1 %shard_map.112 = (f32[128,4096]{1,0:T(8,128)}, f32[128,4096]{1,0:T(8,128)}) custom-call(bf16[128,4096]{1,0:T(8,128)(2,1)} %q_ref.11, bf16[128,4096]{1,0:T(8,128)(2,1)} %k_ref.11, bf16[128,4096]{1,0:T(8,128)(2,1)} %v_ref.11, bf16[128,4096]{1,0:T(8,128)(2,1)} %g_ref.11, f32[16,32,128]{2,1,0:T(8,128)} %bitcast.17, ...), custom_call_target="tpu_custom_call", output_to_operand_aliasing={{0}: (6, {}), {1}: (7, {})} | custom-call | tf_op jit(solution)/shard_map/pallas_call | solution.py:139
  40.2 0.9 %collective-permute-done.3 = f32[16,4224]{1,0:T(8,128)S(1)} collective-permute-done((f32[16,4224]{1,0:T(8,128)S(1)}, f32[16,4224]{1,0:T(8,128)S(1)}, u32[]{:S(2)}, u32[]{:S(2)}) %collective-permute-start.3) | collective-permute-done | bytes 270368 | tf_op jit(solution)/shard_map/ppermute | solution.py:231
  41.1 0.0 collective-permute-start.4
  41.1 1.5 %collective-permute-done.4 = f32[16,4224]{1,0:T(8,128)S(1)} collective-permute-done((f32[16,4224]{1,0:T(8,128)S(1)}, f32[16,4224]{1,0:T(8,128)S(1)}, u32[]{:S(2)}, u32[]{:S(2)}) %collective-permute-start.4) | collective-permute-done | bytes 270368 | tf_op jit(solution)/shard_map/ppermute | solution.py:240
  42.7 0.1 reduce-precision_convert_fusion.3
  42.9 0.8 %fusion.1 = f32[48,256]{1,0:T(8,128)S(1)} fusion(s32[4096]{0:T(1024)S(1)} %copy-done.2, bf16[16,4096]{1,0:T(8,128)(2,1)S(1)} %get-tuple-element.81, bf16[16,4096]{1,0:T(8,128)(2,1)S(1)} %get-tuple-element.80, bf16[16,4096]{1,0:T(8,128)(2,1)S(1)} %get-tuple-element.57), kind=kOutput, calls=%fused_computation.2 | convolution fusion | flops 102891520 | bytes 458752 | tf_op jit(solution)/shard_map/dot_general | solution.py:177
  43.7 0.1 multiply_add_fusion
  43.8 0.1 fusion.38
  44.0 2.7 %collective-permute-start.5 = (f32[16,4224]{1,0:T(8,128)S(1)}, f32[16,4224]{1,0:T(8,128)S(1)}, u32[]{:S(2)}, u32[]{:S(2)}) collective-permute-start(f32[16,4224]{1,0:T(8,128)S(1)} %fusion.38), channel_id=1, source_target_pairs={{0,8},{1,9},{2,10},{3,11},{4,12},{5,13},{6,14},{7,15},{8,0},{9,1},... | collective-permute-start | bytes 811016 | tf_op jit(solution)/shard_map/ppermute | solution.py:231
  46.6 6.1 %shard_map.113 = (f32[128,4096]{1,0:T(8,128)}, f32[128,4096]{1,0:T(8,128)}) custom-call(bf16[128,4096]{1,0:T(8,128)(2,1)} %q_ref.11, bf16[128,4096]{1,0:T(8,128)(2,1)} %k_ref.11, bf16[128,4096]{1,0:T(8,128)(2,1)} %v_ref.11, bf16[128,4096]{1,0:T(8,128)(2,1)} %g_ref.11, f32[16,32,128]{2,1,0:T(8,128)} %bitcast.18, ...), custom_call_target="tpu_custom_call", output_to_operand_aliasing={{0}: (6, {}), {1}: (7, {})} | custom-call | tf_op jit(solution)/shard_map/pallas_call | solution.py:139
  52.7 6.1 %shard_map.114 = (f32[128,4096]{1,0:T(8,128)}, f32[128,4096]{1,0:T(8,128)}) custom-call(bf16[128,4096]{1,0:T(8,128)(2,1)} %q_ref.11, bf16[128,4096]{1,0:T(8,128)(2,1)} %k_ref.11, bf16[128,4096]{1,0:T(8,128)(2,1)} %v_ref.11, bf16[128,4096]{1,0:T(8,128)(2,1)} %g_ref.11, f32[16,32,128]{2,1,0:T(8,128)} %bitcast.19, ...), custom_call_target="tpu_custom_call", output_to_operand_aliasing={{0}: (6, {}), {1}: (7, {})} | custom-call | tf_op jit(solution)/shard_map/pallas_call | solution.py:139
  58.8 0.5 collective-permute-done.5
  59.3 0.0 collective-permute-start.6
  59.3 1.5 %collective-permute-done.6 = f32[16,4224]{1,0:T(8,128)S(1)} collective-permute-done((f32[16,4224]{1,0:T(8,128)S(1)}, f32[16,4224]{1,0:T(8,128)S(1)}, u32[]{:S(2)}, u32[]{:S(2)}) %collective-permute-start.6) | collective-permute-done | bytes 270368 | tf_op jit(solution)/shard_map/ppermute | solution.py:240
  60.8 0.3 reduce-precision_convert_fusion.1
  61.2 0.8 %fusion = f32[48,256]{1,0:T(8,128)S(1)} fusion(s32[4096]{0:T(1024)S(1)} %copy-done.2, bf16[16,4096]{1,0:T(8,128)(2,1)S(1)} %get-tuple-element.79, bf16[16,4096]{1,0:T(8,128)(2,1)S(1)} %get-tuple-element.78, bf16[16,4096]{1,0:T(8,128)(2,1)S(1)} %get-tuple-element.55), kind=kOutput, calls=%fused_computation.1 | convolution fusion | flops 102891520 | bytes 458752 | tf_op jit(solution)/shard_map/dot_general | solution.py:177
  62.0 0.6 multiply_reduce_fusion
  63.3 0.8 copy.21
  64.1 0.2 add_bitcast_fusion.1
  64.3 0.8 copy.20
  65.0 0.6 divide_bitcast_fusion
  65.7 12.1 %shard_map.115 = (bf16[128,4096]{1,0:T(8,128)(2,1)}, bf16[128,4096]{1,0:T(8,128)(2,1)}, bf16[128,4096]{1,0:T(8,128)(2,1)}, bf16[128,4096]{1,0:T(8,128)(2,1)}) custom-call(bf16[128,4096]{1,0:T(8,128)(2,1)} %q_ref.11, bf16[128,4096]{1,0:T(8,128)(2,1)} %k_ref.11, bf16[128,4096]{1,0:T(8,128)(2,1)} %v_ref.11, bf16[128,4096]{1,0:T(8,128)(2,1)} %g_ref.11, ...), custom_call_target="tpu_custom_call" | custom-call | tf_op jit(solution)/shard_map/pallas_call | solution.py:158
  (11 shorter events, 0.3 us)
Async XLA Ops:
  3.8 11.0 %copy-start.2 = (s32[4096]{0:T(1024)S(1)}, s32[4096]{0:T(1024)}, u32[]{:S(2)}) copy-start(s32[4096]{0:T(1024)} %param.13) | copy-start | bytes 49156
  13.8 1.9 %copy-start = (f32[16,4096]{1,0:T(8,128)S(1)}, f32[16,4096]{1,0:T(8,128)}, u32[]{:S(2)}) copy-start(f32[16,4096]{1,0:T(8,128)} %get-tuple-element.29) | copy-start | bytes 786436
  13.8 1.9 %copy-start.1 = (f32[16,4096]{1,0:T(8,128)S(1)}, f32[16,4096]{1,0:T(8,128)}, u32[]{:S(2)}) copy-start(f32[16,4096]{1,0:T(8,128)} %get-tuple-element.30) | copy-start | bytes 786436
  15.7 2.1 %collective-permute-start = (f32[16,8448]{1,0:T(8,128)S(1)}, f32[16,8448]{1,0:T(8,128)S(1)}, u32[]{:S(2)}, u32[]{:S(2)}) collective-permute-start(f32[16,8448]{1,0:T(8,128)S(1)} %pad_maximum_fusion), channel_id=1, source_target_pairs={{0,1},{1,0},{2,3},{3,2},{4,5},{5,4},{6,7},{7,6},{8,9},{9,8},{10,11... | collective-permute-start | bytes 1622024 | tf_op jit(solution)/shard_map/ppermute | solution.py:226
  19.1 10.6 %collective-permute-start.1 = (f32[16,4224]{1,0:T(8,128)S(1)}, f32[16,4224]{1,0:T(8,128)S(1)}, u32[]{:S(2)}, u32[]{:S(2)}) collective-permute-start(f32[16,4224]{1,0:T(8,128)S(1)} %fusion.42), channel_id=1, source_target_pairs={{0,2},{1,3},{2,0},{3,1},{4,6},{5,7},{6,4},{7,5},{8,10},{9,11},{10,... | collective-permute-start | bytes 811016 | tf_op jit(solution)/shard_map/ppermute | solution.py:231
  29.7 1.5 %collective-permute-start.2 = (f32[16,4224]{1,0:T(8,128)S(1)}, f32[16,4224]{1,0:T(8,128)S(1)}, u32[]{:S(2)}, u32[]{:S(2)}) collective-permute-start(f32[16,4224]{1,0:T(8,128)S(1)} %collective-permute-done.1), channel_id=1, source_target_pairs={{0,1},{1,0},{2,3},{3,2},{4,5},{5,4},{6,7},{7,6},{8,9},{9,8},{10,11... | collective-permute-start | bytes 811016 | tf_op jit(solution)/shard_map/ppermute | solution.py:240
  32.5 8.6 %collective-permute-start.3 = (f32[16,4224]{1,0:T(8,128)S(1)}, f32[16,4224]{1,0:T(8,128)S(1)}, u32[]{:S(2)}, u32[]{:S(2)}) collective-permute-start(f32[16,4224]{1,0:T(8,128)S(1)} %fusion.40), channel_id=1, source_target_pairs={{0,4},{1,5},{2,6},{3,7},{4,0},{5,1},{6,2},{7,3},{8,12},{9,13},{10,... | collective-permute-start | bytes 811016 | tf_op jit(solution)/shard_map/ppermute | solution.py:231
  41.1 1.5 %collective-permute-start.4 = (f32[16,4224]{1,0:T(8,128)S(1)}, f32[16,4224]{1,0:T(8,128)S(1)}, u32[]{:S(2)}, u32[]{:S(2)}) collective-permute-start(f32[16,4224]{1,0:T(8,128)S(1)} %collective-permute-done.3), channel_id=1, source_target_pairs={{0,1},{1,0},{2,3},{3,2},{4,5},{5,4},{6,7},{7,6},{8,9},{9,8},{10,11... | collective-permute-start | bytes 811016 | tf_op jit(solution)/shard_map/ppermute | solution.py:240
  44.0 15.3 %collective-permute-start.5 = (f32[16,4224]{1,0:T(8,128)S(1)}, f32[16,4224]{1,0:T(8,128)S(1)}, u32[]{:S(2)}, u32[]{:S(2)}) collective-permute-start(f32[16,4224]{1,0:T(8,128)S(1)} %fusion.38), channel_id=1, source_target_pairs={{0,8},{1,9},{2,10},{3,11},{4,12},{5,13},{6,14},{7,15},{8,0},{9,1},... | collective-permute-start | bytes 811016 | tf_op jit(solution)/shard_map/ppermute | solution.py:231
  59.3 1.5 %collective-permute-start.6 = (f32[16,4224]{1,0:T(8,128)S(1)}, f32[16,4224]{1,0:T(8,128)S(1)}, u32[]{:S(2)}, u32[]{:S(2)}) collective-permute-start(f32[16,4224]{1,0:T(8,128)S(1)} %collective-permute-done.5), channel_id=1, source_target_pairs={{0,1},{1,0},{2,3},{3,2},{4,5},{5,4},{6,7},{7,6},{8,9},{9,8},{10,11... | collective-permute-start | bytes 811016 | tf_op jit(solution)/shard_map/ppermute | solution.py:240

commit v11 on v10

--- a/solution.py
+++ b/solution.py
@@ -42,11 +42,22 @@
         tot_ref[:, cols] = tot
 
 
-def local_kernel(q_ref, k_ref, v_ref, g_ref, p_ref, r_ref, *refs):
+def to_modes(src_ref, stage_ref, dst_ref):
+    modes, width = src_ref.shape
+    lanes = width // LANE
+    for c in range(lanes):
+        stage_ref[c * modes : (c + 1) * modes, :] = src_ref[:, c * LANE : (c + 1) * LANE]
+    for m in range(modes):
+        dst_ref[m] = stage_ref[pl.ds(m, lanes, stride=modes), :]
+
+
+def local_kernel(q_ref, k_ref, v_ref, g_ref, pw_ref, rw_ref, *refs):
     f32 = jnp.float32
-    if len(refs) == 8:
+    if len(refs) == 11:
         refs = refs[2:]
-    filt_out, mg_out, mix_ref, up_ref, filt_ref, mg_ref = refs
+    filt_out, mg_out, mix_ref, up_ref, filt_ref, mg_ref, stage_ref, p_ref, r_ref = refs
+    to_modes(pw_ref, stage_ref, p_ref)
+    to_modes(rw_ref, stage_ref, r_ref)
     rows, width = q_ref.shape
     lanes = width // LANE
     for c in range(lanes):
@@ -78,11 +89,13 @@
 
 
 def correct_kernel(
-    q_ref, k_ref, v_ref, g_ref, fl_ref, ml_ref, p_ref, r_ref, s_ref, b_ref,
+    q_ref, k_ref, v_ref, g_ref, fl_ref, ml_ref, pw_ref, rw_ref, sw_ref, bw_ref,
     ho_ref, qg_ref, kg_ref, vg_ref,
-    filt_ref, mg_ref,
+    filt_ref, mg_ref, stage_ref, p_ref, r_ref, s_ref, b_ref,
 ):
     f32 = jnp.float32
+    for src, dst in ((pw_ref, p_ref), (rw_ref, r_ref), (sw_ref, s_ref), (bw_ref, b_ref)):
+        to_modes(src, stage_ref, dst)
     rows, width = q_ref.shape
     lanes = width // LANE
 
@@ -123,13 +136,13 @@
     )(query_proj, key_proj, value_proj, out_grad, factor)
 
 
-def local_scans(query_proj, key_proj, value_proj, out_grad, factor4, weight4, first, previous):
+def local_scans(query_proj, key_proj, value_proj, out_grad, factor, weight, first, previous):
     rows, width = query_proj.shape
-    modes = factor4.shape[0]
+    modes = factor.shape[0]
     lanes = BLOCK // LANE
     big = pl.BlockSpec((rows, BLOCK), lambda i: (0, i + first))
-    small = pl.BlockSpec((modes, lanes, LANE), lambda i: (0, i + first, 0))
-    operands = [query_proj, key_proj, value_proj, out_grad, factor4, weight4]
+    small = pl.BlockSpec((modes, BLOCK), lambda i: (0, i + first))
+    operands = [query_proj, key_proj, value_proj, out_grad, factor, weight]
     specs = [big, big, big, big, small, small]
     aliases = {}
     if previous is not None:
@@ -142,27 +155,30 @@
         in_specs=specs,
         out_specs=[big, big],
         out_shape=[jax.ShapeDtypeStruct((rows, width), jnp.float32)] * 2,
-        scratch_shapes=[pltpu.VMEM((lanes * rows, LANE), jnp.float32)] * 4,
+        scratch_shapes=[pltpu.VMEM((lanes * rows, LANE), jnp.float32)] * 4
+        + [pltpu.VMEM((lanes * modes, LANE), jnp.float32)]
+        + [pltpu.VMEM((modes, lanes, LANE), jnp.float32)] * 2,
         input_output_aliases=aliases,
     )(*operands)
 
 
-def corrected(query_proj, key_proj, value_proj, out_grad, local, factor4, weight4, state_in, adjoint_in):
+def corrected(query_proj, key_proj, value_proj, out_grad, local, factor, weight, state_in, adjoint_in):
     rows, width = query_proj.shape
-    modes = factor4.shape[0]
+    modes = factor.shape[0]
     lanes = BLOCK // LANE
     big = pl.BlockSpec((rows, BLOCK), lambda i: (0, i))
-    small = pl.BlockSpec((modes, lanes, LANE), lambda i: (0, i, 0))
+    small = pl.BlockSpec((modes, BLOCK), lambda i: (0, i))
     out_big = jax.ShapeDtypeStruct((rows, width), jnp.bfloat16)
-    tiles = [a.reshape(modes, width // LANE, LANE) for a in (state_in, adjoint_in)]
     return pl.pallas_call(
         correct_kernel,
         grid=(width // BLOCK,),
         in_specs=[big] * 6 + [small] * 4,
         out_specs=[big, big, big, big],
         out_shape=[out_big] * 4,
-        scratch_shapes=[pltpu.VMEM((lanes * rows, LANE), jnp.float32)] * 2,
-    )(query_proj, key_proj, value_proj, out_grad, *local, factor4, weight4, *tiles)
+        scratch_shapes=[pltpu.VMEM((lanes * rows, LANE), jnp.float32)] * 2
+        + [pltpu.VMEM((lanes * modes, LANE), jnp.float32)]
+        + [pltpu.VMEM((modes, lanes, LANE), jnp.float32)] * 4,
+    )(query_proj, key_proj, value_proj, out_grad, *local, factor, weight, state_in, adjoint_in)
 
 
 def split_dot(a, member):
@@ -195,8 +211,6 @@
         )
         width = query_proj.shape[1]
         modes = factor.shape[0]
-        factor4 = factor.reshape(modes, width // LANE, LANE)
-        weight4 = weight.reshape(modes, width // LANE, LANE)
         pieces = width // BLOCK
         local = None
         made = 0
@@ -232,7 +246,7 @@
                 if need > made:
                     while made < need:
                         local = local_scans(
-                            query_proj, key_proj, value_proj, out_grad, factor4, weight4, made,
+                            query_proj, key_proj, value_proj, out_grad, factor, weight, made,
                             local,
                         )
                         made += 1
@@ -262,11 +276,11 @@
 
         while made < pieces:
             local = local_scans(
-                query_proj, key_proj, value_proj, out_grad, factor4, weight4, made, local
+                query_proj, key_proj, value_proj, out_grad, factor, weight, made, local
             )
             made += 1
         hyena_out, query_grad, key_grad, value_grad = corrected(
-            query_proj, key_proj, value_proj, out_grad, local, factor4, weight4, state_in, adjoint_in
+            query_proj, key_proj, value_proj, out_grad, local, factor, weight, state_in, adjoint_in
         )
         filter_grad = grad_cube.T
         filter_update = filter_grad / jnp.sqrt(jnp.mean(filter_grad * filter_grad) + 1e-06)

time: 78.2 us -> 78.4 us (level)
  local copies, waits for them, and re-layouts: 3.04 us -> 0.01 us
  other arithmetic: 5.76 us -> 7.8 us
    unnamed x10 -> x6, local copies, waits for them, and re-layouts: 3.04 us -> 0.01 us
    convert_element_type x6, other arithmetic: 2.54 us -> 3.87 us  [split_dot(): hi = top.astype(bf16)]
    add x0 -> x1, other arithmetic: none -> 0.91 us  [on_device(): state_in = state_in + jnp.where(upper, span(offset) * got_fwd, 0.0)]
  transfers between devices with their start and end apart: 7 -> 7, of which waited for: 6 -> 7; matrix products, arithmetic and copies ran while one was open for 2% -> 0% of each run, Pallas kernels for 31% -> 31%
where the time goes in v11:
time: 78.4 us; the launch traced here: 78 us
  Pallas kernels  47.1 us (60%)
  starting transfers between devices  8.16 us (10%)
  other arithmetic  7.8 us (10%)
  waiting for transfers between devices  7.77 us (10%)
  matrix products  5.68 us (7%)
  between operations  1.52 us (2%)
    pallas_call x4, Pallas kernels, local_scans(): pl.pallas_call(local_kernel, grid=(1,), in_specs=specs, out_specs=[big, b...  24.6 us
    pallas_call x1, Pallas kernels, corrected(): pl.pallas_call(correct_kernel, grid=(width // BLOCK,), in_specs=[big] * 6...  12.5 us
    pallas_call x1, Pallas kernels, local_carries(): pl.pallas_call(carry_kernel, grid=(width // BLOCK,), in_specs=[big, big,...  9.96 us
    ppermute x3, starting transfers between devices, on_device(): got_mine = lax.ppermute(mine, 'ctx', pairs)  7.63 us
    dot_general x6, matrix products, split_dot(): jnp.dot(jnp.concatenate([hi, mid, lo], axis=0), member, preferred_element...  5.68 us
    ppermute x3, waiting for transfers between devices, on_device(): lax.ppermute(got_mine, 'ctx', [(i, i ^ 1) for i in range(count)])  4.63 us
    convert_element_type x6, other arithmetic, split_dot(): hi = top.astype(bf16)  3.87 us
    ppermute x3, waiting for transfers between devices, on_device(): got_mine = lax.ppermute(mine, 'ctx', pairs)  1.58 us
  transfers between devices with their start and end apart: 7, of which 7 were waited for; matrix products, arithmetic and copies ran while one was open for 0% of the time, Pallas kernels for 31%

profile of v11, /device:TPU:0, one launch (start us, length us, event | category | flops | bytes accessed | tf_op | source)
XLA Modules:
  0.0 78.0 jit_solution(11467660926701194651)
XLA Ops:
  0.6 0.7 reduce-precision_convert_fusion.11
  1.4 1.6 %fusion.5 = f32[96,4096]{1,0:T(8,128)S(1)} fusion(s32[4096]{0:T(1024)} %param.13, bf16[32,256]{1,0:T(8,128)(2,1)S(1)} %get-tuple-element.90, bf16[32,256]{1,0:T(8,128)(2,1)S(1)} %get-tuple-element.89, bf16[32,256]{1,0:T(8,128)(2,1)S(1)} %get-tuple-element.88), kind=kOutput, calls=%fused_computation.6 | convolution fusion | flops 202522624 | bytes 1638400 | tf_op jit(solution)/shard_map/dot_general | solution.py:193
  3.0 0.1 slice_add_fusion
  3.1 0.8 fusion.58.p_ref.pw_ref
  3.8 0.0 copy-start.2
  3.8 10.0 %shard_map.110 = (f32[16,4096]{1,0:T(8,128)}, f32[16,4096]{1,0:T(8,128)}, f32[16,4096]{1,0:T(8,128)}) custom-call(bf16[128,4096]{1,0:T(8,128)(2,1)} %q_ref.11, bf16[128,4096]{1,0:T(8,128)(2,1)} %k_ref.11, bf16[128,4096]{1,0:T(8,128)(2,1)} %v_ref.11, bf16[128,4096]{1,0:T(8,128)(2,1)} %g_ref.11, f32[16,4096]{1,0:T(8,128)} %fusion.58.p_ref.pw_ref), custom_call_target="tpu_custom_call" | custom-call | tf_op jit(solution)/shard_map/pallas_call | solution.py:129
  13.8 0.0 copy-start
  13.8 0.0 copy-start.1
  13.8 1.1 %reduce-precision_convert_fusion.9 = (bf16[16,4096]{1,0:T(8,128)(2,1)S(1)}, bf16[16,4096]{1,0:T(8,128)(2,1)S(1)}, bf16[16,4096]{1,0:T(8,128)(2,1)S(1)}) fusion(f32[16,4096]{1,0:T(8,128)} %get-tuple-element.31), kind=kLoop, calls=%fused_computation.69 | loop fusion | flops 458752 | bytes 655360 | tf_op jit(solution)/shard_map/convert_element_type | solution.py:189
  14.8 0.0 copy-done.2
  14.8 0.8 %fusion.4 = f32[48,256]{1,0:T(8,128)S(1)} fusion(s32[4096]{0:T(1024)S(1)} %copy-done.2, bf16[16,4096]{1,0:T(8,128)(2,1)S(1)} %get-tuple-element.86, bf16[16,4096]{1,0:T(8,128)(2,1)S(1)} %get-tuple-element.87, bf16[16,4096]{1,0:T(8,128)(2,1)S(1)} %get-tuple-element.85), kind=kOutput, calls=%fused_computation.5 | convolution fusion | flops 102891520 | bytes 458752 | tf_op jit(solution)/shard_map/dot_general | solution.py:193
  15.7 0.0 copy-done
  15.7 0.0 copy-done.1
  15.8 0.5 collective-permute-start
  16.3 1.6 %collective-permute-done = f32[16,8448]{1,0:T(8,128)S(1)} collective-permute-done((f32[16,8448]{1,0:T(8,128)S(1)}, f32[16,8448]{1,0:T(8,128)S(1)}, u32[]{:S(2)}, u32[]{:S(2)}) %collective-permute-start) | collective-permute-done | bytes 540704 | tf_op jit(solution)/shard_map/ppermute | solution.py:240
  17.8 0.8 %reduce-precision_convert_fusion.7 = (bf16[16,4096]{1,0:T(8,128)(2,1)S(1)}, f32[16,4096]{1,0:T(8,128)S(1)}, f32[16,4096]{1,0:T(8,128)S(1)}, f32[16,4096]{1,0:T(8,128)S(1)}, f32[16,4096]{1,0:T(8,128)}) fusion(f32[16,4096]{1,0:T(8,128)S(1)} %copy-done.1, f32[16,8448]{1,0:T(8,128)S(1)} %collective-permute-done, f32[16,4096]{1,0:T(8,128)S(1)} %copy-done, ...), kind=kLoop, calls=%fused_computation.65 | loop fusion | flops 917504 | bytes 2752513 | tf_op jit(solution)/shard_map/convert_element_type | solution.py:189
  18.7 0.8 %fusion.3 = f32[48,256]{1,0:T(8,128)S(1)} fusion(s32[4096]{0:T(1024)S(1)} %copy-done.2, bf16[16,4096]{1,0:T(8,128)(2,1)S(1)} %get-tuple-element.84, bf16[16,4096]{1,0:T(8,128)(2,1)S(1)} %get-tuple-element.83, bf16[16,4096]{1,0:T(8,128)(2,1)S(1)} %get-tuple-element.63), kind=kOutput, calls=%fused_computation.4 | convolution fusion | flops 102891520 | bytes 458752 | tf_op jit(solution)/shard_map/dot_general | solution.py:193
  19.5 0.1 fusion.42
  19.7 3.0 %collective-permute-start.1 = (f32[16,4224]{1,0:T(8,128)S(1)}, f32[16,4224]{1,0:T(8,128)S(1)}, u32[]{:S(2)}, u32[]{:S(2)}) collective-permute-start(f32[16,4224]{1,0:T(8,128)S(1)} %fusion.42), channel_id=1, source_target_pairs={{0,2},{1,3},{2,0},{3,1},{4,6},{5,7},{6,4},{7,5},{8,10},{9,11},{10,... | collective-permute-start | bytes 811016 | tf_op jit(solution)/shard_map/ppermute | solution.py:245
  22.6 6.2 %shard_map.111 = (f32[128,4096]{1,0:T(8,128)}, f32[128,4096]{1,0:T(8,128)}) custom-call(bf16[128,4096]{1,0:T(8,128)(2,1)} %q_ref.11, bf16[128,4096]{1,0:T(8,128)(2,1)} %k_ref.11, bf16[128,4096]{1,0:T(8,128)(2,1)} %v_ref.11, bf16[128,4096]{1,0:T(8,128)(2,1)} %g_ref.11, f32[16,4096]{1,0:T(8,128)} %fusion.58.p_ref.pw_ref, f32[16,4096]{1,0:T(8,128)} %get-tuple-element.76.rw_ref), custom_call_target="tpu_custom_call" | custom-call | tf_op jit(solution)/shard_map/pallas_call | solution.py:152
  28.8 0.6 collective-permute-done.1
  29.4 0.0 collective-permute-start.2
  29.4 1.5 %collective-permute-done.2 = f32[16,4224]{1,0:T(8,128)S(1)} collective-permute-done((f32[16,4224]{1,0:T(8,128)S(1)}, f32[16,4224]{1,0:T(8,128)S(1)}, u32[]{:S(2)}, u32[]{:S(2)}) %collective-permute-start.2) | collective-permute-done | bytes 270368 | tf_op jit(solution)/shard_map/ppermute | solution.py:254
  31.0 0.1 reduce-precision_convert_fusion.5
  31.2 0.1 reduce-precision_convert_fusion.4
  31.3 0.8 %fusion.2 = f32[48,256]{1,0:T(8,128)S(1)} fusion(s32[4096]{0:T(1024)S(1)} %copy-done.2, bf16[16,4096]{1,0:T(8,128)(2,1)S(1)} %get-tuple-element.82, bf16[16,4096]{1,0:T(8,128)(2,1)S(1)} %get-tuple-element.81, bf16[16,4096]{1,0:T(8,128)(2,1)S(1)} %get-tuple-element.60), kind=kOutput, calls=%fused_computation.3 | convolution fusion | flops 102891520 | bytes 458752 | tf_op jit(solution)/shard_map/dot_general | solution.py:193
  32.1 0.1 fusion.40
  32.3 1.9 %collective-permute-start.3 = (f32[16,4224]{1,0:T(8,128)S(1)}, f32[16,4224]{1,0:T(8,128)S(1)}, u32[]{:S(2)}, u32[]{:S(2)}) collective-permute-start(f32[16,4224]{1,0:T(8,128)S(1)} %fusion.40), channel_id=1, source_target_pairs={{0,4},{1,5},{2,6},{3,7},{4,0},{5,1},{6,2},{7,3},{8,12},{9,13},{10,... | collective-permute-start | bytes 811016 | tf_op jit(solution)/shard_map/ppermute | solution.py:245
  34.1 6.1 %shard_map.112 = (f32[128,4096]{1,0:T(8,128)}, f32[128,4096]{1,0:T(8,128)}) custom-call(bf16[128,4096]{1,0:T(8,128)(2,1)} %q_ref.11, bf16[128,4096]{1,0:T(8,128)(2,1)} %k_ref.11, bf16[128,4096]{1,0:T(8,128)(2,1)} %v_ref.11, bf16[128,4096]{1,0:T(8,128)(2,1)} %g_ref.11, f32[16,4096]{1,0:T(8,128)} %fusion.58.p_ref.pw_ref, ...), custom_call_target="tpu_custom_call", output_to_operand_aliasing={{0}: (6, {}), {1}: (7, {})} | custom-call | tf_op jit(solution)/shard_map/pallas_call | solution.py:152
  40.3 0.7 collective-permute-done.3
  40.9 0.0 collective-permute-start.4
  40.9 1.5 %collective-permute-done.4 = f32[16,4224]{1,0:T(8,128)S(1)} collective-permute-done((f32[16,4224]{1,0:T(8,128)S(1)}, f32[16,4224]{1,0:T(8,128)S(1)}, u32[]{:S(2)}, u32[]{:S(2)}) %collective-permute-start.4) | collective-permute-done | bytes 270368 | tf_op jit(solution)/shard_map/ppermute | solution.py:254
  42.5 0.1 reduce-precision_convert_fusion.3
  42.7 0.8 %fusion.1 = f32[48,256]{1,0:T(8,128)S(1)} fusion(s32[4096]{0:T(1024)S(1)} %copy-done.2, bf16[16,4096]{1,0:T(8,128)(2,1)S(1)} %get-tuple-element.80, bf16[16,4096]{1,0:T(8,128)(2,1)S(1)} %get-tuple-element.79, bf16[16,4096]{1,0:T(8,128)(2,1)S(1)} %get-tuple-element.57), kind=kOutput, calls=%fused_computation.2 | convolution fusion | flops 102891520 | bytes 458752 | tf_op jit(solution)/shard_map/dot_general | solution.py:193
  43.5 0.1 multiply_add_fusion
  43.6 0.1 fusion.38
  43.8 2.8 %collective-permute-start.5 = (f32[16,4224]{1,0:T(8,128)S(1)}, f32[16,4224]{1,0:T(8,128)S(1)}, u32[]{:S(2)}, u32[]{:S(2)}) collective-permute-start(f32[16,4224]{1,0:T(8,128)S(1)} %fusion.38), channel_id=1, source_target_pairs={{0,8},{1,9},{2,10},{3,11},{4,12},{5,13},{6,14},{7,15},{8,0},{9,1},... | collective-permute-start | bytes 811016 | tf_op jit(solution)/shard_map/ppermute | solution.py:245
  46.6 6.1 %shard_map.113 = (f32[128,4096]{1,0:T(8,128)}, f32[128,4096]{1,0:T(8,128)}) custom-call(bf16[128,4096]{1,0:T(8,128)(2,1)} %q_ref.11, bf16[128,4096]{1,0:T(8,128)(2,1)} %k_ref.11, bf16[128,4096]{1,0:T(8,128)(2,1)} %v_ref.11, bf16[128,4096]{1,0:T(8,128)(2,1)} %g_ref.11, f32[16,4096]{1,0:T(8,128)} %fusion.58.p_ref.pw_ref, ...), custom_call_target="tpu_custom_call", output_to_operand_aliasing={{0}: (6, {}), {1}: (7, {})} | custom-call | tf_op jit(solution)/shard_map/pallas_call | solution.py:152
  52.7 6.1 %shard_map.114 = (f32[128,4096]{1,0:T(8,128)}, f32[128,4096]{1,0:T(8,128)}) custom-call(bf16[128,4096]{1,0:T(8,128)(2,1)} %q_ref.11, bf16[128,4096]{1,0:T(8,128)(2,1)} %k_ref.11, bf16[128,4096]{1,0:T(8,128)(2,1)} %v_ref.11, bf16[128,4096]{1,0:T(8,128)(2,1)} %g_ref.11, f32[16,4096]{1,0:T(8,128)} %fusion.58.p_ref.pw_ref, ...), custom_call_target="tpu_custom_call", output_to_operand_aliasing={{0}: (6, {}), {1}: (7, {})} | custom-call | tf_op jit(solution)/shard_map/pallas_call | solution.py:152
  58.9 0.3 collective-permute-done.5
  59.2 0.0 collective-permute-start.6
  59.2 1.5 %collective-permute-done.6 = f32[16,4224]{1,0:T(8,128)S(1)} collective-permute-done((f32[16,4224]{1,0:T(8,128)S(1)}, f32[16,4224]{1,0:T(8,128)S(1)}, u32[]{:S(2)}, u32[]{:S(2)}) %collective-permute-start.6) | collective-permute-done | bytes 270368 | tf_op jit(solution)/shard_map/ppermute | solution.py:254
  60.8 1.0 %reduce-precision_convert_fusion.1 = (bf16[16,4096]{1,0:T(8,128)(2,1)S(1)}, f32[16,4096]{1,0:T(8,128)S(1)}, f32[16,4096]{1,0:T(8,128)}) fusion(f32[16,4096]{1,0:T(8,128)S(1)} %multiply_add_fusion, f32[16,4224]{1,0:T(8,128)S(1)} %get-tuple-element.70, f32[16,4224]{1,0:T(8,128)S(1)} %get-tuple-element.71, f32[16,4096]{1,0:T(8,128)S(1)} %get-tuple-element.68, ...), kind=kLoop, calls=%fused_computation.53 | loop fusion | flops 1507328 | bytes 3031056 | tf_op jit(solution)/shard_map/convert_element_type | solution.py:189
  61.8 0.8 %fusion = f32[48,256]{1,0:T(8,128)S(1)} fusion(s32[4096]{0:T(1024)S(1)} %copy-done.2, bf16[16,4096]{1,0:T(8,128)(2,1)S(1)} %get-tuple-element.78, bf16[16,4096]{1,0:T(8,128)(2,1)S(1)} %get-tuple-element.77, bf16[16,4096]{1,0:T(8,128)(2,1)S(1)} %get-tuple-element.55), kind=kOutput, calls=%fused_computation.1 | convolution fusion | flops 102891520 | bytes 458752 | tf_op jit(solution)/shard_map/dot_general | solution.py:193
  62.6 0.6 multiply_reduce_fusion
  63.9 0.6 divide_bitcast_fusion
  64.5 0.9 %select_add_fusion.1.sw_ref = f32[16,4096]{1,0:T(8,128)} fusion(f32[16,4224]{1,0:T(8,128)S(1)} %get-tuple-element.71, f32[16,4224]{1,0:T(8,128)S(1)} %get-tuple-element.73, f32[16,4224]{1,0:T(8,128)S(1)} %get-tuple-element.75, f32[16,8448]{1,0:T(8,128)S(1)} %collective-permute-done, f32[]{:T(128)S(6)} %mul.187, f32[]{:T(128)S(6)} %mul.183, f32[]{:T(128)S(6)} %mul.179, ...), kind=kLoop, calls=%fused_computation.87 | loop fusion | flops 1048576 | bytes 1572880 | tf_op jit(solution)/shard_map/add | solution.py:269
  65.5 12.5 %shard_map.115 = (bf16[128,4096]{1,0:T(8,128)(2,1)}, bf16[128,4096]{1,0:T(8,128)(2,1)}, bf16[128,4096]{1,0:T(8,128)(2,1)}, bf16[128,4096]{1,0:T(8,128)(2,1)}) custom-call(bf16[128,4096]{1,0:T(8,128)(2,1)} %q_ref.11, bf16[128,4096]{1,0:T(8,128)(2,1)} %k_ref.11, bf16[128,4096]{1,0:T(8,128)(2,1)} %v_ref.11, bf16[128,4096]{1,0:T(8,128)(2,1)} %g_ref.11, ...), custom_call_target="tpu_custom_call" | custom-call | tf_op jit(solution)/shard_map/pallas_call | solution.py:172
  (11 shorter events, 0.3 us)
Async XLA Ops:
  3.8 11.0 %copy-start.2 = (s32[4096]{0:T(1024)S(1)}, s32[4096]{0:T(1024)}, u32[]{:S(2)}) copy-start(s32[4096]{0:T(1024)} %param.13) | copy-start | bytes 49156
  13.8 1.9 %copy-start = (f32[16,4096]{1,0:T(8,128)S(1)}, f32[16,4096]{1,0:T(8,128)}, u32[]{:S(2)}) copy-start(f32[16,4096]{1,0:T(8,128)} %get-tuple-element.29) | copy-start | bytes 786436
  13.8 1.9 %copy-start.1 = (f32[16,4096]{1,0:T(8,128)S(1)}, f32[16,4096]{1,0:T(8,128)}, u32[]{:S(2)}) copy-start(f32[16,4096]{1,0:T(8,128)} %get-tuple-element.30) | copy-start | bytes 786436
  15.8 2.1 %collective-permute-start = (f32[16,8448]{1,0:T(8,128)S(1)}, f32[16,8448]{1,0:T(8,128)S(1)}, u32[]{:S(2)}, u32[]{:S(2)}) collective-permute-start(f32[16,8448]{1,0:T(8,128)S(1)} %pad_maximum_fusion), channel_id=1, source_target_pairs={{0,1},{1,0},{2,3},{3,2},{4,5},{5,4},{6,7},{7,6},{8,9},{9,8},{10,11... | collective-permute-start | bytes 1622024 | tf_op jit(solution)/shard_map/ppermute | solution.py:240
  19.7 9.7 %collective-permute-start.1 = (f32[16,4224]{1,0:T(8,128)S(1)}, f32[16,4224]{1,0:T(8,128)S(1)}, u32[]{:S(2)}, u32[]{:S(2)}) collective-permute-start(f32[16,4224]{1,0:T(8,128)S(1)} %fusion.42), channel_id=1, source_target_pairs={{0,2},{1,3},{2,0},{3,1},{4,6},{5,7},{6,4},{7,5},{8,10},{9,11},{10,... | collective-permute-start | bytes 811016 | tf_op jit(solution)/shard_map/ppermute | solution.py:245
  29.4 1.5 %collective-permute-start.2 = (f32[16,4224]{1,0:T(8,128)S(1)}, f32[16,4224]{1,0:T(8,128)S(1)}, u32[]{:S(2)}, u32[]{:S(2)}) collective-permute-start(f32[16,4224]{1,0:T(8,128)S(1)} %collective-permute-done.1), channel_id=1, source_target_pairs={{0,1},{1,0},{2,3},{3,2},{4,5},{5,4},{6,7},{7,6},{8,9},{9,8},{10,11... | collective-permute-start | bytes 811016 | tf_op jit(solution)/shard_map/ppermute | solution.py:254
  32.3 8.6 %collective-permute-start.3 = (f32[16,4224]{1,0:T(8,128)S(1)}, f32[16,4224]{1,0:T(8,128)S(1)}, u32[]{:S(2)}, u32[]{:S(2)}) collective-permute-start(f32[16,4224]{1,0:T(8,128)S(1)} %fusion.40), channel_id=1, source_target_pairs={{0,4},{1,5},{2,6},{3,7},{4,0},{5,1},{6,2},{7,3},{8,12},{9,13},{10,... | collective-permute-start | bytes 811016 | tf_op jit(solution)/shard_map/ppermute | solution.py:245
  40.9 1.5 %collective-permute-start.4 = (f32[16,4224]{1,0:T(8,128)S(1)}, f32[16,4224]{1,0:T(8,128)S(1)}, u32[]{:S(2)}, u32[]{:S(2)}) collective-permute-start(f32[16,4224]{1,0:T(8,128)S(1)} %collective-permute-done.3), channel_id=1, source_target_pairs={{0,1},{1,0},{2,3},{3,2},{4,5},{5,4},{6,7},{7,6},{8,9},{9,8},{10,11... | collective-permute-start | bytes 811016 | tf_op jit(solution)/shard_map/ppermute | solution.py:254
  43.8 15.4 %collective-permute-start.5 = (f32[16,4224]{1,0:T(8,128)S(1)}, f32[16,4224]{1,0:T(8,128)S(1)}, u32[]{:S(2)}, u32[]{:S(2)}) collective-permute-start(f32[16,4224]{1,0:T(8,128)S(1)} %fusion.38), channel_id=1, source_target_pairs={{0,8},{1,9},{2,10},{3,11},{4,12},{5,13},{6,14},{7,15},{8,0},{9,1},... | collective-permute-start | bytes 811016 | tf_op jit(solution)/shard_map/ppermute | solution.py:245
  59.2 1.5 %collective-permute-start.6 = (f32[16,4224]{1,0:T(8,128)S(1)}, f32[16,4224]{1,0:T(8,128)S(1)}, u32[]{:S(2)}, u32[]{:S(2)}) collective-permute-start(f32[16,4224]{1,0:T(8,128)S(1)} %collective-permute-done.5), channel_id=1, source_target_pairs={{0,1},{1,0},{2,3},{3,2},{4,5},{5,4},{6,7},{7,6},{8,9},{9,8},{10,11... | collective-permute-start | bytes 811016 | tf_op jit(solution)/shard_map/ppermute | solution.py:254

commit v12 on v11

--- a/solution.py
+++ b/solution.py
@@ -109,7 +109,7 @@
 
     p = p_ref[...]
     r = r_ref[...]
-    lax.fori_loop(0, rows, body, ((r * p) * s_ref[...], (r * p) * b_ref[...]), unroll=2)
+    lax.fori_loop(0, rows, body, ((r * p) * s_ref[...], (r * p) * b_ref[...]), unroll=4)
     for c in range(lanes):
         cols = slice(c * LANE, (c + 1) * LANE)
         band = slice(c * rows, (c + 1) * rows)

time: 78.4 us -> 76.8 us (0.980)
  Pallas kernels: 47.1 us -> 45.4 us
    pallas_call x1, Pallas kernels: 12.5 us -> 10.9 us  [corrected(): pl.pallas_call(correct_kernel, grid=(width // BLOCK,), in_specs=[big] * 6...]
  transfers between devices with their start and end apart: 7 -> 7, of which waited for: 7 -> 7; matrix products, arithmetic and copies ran while one was open for 0% -> 0% of each run, Pallas kernels for 31% -> 32%
where the time goes in v12:
time: 76.8 us; the launch traced here: 76.4 us
  Pallas kernels  45.4 us (59%)
  starting transfers between devices  8.16 us (11%)
  other arithmetic  7.8 us (10%)
  waiting for transfers between devices  7.77 us (10%)
  matrix products  5.68 us (7%)
  between operations  1.52 us (2%)
    pallas_call x4, Pallas kernels, local_scans(): pl.pallas_call(local_kernel, grid=(1,), in_specs=specs, out_specs=[big, b...  24.6 us
    pallas_call x1, Pallas kernels, corrected(): pl.pallas_call(correct_kernel, grid=(width // BLOCK,), in_specs=[big] * 6...  10.9 us
    pallas_call x1, Pallas kernels, local_carries(): pl.pallas_call(carry_kernel, grid=(width // BLOCK,), in_specs=[big, big,...  9.96 us
    ppermute x3, starting transfers between devices, on_device(): got_mine = lax.ppermute(mine, 'ctx', pairs)  7.63 us
    dot_general x6, matrix products, split_dot(): jnp.dot(jnp.concatenate([hi, mid, lo], axis=0), member, preferred_element...  5.68 us
    ppermute x3, waiting for transfers between devices, on_device(): lax.ppermute(got_mine, 'ctx', [(i, i ^ 1) for i in range(count)])  4.63 us
    convert_element_type x6, other arithmetic, split_dot(): hi = top.astype(bf16)  3.87 us
    ppermute x3, waiting for transfers between devices, on_device(): got_mine = lax.ppermute(mine, 'ctx', pairs)  1.58 us
  transfers between devices with their start and end apart: 7, of which 7 were waited for; matrix products, arithmetic and copies ran while one was open for 0% of the time, Pallas kernels for 32%

profile of v12, /device:TPU:0, one launch (start us, length us, event | category | flops | bytes accessed | tf_op | source)
XLA Modules:
  0.0 76.4 jit_solution(4372385340604382815)
XLA Ops:
  0.6 0.7 reduce-precision_convert_fusion.11
  1.4 1.6 %fusion.5 = f32[96,4096]{1,0:T(8,128)S(1)} fusion(s32[4096]{0:T(1024)} %param.13, bf16[32,256]{1,0:T(8,128)(2,1)S(1)} %get-tuple-element.90, bf16[32,256]{1,0:T(8,128)(2,1)S(1)} %get-tuple-element.89, bf16[32,256]{1,0:T(8,128)(2,1)S(1)} %get-tuple-element.88), kind=kOutput, calls=%fused_computation.6 | convolution fusion | flops 202522624 | bytes 1638400 | tf_op jit(solution)/shard_map/dot_general | solution.py:193
  3.0 0.1 slice_add_fusion
  3.1 0.8 fusion.58.p_ref.pw_ref
  3.8 0.0 copy-start.2
  3.8 10.0 %shard_map.110 = (f32[16,4096]{1,0:T(8,128)}, f32[16,4096]{1,0:T(8,128)}, f32[16,4096]{1,0:T(8,128)}) custom-call(bf16[128,4096]{1,0:T(8,128)(2,1)} %q_ref.11, bf16[128,4096]{1,0:T(8,128)(2,1)} %k_ref.11, bf16[128,4096]{1,0:T(8,128)(2,1)} %v_ref.11, bf16[128,4096]{1,0:T(8,128)(2,1)} %g_ref.11, f32[16,4096]{1,0:T(8,128)} %fusion.58.p_ref.pw_ref), custom_call_target="tpu_custom_call" | custom-call | tf_op jit(solution)/shard_map/pallas_call | solution.py:129
  13.8 0.0 copy-start
  13.8 0.0 copy-start.1
  13.8 1.1 %reduce-precision_convert_fusion.9 = (bf16[16,4096]{1,0:T(8,128)(2,1)S(1)}, bf16[16,4096]{1,0:T(8,128)(2,1)S(1)}, bf16[16,4096]{1,0:T(8,128)(2,1)S(1)}) fusion(f32[16,4096]{1,0:T(8,128)} %get-tuple-element.31), kind=kLoop, calls=%fused_computation.69 | loop fusion | flops 458752 | bytes 655360 | tf_op jit(solution)/shard_map/convert_element_type | solution.py:189
  14.8 0.0 copy-done.2
  14.8 0.8 %fusion.4 = f32[48,256]{1,0:T(8,128)S(1)} fusion(s32[4096]{0:T(1024)S(1)} %copy-done.2, bf16[16,4096]{1,0:T(8,128)(2,1)S(1)} %get-tuple-element.86, bf16[16,4096]{1,0:T(8,128)(2,1)S(1)} %get-tuple-element.87, bf16[16,4096]{1,0:T(8,128)(2,1)S(1)} %get-tuple-element.85), kind=kOutput, calls=%fused_computation.5 | convolution fusion | flops 102891520 | bytes 458752 | tf_op jit(solution)/shard_map/dot_general | solution.py:193
  15.7 0.0 copy-done
  15.7 0.0 copy-done.1
  15.8 0.5 collective-permute-start
  16.3 1.6 %collective-permute-done = f32[16,8448]{1,0:T(8,128)S(1)} collective-permute-done((f32[16,8448]{1,0:T(8,128)S(1)}, f32[16,8448]{1,0:T(8,128)S(1)}, u32[]{:S(2)}, u32[]{:S(2)}) %collective-permute-start) | collective-permute-done | bytes 540704 | tf_op jit(solution)/shard_map/ppermute | solution.py:240
  17.8 0.8 %reduce-precision_convert_fusion.7 = (bf16[16,4096]{1,0:T(8,128)(2,1)S(1)}, f32[16,4096]{1,0:T(8,128)S(1)}, f32[16,4096]{1,0:T(8,128)S(1)}, f32[16,4096]{1,0:T(8,128)S(1)}, f32[16,4096]{1,0:T(8,128)}) fusion(f32[16,4096]{1,0:T(8,128)S(1)} %copy-done.1, f32[16,8448]{1,0:T(8,128)S(1)} %collective-permute-done, f32[16,4096]{1,0:T(8,128)S(1)} %copy-done, ...), kind=kLoop, calls=%fused_computation.65 | loop fusion | flops 917504 | bytes 2752513 | tf_op jit(solution)/shard_map/convert_element_type | solution.py:189
  18.7 0.8 %fusion.3 = f32[48,256]{1,0:T(8,128)S(1)} fusion(s32[4096]{0:T(1024)S(1)} %copy-done.2, bf16[16,4096]{1,0:T(8,128)(2,1)S(1)} %get-tuple-element.84, bf16[16,4096]{1,0:T(8,128)(2,1)S(1)} %get-tuple-element.83, bf16[16,4096]{1,0:T(8,128)(2,1)S(1)} %get-tuple-element.63), kind=kOutput, calls=%fused_computation.4 | convolution fusion | flops 102891520 | bytes 458752 | tf_op jit(solution)/shard_map/dot_general | solution.py:193
  19.5 0.1 fusion.42
  19.7 3.0 %collective-permute-start.1 = (f32[16,4224]{1,0:T(8,128)S(1)}, f32[16,4224]{1,0:T(8,128)S(1)}, u32[]{:S(2)}, u32[]{:S(2)}) collective-permute-start(f32[16,4224]{1,0:T(8,128)S(1)} %fusion.42), channel_id=1, source_target_pairs={{0,2},{1,3},{2,0},{3,1},{4,6},{5,7},{6,4},{7,5},{8,10},{9,11},{10,... | collective-permute-start | bytes 811016 | tf_op jit(solution)/shard_map/ppermute | solution.py:245
  22.6 6.2 %shard_map.111 = (f32[128,4096]{1,0:T(8,128)}, f32[128,4096]{1,0:T(8,128)}) custom-call(bf16[128,4096]{1,0:T(8,128)(2,1)} %q_ref.11, bf16[128,4096]{1,0:T(8,128)(2,1)} %k_ref.11, bf16[128,4096]{1,0:T(8,128)(2,1)} %v_ref.11, bf16[128,4096]{1,0:T(8,128)(2,1)} %g_ref.11, f32[16,4096]{1,0:T(8,128)} %fusion.58.p_ref.pw_ref, f32[16,4096]{1,0:T(8,128)} %get-tuple-element.76.rw_ref), custom_call_target="tpu_custom_call" | custom-call | tf_op jit(solution)/shard_map/pallas_call | solution.py:152
  28.8 0.6 collective-permute-done.1
  29.4 0.0 collective-permute-start.2
  29.4 1.5 %collective-permute-done.2 = f32[16,4224]{1,0:T(8,128)S(1)} collective-permute-done((f32[16,4224]{1,0:T(8,128)S(1)}, f32[16,4224]{1,0:T(8,128)S(1)}, u32[]{:S(2)}, u32[]{:S(2)}) %collective-permute-start.2) | collective-permute-done | bytes 270368 | tf_op jit(solution)/shard_map/ppermute | solution.py:254
  31.0 0.1 reduce-precision_convert_fusion.5
  31.2 0.1 reduce-precision_convert_fusion.4
  31.3 0.8 %fusion.2 = f32[48,256]{1,0:T(8,128)S(1)} fusion(s32[4096]{0:T(1024)S(1)} %copy-done.2, bf16[16,4096]{1,0:T(8,128)(2,1)S(1)} %get-tuple-element.82, bf16[16,4096]{1,0:T(8,128)(2,1)S(1)} %get-tuple-element.81, bf16[16,4096]{1,0:T(8,128)(2,1)S(1)} %get-tuple-element.60), kind=kOutput, calls=%fused_computation.3 | convolution fusion | flops 102891520 | bytes 458752 | tf_op jit(solution)/shard_map/dot_general | solution.py:193
  32.1 0.1 fusion.40
  32.3 1.9 %collective-permute-start.3 = (f32[16,4224]{1,0:T(8,128)S(1)}, f32[16,4224]{1,0:T(8,128)S(1)}, u32[]{:S(2)}, u32[]{:S(2)}) collective-permute-start(f32[16,4224]{1,0:T(8,128)S(1)} %fusion.40), channel_id=1, source_target_pairs={{0,4},{1,5},{2,6},{3,7},{4,0},{5,1},{6,2},{7,3},{8,12},{9,13},{10,... | collective-permute-start | bytes 811016 | tf_op jit(solution)/shard_map/ppermute | solution.py:245
  34.1 6.1 %shard_map.112 = (f32[128,4096]{1,0:T(8,128)}, f32[128,4096]{1,0:T(8,128)}) custom-call(bf16[128,4096]{1,0:T(8,128)(2,1)} %q_ref.11, bf16[128,4096]{1,0:T(8,128)(2,1)} %k_ref.11, bf16[128,4096]{1,0:T(8,128)(2,1)} %v_ref.11, bf16[128,4096]{1,0:T(8,128)(2,1)} %g_ref.11, f32[16,4096]{1,0:T(8,128)} %fusion.58.p_ref.pw_ref, ...), custom_call_target="tpu_custom_call", output_to_operand_aliasing={{0}: (6, {}), {1}: (7, {})} | custom-call | tf_op jit(solution)/shard_map/pallas_call | solution.py:152
  40.3 0.7 collective-permute-done.3
  40.9 0.0 collective-permute-start.4
  40.9 1.5 %collective-permute-done.4 = f32[16,4224]{1,0:T(8,128)S(1)} collective-permute-done((f32[16,4224]{1,0:T(8,128)S(1)}, f32[16,4224]{1,0:T(8,128)S(1)}, u32[]{:S(2)}, u32[]{:S(2)}) %collective-permute-start.4) | collective-permute-done | bytes 270368 | tf_op jit(solution)/shard_map/ppermute | solution.py:254
  42.5 0.1 reduce-precision_convert_fusion.3
  42.7 0.8 %fusion.1 = f32[48,256]{1,0:T(8,128)S(1)} fusion(s32[4096]{0:T(1024)S(1)} %copy-done.2, bf16[16,4096]{1,0:T(8,128)(2,1)S(1)} %get-tuple-element.80, bf16[16,4096]{1,0:T(8,128)(2,1)S(1)} %get-tuple-element.79, bf16[16,4096]{1,0:T(8,128)(2,1)S(1)} %get-tuple-element.57), kind=kOutput, calls=%fused_computation.2 | convolution fusion | flops 102891520 | bytes 458752 | tf_op jit(solution)/shard_map/dot_general | solution.py:193
  43.5 0.1 multiply_add_fusion
  43.6 0.1 fusion.38
  43.8 2.8 %collective-permute-start.5 = (f32[16,4224]{1,0:T(8,128)S(1)}, f32[16,4224]{1,0:T(8,128)S(1)}, u32[]{:S(2)}, u32[]{:S(2)}) collective-permute-start(f32[16,4224]{1,0:T(8,128)S(1)} %fusion.38), channel_id=1, source_target_pairs={{0,8},{1,9},{2,10},{3,11},{4,12},{5,13},{6,14},{7,15},{8,0},{9,1},... | collective-permute-start | bytes 811016 | tf_op jit(solution)/shard_map/ppermute | solution.py:245
  46.6 6.1 %shard_map.113 = (f32[128,4096]{1,0:T(8,128)}, f32[128,4096]{1,0:T(8,128)}) custom-call(bf16[128,4096]{1,0:T(8,128)(2,1)} %q_ref.11, bf16[128,4096]{1,0:T(8,128)(2,1)} %k_ref.11, bf16[128,4096]{1,0:T(8,128)(2,1)} %v_ref.11, bf16[128,4096]{1,0:T(8,128)(2,1)} %g_ref.11, f32[16,4096]{1,0:T(8,128)} %fusion.58.p_ref.pw_ref, ...), custom_call_target="tpu_custom_call", output_to_operand_aliasing={{0}: (6, {}), {1}: (7, {})} | custom-call | tf_op jit(solution)/shard_map/pallas_call | solution.py:152
  52.7 6.1 %shard_map.114 = (f32[128,4096]{1,0:T(8,128)}, f32[128,4096]{1,0:T(8,128)}) custom-call(bf16[128,4096]{1,0:T(8,128)(2,1)} %q_ref.11, bf16[128,4096]{1,0:T(8,128)(2,1)} %k_ref.11, bf16[128,4096]{1,0:T(8,128)(2,1)} %v_ref.11, bf16[128,4096]{1,0:T(8,128)(2,1)} %g_ref.11, f32[16,4096]{1,0:T(8,128)} %fusion.58.p_ref.pw_ref, ...), custom_call_target="tpu_custom_call", output_to_operand_aliasing={{0}: (6, {}), {1}: (7, {})} | custom-call | tf_op jit(solution)/shard_map/pallas_call | solution.py:152
  58.9 0.3 collective-permute-done.5
  59.2 0.0 collective-permute-start.6
  59.2 1.5 %collective-permute-done.6 = f32[16,4224]{1,0:T(8,128)S(1)} collective-permute-done((f32[16,4224]{1,0:T(8,128)S(1)}, f32[16,4224]{1,0:T(8,128)S(1)}, u32[]{:S(2)}, u32[]{:S(2)}) %collective-permute-start.6) | collective-permute-done | bytes 270368 | tf_op jit(solution)/shard_map/ppermute | solution.py:254
  60.8 1.0 %reduce-precision_convert_fusion.1 = (bf16[16,4096]{1,0:T(8,128)(2,1)S(1)}, f32[16,4096]{1,0:T(8,128)S(1)}, f32[16,4096]{1,0:T(8,128)}) fusion(f32[16,4096]{1,0:T(8,128)S(1)} %multiply_add_fusion, f32[16,4224]{1,0:T(8,128)S(1)} %get-tuple-element.70, f32[16,4224]{1,0:T(8,128)S(1)} %get-tuple-element.71, f32[16,4096]{1,0:T(8,128)S(1)} %get-tuple-element.68, ...), kind=kLoop, calls=%fused_computation.53 | loop fusion | flops 1507328 | bytes 3031056 | tf_op jit(solution)/shard_map/convert_element_type | solution.py:189
  61.8 0.8 %fusion = f32[48,256]{1,0:T(8,128)S(1)} fusion(s32[4096]{0:T(1024)S(1)} %copy-done.2, bf16[16,4096]{1,0:T(8,128)(2,1)S(1)} %get-tuple-element.78, bf16[16,4096]{1,0:T(8,128)(2,1)S(1)} %get-tuple-element.77, bf16[16,4096]{1,0:T(8,128)(2,1)S(1)} %get-tuple-element.55), kind=kOutput, calls=%fused_computation.1 | convolution fusion | flops 102891520 | bytes 458752 | tf_op jit(solution)/shard_map/dot_general | solution.py:193
  62.6 0.6 multiply_reduce_fusion
  63.9 0.6 divide_bitcast_fusion
  64.5 0.9 %select_add_fusion.1.sw_ref = f32[16,4096]{1,0:T(8,128)} fusion(f32[16,4224]{1,0:T(8,128)S(1)} %get-tuple-element.71, f32[16,4224]{1,0:T(8,128)S(1)} %get-tuple-element.73, f32[16,4224]{1,0:T(8,128)S(1)} %get-tuple-element.75, f32[16,8448]{1,0:T(8,128)S(1)} %collective-permute-done, f32[]{:T(128)S(6)} %mul.187, f32[]{:T(128)S(6)} %mul.183, f32[]{:T(128)S(6)} %mul.179, ...), kind=kLoop, calls=%fused_computation.87 | loop fusion | flops 1048576 | bytes 1572880 | tf_op jit(solution)/shard_map/add | solution.py:269
  65.5 10.9 %shard_map.115 = (bf16[128,4096]{1,0:T(8,128)(2,1)}, bf16[128,4096]{1,0:T(8,128)(2,1)}, bf16[128,4096]{1,0:T(8,128)(2,1)}, bf16[128,4096]{1,0:T(8,128)(2,1)}) custom-call(bf16[128,4096]{1,0:T(8,128)(2,1)} %q_ref.11, bf16[128,4096]{1,0:T(8,128)(2,1)} %k_ref.11, bf16[128,4096]{1,0:T(8,128)(2,1)} %v_ref.11, bf16[128,4096]{1,0:T(8,128)(2,1)} %g_ref.11, ...), custom_call_target="tpu_custom_call" | custom-call | tf_op jit(solution)/shard_map/pallas_call | solution.py:172
  (11 shorter events, 0.3 us)
Async XLA Ops:
  3.8 11.0 %copy-start.2 = (s32[4096]{0:T(1024)S(1)}, s32[4096]{0:T(1024)}, u32[]{:S(2)}) copy-start(s32[4096]{0:T(1024)} %param.13) | copy-start | bytes 49156
  13.8 1.9 %copy-start = (f32[16,4096]{1,0:T(8,128)S(1)}, f32[16,4096]{1,0:T(8,128)}, u32[]{:S(2)}) copy-start(f32[16,4096]{1,0:T(8,128)} %get-tuple-element.29) | copy-start | bytes 786436
  13.8 1.9 %copy-start.1 = (f32[16,4096]{1,0:T(8,128)S(1)}, f32[16,4096]{1,0:T(8,128)}, u32[]{:S(2)}) copy-start(f32[16,4096]{1,0:T(8,128)} %get-tuple-element.30) | copy-start | bytes 786436
  15.8 2.1 %collective-permute-start = (f32[16,8448]{1,0:T(8,128)S(1)}, f32[16,8448]{1,0:T(8,128)S(1)}, u32[]{:S(2)}, u32[]{:S(2)}) collective-permute-start(f32[16,8448]{1,0:T(8,128)S(1)} %pad_maximum_fusion), channel_id=1, source_target_pairs={{0,1},{1,0},{2,3},{3,2},{4,5},{5,4},{6,7},{7,6},{8,9},{9,8},{10,11... | collective-permute-start | bytes 1622024 | tf_op jit(solution)/shard_map/ppermute | solution.py:240
  19.7 9.7 %collective-permute-start.1 = (f32[16,4224]{1,0:T(8,128)S(1)}, f32[16,4224]{1,0:T(8,128)S(1)}, u32[]{:S(2)}, u32[]{:S(2)}) collective-permute-start(f32[16,4224]{1,0:T(8,128)S(1)} %fusion.42), channel_id=1, source_target_pairs={{0,2},{1,3},{2,0},{3,1},{4,6},{5,7},{6,4},{7,5},{8,10},{9,11},{10,... | collective-permute-start | bytes 811016 | tf_op jit(solution)/shard_map/ppermute | solution.py:245
  29.4 1.5 %collective-permute-start.2 = (f32[16,4224]{1,0:T(8,128)S(1)}, f32[16,4224]{1,0:T(8,128)S(1)}, u32[]{:S(2)}, u32[]{:S(2)}) collective-permute-start(f32[16,4224]{1,0:T(8,128)S(1)} %collective-permute-done.1), channel_id=1, source_target_pairs={{0,1},{1,0},{2,3},{3,2},{4,5},{5,4},{6,7},{7,6},{8,9},{9,8},{10,11... | collective-permute-start | bytes 811016 | tf_op jit(solution)/shard_map/ppermute | solution.py:254
  32.3 8.6 %collective-permute-start.3 = (f32[16,4224]{1,0:T(8,128)S(1)}, f32[16,4224]{1,0:T(8,128)S(1)}, u32[]{:S(2)}, u32[]{:S(2)}) collective-permute-start(f32[16,4224]{1,0:T(8,128)S(1)} %fusion.40), channel_id=1, source_target_pairs={{0,4},{1,5},{2,6},{3,7},{4,0},{5,1},{6,2},{7,3},{8,12},{9,13},{10,... | collective-permute-start | bytes 811016 | tf_op jit(solution)/shard_map/ppermute | solution.py:245
  40.9 1.5 %collective-permute-start.4 = (f32[16,4224]{1,0:T(8,128)S(1)}, f32[16,4224]{1,0:T(8,128)S(1)}, u32[]{:S(2)}, u32[]{:S(2)}) collective-permute-start(f32[16,4224]{1,0:T(8,128)S(1)} %collective-permute-done.3), channel_id=1, source_target_pairs={{0,1},{1,0},{2,3},{3,2},{4,5},{5,4},{6,7},{7,6},{8,9},{9,8},{10,11... | collective-permute-start | bytes 811016 | tf_op jit(solution)/shard_map/ppermute | solution.py:254
  43.8 15.4 %collective-permute-start.5 = (f32[16,4224]{1,0:T(8,128)S(1)}, f32[16,4224]{1,0:T(8,128)S(1)}, u32[]{:S(2)}, u32[]{:S(2)}) collective-permute-start(f32[16,4224]{1,0:T(8,128)S(1)} %fusion.38), channel_id=1, source_target_pairs={{0,8},{1,9},{2,10},{3,11},{4,12},{5,13},{6,14},{7,15},{8,0},{9,1},... | collective-permute-start | bytes 811016 | tf_op jit(solution)/shard_map/ppermute | solution.py:245
  59.2 1.5 %collective-permute-start.6 = (f32[16,4224]{1,0:T(8,128)S(1)}, f32[16,4224]{1,0:T(8,128)S(1)}, u32[]{:S(2)}, u32[]{:S(2)}) collective-permute-start(f32[16,4224]{1,0:T(8,128)S(1)} %collective-permute-done.5), channel_id=1, source_target_pairs={{0,1},{1,0},{2,3},{3,2},{4,5},{5,4},{6,7},{7,6},{8,9},{9,8},{10,11... | collective-permute-start | bytes 811016 | tf_op jit(solution)/shard_map/ppermute | solution.py:254

commit v13 on v12

--- a/solution.py
+++ b/solution.py
@@ -80,7 +80,7 @@
         return x, a
 
     zero = jnp.zeros(p_ref.shape, f32)
-    lax.fori_loop(0, rows, body, (zero, zero), unroll=2)
+    lax.fori_loop(0, rows, body, (zero, zero), unroll=4)
     for c in range(lanes):
         cols = slice(c * LANE, (c + 1) * LANE)
         band = slice(c * rows, (c + 1) * rows)

time: 76.8 us -> 76.8 us (level)
  waiting for transfers between devices: 7.77 us -> 9.08 us
  Pallas kernels: 45.4 us -> 44.1 us
    pallas_call x4, Pallas kernels: 24.6 us -> 23.3 us  [local_scans(): pl.pallas_call(local_kernel, grid=(1,), in_specs=specs, out_specs=[big, b...]
    ppermute x3, waiting for transfers between devices: 1.58 us -> 2.89 us  [on_device(): got_mine = lax.ppermute(mine, 'ctx', pairs)]
  transfers between devices with their start and end apart: 7 -> 7, of which waited for: 7 -> 7; matrix products, arithmetic and copies ran while one was open for 0% -> 0% of each run, Pallas kernels for 32% -> 30%
where the time goes in v13:
time: 76.8 us; the launch traced here: 76.4 us
  Pallas kernels  44.1 us (57%)
  waiting for transfers between devices  9.08 us (12%)
  starting transfers between devices  8.16 us (11%)
  other arithmetic  7.8 us (10%)
  matrix products  5.68 us (7%)
  between operations  1.52 us (2%)
    pallas_call x4, Pallas kernels, local_scans(): pl.pallas_call(local_kernel, grid=(1,), in_specs=specs, out_specs=[big, b...  23.3 us
    pallas_call x1, Pallas kernels, corrected(): pl.pallas_call(correct_kernel, grid=(width // BLOCK,), in_specs=[big] * 6...  10.9 us
    pallas_call x1, Pallas kernels, local_carries(): pl.pallas_call(carry_kernel, grid=(width // BLOCK,), in_specs=[big, big,...  9.96 us
    ppermute x3, starting transfers between devices, on_device(): got_mine = lax.ppermute(mine, 'ctx', pairs)  7.63 us
    dot_general x6, matrix products, split_dot(): jnp.dot(jnp.concatenate([hi, mid, lo], axis=0), member, preferred_element...  5.68 us
    ppermute x3, waiting for transfers between devices, on_device(): lax.ppermute(got_mine, 'ctx', [(i, i ^ 1) for i in range(count)])  4.63 us
    convert_element_type x6, other arithmetic, split_dot(): hi = top.astype(bf16)  3.87 us
    ppermute x3, waiting for transfers between devices, on_device(): got_mine = lax.ppermute(mine, 'ctx', pairs)  2.89 us
  transfers between devices with their start and end apart: 7, of which 7 were waited for; matrix products, arithmetic and copies ran while one was open for 0% of the time, Pallas kernels for 30%

profile of v13, /device:TPU:0, one launch (start us, length us, event | category | flops | bytes accessed | tf_op | source)
XLA Modules:
  0.0 76.4 jit_solution(12857174094964629565)
XLA Ops:
  0.6 0.7 reduce-precision_convert_fusion.11
  1.4 1.6 %fusion.5 = f32[96,4096]{1,0:T(8,128)S(1)} fusion(s32[4096]{0:T(1024)} %param.13, bf16[32,256]{1,0:T(8,128)(2,1)S(1)} %get-tuple-element.90, bf16[32,256]{1,0:T(8,128)(2,1)S(1)} %get-tuple-element.89, bf16[32,256]{1,0:T(8,128)(2,1)S(1)} %get-tuple-element.88), kind=kOutput, calls=%fused_computation.6 | convolution fusion | flops 202522624 | bytes 1638400 | tf_op jit(solution)/shard_map/dot_general | solution.py:193
  3.0 0.1 slice_add_fusion
  3.1 0.8 fusion.58.p_ref.pw_ref
  3.8 0.0 copy-start.2
  3.8 10.0 %shard_map.110 = (f32[16,4096]{1,0:T(8,128)}, f32[16,4096]{1,0:T(8,128)}, f32[16,4096]{1,0:T(8,128)}) custom-call(bf16[128,4096]{1,0:T(8,128)(2,1)} %q_ref.11, bf16[128,4096]{1,0:T(8,128)(2,1)} %k_ref.11, bf16[128,4096]{1,0:T(8,128)(2,1)} %v_ref.11, bf16[128,4096]{1,0:T(8,128)(2,1)} %g_ref.11, f32[16,4096]{1,0:T(8,128)} %fusion.58.p_ref.pw_ref), custom_call_target="tpu_custom_call" | custom-call | tf_op jit(solution)/shard_map/pallas_call | solution.py:129
  13.8 0.0 copy-start
  13.8 0.0 copy-start.1
  13.8 1.1 %reduce-precision_convert_fusion.9 = (bf16[16,4096]{1,0:T(8,128)(2,1)S(1)}, bf16[16,4096]{1,0:T(8,128)(2,1)S(1)}, bf16[16,4096]{1,0:T(8,128)(2,1)S(1)}) fusion(f32[16,4096]{1,0:T(8,128)} %get-tuple-element.31), kind=kLoop, calls=%fused_computation.69 | loop fusion | flops 458752 | bytes 655360 | tf_op jit(solution)/shard_map/convert_element_type | solution.py:189
  14.8 0.0 copy-done.2
  14.8 0.8 %fusion.4 = f32[48,256]{1,0:T(8,128)S(1)} fusion(s32[4096]{0:T(1024)S(1)} %copy-done.2, bf16[16,4096]{1,0:T(8,128)(2,1)S(1)} %get-tuple-element.86, bf16[16,4096]{1,0:T(8,128)(2,1)S(1)} %get-tuple-element.87, bf16[16,4096]{1,0:T(8,128)(2,1)S(1)} %get-tuple-element.85), kind=kOutput, calls=%fused_computation.5 | convolution fusion | flops 102891520 | bytes 458752 | tf_op jit(solution)/shard_map/dot_general | solution.py:193
  15.7 0.0 copy-done
  15.7 0.0 copy-done.1
  15.8 0.5 collective-permute-start
  16.3 1.6 %collective-permute-done = f32[16,8448]{1,0:T(8,128)S(1)} collective-permute-done((f32[16,8448]{1,0:T(8,128)S(1)}, f32[16,8448]{1,0:T(8,128)S(1)}, u32[]{:S(2)}, u32[]{:S(2)}) %collective-permute-start) | collective-permute-done | bytes 540704 | tf_op jit(solution)/shard_map/ppermute | solution.py:240
  17.8 0.8 %reduce-precision_convert_fusion.7 = (bf16[16,4096]{1,0:T(8,128)(2,1)S(1)}, f32[16,4096]{1,0:T(8,128)S(1)}, f32[16,4096]{1,0:T(8,128)S(1)}, f32[16,4096]{1,0:T(8,128)S(1)}, f32[16,4096]{1,0:T(8,128)}) fusion(f32[16,4096]{1,0:T(8,128)S(1)} %copy-done.1, f32[16,8448]{1,0:T(8,128)S(1)} %collective-permute-done, f32[16,4096]{1,0:T(8,128)S(1)} %copy-done, ...), kind=kLoop, calls=%fused_computation.65 | loop fusion | flops 917504 | bytes 2752513 | tf_op jit(solution)/shard_map/convert_element_type | solution.py:189
  18.7 0.8 %fusion.3 = f32[48,256]{1,0:T(8,128)S(1)} fusion(s32[4096]{0:T(1024)S(1)} %copy-done.2, bf16[16,4096]{1,0:T(8,128)(2,1)S(1)} %get-tuple-element.84, bf16[16,4096]{1,0:T(8,128)(2,1)S(1)} %get-tuple-element.83, bf16[16,4096]{1,0:T(8,128)(2,1)S(1)} %get-tuple-element.63), kind=kOutput, calls=%fused_computation.4 | convolution fusion | flops 102891520 | bytes 458752 | tf_op jit(solution)/shard_map/dot_general | solution.py:193
  19.5 0.1 fusion.42
  19.7 3.0 %collective-permute-start.1 = (f32[16,4224]{1,0:T(8,128)S(1)}, f32[16,4224]{1,0:T(8,128)S(1)}, u32[]{:S(2)}, u32[]{:S(2)}) collective-permute-start(f32[16,4224]{1,0:T(8,128)S(1)} %fusion.42), channel_id=1, source_target_pairs={{0,2},{1,3},{2,0},{3,1},{4,6},{5,7},{6,4},{7,5},{8,10},{9,11},{10,... | collective-permute-start | bytes 811016 | tf_op jit(solution)/shard_map/ppermute | solution.py:245
  22.6 5.9 %shard_map.111 = (f32[128,4096]{1,0:T(8,128)}, f32[128,4096]{1,0:T(8,128)}) custom-call(bf16[128,4096]{1,0:T(8,128)(2,1)} %q_ref.11, bf16[128,4096]{1,0:T(8,128)(2,1)} %k_ref.11, bf16[128,4096]{1,0:T(8,128)(2,1)} %v_ref.11, bf16[128,4096]{1,0:T(8,128)(2,1)} %g_ref.11, f32[16,4096]{1,0:T(8,128)} %fusion.58.p_ref.pw_ref, f32[16,4096]{1,0:T(8,128)} %get-tuple-element.76.rw_ref), custom_call_target="tpu_custom_call" | custom-call | tf_op jit(solution)/shard_map/pallas_call | solution.py:152
  28.5 0.9 %collective-permute-done.1 = f32[16,4224]{1,0:T(8,128)S(1)} collective-permute-done((f32[16,4224]{1,0:T(8,128)S(1)}, f32[16,4224]{1,0:T(8,128)S(1)}, u32[]{:S(2)}, u32[]{:S(2)}) %collective-permute-start.1) | collective-permute-done | bytes 270368 | tf_op jit(solution)/shard_map/ppermute | solution.py:245
  29.4 0.0 collective-permute-start.2
  29.4 1.5 %collective-permute-done.2 = f32[16,4224]{1,0:T(8,128)S(1)} collective-permute-done((f32[16,4224]{1,0:T(8,128)S(1)}, f32[16,4224]{1,0:T(8,128)S(1)}, u32[]{:S(2)}, u32[]{:S(2)}) %collective-permute-start.2) | collective-permute-done | bytes 270368 | tf_op jit(solution)/shard_map/ppermute | solution.py:254
  31.0 0.1 reduce-precision_convert_fusion.5
  31.2 0.1 reduce-precision_convert_fusion.4
  31.3 0.8 %fusion.2 = f32[48,256]{1,0:T(8,128)S(1)} fusion(s32[4096]{0:T(1024)S(1)} %copy-done.2, bf16[16,4096]{1,0:T(8,128)(2,1)S(1)} %get-tuple-element.82, bf16[16,4096]{1,0:T(8,128)(2,1)S(1)} %get-tuple-element.81, bf16[16,4096]{1,0:T(8,128)(2,1)S(1)} %get-tuple-element.60), kind=kOutput, calls=%fused_computation.3 | convolution fusion | flops 102891520 | bytes 458752 | tf_op jit(solution)/shard_map/dot_general | solution.py:193
  32.1 0.1 fusion.40
  32.3 1.9 %collective-permute-start.3 = (f32[16,4224]{1,0:T(8,128)S(1)}, f32[16,4224]{1,0:T(8,128)S(1)}, u32[]{:S(2)}, u32[]{:S(2)}) collective-permute-start(f32[16,4224]{1,0:T(8,128)S(1)} %fusion.40), channel_id=1, source_target_pairs={{0,4},{1,5},{2,6},{3,7},{4,0},{5,1},{6,2},{7,3},{8,12},{9,13},{10,... | collective-permute-start | bytes 811016 | tf_op jit(solution)/shard_map/ppermute | solution.py:245
  34.1 5.8 %shard_map.112 = (f32[128,4096]{1,0:T(8,128)}, f32[128,4096]{1,0:T(8,128)}) custom-call(bf16[128,4096]{1,0:T(8,128)(2,1)} %q_ref.11, bf16[128,4096]{1,0:T(8,128)(2,1)} %k_ref.11, bf16[128,4096]{1,0:T(8,128)(2,1)} %v_ref.11, bf16[128,4096]{1,0:T(8,128)(2,1)} %g_ref.11, f32[16,4096]{1,0:T(8,128)} %fusion.58.p_ref.pw_ref, ...), custom_call_target="tpu_custom_call", output_to_operand_aliasing={{0}: (6, {}), {1}: (7, {})} | custom-call | tf_op jit(solution)/shard_map/pallas_call | solution.py:152
  39.9 1.0 %collective-permute-done.3 = f32[16,4224]{1,0:T(8,128)S(1)} collective-permute-done((f32[16,4224]{1,0:T(8,128)S(1)}, f32[16,4224]{1,0:T(8,128)S(1)}, u32[]{:S(2)}, u32[]{:S(2)}) %collective-permute-start.3) | collective-permute-done | bytes 270368 | tf_op jit(solution)/shard_map/ppermute | solution.py:245
  40.9 0.0 collective-permute-start.4
  40.9 1.5 %collective-permute-done.4 = f32[16,4224]{1,0:T(8,128)S(1)} collective-permute-done((f32[16,4224]{1,0:T(8,128)S(1)}, f32[16,4224]{1,0:T(8,128)S(1)}, u32[]{:S(2)}, u32[]{:S(2)}) %collective-permute-start.4) | collective-permute-done | bytes 270368 | tf_op jit(solution)/shard_map/ppermute | solution.py:254
  42.5 0.1 reduce-precision_convert_fusion.3
  42.7 0.8 %fusion.1 = f32[48,256]{1,0:T(8,128)S(1)} fusion(s32[4096]{0:T(1024)S(1)} %copy-done.2, bf16[16,4096]{1,0:T(8,128)(2,1)S(1)} %get-tuple-element.80, bf16[16,4096]{1,0:T(8,128)(2,1)S(1)} %get-tuple-element.79, bf16[16,4096]{1,0:T(8,128)(2,1)S(1)} %get-tuple-element.57), kind=kOutput, calls=%fused_computation.2 | convolution fusion | flops 102891520 | bytes 458752 | tf_op jit(solution)/shard_map/dot_general | solution.py:193
  43.5 0.1 multiply_add_fusion
  43.6 0.1 fusion.38
  43.8 2.8 %collective-permute-start.5 = (f32[16,4224]{1,0:T(8,128)S(1)}, f32[16,4224]{1,0:T(8,128)S(1)}, u32[]{:S(2)}, u32[]{:S(2)}) collective-permute-start(f32[16,4224]{1,0:T(8,128)S(1)} %fusion.38), channel_id=1, source_target_pairs={{0,8},{1,9},{2,10},{3,11},{4,12},{5,13},{6,14},{7,15},{8,0},{9,1},... | collective-permute-start | bytes 811016 | tf_op jit(solution)/shard_map/ppermute | solution.py:245
  46.6 5.8 %shard_map.113 = (f32[128,4096]{1,0:T(8,128)}, f32[128,4096]{1,0:T(8,128)}) custom-call(bf16[128,4096]{1,0:T(8,128)(2,1)} %q_ref.11, bf16[128,4096]{1,0:T(8,128)(2,1)} %k_ref.11, bf16[128,4096]{1,0:T(8,128)(2,1)} %v_ref.11, bf16[128,4096]{1,0:T(8,128)(2,1)} %g_ref.11, f32[16,4096]{1,0:T(8,128)} %fusion.58.p_ref.pw_ref, ...), custom_call_target="tpu_custom_call", output_to_operand_aliasing={{0}: (6, {}), {1}: (7, {})} | custom-call | tf_op jit(solution)/shard_map/pallas_call | solution.py:152
  52.4 5.8 %shard_map.114 = (f32[128,4096]{1,0:T(8,128)}, f32[128,4096]{1,0:T(8,128)}) custom-call(bf16[128,4096]{1,0:T(8,128)(2,1)} %q_ref.11, bf16[128,4096]{1,0:T(8,128)(2,1)} %k_ref.11, bf16[128,4096]{1,0:T(8,128)(2,1)} %v_ref.11, bf16[128,4096]{1,0:T(8,128)(2,1)} %g_ref.11, f32[16,4096]{1,0:T(8,128)} %fusion.58.p_ref.pw_ref, ...), custom_call_target="tpu_custom_call", output_to_operand_aliasing={{0}: (6, {}), {1}: (7, {})} | custom-call | tf_op jit(solution)/shard_map/pallas_call | solution.py:152
  58.2 1.0 %collective-permute-done.5 = f32[16,4224]{1,0:T(8,128)S(1)} collective-permute-done((f32[16,4224]{1,0:T(8,128)S(1)}, f32[16,4224]{1,0:T(8,128)S(1)}, u32[]{:S(2)}, u32[]{:S(2)}) %collective-permute-start.5) | collective-permute-done | bytes 270368 | tf_op jit(solution)/shard_map/ppermute | solution.py:245
  59.2 0.0 collective-permute-start.6
  59.2 1.5 %collective-permute-done.6 = f32[16,4224]{1,0:T(8,128)S(1)} collective-permute-done((f32[16,4224]{1,0:T(8,128)S(1)}, f32[16,4224]{1,0:T(8,128)S(1)}, u32[]{:S(2)}, u32[]{:S(2)}) %collective-permute-start.6) | collective-permute-done | bytes 270368 | tf_op jit(solution)/shard_map/ppermute | solution.py:254
  60.8 1.0 %reduce-precision_convert_fusion.1 = (bf16[16,4096]{1,0:T(8,128)(2,1)S(1)}, f32[16,4096]{1,0:T(8,128)S(1)}, f32[16,4096]{1,0:T(8,128)}) fusion(f32[16,4096]{1,0:T(8,128)S(1)} %multiply_add_fusion, f32[16,4224]{1,0:T(8,128)S(1)} %get-tuple-element.70, f32[16,4224]{1,0:T(8,128)S(1)} %get-tuple-element.71, f32[16,4096]{1,0:T(8,128)S(1)} %get-tuple-element.68, ...), kind=kLoop, calls=%fused_computation.53 | loop fusion | flops 1507328 | bytes 3031056 | tf_op jit(solution)/shard_map/convert_element_type | solution.py:189
  61.8 0.8 %fusion = f32[48,256]{1,0:T(8,128)S(1)} fusion(s32[4096]{0:T(1024)S(1)} %copy-done.2, bf16[16,4096]{1,0:T(8,128)(2,1)S(1)} %get-tuple-element.78, bf16[16,4096]{1,0:T(8,128)(2,1)S(1)} %get-tuple-element.77, bf16[16,4096]{1,0:T(8,128)(2,1)S(1)} %get-tuple-element.55), kind=kOutput, calls=%fused_computation.1 | convolution fusion | flops 102891520 | bytes 458752 | tf_op jit(solution)/shard_map/dot_general | solution.py:193
  62.6 0.6 multiply_reduce_fusion
  63.9 0.6 divide_bitcast_fusion
  64.5 0.9 %select_add_fusion.1.sw_ref = f32[16,4096]{1,0:T(8,128)} fusion(f32[16,4224]{1,0:T(8,128)S(1)} %get-tuple-element.71, f32[16,4224]{1,0:T(8,128)S(1)} %get-tuple-element.73, f32[16,4224]{1,0:T(8,128)S(1)} %get-tuple-element.75, f32[16,8448]{1,0:T(8,128)S(1)} %collective-permute-done, f32[]{:T(128)S(6)} %mul.187, f32[]{:T(128)S(6)} %mul.183, f32[]{:T(128)S(6)} %mul.179, ...), kind=kLoop, calls=%fused_computation.87 | loop fusion | flops 1048576 | bytes 1572880 | tf_op jit(solution)/shard_map/add | solution.py:269
  65.5 10.9 %shard_map.115 = (bf16[128,4096]{1,0:T(8,128)(2,1)}, bf16[128,4096]{1,0:T(8,128)(2,1)}, bf16[128,4096]{1,0:T(8,128)(2,1)}, bf16[128,4096]{1,0:T(8,128)(2,1)}) custom-call(bf16[128,4096]{1,0:T(8,128)(2,1)} %q_ref.11, bf16[128,4096]{1,0:T(8,128)(2,1)} %k_ref.11, bf16[128,4096]{1,0:T(8,128)(2,1)} %v_ref.11, bf16[128,4096]{1,0:T(8,128)(2,1)} %g_ref.11, ...), custom_call_target="tpu_custom_call" | custom-call | tf_op jit(solution)/shard_map/pallas_call | solution.py:172
  (11 shorter events, 0.3 us)
Async XLA Ops:
  3.8 11.0 %copy-start.2 = (s32[4096]{0:T(1024)S(1)}, s32[4096]{0:T(1024)}, u32[]{:S(2)}) copy-start(s32[4096]{0:T(1024)} %param.13) | copy-start | bytes 49156
  13.8 1.9 %copy-start = (f32[16,4096]{1,0:T(8,128)S(1)}, f32[16,4096]{1,0:T(8,128)}, u32[]{:S(2)}) copy-start(f32[16,4096]{1,0:T(8,128)} %get-tuple-element.29) | copy-start | bytes 786436
  13.8 1.9 %copy-start.1 = (f32[16,4096]{1,0:T(8,128)S(1)}, f32[16,4096]{1,0:T(8,128)}, u32[]{:S(2)}) copy-start(f32[16,4096]{1,0:T(8,128)} %get-tuple-element.30) | copy-start | bytes 786436
  15.8 2.1 %collective-permute-start = (f32[16,8448]{1,0:T(8,128)S(1)}, f32[16,8448]{1,0:T(8,128)S(1)}, u32[]{:S(2)}, u32[]{:S(2)}) collective-permute-start(f32[16,8448]{1,0:T(8,128)S(1)} %pad_maximum_fusion), channel_id=1, source_target_pairs={{0,1},{1,0},{2,3},{3,2},{4,5},{5,4},{6,7},{7,6},{8,9},{9,8},{10,11... | collective-permute-start | bytes 1622024 | tf_op jit(solution)/shard_map/ppermute | solution.py:240
  19.7 9.7 %collective-permute-start.1 = (f32[16,4224]{1,0:T(8,128)S(1)}, f32[16,4224]{1,0:T(8,128)S(1)}, u32[]{:S(2)}, u32[]{:S(2)}) collective-permute-start(f32[16,4224]{1,0:T(8,128)S(1)} %fusion.42), channel_id=1, source_target_pairs={{0,2},{1,3},{2,0},{3,1},{4,6},{5,7},{6,4},{7,5},{8,10},{9,11},{10,... | collective-permute-start | bytes 811016 | tf_op jit(solution)/shard_map/ppermute | solution.py:245
  29.4 1.5 %collective-permute-start.2 = (f32[16,4224]{1,0:T(8,128)S(1)}, f32[16,4224]{1,0:T(8,128)S(1)}, u32[]{:S(2)}, u32[]{:S(2)}) collective-permute-start(f32[16,4224]{1,0:T(8,128)S(1)} %collective-permute-done.1), channel_id=1, source_target_pairs={{0,1},{1,0},{2,3},{3,2},{4,5},{5,4},{6,7},{7,6},{8,9},{9,8},{10,11... | collective-permute-start | bytes 811016 | tf_op jit(solution)/shard_map/ppermute | solution.py:254
  32.3 8.6 %collective-permute-start.3 = (f32[16,4224]{1,0:T(8,128)S(1)}, f32[16,4224]{1,0:T(8,128)S(1)}, u32[]{:S(2)}, u32[]{:S(2)}) collective-permute-start(f32[16,4224]{1,0:T(8,128)S(1)} %fusion.40), channel_id=1, source_target_pairs={{0,4},{1,5},{2,6},{3,7},{4,0},{5,1},{6,2},{7,3},{8,12},{9,13},{10,... | collective-permute-start | bytes 811016 | tf_op jit(solution)/shard_map/ppermute | solution.py:245
  40.9 1.5 %collective-permute-start.4 = (f32[16,4224]{1,0:T(8,128)S(1)}, f32[16,4224]{1,0:T(8,128)S(1)}, u32[]{:S(2)}, u32[]{:S(2)}) collective-permute-start(f32[16,4224]{1,0:T(8,128)S(1)} %collective-permute-done.3), channel_id=1, source_target_pairs={{0,1},{1,0},{2,3},{3,2},{4,5},{5,4},{6,7},{7,6},{8,9},{9,8},{10,11... | collective-permute-start | bytes 811016 | tf_op jit(solution)/shard_map/ppermute | solution.py:254
  43.8 15.4 %collective-permute-start.5 = (f32[16,4224]{1,0:T(8,128)S(1)}, f32[16,4224]{1,0:T(8,128)S(1)}, u32[]{:S(2)}, u32[]{:S(2)}) collective-permute-start(f32[16,4224]{1,0:T(8,128)S(1)} %fusion.38), channel_id=1, source_target_pairs={{0,8},{1,9},{2,10},{3,11},{4,12},{5,13},{6,14},{7,15},{8,0},{9,1},... | collective-permute-start | bytes 811016 | tf_op jit(solution)/shard_map/ppermute | solution.py:245
  59.2 1.5 %collective-permute-start.6 = (f32[16,4224]{1,0:T(8,128)S(1)}, f32[16,4224]{1,0:T(8,128)S(1)}, u32[]{:S(2)}, u32[]{:S(2)}) collective-permute-start(f32[16,4224]{1,0:T(8,128)S(1)} %collective-permute-done.5), channel_id=1, source_target_pairs={{0,1},{1,0},{2,3},{3,2},{4,5},{5,4},{6,7},{7,6},{8,9},{9,8},{10,11... | collective-permute-start | bytes 811016 | tf_op jit(solution)/shard_map/ppermute | solution.py:254

commit v14 on v13

--- a/solution.py
+++ b/solution.py
@@ -11,8 +11,9 @@
 LANE = 128
 
 
-def carry_kernel(q_ref, k_ref, v_ref, g_ref, p_ref, xend_ref, head_ref, tot_ref, mix_ref, up_ref):
+def carry_kernel(q_ref, k_ref, v_ref, g_ref, rate_ref, xend_ref, head_ref, tot_ref, p_ref, mix_ref, up_ref):
     f32 = jnp.float32
+    p_ref[...] = jnp.exp(-rate_ref[...])
     mix_ref[...] = (k_ref[...].astype(f32) * v_ref[...].astype(f32)).astype(jnp.bfloat16).astype(f32)
     up_ref[...] = g_ref[...].astype(f32) * q_ref[...].astype(f32)
     rows, width = mix_ref.shape
@@ -121,19 +122,19 @@
         vg_ref[:, cols] = (mg * k_ref[:, cols].astype(f32)).astype(jnp.bfloat16)
 
 
-def local_carries(query_proj, key_proj, value_proj, out_grad, factor):
+def local_carries(query_proj, key_proj, value_proj, out_grad, rate):
     rows, width = query_proj.shape
-    modes = factor.shape[0]
+    modes = rate.shape[0]
     big = pl.BlockSpec((rows, BLOCK), lambda i: (0, i))
     small = pl.BlockSpec((modes, BLOCK), lambda i: (0, i))
     return pl.pallas_call(
         carry_kernel,
         grid=(width // BLOCK,),
         in_specs=[big, big, big, big, small],
-        out_specs=[small, small, small],
-        out_shape=[jax.ShapeDtypeStruct((modes, width), jnp.float32)] * 3,
+        out_specs=[small, small, small, small],
+        out_shape=[jax.ShapeDtypeStruct((modes, width), jnp.float32)] * 4,
         scratch_shapes=[pltpu.VMEM((rows, BLOCK), jnp.float32)] * 2,
-    )(query_proj, key_proj, value_proj, out_grad, factor)
+    )(query_proj, key_proj, value_proj, out_grad, rate)
 
 
 def local_scans(query_proj, key_proj, value_proj, out_grad, factor, weight, first, previous):
@@ -201,13 +202,10 @@
         member = (group_of[None, :] == jnp.arange(group_count, dtype=jnp.int32)[:, None]).astype(
             jnp.bfloat16
         )
-        modes = decay_rate.shape[1]
-        params = split_dot(jnp.concatenate([decay_rate.T, residue.T], axis=0), member)
-        rate = params[:modes]
-        weight = params[modes:]
-        factor = jnp.exp(-rate)
-        end_state, head_adjoint, local_total = local_carries(
-            query_proj, key_proj, value_proj, out_grad, factor
+        rate = split_dot(decay_rate.T, member)
+        weight = split_dot(residue.T, member)
+        end_state, head_adjoint, local_total, factor = local_carries(
+            query_proj, key_proj, value_proj, out_grad, rate
         )
         width = query_proj.shape[1]
         modes = factor.shape[0]

time: 76.8 us -> 79.7 us (1.038)
  other arithmetic: 7.8 us -> 10.6 us
  waiting for transfers between devices: 9.08 us -> 7.1 us
    select_n x3, other arithmetic: 0.11 us -> 2.1 us  [on_device(): second = jnp.where(core == 0, got_other, got_mine)]
    add x2 -> x3, other arithmetic: 0.09 us -> 1.49 us  [split_dot(): return out[:rows] + out[rows:2 * rows] + out[2 * rows:]]
    ppermute x1, waiting for transfers between devices: 1.56 us -> 0.72 us  [on_device(): got = lax.ppermute(packed, 'ctx', pairs)]
    dot_general x6 -> x7, matrix products: 5.68 us -> 6.46 us  [split_dot(): jnp.dot(jnp.concatenate([hi, mid, lo], axis=0), member, preferred_element...]
    convert_element_type x6 -> x7, other arithmetic: 3.87 us -> 3.28 us  [split_dot(): hi = top.astype(bf16)]
  transfers between devices with their start and end apart: 7 -> 7, of which waited for: 7 -> 7; matrix products, arithmetic and copies ran while one was open for 0% -> 2% of each run, Pallas kernels for 30% -> 30%
where the time goes in v14:
time: 79.7 us; the launch traced here: 79.2 us
  Pallas kernels  44.7 us (56%)
  other arithmetic  10.6 us (13%)
  starting transfers between devices  8.09 us (10%)
  waiting for transfers between devices  7.1 us (9%)
  matrix products  6.46 us (8%)
  between operations  1.57 us (2%)
    pallas_call x4, Pallas kernels, local_scans(): pl.pallas_call(local_kernel, grid=(1,), in_specs=specs, out_specs=[big, b...  23.4 us
    pallas_call x1, Pallas kernels, corrected(): pl.pallas_call(correct_kernel, grid=(width // BLOCK,), in_specs=[big] * 6...  10.9 us
    pallas_call x1, Pallas kernels, local_carries(): pl.pallas_call(carry_kernel, grid=(width // BLOCK,), in_specs=[big, big,...  10.3 us
    ppermute x3, starting transfers between devices, on_device(): got_mine = lax.ppermute(mine, 'ctx', pairs)  7.57 us
    dot_general x7, matrix products, split_dot(): jnp.dot(jnp.concatenate([hi, mid, lo], axis=0), member, preferred_element...  6.46 us
    ppermute x3, waiting for transfers between devices, on_device(): lax.ppermute(got_mine, 'ctx', [(i, i ^ 1) for i in range(count)])  4.2 us
    convert_element_type x7, other arithmetic, split_dot(): hi = top.astype(bf16)  3.28 us
    ppermute x3, waiting for transfers between devices, on_device(): got_mine = lax.ppermute(mine, 'ctx', pairs)  2.19 us
  transfers between devices with their start and end apart: 7, of which 7 were waited for; matrix products, arithmetic and copies ran while one was open for 2% of the time, Pallas kernels for 30%

profile of v14, /device:TPU:0, one launch (start us, length us, event | category | flops | bytes accessed | tf_op | source)
XLA Modules:
  0.0 79.2 jit_solution(7091713685942510402)
XLA Ops:
  0.6 0.7 reduce-precision_convert_fusion.13
  1.4 1.5 %fusion.6 = f32[48,4096]{1,0:T(8,128)S(1)} fusion(s32[4096]{0:T(1024)} %param.13, bf16[16,256]{1,0:T(8,128)(2,1)S(1)} %get-tuple-element.93, bf16[16,256]{1,0:T(8,128)(2,1)S(1)} %get-tuple-element.94, bf16[16,256]{1,0:T(8,128)(2,1)S(1)} %get-tuple-element.92), kind=kOutput, calls=%fused_computation.7 | convolution fusion | flops 101785600 | bytes 827392 | tf_op jit(solution)/shard_map/dot_general | solution.py:194
  2.9 0.7 slice_add_fusion.2.rate_ref
  3.6 0.0 copy-start.8
  3.6 10.3 %shard_map.110 = (f32[16,4096]{1,0:T(8,128)}, f32[16,4096]{1,0:T(8,128)}, f32[16,4096]{1,0:T(8,128)}, f32[16,4096]{1,0:T(8,128)}) custom-call(bf16[128,4096]{1,0:T(8,128)(2,1)} %q_ref.11, bf16[128,4096]{1,0:T(8,128)(2,1)} %k_ref.11, bf16[128,4096]{1,0:T(8,128)(2,1)} %v_ref.11, bf16[128,4096]{1,0:T(8,128)(2,1)} %g_ref.11, f32[16,4096]{1,0:T(8,128)} %slice_add_fusion.2.rate_ref), custom_call_target="tpu_custom_call" | custom-call | tf_op jit(solution)/shard_map/pallas_call | solution.py:130
  14.0 0.0 copy-start.4
  14.0 0.0 copy-start.5
  14.0 0.0 copy-start.7
  14.0 1.1 %reduce-precision_convert_fusion.9 = (bf16[16,4096]{1,0:T(8,128)(2,1)S(1)}, bf16[16,4096]{1,0:T(8,128)(2,1)S(1)}, bf16[16,4096]{1,0:T(8,128)(2,1)S(1)}) fusion(f32[16,4096]{1,0:T(8,128)} %get-tuple-element.32), kind=kLoop, calls=%fused_computation.69 | loop fusion | flops 458752 | bytes 655360 | tf_op jit(solution)/shard_map/convert_element_type | solution.py:190
  15.1 0.0 copy-done.8
  15.1 0.0 copy-start
  15.1 0.8 %fusion.5 = f32[48,256]{1,0:T(8,128)S(1)} fusion(s32[4096]{0:T(1024)S(1)} %copy-done.8, bf16[16,4096]{1,0:T(8,128)(2,1)S(1)} %get-tuple-element.87, bf16[16,4096]{1,0:T(8,128)(2,1)S(1)} %get-tuple-element.88, bf16[16,4096]{1,0:T(8,128)(2,1)S(1)} %get-tuple-element.86), kind=kOutput, calls=%fused_computation.6 | convolution fusion | flops 102891520 | bytes 458752 | tf_op jit(solution)/shard_map/dot_general | solution.py:194
  15.9 0.0 copy-done.4
  16.0 0.0 copy-done.5
  16.0 0.5 collective-permute-start
  16.5 0.0 copy-done.7
  16.5 0.8 %fusion.3 = f32[48,4096]{1,0:T(8,128)S(1)} fusion(s32[4096]{0:T(1024)S(1)} %copy-done.8, bf16[16,256]{1,0:T(8,128)(2,1)S(1)} %get-tuple-element.90, bf16[16,256]{1,0:T(8,128)(2,1)S(1)} %get-tuple-element.91, bf16[16,256]{1,0:T(8,128)(2,1)S(1)} %get-tuple-element.89), kind=kOutput, calls=%fused_computation.4 | convolution fusion | flops 101785600 | bytes 827392 | tf_op jit(solution)/shard_map/dot_general | solution.py:194
  17.4 0.7 collective-permute-done
  18.1 0.0 copy-done
  18.1 0.1 reduce-precision_convert_fusion.7
  18.3 0.8 %fusion.4 = f32[48,256]{1,0:T(8,128)S(1)} fusion(s32[4096]{0:T(1024)S(1)} %copy-done.8, bf16[16,4096]{1,0:T(8,128)(2,1)S(1)} %get-tuple-element.85, bf16[16,4096]{1,0:T(8,128)(2,1)S(1)} %get-tuple-element.84, bf16[16,4096]{1,0:T(8,128)(2,1)S(1)} %get-tuple-element.65), kind=kOutput, calls=%fused_computation.5 | convolution fusion | flops 102891520 | bytes 458752 | tf_op jit(solution)/shard_map/dot_general | solution.py:194
  19.1 0.1 fusion.44
  19.3 3.0 %collective-permute-start.1 = (f32[16,4224]{1,0:T(8,128)S(1)}, f32[16,4224]{1,0:T(8,128)S(1)}, u32[]{:S(2)}, u32[]{:S(2)}) collective-permute-start(f32[16,4224]{1,0:T(8,128)S(1)} %fusion.44), channel_id=1, source_target_pairs={{0,2},{1,3},{2,0},{3,1},{4,6},{5,7},{6,4},{7,5},{8,10},{9,11},{10,... | collective-permute-start | bytes 811016 | tf_op jit(solution)/shard_map/ppermute | solution.py:243
  22.2 0.7 slice_add_fusion.rw_ref
  23.0 0.0 copy-start.1
  23.0 5.8 %shard_map.111 = (f32[128,4096]{1,0:T(8,128)}, f32[128,4096]{1,0:T(8,128)}) custom-call(bf16[128,4096]{1,0:T(8,128)(2,1)} %q_ref.11, bf16[128,4096]{1,0:T(8,128)(2,1)} %k_ref.11, bf16[128,4096]{1,0:T(8,128)(2,1)} %v_ref.11, bf16[128,4096]{1,0:T(8,128)(2,1)} %g_ref.11, f32[16,4096]{1,0:T(8,128)} %get-tuple-element.33.pw_ref, f32[16,4096]{1,0:T(8,128)} %slice_add_fusion.rw_ref), custom_call_target="tpu_custom_call" | custom-call | tf_op jit(solution)/shard_map/pallas_call | solution.py:153
  28.8 0.2 collective-permute-done.1
  29.0 0.0 collective-permute-start.2
  29.0 1.5 %collective-permute-done.2 = f32[16,4224]{1,0:T(8,128)S(1)} collective-permute-done((f32[16,4224]{1,0:T(8,128)S(1)}, f32[16,4224]{1,0:T(8,128)S(1)}, u32[]{:S(2)}, u32[]{:S(2)}) %collective-permute-start.2) | collective-permute-done | bytes 270368 | tf_op jit(solution)/shard_map/ppermute | solution.py:252
  30.6 0.0 copy-done.1
  30.6 0.1 reduce-precision_convert_fusion.5
  30.8 0.1 reduce-precision_convert_fusion.4
  30.9 0.8 %fusion.2 = f32[48,256]{1,0:T(8,128)S(1)} fusion(s32[4096]{0:T(1024)S(1)} %copy-done.8, bf16[16,4096]{1,0:T(8,128)(2,1)S(1)} %get-tuple-element.83, bf16[16,4096]{1,0:T(8,128)(2,1)S(1)} %get-tuple-element.82, bf16[16,4096]{1,0:T(8,128)(2,1)S(1)} %get-tuple-element.62), kind=kOutput, calls=%fused_computation.3 | convolution fusion | flops 102891520 | bytes 458752 | tf_op jit(solution)/shard_map/dot_general | solution.py:194
  31.8 0.1 fusion.42
  31.9 0.0 copy-start.2
  31.9 1.9 %collective-permute-start.3 = (f32[16,4224]{1,0:T(8,128)S(1)}, f32[16,4224]{1,0:T(8,128)S(1)}, u32[]{:S(2)}, u32[]{:S(2)}) collective-permute-start(f32[16,4224]{1,0:T(8,128)S(1)} %fusion.42), channel_id=1, source_target_pairs={{0,4},{1,5},{2,6},{3,7},{4,0},{5,1},{6,2},{7,3},{8,12},{9,13},{10,... | collective-permute-start | bytes 811016 | tf_op jit(solution)/shard_map/ppermute | solution.py:243
  33.8 5.8 %shard_map.112 = (f32[128,4096]{1,0:T(8,128)}, f32[128,4096]{1,0:T(8,128)}) custom-call(bf16[128,4096]{1,0:T(8,128)(2,1)} %q_ref.11, bf16[128,4096]{1,0:T(8,128)(2,1)} %k_ref.11, bf16[128,4096]{1,0:T(8,128)(2,1)} %v_ref.11, bf16[128,4096]{1,0:T(8,128)(2,1)} %g_ref.11, ...), custom_call_target="tpu_custom_call", output_to_operand_aliasing={{0}: (6, {}), {1}: (7, {})} | custom-call | tf_op jit(solution)/shard_map/pallas_call | solution.py:153
  39.6 0.9 %collective-permute-done.3 = f32[16,4224]{1,0:T(8,128)S(1)} collective-permute-done((f32[16,4224]{1,0:T(8,128)S(1)}, f32[16,4224]{1,0:T(8,128)S(1)}, u32[]{:S(2)}, u32[]{:S(2)}) %collective-permute-start.3) | collective-permute-done | bytes 270368 | tf_op jit(solution)/shard_map/ppermute | solution.py:243
  40.6 0.0 collective-permute-start.4
  40.6 1.7 %collective-permute-done.4 = f32[16,4224]{1,0:T(8,128)} collective-permute-done((f32[16,4224]{1,0:T(8,128)S(1)}, f32[16,4224]{1,0:T(8,128)}, u32[]{:S(2)}, u32[]{:S(2)}) %collective-permute-start.4) | collective-permute-done | bytes 270368 | tf_op jit(solution)/shard_map/ppermute | solution.py:252
  42.2 1.0 %broadcast_select_fusion.2 = (f32[16,4224]{1,0:T(8,128)S(1)}, f32[16,4224]{1,0:T(8,128)S(1)}) fusion(f32[16,4224]{1,0:T(8,128)} %collective-permute-done.4, f32[16,4224]{1,0:T(8,128)S(1)} %collective-permute-done.3, pred[]{:T(512)S(6)} %eq.32), kind=kLoop, calls=%fused_computation.110 | loop fusion | flops 135168 | bytes 1081345 | tf_op jit(solution)/shard_map/jit(_where)/select_n | solution.py:254
  43.2 0.0 copy-done.2
  43.2 0.2 reduce-precision_convert_fusion.3
  43.5 0.8 %fusion.1 = f32[48,256]{1,0:T(8,128)S(1)} fusion(s32[4096]{0:T(1024)S(1)} %copy-done.8, bf16[16,4096]{1,0:T(8,128)(2,1)S(1)} %get-tuple-element.81, bf16[16,4096]{1,0:T(8,128)(2,1)S(1)} %get-tuple-element.80, bf16[16,4096]{1,0:T(8,128)(2,1)S(1)} %get-tuple-element.59), kind=kOutput, calls=%fused_computation.2 | convolution fusion | flops 102891520 | bytes 458752 | tf_op jit(solution)/shard_map/dot_general | solution.py:194
  44.3 0.1 multiply_add_fusion
  44.4 0.8 %fusion.40 = f32[16,4224]{1,0:T(8,128)} fusion(s32[]{:T(128)S(6)} %select_n.212, f32[16,4096]{1,0:T(8,128)S(1)} %get-tuple-element.76, f32[16,4096]{1,0:T(8,128)S(1)} %multiply_add_fusion, f32[16,256]{1,0:T(8,128)S(1)} %fusion.63), kind=kLoop, calls=%fused_computation.71 | loop fusion | flops 135168 | bytes 811012 | tf_op jit(solution)/shard_map/concatenate | solution.py:234
  45.3 2.8 %collective-permute-start.5 = (f32[16,4224]{1,0:T(8,128)}, f32[16,4224]{1,0:T(8,128)S(1)}, u32[]{:S(2)}, u32[]{:S(2)}) collective-permute-start(f32[16,4224]{1,0:T(8,128)} %fusion.40), channel_id=1, source_target_pairs={{0,8},{1,9},{2,10},{3,11},{4,12},{5,13},{6,14},{7,15},{8,0},{9,1},... | collective-permute-start | bytes 811016 | tf_op jit(solution)/shard_map/ppermute | solution.py:243
  48.0 5.9 %shard_map.113 = (f32[128,4096]{1,0:T(8,128)}, f32[128,4096]{1,0:T(8,128)}) custom-call(bf16[128,4096]{1,0:T(8,128)(2,1)} %q_ref.11, bf16[128,4096]{1,0:T(8,128)(2,1)} %k_ref.11, bf16[128,4096]{1,0:T(8,128)(2,1)} %v_ref.11, bf16[128,4096]{1,0:T(8,128)(2,1)} %g_ref.11, ...), custom_call_target="tpu_custom_call", output_to_operand_aliasing={{0}: (6, {}), {1}: (7, {})} | custom-call | tf_op jit(solution)/shard_map/pallas_call | solution.py:153
  53.9 0.0 copy-start.3
  53.9 5.9 %shard_map.114 = (f32[128,4096]{1,0:T(8,128)}, f32[128,4096]{1,0:T(8,128)}) custom-call(bf16[128,4096]{1,0:T(8,128)(2,1)} %q_ref.11, bf16[128,4096]{1,0:T(8,128)(2,1)} %k_ref.11, bf16[128,4096]{1,0:T(8,128)(2,1)} %v_ref.11, bf16[128,4096]{1,0:T(8,128)(2,1)} %g_ref.11, ...), custom_call_target="tpu_custom_call", output_to_operand_aliasing={{0}: (6, {}), {1}: (7, {})} | custom-call | tf_op jit(solution)/shard_map/pallas_call | solution.py:153
  59.7 1.1 %collective-permute-done.5 = f32[16,4224]{1,0:T(8,128)S(1)} collective-permute-done((f32[16,4224]{1,0:T(8,128)}, f32[16,4224]{1,0:T(8,128)S(1)}, u32[]{:S(2)}, u32[]{:S(2)}) %collective-permute-start.5) | collective-permute-done | bytes 270368 | tf_op jit(solution)/shard_map/ppermute | solution.py:243
  60.8 0.0 copy-start.6
  60.8 0.0 collective-permute-start.6
  60.8 0.7 copy-done.6
  61.5 1.0 %collective-permute-done.6 = f32[16,4224]{1,0:T(8,128)} collective-permute-done((f32[16,4224]{1,0:T(8,128)S(1)}, f32[16,4224]{1,0:T(8,128)}, u32[]{:S(2)}, u32[]{:S(2)}) %collective-permute-start.6) | collective-permute-done | bytes 270368 | tf_op jit(solution)/shard_map/ppermute | solution.py:252
  62.5 1.1 %broadcast_select_fusion = (f32[16,4224]{1,0:T(8,128)S(1)}, f32[16,4224]{1,0:T(8,128)S(1)}) fusion(f32[16,4224]{1,0:T(8,128)} %collective-permute-done.6, f32[16,4224]{1,0:T(8,128)} %copy-done.6, pred[]{:T(512)S(6)} %eq.32), kind=kLoop, calls=%fused_computation.108 | loop fusion | flops 135168 | bytes 1081345 | tf_op jit(solution)/shard_map/jit(_where)/select_n | solution.py:254
  63.5 0.0 copy-done.3
  63.6 1.0 %reduce-precision_convert_fusion.1 = (bf16[16,4096]{1,0:T(8,128)(2,1)S(1)}, f32[16,4096]{1,0:T(8,128)S(1)}, f32[16,4096]{1,0:T(8,128)}) fusion(f32[16,4096]{1,0:T(8,128)S(1)} %multiply_add_fusion, f32[16,4224]{1,0:T(8,128)S(1)} %get-tuple-element.70, f32[16,4224]{1,0:T(8,128)S(1)} %get-tuple-element.71, f32[16,4096]{1,0:T(8,128)S(1)} %copy-done.3, ...), kind=kLoop, calls=%fused_computation.53 | loop fusion | flops 1638400 | bytes 3817488 | tf_op jit(solution)/shard_map/convert_element_type | solution.py:190
  64.7 0.8 %fusion = f32[48,256]{1,0:T(8,128)S(1)} fusion(s32[4096]{0:T(1024)S(1)} %copy-done.8, bf16[16,4096]{1,0:T(8,128)(2,1)S(1)} %get-tuple-element.79, bf16[16,4096]{1,0:T(8,128)(2,1)S(1)} %get-tuple-element.78, bf16[16,4096]{1,0:T(8,128)(2,1)S(1)} %get-tuple-element.57), kind=kOutput, calls=%fused_computation.1 | convolution fusion | flops 102891520 | bytes 458752 | tf_op jit(solution)/shard_map/dot_general | solution.py:194
  65.5 0.6 multiply_reduce_fusion
  66.8 0.6 divide_bitcast_fusion
  67.4 0.9 %select_add_fusion.1.sw_ref = f32[16,4096]{1,0:T(8,128)} fusion(f32[16,4224]{1,0:T(8,128)S(1)} %get-tuple-element.71, f32[16,4224]{1,0:T(8,128)S(1)} %get-tuple-element.73, f32[16,4224]{1,0:T(8,128)S(1)} %get-tuple-element.75, f32[16,8448]{1,0:T(8,128)S(1)} %collective-permute-done, f32[]{:T(128)S(6)} %mul.187, f32[]{:T(128)S(6)} %mul.183, f32[]{:T(128)S(6)} %mul.179, ...), kind=kLoop, calls=%fused_computation.90 | loop fusion | flops 1179648 | bytes 2097168 | tf_op jit(solution)/shard_map/add | solution.py:267
  68.3 10.9 %shard_map.115 = (bf16[128,4096]{1,0:T(8,128)(2,1)}, bf16[128,4096]{1,0:T(8,128)(2,1)}, bf16[128,4096]{1,0:T(8,128)(2,1)}, bf16[128,4096]{1,0:T(8,128)(2,1)}) custom-call(bf16[128,4096]{1,0:T(8,128)(2,1)} %q_ref.11, bf16[128,4096]{1,0:T(8,128)(2,1)} %k_ref.11, bf16[128,4096]{1,0:T(8,128)(2,1)} %v_ref.11, bf16[128,4096]{1,0:T(8,128)(2,1)} %g_ref.11, ...), custom_call_target="tpu_custom_call" | custom-call | tf_op jit(solution)/shard_map/pallas_call | solution.py:173
  (10 shorter events, 0.3 us)
Async XLA Ops:
  3.6 11.4 %copy-start.8 = (s32[4096]{0:T(1024)S(1)}, s32[4096]{0:T(1024)}, u32[]{:S(2)}) copy-start(s32[4096]{0:T(1024)} %param.13) | copy-start | bytes 49156
  14.0 2.0 %copy-start.4 = (f32[16,4096]{1,0:T(8,128)S(1)}, f32[16,4096]{1,0:T(8,128)}, u32[]{:S(2)}) copy-start(f32[16,4096]{1,0:T(8,128)} %get-tuple-element.30) | copy-start | bytes 786436
  14.0 2.0 %copy-start.5 = (f32[16,4096]{1,0:T(8,128)S(1)}, f32[16,4096]{1,0:T(8,128)}, u32[]{:S(2)}) copy-start(f32[16,4096]{1,0:T(8,128)} %get-tuple-element.31) | copy-start | bytes 786436
  14.0 2.5 %copy-start.7 = (f32[256,16]{0,1:T(8,128)S(1)}, f32[256,16]{0,1:T(8,128)}, u32[]{:S(2)}) copy-start(f32[256,16]{0,1:T(8,128)} %param.12) | copy-start | bytes 49156
  15.1 3.0 %copy-start = (f32[16,4096]{1,0:T(8,128)S(1)}, f32[16,4096]{1,0:T(8,128)}, u32[]{:S(2)}) copy-start(f32[16,4096]{1,0:T(8,128)} %get-tuple-element.33.pw_ref) | copy-start | bytes 786436
  16.0 2.1 %collective-permute-start = (f32[16,8448]{1,0:T(8,128)S(1)}, f32[16,8448]{1,0:T(8,128)S(1)}, u32[]{:S(2)}, u32[]{:S(2)}) collective-permute-start(f32[16,8448]{1,0:T(8,128)S(1)} %pad_maximum_fusion), channel_id=1, source_target_pairs={{0,1},{1,0},{2,3},{3,2},{4,5},{5,4},{6,7},{7,6},{8,9},{9,8},{10,11... | collective-permute-start | bytes 1622024 | tf_op jit(solution)/shard_map/ppermute | solution.py:238
  19.3 9.7 %collective-permute-start.1 = (f32[16,4224]{1,0:T(8,128)S(1)}, f32[16,4224]{1,0:T(8,128)S(1)}, u32[]{:S(2)}, u32[]{:S(2)}) collective-permute-start(f32[16,4224]{1,0:T(8,128)S(1)} %fusion.44), channel_id=1, source_target_pairs={{0,2},{1,3},{2,0},{3,1},{4,6},{5,7},{6,4},{7,5},{8,10},{9,11},{10,... | collective-permute-start | bytes 811016 | tf_op jit(solution)/shard_map/ppermute | solution.py:243
  23.0 7.6 %copy-start.1 = (f32[16,4096]{1,0:T(8,128)S(1)}, f32[16,4096]{1,0:T(8,128)}, u32[]{:S(2)}) copy-start(f32[16,4096]{1,0:T(8,128)} %get-tuple-element.33.pw_ref) | copy-start | bytes 786436
  29.0 1.5 %collective-permute-start.2 = (f32[16,4224]{1,0:T(8,128)S(1)}, f32[16,4224]{1,0:T(8,128)S(1)}, u32[]{:S(2)}, u32[]{:S(2)}) collective-permute-start(f32[16,4224]{1,0:T(8,128)S(1)} %collective-permute-done.1), channel_id=1, source_target_pairs={{0,1},{1,0},{2,3},{3,2},{4,5},{5,4},{6,7},{7,6},{8,9},{9,8},{10,11... | collective-permute-start | bytes 811016 | tf_op jit(solution)/shard_map/ppermute | solution.py:252
  31.9 11.3 %copy-start.2 = (f32[16,4096]{1,0:T(8,128)S(1)}, f32[16,4096]{1,0:T(8,128)}, u32[]{:S(2)}) copy-start(f32[16,4096]{1,0:T(8,128)} %get-tuple-element.33.pw_ref) | copy-start | bytes 786436
  31.9 8.6 %collective-permute-start.3 = (f32[16,4224]{1,0:T(8,128)S(1)}, f32[16,4224]{1,0:T(8,128)S(1)}, u32[]{:S(2)}, u32[]{:S(2)}) collective-permute-start(f32[16,4224]{1,0:T(8,128)S(1)} %fusion.42), channel_id=1, source_target_pairs={{0,4},{1,5},{2,6},{3,7},{4,0},{5,1},{6,2},{7,3},{8,12},{9,13},{10,... | collective-permute-start | bytes 811016 | tf_op jit(solution)/shard_map/ppermute | solution.py:243
  40.6 1.7 %collective-permute-start.4 = (f32[16,4224]{1,0:T(8,128)S(1)}, f32[16,4224]{1,0:T(8,128)}, u32[]{:S(2)}, u32[]{:S(2)}) collective-permute-start(f32[16,4224]{1,0:T(8,128)S(1)} %collective-permute-done.3), channel_id=1, source_target_pairs={{0,1},{1,0},{2,3},{3,2},{4,5},{5,4},{6,7},{7,6},{8,9},{9,8},{10,11... | collective-permute-start | bytes 811016 | tf_op jit(solution)/shard_map/ppermute | solution.py:252
  45.3 15.5 %collective-permute-start.5 = (f32[16,4224]{1,0:T(8,128)}, f32[16,4224]{1,0:T(8,128)S(1)}, u32[]{:S(2)}, u32[]{:S(2)}) collective-permute-start(f32[16,4224]{1,0:T(8,128)} %fusion.40), channel_id=1, source_target_pairs={{0,8},{1,9},{2,10},{3,11},{4,12},{5,13},{6,14},{7,15},{8,0},{9,1},... | collective-permute-start | bytes 811016 | tf_op jit(solution)/shard_map/ppermute | solution.py:243
  53.9 9.7 %copy-start.3 = (f32[16,4096]{1,0:T(8,128)S(1)}, f32[16,4096]{1,0:T(8,128)}, u32[]{:S(2)}) copy-start(f32[16,4096]{1,0:T(8,128)} %get-tuple-element.33.pw_ref) | copy-start | bytes 786436
  60.8 0.7 copy-start.6
  60.8 1.7 %collective-permute-start.6 = (f32[16,4224]{1,0:T(8,128)S(1)}, f32[16,4224]{1,0:T(8,128)}, u32[]{:S(2)}, u32[]{:S(2)}) collective-permute-start(f32[16,4224]{1,0:T(8,128)S(1)} %collective-permute-done.5), channel_id=1, source_target_pairs={{0,1},{1,0},{2,3},{3,2},{4,5},{5,4},{6,7},{7,6},{8,9},{9,8},{10,11... | collective-permute-start | bytes 811016 | tf_op jit(solution)/shard_map/ppermute | solution.py:252

commit v15 on v13

--- a/solution.py
+++ b/solution.py
@@ -109,7 +109,7 @@
 
     p = p_ref[...]
     r = r_ref[...]
-    lax.fori_loop(0, rows, body, ((r * p) * s_ref[...], (r * p) * b_ref[...]), unroll=4)
+    lax.fori_loop(0, rows, body, ((r * p) * s_ref[...], (r * p) * b_ref[...]), unroll=8)
     for c in range(lanes):
         cols = slice(c * LANE, (c + 1) * LANE)
         band = slice(c * rows, (c + 1) * rows)

time: 76.8 us -> 76 us (0.990)
  Pallas kernels: 44.1 us -> 43.3 us
    pallas_call x1, Pallas kernels: 10.9 us -> 10.1 us  [corrected(): pl.pallas_call(correct_kernel, grid=(width // BLOCK,), in_specs=[big] * 6...]
  transfers between devices with their start and end apart: 7 -> 7, of which waited for: 7 -> 7; matrix products, arithmetic and copies ran while one was open for 0% -> 0% of each run, Pallas kernels for 30% -> 31%
where the time goes in v15:
time: 76 us; the launch traced here: 75.5 us
  Pallas kernels  43.3 us (57%)
  waiting for transfers between devices  9.08 us (12%)
  starting transfers between devices  8.16 us (11%)
  other arithmetic  7.8 us (10%)
  matrix products  5.68 us (7%)
  between operations  1.52 us (2%)
    pallas_call x4, Pallas kernels, local_scans(): pl.pallas_call(local_kernel, grid=(1,), in_specs=specs, out_specs=[big, b...  23.3 us
    pallas_call x1, Pallas kernels, corrected(): pl.pallas_call(correct_kernel, grid=(width // BLOCK,), in_specs=[big] * 6...  10.1 us
    pallas_call x1, Pallas kernels, local_carries(): pl.pallas_call(carry_kernel, grid=(width // BLOCK,), in_specs=[big, big,...  9.96 us
    ppermute x3, starting transfers between devices, on_device(): got_mine = lax.ppermute(mine, 'ctx', pairs)  7.63 us
    dot_general x6, matrix products, split_dot(): jnp.dot(jnp.concatenate([hi, mid, lo], axis=0), member, preferred_element...  5.68 us
    ppermute x3, waiting for transfers between devices, on_device(): lax.ppermute(got_mine, 'ctx', [(i, i ^ 1) for i in range(count)])  4.63 us
    convert_element_type x6, other arithmetic, split_dot(): hi = top.astype(bf16)  3.87 us
    ppermute x3, waiting for transfers between devices, on_device(): got_mine = lax.ppermute(mine, 'ctx', pairs)  2.89 us
  transfers between devices with their start and end apart: 7, of which 7 were waited for; matrix products, arithmetic and copies ran while one was open for 0% of the time, Pallas kernels for 31%

profile of v15, /device:TPU:0, one launch (start us, length us, event | category | flops | bytes accessed | tf_op | source)
XLA Modules:
  0.0 75.5 jit_solution(9924242092875331411)
XLA Ops:
  0.6 0.7 reduce-precision_convert_fusion.11
  1.4 1.6 %fusion.5 = f32[96,4096]{1,0:T(8,128)S(1)} fusion(s32[4096]{0:T(1024)} %param.13, bf16[32,256]{1,0:T(8,128)(2,1)S(1)} %get-tuple-element.90, bf16[32,256]{1,0:T(8,128)(2,1)S(1)} %get-tuple-element.89, bf16[32,256]{1,0:T(8,128)(2,1)S(1)} %get-tuple-element.88), kind=kOutput, calls=%fused_computation.6 | convolution fusion | flops 202522624 | bytes 1638400 | tf_op jit(solution)/shard_map/dot_general | solution.py:193
  3.0 0.1 slice_add_fusion
  3.1 0.8 fusion.58.p_ref.pw_ref
  3.8 0.0 copy-start.2
  3.8 10.0 %shard_map.110 = (f32[16,4096]{1,0:T(8,128)}, f32[16,4096]{1,0:T(8,128)}, f32[16,4096]{1,0:T(8,128)}) custom-call(bf16[128,4096]{1,0:T(8,128)(2,1)} %q_ref.11, bf16[128,4096]{1,0:T(8,128)(2,1)} %k_ref.11, bf16[128,4096]{1,0:T(8,128)(2,1)} %v_ref.11, bf16[128,4096]{1,0:T(8,128)(2,1)} %g_ref.11, f32[16,4096]{1,0:T(8,128)} %fusion.58.p_ref.pw_ref), custom_call_target="tpu_custom_call" | custom-call | tf_op jit(solution)/shard_map/pallas_call | solution.py:129
  13.8 0.0 copy-start
  13.8 0.0 copy-start.1
  13.8 1.1 %reduce-precision_convert_fusion.9 = (bf16[16,4096]{1,0:T(8,128)(2,1)S(1)}, bf16[16,4096]{1,0:T(8,128)(2,1)S(1)}, bf16[16,4096]{1,0:T(8,128)(2,1)S(1)}) fusion(f32[16,4096]{1,0:T(8,128)} %get-tuple-element.31), kind=kLoop, calls=%fused_computation.69 | loop fusion | flops 458752 | bytes 655360 | tf_op jit(solution)/shard_map/convert_element_type | solution.py:189
  14.8 0.0 copy-done.2
  14.8 0.8 %fusion.4 = f32[48,256]{1,0:T(8,128)S(1)} fusion(s32[4096]{0:T(1024)S(1)} %copy-done.2, bf16[16,4096]{1,0:T(8,128)(2,1)S(1)} %get-tuple-element.86, bf16[16,4096]{1,0:T(8,128)(2,1)S(1)} %get-tuple-element.87, bf16[16,4096]{1,0:T(8,128)(2,1)S(1)} %get-tuple-element.85), kind=kOutput, calls=%fused_computation.5 | convolution fusion | flops 102891520 | bytes 458752 | tf_op jit(solution)/shard_map/dot_general | solution.py:193
  15.7 0.0 copy-done
  15.7 0.0 copy-done.1
  15.8 0.5 collective-permute-start
  16.3 1.6 %collective-permute-done = f32[16,8448]{1,0:T(8,128)S(1)} collective-permute-done((f32[16,8448]{1,0:T(8,128)S(1)}, f32[16,8448]{1,0:T(8,128)S(1)}, u32[]{:S(2)}, u32[]{:S(2)}) %collective-permute-start) | collective-permute-done | bytes 540704 | tf_op jit(solution)/shard_map/ppermute | solution.py:240
  17.8 0.8 %reduce-precision_convert_fusion.7 = (bf16[16,4096]{1,0:T(8,128)(2,1)S(1)}, f32[16,4096]{1,0:T(8,128)S(1)}, f32[16,4096]{1,0:T(8,128)S(1)}, f32[16,4096]{1,0:T(8,128)S(1)}, f32[16,4096]{1,0:T(8,128)}) fusion(f32[16,4096]{1,0:T(8,128)S(1)} %copy-done.1, f32[16,8448]{1,0:T(8,128)S(1)} %collective-permute-done, f32[16,4096]{1,0:T(8,128)S(1)} %copy-done, ...), kind=kLoop, calls=%fused_computation.65 | loop fusion | flops 917504 | bytes 2752513 | tf_op jit(solution)/shard_map/convert_element_type | solution.py:189
  18.7 0.8 %fusion.3 = f32[48,256]{1,0:T(8,128)S(1)} fusion(s32[4096]{0:T(1024)S(1)} %copy-done.2, bf16[16,4096]{1,0:T(8,128)(2,1)S(1)} %get-tuple-element.84, bf16[16,4096]{1,0:T(8,128)(2,1)S(1)} %get-tuple-element.83, bf16[16,4096]{1,0:T(8,128)(2,1)S(1)} %get-tuple-element.63), kind=kOutput, calls=%fused_computation.4 | convolution fusion | flops 102891520 | bytes 458752 | tf_op jit(solution)/shard_map/dot_general | solution.py:193
  19.5 0.1 fusion.42
  19.7 3.0 %collective-permute-start.1 = (f32[16,4224]{1,0:T(8,128)S(1)}, f32[16,4224]{1,0:T(8,128)S(1)}, u32[]{:S(2)}, u32[]{:S(2)}) collective-permute-start(f32[16,4224]{1,0:T(8,128)S(1)} %fusion.42), channel_id=1, source_target_pairs={{0,2},{1,3},{2,0},{3,1},{4,6},{5,7},{6,4},{7,5},{8,10},{9,11},{10,... | collective-permute-start | bytes 811016 | tf_op jit(solution)/shard_map/ppermute | solution.py:245
  22.6 5.9 %shard_map.111 = (f32[128,4096]{1,0:T(8,128)}, f32[128,4096]{1,0:T(8,128)}) custom-call(bf16[128,4096]{1,0:T(8,128)(2,1)} %q_ref.11, bf16[128,4096]{1,0:T(8,128)(2,1)} %k_ref.11, bf16[128,4096]{1,0:T(8,128)(2,1)} %v_ref.11, bf16[128,4096]{1,0:T(8,128)(2,1)} %g_ref.11, f32[16,4096]{1,0:T(8,128)} %fusion.58.p_ref.pw_ref, f32[16,4096]{1,0:T(8,128)} %get-tuple-element.76.rw_ref), custom_call_target="tpu_custom_call" | custom-call | tf_op jit(solution)/shard_map/pallas_call | solution.py:152
  28.5 0.9 %collective-permute-done.1 = f32[16,4224]{1,0:T(8,128)S(1)} collective-permute-done((f32[16,4224]{1,0:T(8,128)S(1)}, f32[16,4224]{1,0:T(8,128)S(1)}, u32[]{:S(2)}, u32[]{:S(2)}) %collective-permute-start.1) | collective-permute-done | bytes 270368 | tf_op jit(solution)/shard_map/ppermute | solution.py:245
  29.4 0.0 collective-permute-start.2
  29.4 1.5 %collective-permute-done.2 = f32[16,4224]{1,0:T(8,128)S(1)} collective-permute-done((f32[16,4224]{1,0:T(8,128)S(1)}, f32[16,4224]{1,0:T(8,128)S(1)}, u32[]{:S(2)}, u32[]{:S(2)}) %collective-permute-start.2) | collective-permute-done | bytes 270368 | tf_op jit(solution)/shard_map/ppermute | solution.py:254
  31.0 0.1 reduce-precision_convert_fusion.5
  31.2 0.1 reduce-precision_convert_fusion.4
  31.3 0.8 %fusion.2 = f32[48,256]{1,0:T(8,128)S(1)} fusion(s32[4096]{0:T(1024)S(1)} %copy-done.2, bf16[16,4096]{1,0:T(8,128)(2,1)S(1)} %get-tuple-element.82, bf16[16,4096]{1,0:T(8,128)(2,1)S(1)} %get-tuple-element.81, bf16[16,4096]{1,0:T(8,128)(2,1)S(1)} %get-tuple-element.60), kind=kOutput, calls=%fused_computation.3 | convolution fusion | flops 102891520 | bytes 458752 | tf_op jit(solution)/shard_map/dot_general | solution.py:193
  32.1 0.1 fusion.40
  32.3 1.9 %collective-permute-start.3 = (f32[16,4224]{1,0:T(8,128)S(1)}, f32[16,4224]{1,0:T(8,128)S(1)}, u32[]{:S(2)}, u32[]{:S(2)}) collective-permute-start(f32[16,4224]{1,0:T(8,128)S(1)} %fusion.40), channel_id=1, source_target_pairs={{0,4},{1,5},{2,6},{3,7},{4,0},{5,1},{6,2},{7,3},{8,12},{9,13},{10,... | collective-permute-start | bytes 811016 | tf_op jit(solution)/shard_map/ppermute | solution.py:245
  34.1 5.8 %shard_map.112 = (f32[128,4096]{1,0:T(8,128)}, f32[128,4096]{1,0:T(8,128)}) custom-call(bf16[128,4096]{1,0:T(8,128)(2,1)} %q_ref.11, bf16[128,4096]{1,0:T(8,128)(2,1)} %k_ref.11, bf16[128,4096]{1,0:T(8,128)(2,1)} %v_ref.11, bf16[128,4096]{1,0:T(8,128)(2,1)} %g_ref.11, f32[16,4096]{1,0:T(8,128)} %fusion.58.p_ref.pw_ref, ...), custom_call_target="tpu_custom_call", output_to_operand_aliasing={{0}: (6, {}), {1}: (7, {})} | custom-call | tf_op jit(solution)/shard_map/pallas_call | solution.py:152
  39.9 1.0 %collective-permute-done.3 = f32[16,4224]{1,0:T(8,128)S(1)} collective-permute-done((f32[16,4224]{1,0:T(8,128)S(1)}, f32[16,4224]{1,0:T(8,128)S(1)}, u32[]{:S(2)}, u32[]{:S(2)}) %collective-permute-start.3) | collective-permute-done | bytes 270368 | tf_op jit(solution)/shard_map/ppermute | solution.py:245
  40.9 0.0 collective-permute-start.4
  40.9 1.5 %collective-permute-done.4 = f32[16,4224]{1,0:T(8,128)S(1)} collective-permute-done((f32[16,4224]{1,0:T(8,128)S(1)}, f32[16,4224]{1,0:T(8,128)S(1)}, u32[]{:S(2)}, u32[]{:S(2)}) %collective-permute-start.4) | collective-permute-done | bytes 270368 | tf_op jit(solution)/shard_map/ppermute | solution.py:254
  42.5 0.1 reduce-precision_convert_fusion.3
  42.7 0.8 %fusion.1 = f32[48,256]{1,0:T(8,128)S(1)} fusion(s32[4096]{0:T(1024)S(1)} %copy-done.2, bf16[16,4096]{1,0:T(8,128)(2,1)S(1)} %get-tuple-element.80, bf16[16,4096]{1,0:T(8,128)(2,1)S(1)} %get-tuple-element.79, bf16[16,4096]{1,0:T(8,128)(2,1)S(1)} %get-tuple-element.57), kind=kOutput, calls=%fused_computation.2 | convolution fusion | flops 102891520 | bytes 458752 | tf_op jit(solution)/shard_map/dot_general | solution.py:193
  43.5 0.1 multiply_add_fusion
  43.6 0.1 fusion.38
  43.8 2.8 %collective-permute-start.5 = (f32[16,4224]{1,0:T(8,128)S(1)}, f32[16,4224]{1,0:T(8,128)S(1)}, u32[]{:S(2)}, u32[]{:S(2)}) collective-permute-start(f32[16,4224]{1,0:T(8,128)S(1)} %fusion.38), channel_id=1, source_target_pairs={{0,8},{1,9},{2,10},{3,11},{4,12},{5,13},{6,14},{7,15},{8,0},{9,1},... | collective-permute-start | bytes 811016 | tf_op jit(solution)/shard_map/ppermute | solution.py:245
  46.6 5.8 %shard_map.113 = (f32[128,4096]{1,0:T(8,128)}, f32[128,4096]{1,0:T(8,128)}) custom-call(bf16[128,4096]{1,0:T(8,128)(2,1)} %q_ref.11, bf16[128,4096]{1,0:T(8,128)(2,1)} %k_ref.11, bf16[128,4096]{1,0:T(8,128)(2,1)} %v_ref.11, bf16[128,4096]{1,0:T(8,128)(2,1)} %g_ref.11, f32[16,4096]{1,0:T(8,128)} %fusion.58.p_ref.pw_ref, ...), custom_call_target="tpu_custom_call", output_to_operand_aliasing={{0}: (6, {}), {1}: (7, {})} | custom-call | tf_op jit(solution)/shard_map/pallas_call | solution.py:152
  52.4 5.8 %shard_map.114 = (f32[128,4096]{1,0:T(8,128)}, f32[128,4096]{1,0:T(8,128)}) custom-call(bf16[128,4096]{1,0:T(8,128)(2,1)} %q_ref.11, bf16[128,4096]{1,0:T(8,128)(2,1)} %k_ref.11, bf16[128,4096]{1,0:T(8,128)(2,1)} %v_ref.11, bf16[128,4096]{1,0:T(8,128)(2,1)} %g_ref.11, f32[16,4096]{1,0:T(8,128)} %fusion.58.p_ref.pw_ref, ...), custom_call_target="tpu_custom_call", output_to_operand_aliasing={{0}: (6, {}), {1}: (7, {})} | custom-call | tf_op jit(solution)/shard_map/pallas_call | solution.py:152
  58.2 1.0 %collective-permute-done.5 = f32[16,4224]{1,0:T(8,128)S(1)} collective-permute-done((f32[16,4224]{1,0:T(8,128)S(1)}, f32[16,4224]{1,0:T(8,128)S(1)}, u32[]{:S(2)}, u32[]{:S(2)}) %collective-permute-start.5) | collective-permute-done | bytes 270368 | tf_op jit(solution)/shard_map/ppermute | solution.py:245
  59.2 0.0 collective-permute-start.6
  59.2 1.5 %collective-permute-done.6 = f32[16,4224]{1,0:T(8,128)S(1)} collective-permute-done((f32[16,4224]{1,0:T(8,128)S(1)}, f32[16,4224]{1,0:T(8,128)S(1)}, u32[]{:S(2)}, u32[]{:S(2)}) %collective-permute-start.6) | collective-permute-done | bytes 270368 | tf_op jit(solution)/shard_map/ppermute | solution.py:254
  60.8 1.0 %reduce-precision_convert_fusion.1 = (bf16[16,4096]{1,0:T(8,128)(2,1)S(1)}, f32[16,4096]{1,0:T(8,128)S(1)}, f32[16,4096]{1,0:T(8,128)}) fusion(f32[16,4096]{1,0:T(8,128)S(1)} %multiply_add_fusion, f32[16,4224]{1,0:T(8,128)S(1)} %get-tuple-element.70, f32[16,4224]{1,0:T(8,128)S(1)} %get-tuple-element.71, f32[16,4096]{1,0:T(8,128)S(1)} %get-tuple-element.68, ...), kind=kLoop, calls=%fused_computation.53 | loop fusion | flops 1507328 | bytes 3031056 | tf_op jit(solution)/shard_map/convert_element_type | solution.py:189
  61.8 0.8 %fusion = f32[48,256]{1,0:T(8,128)S(1)} fusion(s32[4096]{0:T(1024)S(1)} %copy-done.2, bf16[16,4096]{1,0:T(8,128)(2,1)S(1)} %get-tuple-element.78, bf16[16,4096]{1,0:T(8,128)(2,1)S(1)} %get-tuple-element.77, bf16[16,4096]{1,0:T(8,128)(2,1)S(1)} %get-tuple-element.55), kind=kOutput, calls=%fused_computation.1 | convolution fusion | flops 102891520 | bytes 458752 | tf_op jit(solution)/shard_map/dot_general | solution.py:193
  62.6 0.6 multiply_reduce_fusion
  63.9 0.6 divide_bitcast_fusion
  64.5 0.9 %select_add_fusion.1.sw_ref = f32[16,4096]{1,0:T(8,128)} fusion(f32[16,4224]{1,0:T(8,128)S(1)} %get-tuple-element.71, f32[16,4224]{1,0:T(8,128)S(1)} %get-tuple-element.73, f32[16,4224]{1,0:T(8,128)S(1)} %get-tuple-element.75, f32[16,8448]{1,0:T(8,128)S(1)} %collective-permute-done, f32[]{:T(128)S(6)} %mul.187, f32[]{:T(128)S(6)} %mul.183, f32[]{:T(128)S(6)} %mul.179, ...), kind=kLoop, calls=%fused_computation.87 | loop fusion | flops 1048576 | bytes 1572880 | tf_op jit(solution)/shard_map/add | solution.py:269
  65.5 10.1 %shard_map.115 = (bf16[128,4096]{1,0:T(8,128)(2,1)}, bf16[128,4096]{1,0:T(8,128)(2,1)}, bf16[128,4096]{1,0:T(8,128)(2,1)}, bf16[128,4096]{1,0:T(8,128)(2,1)}) custom-call(bf16[128,4096]{1,0:T(8,128)(2,1)} %q_ref.11, bf16[128,4096]{1,0:T(8,128)(2,1)} %k_ref.11, bf16[128,4096]{1,0:T(8,128)(2,1)} %v_ref.11, bf16[128,4096]{1,0:T(8,128)(2,1)} %g_ref.11, ...), custom_call_target="tpu_custom_call" | custom-call | tf_op jit(solution)/shard_map/pallas_call | solution.py:172
  (11 shorter events, 0.3 us)
Async XLA Ops:
  3.8 11.0 %copy-start.2 = (s32[4096]{0:T(1024)S(1)}, s32[4096]{0:T(1024)}, u32[]{:S(2)}) copy-start(s32[4096]{0:T(1024)} %param.13) | copy-start | bytes 49156
  13.8 1.9 %copy-start = (f32[16,4096]{1,0:T(8,128)S(1)}, f32[16,4096]{1,0:T(8,128)}, u32[]{:S(2)}) copy-start(f32[16,4096]{1,0:T(8,128)} %get-tuple-element.29) | copy-start | bytes 786436
  13.8 1.9 %copy-start.1 = (f32[16,4096]{1,0:T(8,128)S(1)}, f32[16,4096]{1,0:T(8,128)}, u32[]{:S(2)}) copy-start(f32[16,4096]{1,0:T(8,128)} %get-tuple-element.30) | copy-start | bytes 786436
  15.8 2.1 %collective-permute-start = (f32[16,8448]{1,0:T(8,128)S(1)}, f32[16,8448]{1,0:T(8,128)S(1)}, u32[]{:S(2)}, u32[]{:S(2)}) collective-permute-start(f32[16,8448]{1,0:T(8,128)S(1)} %pad_maximum_fusion), channel_id=1, source_target_pairs={{0,1},{1,0},{2,3},{3,2},{4,5},{5,4},{6,7},{7,6},{8,9},{9,8},{10,11... | collective-permute-start | bytes 1622024 | tf_op jit(solution)/shard_map/ppermute | solution.py:240
  19.7 9.7 %collective-permute-start.1 = (f32[16,4224]{1,0:T(8,128)S(1)}, f32[16,4224]{1,0:T(8,128)S(1)}, u32[]{:S(2)}, u32[]{:S(2)}) collective-permute-start(f32[16,4224]{1,0:T(8,128)S(1)} %fusion.42), channel_id=1, source_target_pairs={{0,2},{1,3},{2,0},{3,1},{4,6},{5,7},{6,4},{7,5},{8,10},{9,11},{10,... | collective-permute-start | bytes 811016 | tf_op jit(solution)/shard_map/ppermute | solution.py:245
  29.4 1.5 %collective-permute-start.2 = (f32[16,4224]{1,0:T(8,128)S(1)}, f32[16,4224]{1,0:T(8,128)S(1)}, u32[]{:S(2)}, u32[]{:S(2)}) collective-permute-start(f32[16,4224]{1,0:T(8,128)S(1)} %collective-permute-done.1), channel_id=1, source_target_pairs={{0,1},{1,0},{2,3},{3,2},{4,5},{5,4},{6,7},{7,6},{8,9},{9,8},{10,11... | collective-permute-start | bytes 811016 | tf_op jit(solution)/shard_map/ppermute | solution.py:254
  32.3 8.6 %collective-permute-start.3 = (f32[16,4224]{1,0:T(8,128)S(1)}, f32[16,4224]{1,0:T(8,128)S(1)}, u32[]{:S(2)}, u32[]{:S(2)}) collective-permute-start(f32[16,4224]{1,0:T(8,128)S(1)} %fusion.40), channel_id=1, source_target_pairs={{0,4},{1,5},{2,6},{3,7},{4,0},{5,1},{6,2},{7,3},{8,12},{9,13},{10,... | collective-permute-start | bytes 811016 | tf_op jit(solution)/shard_map/ppermute | solution.py:245
  40.9 1.5 %collective-permute-start.4 = (f32[16,4224]{1,0:T(8,128)S(1)}, f32[16,4224]{1,0:T(8,128)S(1)}, u32[]{:S(2)}, u32[]{:S(2)}) collective-permute-start(f32[16,4224]{1,0:T(8,128)S(1)} %collective-permute-done.3), channel_id=1, source_target_pairs={{0,1},{1,0},{2,3},{3,2},{4,5},{5,4},{6,7},{7,6},{8,9},{9,8},{10,11... | collective-permute-start | bytes 811016 | tf_op jit(solution)/shard_map/ppermute | solution.py:254
  43.8 15.4 %collective-permute-start.5 = (f32[16,4224]{1,0:T(8,128)S(1)}, f32[16,4224]{1,0:T(8,128)S(1)}, u32[]{:S(2)}, u32[]{:S(2)}) collective-permute-start(f32[16,4224]{1,0:T(8,128)S(1)} %fusion.38), channel_id=1, source_target_pairs={{0,8},{1,9},{2,10},{3,11},{4,12},{5,13},{6,14},{7,15},{8,0},{9,1},... | collective-permute-start | bytes 811016 | tf_op jit(solution)/shard_map/ppermute | solution.py:245
  59.2 1.5 %collective-permute-start.6 = (f32[16,4224]{1,0:T(8,128)S(1)}, f32[16,4224]{1,0:T(8,128)S(1)}, u32[]{:S(2)}, u32[]{:S(2)}) collective-permute-start(f32[16,4224]{1,0:T(8,128)S(1)} %collective-permute-done.5), channel_id=1, source_target_pairs={{0,1},{1,0},{2,3},{3,2},{4,5},{5,4},{6,7},{7,6},{8,9},{9,8},{10,11... | collective-permute-start | bytes 811016 | tf_op jit(solution)/shard_map/ppermute | solution.py:254

commit v16 on v15

--- a/solution.py
+++ b/solution.py
@@ -80,7 +80,7 @@
         return x, a
 
     zero = jnp.zeros(p_ref.shape, f32)
-    lax.fori_loop(0, rows, body, (zero, zero), unroll=4)
+    lax.fori_loop(0, rows, body, (zero, zero), unroll=8)
     for c in range(lanes):
         cols = slice(c * LANE, (c + 1) * LANE)
         band = slice(c * rows, (c + 1) * rows)

time: 76 us -> 76 us (level)
  transfers between devices with their start and end apart: 7 -> 7, of which waited for: 7 -> 7; matrix products, arithmetic and copies ran while one was open for 0% -> 0% of each run, Pallas kernels for 31% -> 30%
where the time goes in v16:
time: 76 us; the launch traced here: 75.5 us
  Pallas kernels  42.9 us (56%)
  waiting for transfers between devices  9.42 us (12%)
  starting transfers between devices  8.16 us (11%)
  other arithmetic  7.8 us (10%)
  matrix products  5.68 us (7%)
  between operations  1.52 us (2%)
    pallas_call x4, Pallas kernels, local_scans(): pl.pallas_call(local_kernel, grid=(1,), in_specs=specs, out_specs=[big, b...  22.9 us
    pallas_call x1, Pallas kernels, corrected(): pl.pallas_call(correct_kernel, grid=(width // BLOCK,), in_specs=[big] * 6...  10.1 us
    pallas_call x1, Pallas kernels, local_carries(): pl.pallas_call(carry_kernel, grid=(width // BLOCK,), in_specs=[big, big,...  9.96 us
    ppermute x3, starting transfers between devices, on_device(): got_mine = lax.ppermute(mine, 'ctx', pairs)  7.63 us
    dot_general x6, matrix products, split_dot(): jnp.dot(jnp.concatenate([hi, mid, lo], axis=0), member, preferred_element...  5.68 us
    ppermute x3, waiting for transfers between devices, on_device(): lax.ppermute(got_mine, 'ctx', [(i, i ^ 1) for i in range(count)])  4.63 us
    convert_element_type x6, other arithmetic, split_dot(): hi = top.astype(bf16)  3.87 us
    ppermute x3, waiting for transfers between devices, on_device(): got_mine = lax.ppermute(mine, 'ctx', pairs)  3.23 us
  transfers between devices with their start and end apart: 7, of which 7 were waited for; matrix products, arithmetic and copies ran while one was open for 0% of the time, Pallas kernels for 30%

profile of v16, /device:TPU:0, one launch (start us, length us, event | category | flops | bytes accessed | tf_op | source)
XLA Modules:
  0.0 75.5 jit_solution(11501084241759752633)
XLA Ops:
  0.6 0.7 reduce-precision_convert_fusion.11
  1.4 1.6 %fusion.5 = f32[96,4096]{1,0:T(8,128)S(1)} fusion(s32[4096]{0:T(1024)} %param.13, bf16[32,256]{1,0:T(8,128)(2,1)S(1)} %get-tuple-element.90, bf16[32,256]{1,0:T(8,128)(2,1)S(1)} %get-tuple-element.89, bf16[32,256]{1,0:T(8,128)(2,1)S(1)} %get-tuple-element.88), kind=kOutput, calls=%fused_computation.6 | convolution fusion | flops 202522624 | bytes 1638400 | tf_op jit(solution)/shard_map/dot_general | solution.py:193
  3.0 0.1 slice_add_fusion
  3.1 0.8 fusion.58.p_ref.pw_ref
  3.8 0.0 copy-start.2
  3.8 10.0 %shard_map.110 = (f32[16,4096]{1,0:T(8,128)}, f32[16,4096]{1,0:T(8,128)}, f32[16,4096]{1,0:T(8,128)}) custom-call(bf16[128,4096]{1,0:T(8,128)(2,1)} %q_ref.11, bf16[128,4096]{1,0:T(8,128)(2,1)} %k_ref.11, bf16[128,4096]{1,0:T(8,128)(2,1)} %v_ref.11, bf16[128,4096]{1,0:T(8,128)(2,1)} %g_ref.11, f32[16,4096]{1,0:T(8,128)} %fusion.58.p_ref.pw_ref), custom_call_target="tpu_custom_call" | custom-call | tf_op jit(solution)/shard_map/pallas_call | solution.py:129
  13.8 0.0 copy-start
  13.8 0.0 copy-start.1
  13.8 1.1 %reduce-precision_convert_fusion.9 = (bf16[16,4096]{1,0:T(8,128)(2,1)S(1)}, bf16[16,4096]{1,0:T(8,128)(2,1)S(1)}, bf16[16,4096]{1,0:T(8,128)(2,1)S(1)}) fusion(f32[16,4096]{1,0:T(8,128)} %get-tuple-element.31), kind=kLoop, calls=%fused_computation.69 | loop fusion | flops 458752 | bytes 655360 | tf_op jit(solution)/shard_map/convert_element_type | solution.py:189
  14.8 0.0 copy-done.2
  14.8 0.8 %fusion.4 = f32[48,256]{1,0:T(8,128)S(1)} fusion(s32[4096]{0:T(1024)S(1)} %copy-done.2, bf16[16,4096]{1,0:T(8,128)(2,1)S(1)} %get-tuple-element.86, bf16[16,4096]{1,0:T(8,128)(2,1)S(1)} %get-tuple-element.87, bf16[16,4096]{1,0:T(8,128)(2,1)S(1)} %get-tuple-element.85), kind=kOutput, calls=%fused_computation.5 | convolution fusion | flops 102891520 | bytes 458752 | tf_op jit(solution)/shard_map/dot_general | solution.py:193
  15.7 0.0 copy-done
  15.7 0.0 copy-done.1
  15.8 0.5 collective-permute-start
  16.3 1.6 %collective-permute-done = f32[16,8448]{1,0:T(8,128)S(1)} collective-permute-done((f32[16,8448]{1,0:T(8,128)S(1)}, f32[16,8448]{1,0:T(8,128)S(1)}, u32[]{:S(2)}, u32[]{:S(2)}) %collective-permute-start) | collective-permute-done | bytes 540704 | tf_op jit(solution)/shard_map/ppermute | solution.py:240
  17.8 0.8 %reduce-precision_convert_fusion.7 = (bf16[16,4096]{1,0:T(8,128)(2,1)S(1)}, f32[16,4096]{1,0:T(8,128)S(1)}, f32[16,4096]{1,0:T(8,128)S(1)}, f32[16,4096]{1,0:T(8,128)S(1)}, f32[16,4096]{1,0:T(8,128)}) fusion(f32[16,4096]{1,0:T(8,128)S(1)} %copy-done.1, f32[16,8448]{1,0:T(8,128)S(1)} %collective-permute-done, f32[16,4096]{1,0:T(8,128)S(1)} %copy-done, ...), kind=kLoop, calls=%fused_computation.65 | loop fusion | flops 917504 | bytes 2752513 | tf_op jit(solution)/shard_map/convert_element_type | solution.py:189
  18.7 0.8 %fusion.3 = f32[48,256]{1,0:T(8,128)S(1)} fusion(s32[4096]{0:T(1024)S(1)} %copy-done.2, bf16[16,4096]{1,0:T(8,128)(2,1)S(1)} %get-tuple-element.84, bf16[16,4096]{1,0:T(8,128)(2,1)S(1)} %get-tuple-element.83, bf16[16,4096]{1,0:T(8,128)(2,1)S(1)} %get-tuple-element.63), kind=kOutput, calls=%fused_computation.4 | convolution fusion | flops 102891520 | bytes 458752 | tf_op jit(solution)/shard_map/dot_general | solution.py:193
  19.5 0.1 fusion.42
  19.7 3.0 %collective-permute-start.1 = (f32[16,4224]{1,0:T(8,128)S(1)}, f32[16,4224]{1,0:T(8,128)S(1)}, u32[]{:S(2)}, u32[]{:S(2)}) collective-permute-start(f32[16,4224]{1,0:T(8,128)S(1)} %fusion.42), channel_id=1, source_target_pairs={{0,2},{1,3},{2,0},{3,1},{4,6},{5,7},{6,4},{7,5},{8,10},{9,11},{10,... | collective-permute-start | bytes 811016 | tf_op jit(solution)/shard_map/ppermute | solution.py:245
  22.6 5.8 %shard_map.111 = (f32[128,4096]{1,0:T(8,128)}, f32[128,4096]{1,0:T(8,128)}) custom-call(bf16[128,4096]{1,0:T(8,128)(2,1)} %q_ref.11, bf16[128,4096]{1,0:T(8,128)(2,1)} %k_ref.11, bf16[128,4096]{1,0:T(8,128)(2,1)} %v_ref.11, bf16[128,4096]{1,0:T(8,128)(2,1)} %g_ref.11, f32[16,4096]{1,0:T(8,128)} %fusion.58.p_ref.pw_ref, f32[16,4096]{1,0:T(8,128)} %get-tuple-element.76.rw_ref), custom_call_target="tpu_custom_call" | custom-call | tf_op jit(solution)/shard_map/pallas_call | solution.py:152
  28.4 1.0 %collective-permute-done.1 = f32[16,4224]{1,0:T(8,128)S(1)} collective-permute-done((f32[16,4224]{1,0:T(8,128)S(1)}, f32[16,4224]{1,0:T(8,128)S(1)}, u32[]{:S(2)}, u32[]{:S(2)}) %collective-permute-start.1) | collective-permute-done | bytes 270368 | tf_op jit(solution)/shard_map/ppermute | solution.py:245
  29.4 0.0 collective-permute-start.2
  29.4 1.5 %collective-permute-done.2 = f32[16,4224]{1,0:T(8,128)S(1)} collective-permute-done((f32[16,4224]{1,0:T(8,128)S(1)}, f32[16,4224]{1,0:T(8,128)S(1)}, u32[]{:S(2)}, u32[]{:S(2)}) %collective-permute-start.2) | collective-permute-done | bytes 270368 | tf_op jit(solution)/shard_map/ppermute | solution.py:254
  31.0 0.1 reduce-precision_convert_fusion.5
  31.2 0.1 reduce-precision_convert_fusion.4
  31.3 0.8 %fusion.2 = f32[48,256]{1,0:T(8,128)S(1)} fusion(s32[4096]{0:T(1024)S(1)} %copy-done.2, bf16[16,4096]{1,0:T(8,128)(2,1)S(1)} %get-tuple-element.82, bf16[16,4096]{1,0:T(8,128)(2,1)S(1)} %get-tuple-element.81, bf16[16,4096]{1,0:T(8,128)(2,1)S(1)} %get-tuple-element.60), kind=kOutput, calls=%fused_computation.3 | convolution fusion | flops 102891520 | bytes 458752 | tf_op jit(solution)/shard_map/dot_general | solution.py:193
  32.1 0.1 fusion.40
  32.3 1.9 %collective-permute-start.3 = (f32[16,4224]{1,0:T(8,128)S(1)}, f32[16,4224]{1,0:T(8,128)S(1)}, u32[]{:S(2)}, u32[]{:S(2)}) collective-permute-start(f32[16,4224]{1,0:T(8,128)S(1)} %fusion.40), channel_id=1, source_target_pairs={{0,4},{1,5},{2,6},{3,7},{4,0},{5,1},{6,2},{7,3},{8,12},{9,13},{10,... | collective-permute-start | bytes 811016 | tf_op jit(solution)/shard_map/ppermute | solution.py:245
  34.1 5.7 %shard_map.112 = (f32[128,4096]{1,0:T(8,128)}, f32[128,4096]{1,0:T(8,128)}) custom-call(bf16[128,4096]{1,0:T(8,128)(2,1)} %q_ref.11, bf16[128,4096]{1,0:T(8,128)(2,1)} %k_ref.11, bf16[128,4096]{1,0:T(8,128)(2,1)} %v_ref.11, bf16[128,4096]{1,0:T(8,128)(2,1)} %g_ref.11, f32[16,4096]{1,0:T(8,128)} %fusion.58.p_ref.pw_ref, ...), custom_call_target="tpu_custom_call", output_to_operand_aliasing={{0}: (6, {}), {1}: (7, {})} | custom-call | tf_op jit(solution)/shard_map/pallas_call | solution.py:152
  39.8 1.1 %collective-permute-done.3 = f32[16,4224]{1,0:T(8,128)S(1)} collective-permute-done((f32[16,4224]{1,0:T(8,128)S(1)}, f32[16,4224]{1,0:T(8,128)S(1)}, u32[]{:S(2)}, u32[]{:S(2)}) %collective-permute-start.3) | collective-permute-done | bytes 270368 | tf_op jit(solution)/shard_map/ppermute | solution.py:245
  40.9 0.0 collective-permute-start.4
  40.9 1.5 %collective-permute-done.4 = f32[16,4224]{1,0:T(8,128)S(1)} collective-permute-done((f32[16,4224]{1,0:T(8,128)S(1)}, f32[16,4224]{1,0:T(8,128)S(1)}, u32[]{:S(2)}, u32[]{:S(2)}) %collective-permute-start.4) | collective-permute-done | bytes 270368 | tf_op jit(solution)/shard_map/ppermute | solution.py:254
  42.5 0.1 reduce-precision_convert_fusion.3
  42.7 0.8 %fusion.1 = f32[48,256]{1,0:T(8,128)S(1)} fusion(s32[4096]{0:T(1024)S(1)} %copy-done.2, bf16[16,4096]{1,0:T(8,128)(2,1)S(1)} %get-tuple-element.80, bf16[16,4096]{1,0:T(8,128)(2,1)S(1)} %get-tuple-element.79, bf16[16,4096]{1,0:T(8,128)(2,1)S(1)} %get-tuple-element.57), kind=kOutput, calls=%fused_computation.2 | convolution fusion | flops 102891520 | bytes 458752 | tf_op jit(solution)/shard_map/dot_general | solution.py:193
  43.5 0.1 multiply_add_fusion
  43.6 0.1 fusion.38
  43.8 2.8 %collective-permute-start.5 = (f32[16,4224]{1,0:T(8,128)S(1)}, f32[16,4224]{1,0:T(8,128)S(1)}, u32[]{:S(2)}, u32[]{:S(2)}) collective-permute-start(f32[16,4224]{1,0:T(8,128)S(1)} %fusion.38), channel_id=1, source_target_pairs={{0,8},{1,9},{2,10},{3,11},{4,12},{5,13},{6,14},{7,15},{8,0},{9,1},... | collective-permute-start | bytes 811016 | tf_op jit(solution)/shard_map/ppermute | solution.py:245
  46.6 5.7 %shard_map.113 = (f32[128,4096]{1,0:T(8,128)}, f32[128,4096]{1,0:T(8,128)}) custom-call(bf16[128,4096]{1,0:T(8,128)(2,1)} %q_ref.11, bf16[128,4096]{1,0:T(8,128)(2,1)} %k_ref.11, bf16[128,4096]{1,0:T(8,128)(2,1)} %v_ref.11, bf16[128,4096]{1,0:T(8,128)(2,1)} %g_ref.11, f32[16,4096]{1,0:T(8,128)} %fusion.58.p_ref.pw_ref, ...), custom_call_target="tpu_custom_call", output_to_operand_aliasing={{0}: (6, {}), {1}: (7, {})} | custom-call | tf_op jit(solution)/shard_map/pallas_call | solution.py:152
  52.3 5.7 %shard_map.114 = (f32[128,4096]{1,0:T(8,128)}, f32[128,4096]{1,0:T(8,128)}) custom-call(bf16[128,4096]{1,0:T(8,128)(2,1)} %q_ref.11, bf16[128,4096]{1,0:T(8,128)(2,1)} %k_ref.11, bf16[128,4096]{1,0:T(8,128)(2,1)} %v_ref.11, bf16[128,4096]{1,0:T(8,128)(2,1)} %g_ref.11, f32[16,4096]{1,0:T(8,128)} %fusion.58.p_ref.pw_ref, ...), custom_call_target="tpu_custom_call", output_to_operand_aliasing={{0}: (6, {}), {1}: (7, {})} | custom-call | tf_op jit(solution)/shard_map/pallas_call | solution.py:152
  58.0 1.1 %collective-permute-done.5 = f32[16,4224]{1,0:T(8,128)S(1)} collective-permute-done((f32[16,4224]{1,0:T(8,128)S(1)}, f32[16,4224]{1,0:T(8,128)S(1)}, u32[]{:S(2)}, u32[]{:S(2)}) %collective-permute-start.5) | collective-permute-done | bytes 270368 | tf_op jit(solution)/shard_map/ppermute | solution.py:245
  59.2 0.0 collective-permute-start.6
  59.2 1.5 %collective-permute-done.6 = f32[16,4224]{1,0:T(8,128)S(1)} collective-permute-done((f32[16,4224]{1,0:T(8,128)S(1)}, f32[16,4224]{1,0:T(8,128)S(1)}, u32[]{:S(2)}, u32[]{:S(2)}) %collective-permute-start.6) | collective-permute-done | bytes 270368 | tf_op jit(solution)/shard_map/ppermute | solution.py:254
  60.8 1.0 %reduce-precision_convert_fusion.1 = (bf16[16,4096]{1,0:T(8,128)(2,1)S(1)}, f32[16,4096]{1,0:T(8,128)S(1)}, f32[16,4096]{1,0:T(8,128)}) fusion(f32[16,4096]{1,0:T(8,128)S(1)} %multiply_add_fusion, f32[16,4224]{1,0:T(8,128)S(1)} %get-tuple-element.70, f32[16,4224]{1,0:T(8,128)S(1)} %get-tuple-element.71, f32[16,4096]{1,0:T(8,128)S(1)} %get-tuple-element.68, ...), kind=kLoop, calls=%fused_computation.53 | loop fusion | flops 1507328 | bytes 3031056 | tf_op jit(solution)/shard_map/convert_element_type | solution.py:189
  61.8 0.8 %fusion = f32[48,256]{1,0:T(8,128)S(1)} fusion(s32[4096]{0:T(1024)S(1)} %copy-done.2, bf16[16,4096]{1,0:T(8,128)(2,1)S(1)} %get-tuple-element.78, bf16[16,4096]{1,0:T(8,128)(2,1)S(1)} %get-tuple-element.77, bf16[16,4096]{1,0:T(8,128)(2,1)S(1)} %get-tuple-element.55), kind=kOutput, calls=%fused_computation.1 | convolution fusion | flops 102891520 | bytes 458752 | tf_op jit(solution)/shard_map/dot_general | solution.py:193
  62.6 0.6 multiply_reduce_fusion
  63.9 0.6 divide_bitcast_fusion
  64.5 0.9 %select_add_fusion.1.sw_ref = f32[16,4096]{1,0:T(8,128)} fusion(f32[16,4224]{1,0:T(8,128)S(1)} %get-tuple-element.71, f32[16,4224]{1,0:T(8,128)S(1)} %get-tuple-element.73, f32[16,4224]{1,0:T(8,128)S(1)} %get-tuple-element.75, f32[16,8448]{1,0:T(8,128)S(1)} %collective-permute-done, f32[]{:T(128)S(6)} %mul.187, f32[]{:T(128)S(6)} %mul.183, f32[]{:T(128)S(6)} %mul.179, ...), kind=kLoop, calls=%fused_computation.87 | loop fusion | flops 1048576 | bytes 1572880 | tf_op jit(solution)/shard_map/add | solution.py:269
  65.5 10.1 %shard_map.115 = (bf16[128,4096]{1,0:T(8,128)(2,1)}, bf16[128,4096]{1,0:T(8,128)(2,1)}, bf16[128,4096]{1,0:T(8,128)(2,1)}, bf16[128,4096]{1,0:T(8,128)(2,1)}) custom-call(bf16[128,4096]{1,0:T(8,128)(2,1)} %q_ref.11, bf16[128,4096]{1,0:T(8,128)(2,1)} %k_ref.11, bf16[128,4096]{1,0:T(8,128)(2,1)} %v_ref.11, bf16[128,4096]{1,0:T(8,128)(2,1)} %g_ref.11, ...), custom_call_target="tpu_custom_call" | custom-call | tf_op jit(solution)/shard_map/pallas_call | solution.py:172
  (11 shorter events, 0.3 us)
Async XLA Ops:
  3.8 11.0 %copy-start.2 = (s32[4096]{0:T(1024)S(1)}, s32[4096]{0:T(1024)}, u32[]{:S(2)}) copy-start(s32[4096]{0:T(1024)} %param.13) | copy-start | bytes 49156
  13.8 1.9 %copy-start = (f32[16,4096]{1,0:T(8,128)S(1)}, f32[16,4096]{1,0:T(8,128)}, u32[]{:S(2)}) copy-start(f32[16,4096]{1,0:T(8,128)} %get-tuple-element.29) | copy-start | bytes 786436
  13.8 1.9 %copy-start.1 = (f32[16,4096]{1,0:T(8,128)S(1)}, f32[16,4096]{1,0:T(8,128)}, u32[]{:S(2)}) copy-start(f32[16,4096]{1,0:T(8,128)} %get-tuple-element.30) | copy-start | bytes 786436
  15.8 2.1 %collective-permute-start = (f32[16,8448]{1,0:T(8,128)S(1)}, f32[16,8448]{1,0:T(8,128)S(1)}, u32[]{:S(2)}, u32[]{:S(2)}) collective-permute-start(f32[16,8448]{1,0:T(8,128)S(1)} %pad_maximum_fusion), channel_id=1, source_target_pairs={{0,1},{1,0},{2,3},{3,2},{4,5},{5,4},{6,7},{7,6},{8,9},{9,8},{10,11... | collective-permute-start | bytes 1622024 | tf_op jit(solution)/shard_map/ppermute | solution.py:240
  19.7 9.7 %collective-permute-start.1 = (f32[16,4224]{1,0:T(8,128)S(1)}, f32[16,4224]{1,0:T(8,128)S(1)}, u32[]{:S(2)}, u32[]{:S(2)}) collective-permute-start(f32[16,4224]{1,0:T(8,128)S(1)} %fusion.42), channel_id=1, source_target_pairs={{0,2},{1,3},{2,0},{3,1},{4,6},{5,7},{6,4},{7,5},{8,10},{9,11},{10,... | collective-permute-start | bytes 811016 | tf_op jit(solution)/shard_map/ppermute | solution.py:245
  29.4 1.5 %collective-permute-start.2 = (f32[16,4224]{1,0:T(8,128)S(1)}, f32[16,4224]{1,0:T(8,128)S(1)}, u32[]{:S(2)}, u32[]{:S(2)}) collective-permute-start(f32[16,4224]{1,0:T(8,128)S(1)} %collective-permute-done.1), channel_id=1, source_target_pairs={{0,1},{1,0},{2,3},{3,2},{4,5},{5,4},{6,7},{7,6},{8,9},{9,8},{10,11... | collective-permute-start | bytes 811016 | tf_op jit(solution)/shard_map/ppermute | solution.py:254
  32.3 8.6 %collective-permute-start.3 = (f32[16,4224]{1,0:T(8,128)S(1)}, f32[16,4224]{1,0:T(8,128)S(1)}, u32[]{:S(2)}, u32[]{:S(2)}) collective-permute-start(f32[16,4224]{1,0:T(8,128)S(1)} %fusion.40), channel_id=1, source_target_pairs={{0,4},{1,5},{2,6},{3,7},{4,0},{5,1},{6,2},{7,3},{8,12},{9,13},{10,... | collective-permute-start | bytes 811016 | tf_op jit(solution)/shard_map/ppermute | solution.py:245
  40.9 1.5 %collective-permute-start.4 = (f32[16,4224]{1,0:T(8,128)S(1)}, f32[16,4224]{1,0:T(8,128)S(1)}, u32[]{:S(2)}, u32[]{:S(2)}) collective-permute-start(f32[16,4224]{1,0:T(8,128)S(1)} %collective-permute-done.3), channel_id=1, source_target_pairs={{0,1},{1,0},{2,3},{3,2},{4,5},{5,4},{6,7},{7,6},{8,9},{9,8},{10,11... | collective-permute-start | bytes 811016 | tf_op jit(solution)/shard_map/ppermute | solution.py:254
  43.8 15.4 %collective-permute-start.5 = (f32[16,4224]{1,0:T(8,128)S(1)}, f32[16,4224]{1,0:T(8,128)S(1)}, u32[]{:S(2)}, u32[]{:S(2)}) collective-permute-start(f32[16,4224]{1,0:T(8,128)S(1)} %fusion.38), channel_id=1, source_target_pairs={{0,8},{1,9},{2,10},{3,11},{4,12},{5,13},{6,14},{7,15},{8,0},{9,1},... | collective-permute-start | bytes 811016 | tf_op jit(solution)/shard_map/ppermute | solution.py:245
  59.2 1.5 %collective-permute-start.6 = (f32[16,4224]{1,0:T(8,128)S(1)}, f32[16,4224]{1,0:T(8,128)S(1)}, u32[]{:S(2)}, u32[]{:S(2)}) collective-permute-start(f32[16,4224]{1,0:T(8,128)S(1)} %collective-permute-done.5), channel_id=1, source_target_pairs={{0,1},{1,0},{2,3},{3,2},{4,5},{5,4},{6,7},{7,6},{8,9},{9,8},{10,11... | collective-permute-start | bytes 811016 | tf_op jit(solution)/shard_map/ppermute | solution.py:254

commit v17 on v15

--- a/solution.py
+++ b/solution.py
@@ -11,8 +11,28 @@
 LANE = 128
 
 
-def carry_kernel(q_ref, k_ref, v_ref, g_ref, p_ref, xend_ref, head_ref, tot_ref, mix_ref, up_ref):
+def carry_kernel(
+    q_ref, k_ref, v_ref, g_ref, grp_ref, par_ref,
+    xend_ref, head_ref, tot_ref, rate_ref, p_ref, w_ref, mix_ref, up_ref,
+):
     f32 = jnp.float32
+    bf16 = jnp.bfloat16
+    groups = par_ref.shape[1]
+    modes = rate_ref.shape[0]
+    ids = lax.broadcasted_iota(jnp.int32, (groups, grp_ref.shape[1]), 0)
+    member = (ids == grp_ref[...]).astype(bf16)
+    par = par_ref[...]
+    hi = par.astype(bf16)
+    rest = par - hi.astype(f32)
+    mid = rest.astype(bf16)
+    lo = (rest - mid.astype(f32)).astype(bf16)
+    prod = jnp.dot(jnp.concatenate([hi, mid, lo], axis=0), member, preferred_element_type=f32)
+    both = 2 * modes
+    rate = (prod[0:modes] + prod[both : both + modes]) + prod[2 * both : 2 * both + modes]
+    weight = (prod[modes:both] + prod[both + modes : 2 * both]) + prod[2 * both + modes :]
+    rate_ref[...] = rate
+    w_ref[...] = weight
+    p_ref[...] = jnp.exp(-rate)
     mix_ref[...] = (k_ref[...].astype(f32) * v_ref[...].astype(f32)).astype(jnp.bfloat16).astype(f32)
     up_ref[...] = g_ref[...].astype(f32) * q_ref[...].astype(f32)
     rows, width = mix_ref.shape
@@ -121,19 +141,21 @@
         vg_ref[:, cols] = (mg * k_ref[:, cols].astype(f32)).astype(jnp.bfloat16)
 
 
-def local_carries(query_proj, key_proj, value_proj, out_grad, factor):
+def local_carries(query_proj, key_proj, value_proj, out_grad, group_row, params):
     rows, width = query_proj.shape
-    modes = factor.shape[0]
+    modes = params.shape[0] // 2
     big = pl.BlockSpec((rows, BLOCK), lambda i: (0, i))
     small = pl.BlockSpec((modes, BLOCK), lambda i: (0, i))
+    row = pl.BlockSpec((1, BLOCK), lambda i: (0, i))
+    whole = pl.BlockSpec(params.shape, lambda i: (0, 0))
     return pl.pallas_call(
         carry_kernel,
         grid=(width // BLOCK,),
-        in_specs=[big, big, big, big, small],
-        out_specs=[small, small, small],
-        out_shape=[jax.ShapeDtypeStruct((modes, width), jnp.float32)] * 3,
+        in_specs=[big, big, big, big, row, whole],
+        out_specs=[small] * 6,
+        out_shape=[jax.ShapeDtypeStruct((modes, width), jnp.float32)] * 6,
         scratch_shapes=[pltpu.VMEM((rows, BLOCK), jnp.float32)] * 2,
-    )(query_proj, key_proj, value_proj, out_grad, factor)
+    )(query_proj, key_proj, value_proj, out_grad, group_row, params)
 
 
 def local_scans(query_proj, key_proj, value_proj, out_grad, factor, weight, first, previous):
@@ -201,13 +223,9 @@
         member = (group_of[None, :] == jnp.arange(group_count, dtype=jnp.int32)[:, None]).astype(
             jnp.bfloat16
         )
-        modes = decay_rate.shape[1]
-        params = split_dot(jnp.concatenate([decay_rate.T, residue.T], axis=0), member)
-        rate = params[:modes]
-        weight = params[modes:]
-        factor = jnp.exp(-rate)
-        end_state, head_adjoint, local_total = local_carries(
-            query_proj, key_proj, value_proj, out_grad, factor
+        params = jnp.concatenate([decay_rate.T, residue.T], axis=0)
+        end_state, head_adjoint, local_total, rate, factor, weight = local_carries(
+            query_proj, key_proj, value_proj, out_grad, group_of.reshape(1, -1), params
         )
         width = query_proj.shape[1]
         modes = factor.shape[0]

time: 76 us -> 75 us (0.987)
  Pallas kernels: 43.3 us -> 44.9 us
  matrix products: 5.68 us -> 4.1 us
  other arithmetic: 7.8 us -> 6.93 us
    dot_general x6 -> x5, matrix products: 5.68 us -> 4.1 us  [split_dot(): jnp.dot(jnp.concatenate([hi, mid, lo], axis=0), member, preferred_element...]
    pallas_call x1, Pallas kernels: 9.96 us -> 11.5 us  [local_carries(): pl.pallas_call(carry_kernel, grid=(width // BLOCK,), in_specs=[big, big,...]
    convert_element_type x6 -> x5, other arithmetic: 3.87 us -> 2.48 us  [split_dot(): hi = top.astype(bf16)]
    concatenate x0 -> x1, other arithmetic: none -> 1.34 us  [on_device(): params = jnp.concatenate([decay_rate.T, residue.T], axis=0)]
where the time goes in v17:
time: 75 us; the launch traced here: 74.7 us
  Pallas kernels  44.9 us (60%)
  waiting for transfers between devices  8.97 us (12%)
  starting transfers between devices  8.16 us (11%)
  other arithmetic  6.93 us (9%)
  matrix products  4.1 us (5%)
  between operations  1.57 us (2%)
    pallas_call x4, Pallas kernels, local_scans(): pl.pallas_call(local_kernel, grid=(1,), in_specs=specs, out_specs=[big, b...  23.4 us
    pallas_call x1, Pallas kernels, local_carries(): pl.pallas_call(carry_kernel, grid=(width // BLOCK,), in_specs=[big, big,...  11.5 us
    pallas_call x1, Pallas kernels, corrected(): pl.pallas_call(correct_kernel, grid=(width // BLOCK,), in_specs=[big] * 6...  10.1 us
    ppermute x3, starting transfers between devices, on_device(): got_mine = lax.ppermute(mine, 'ctx', pairs)  7.64 us
    ppermute x3, waiting for transfers between devices, on_device(): lax.ppermute(got_mine, 'ctx', [(i, i ^ 1) for i in range(count)])  4.63 us
    dot_general x5, matrix products, split_dot(): jnp.dot(jnp.concatenate([hi, mid, lo], axis=0), member, preferred_element...  4.1 us
    ppermute x3, waiting for transfers between devices, on_device(): got_mine = lax.ppermute(mine, 'ctx', pairs)  2.78 us
    convert_element_type x5, other arithmetic, split_dot(): hi = top.astype(bf16)  2.48 us
  transfers between devices with their start and end apart: 7, of which 7 were waited for; matrix products, arithmetic and copies ran while one was open for 0% of the time, Pallas kernels for 31%

profile of v17, /device:TPU:0, one launch (start us, length us, event | category | flops | bytes accessed | tf_op | source)
XLA Modules:
  0.0 74.7 jit_solution(4432884164381023327)
XLA Ops:
  0.6 1.3 %pad_maximum_fusion.4.par_ref = f32[32,256]{1,0:T(8,128)} fusion(f32[16,256]{1,0:T(8,128)} %bitcast.6, f32[16,256]{1,0:T(8,128)} %bitcast.7), kind=kLoop, calls=%fused_computation.108 | loop fusion | flops 8192 | bytes 65536 | tf_op jit(solution)/shard_map/concatenate | solution.py:226
  2.0 0.0 copy-start.7
  2.0 11.5 %shard_map.110 = (f32[16,4096]{1,0:T(8,128)}, f32[16,4096]{1,0:T(8,128)}, f32[16,4096]{1,0:T(8,128)}, f32[16,4096]{1,0:T(8,128)}, f32[16,4096]{1,0:T(8,128)}, /*index=5*/f32[16,4096]{1,0:T(8,128)}) custom-call(bf16[128,4096]{1,0:T(8,128)(2,1)} %q_ref.11, bf16[128,4096]{1,0:T(8,128)(2,1)} %k_ref.11, bf16[128,4096]{1,0:T(8,128)(2,1)} %v_ref.11, ...), custom_call_target="tpu_custom_call" | custom-call | tf_op jit(solution)/shard_map/pallas_call | solution.py:151
  13.4 0.0 copy-start.5
  13.5 0.0 copy-start.6
  13.5 0.0 copy-start
  13.5 0.0 copy-start.4
  13.5 1.1 %reduce-precision_convert_fusion.9 = (bf16[16,4096]{1,0:T(8,128)(2,1)S(1)}, bf16[16,4096]{1,0:T(8,128)(2,1)S(1)}, bf16[16,4096]{1,0:T(8,128)(2,1)S(1)}) fusion(f32[16,4096]{1,0:T(8,128)} %get-tuple-element.34), kind=kLoop, calls=%fused_computation.65 | loop fusion | flops 458752 | bytes 655360 | tf_op jit(solution)/shard_map/convert_element_type | solution.py:211
  14.6 0.0 copy-done.7
  14.6 0.8 %fusion.4 = f32[48,256]{1,0:T(8,128)S(1)} fusion(s32[4096]{0:T(1024)S(1)} %copy-done.7, bf16[16,4096]{1,0:T(8,128)(2,1)S(1)} %get-tuple-element.91, bf16[16,4096]{1,0:T(8,128)(2,1)S(1)} %get-tuple-element.92, bf16[16,4096]{1,0:T(8,128)(2,1)S(1)} %get-tuple-element.90), kind=kOutput, calls=%fused_computation.5 | convolution fusion | flops 102891520 | bytes 458752 | tf_op jit(solution)/shard_map/dot_general | solution.py:215
  15.4 0.0 copy-done.5
  15.4 0.0 copy-done.6
  15.5 0.5 collective-permute-start
  16.0 1.6 %collective-permute-done = f32[16,8448]{1,0:T(8,128)S(1)} collective-permute-done((f32[16,8448]{1,0:T(8,128)S(1)}, f32[16,8448]{1,0:T(8,128)S(1)}, u32[]{:S(2)}, u32[]{:S(2)}) %collective-permute-start) | collective-permute-done | bytes 540704 | tf_op jit(solution)/shard_map/ppermute | solution.py:258
  17.6 0.0 copy-done
  17.6 0.0 copy-done.4
  17.6 0.1 reduce-precision_convert_fusion.7
  17.8 0.8 %fusion.3 = f32[48,256]{1,0:T(8,128)S(1)} fusion(s32[4096]{0:T(1024)S(1)} %copy-done.7, bf16[16,4096]{1,0:T(8,128)(2,1)S(1)} %get-tuple-element.89, bf16[16,4096]{1,0:T(8,128)(2,1)S(1)} %get-tuple-element.88, bf16[16,4096]{1,0:T(8,128)(2,1)S(1)} %get-tuple-element.69), kind=kOutput, calls=%fused_computation.4 | convolution fusion | flops 102891520 | bytes 458752 | tf_op jit(solution)/shard_map/dot_general | solution.py:215
  18.6 0.1 fusion.40
  18.8 3.0 %collective-permute-start.1 = (f32[16,4224]{1,0:T(8,128)S(1)}, f32[16,4224]{1,0:T(8,128)S(1)}, u32[]{:S(2)}, u32[]{:S(2)}) collective-permute-start(f32[16,4224]{1,0:T(8,128)S(1)} %fusion.40), channel_id=1, source_target_pairs={{0,2},{1,3},{2,0},{3,1},{4,6},{5,7},{6,4},{7,5},{8,10},{9,11},{10,... | collective-permute-start | bytes 811016 | tf_op jit(solution)/shard_map/ppermute | solution.py:263
  21.7 0.0 copy-start.1
  21.7 5.8 %shard_map.111 = (f32[128,4096]{1,0:T(8,128)}, f32[128,4096]{1,0:T(8,128)}) custom-call(bf16[128,4096]{1,0:T(8,128)(2,1)} %q_ref.11, bf16[128,4096]{1,0:T(8,128)(2,1)} %k_ref.11, bf16[128,4096]{1,0:T(8,128)(2,1)} %v_ref.11, bf16[128,4096]{1,0:T(8,128)(2,1)} %g_ref.11, f32[16,4096]{1,0:T(8,128)} %get-tuple-element.36.pw_ref, f32[16,4096]{1,0:T(8,128)} %get-tuple-element.37.rw_ref), custom_call_target="tpu_custom_call" | custom-call | tf_op jit(solution)/shard_map/pallas_call | solution.py:174
  27.6 0.9 %collective-permute-done.1 = f32[16,4224]{1,0:T(8,128)S(1)} collective-permute-done((f32[16,4224]{1,0:T(8,128)S(1)}, f32[16,4224]{1,0:T(8,128)S(1)}, u32[]{:S(2)}, u32[]{:S(2)}) %collective-permute-start.1) | collective-permute-done | bytes 270368 | tf_op jit(solution)/shard_map/ppermute | solution.py:263
  28.5 0.0 collective-permute-start.2
  28.5 1.5 %collective-permute-done.2 = f32[16,4224]{1,0:T(8,128)S(1)} collective-permute-done((f32[16,4224]{1,0:T(8,128)S(1)}, f32[16,4224]{1,0:T(8,128)S(1)}, u32[]{:S(2)}, u32[]{:S(2)}) %collective-permute-start.2) | collective-permute-done | bytes 270368 | tf_op jit(solution)/shard_map/ppermute | solution.py:272
  30.1 0.0 copy-done.1
  30.1 0.1 reduce-precision_convert_fusion.5
  30.2 0.1 reduce-precision_convert_fusion.4
  30.4 0.8 %fusion.2 = f32[48,256]{1,0:T(8,128)S(1)} fusion(s32[4096]{0:T(1024)S(1)} %copy-done.7, bf16[16,4096]{1,0:T(8,128)(2,1)S(1)} %get-tuple-element.87, bf16[16,4096]{1,0:T(8,128)(2,1)S(1)} %get-tuple-element.86, bf16[16,4096]{1,0:T(8,128)(2,1)S(1)} %get-tuple-element.66), kind=kOutput, calls=%fused_computation.3 | convolution fusion | flops 102891520 | bytes 458752 | tf_op jit(solution)/shard_map/dot_general | solution.py:215
  31.2 0.1 fusion.38
  31.4 0.0 copy-start.2
  31.4 1.9 %collective-permute-start.3 = (f32[16,4224]{1,0:T(8,128)S(1)}, f32[16,4224]{1,0:T(8,128)S(1)}, u32[]{:S(2)}, u32[]{:S(2)}) collective-permute-start(f32[16,4224]{1,0:T(8,128)S(1)} %fusion.38), channel_id=1, source_target_pairs={{0,4},{1,5},{2,6},{3,7},{4,0},{5,1},{6,2},{7,3},{8,12},{9,13},{10,... | collective-permute-start | bytes 811016 | tf_op jit(solution)/shard_map/ppermute | solution.py:263
  33.2 5.8 %shard_map.112 = (f32[128,4096]{1,0:T(8,128)}, f32[128,4096]{1,0:T(8,128)}) custom-call(bf16[128,4096]{1,0:T(8,128)(2,1)} %q_ref.11, bf16[128,4096]{1,0:T(8,128)(2,1)} %k_ref.11, bf16[128,4096]{1,0:T(8,128)(2,1)} %v_ref.11, bf16[128,4096]{1,0:T(8,128)(2,1)} %g_ref.11, ...), custom_call_target="tpu_custom_call", output_to_operand_aliasing={{0}: (6, {}), {1}: (7, {})} | custom-call | tf_op jit(solution)/shard_map/pallas_call | solution.py:174
  39.0 1.0 %collective-permute-done.3 = f32[16,4224]{1,0:T(8,128)S(1)} collective-permute-done((f32[16,4224]{1,0:T(8,128)S(1)}, f32[16,4224]{1,0:T(8,128)S(1)}, u32[]{:S(2)}, u32[]{:S(2)}) %collective-permute-start.3) | collective-permute-done | bytes 270368 | tf_op jit(solution)/shard_map/ppermute | solution.py:263
  40.0 0.0 collective-permute-start.4
  40.0 1.5 %collective-permute-done.4 = f32[16,4224]{1,0:T(8,128)S(1)} collective-permute-done((f32[16,4224]{1,0:T(8,128)S(1)}, f32[16,4224]{1,0:T(8,128)S(1)}, u32[]{:S(2)}, u32[]{:S(2)}) %collective-permute-start.4) | collective-permute-done | bytes 270368 | tf_op jit(solution)/shard_map/ppermute | solution.py:272
  41.6 0.0 copy-done.2
  41.6 0.1 reduce-precision_convert_fusion.3
  41.8 0.8 %fusion.1 = f32[48,256]{1,0:T(8,128)S(1)} fusion(s32[4096]{0:T(1024)S(1)} %copy-done.7, bf16[16,4096]{1,0:T(8,128)(2,1)S(1)} %get-tuple-element.85, bf16[16,4096]{1,0:T(8,128)(2,1)S(1)} %get-tuple-element.84, bf16[16,4096]{1,0:T(8,128)(2,1)S(1)} %get-tuple-element.63), kind=kOutput, calls=%fused_computation.2 | convolution fusion | flops 102891520 | bytes 458752 | tf_op jit(solution)/shard_map/dot_general | solution.py:215
  42.6 0.1 multiply_add_fusion
  42.7 0.1 fusion.36
  42.9 2.8 %collective-permute-start.5 = (f32[16,4224]{1,0:T(8,128)S(1)}, f32[16,4224]{1,0:T(8,128)S(1)}, u32[]{:S(2)}, u32[]{:S(2)}) collective-permute-start(f32[16,4224]{1,0:T(8,128)S(1)} %fusion.36), channel_id=1, source_target_pairs={{0,8},{1,9},{2,10},{3,11},{4,12},{5,13},{6,14},{7,15},{8,0},{9,1},... | collective-permute-start | bytes 811016 | tf_op jit(solution)/shard_map/ppermute | solution.py:263
  45.7 5.9 %shard_map.113 = (f32[128,4096]{1,0:T(8,128)}, f32[128,4096]{1,0:T(8,128)}) custom-call(bf16[128,4096]{1,0:T(8,128)(2,1)} %q_ref.11, bf16[128,4096]{1,0:T(8,128)(2,1)} %k_ref.11, bf16[128,4096]{1,0:T(8,128)(2,1)} %v_ref.11, bf16[128,4096]{1,0:T(8,128)(2,1)} %g_ref.11, ...), custom_call_target="tpu_custom_call", output_to_operand_aliasing={{0}: (6, {}), {1}: (7, {})} | custom-call | tf_op jit(solution)/shard_map/pallas_call | solution.py:174
  51.6 0.0 copy-start.3
  51.6 5.8 %shard_map.114 = (f32[128,4096]{1,0:T(8,128)}, f32[128,4096]{1,0:T(8,128)}) custom-call(bf16[128,4096]{1,0:T(8,128)(2,1)} %q_ref.11, bf16[128,4096]{1,0:T(8,128)(2,1)} %k_ref.11, bf16[128,4096]{1,0:T(8,128)(2,1)} %v_ref.11, bf16[128,4096]{1,0:T(8,128)(2,1)} %g_ref.11, ...), custom_call_target="tpu_custom_call", output_to_operand_aliasing={{0}: (6, {}), {1}: (7, {})} | custom-call | tf_op jit(solution)/shard_map/pallas_call | solution.py:174
  57.4 0.9 %collective-permute-done.5 = f32[16,4224]{1,0:T(8,128)S(1)} collective-permute-done((f32[16,4224]{1,0:T(8,128)S(1)}, f32[16,4224]{1,0:T(8,128)S(1)}, u32[]{:S(2)}, u32[]{:S(2)}) %collective-permute-start.5) | collective-permute-done | bytes 270368 | tf_op jit(solution)/shard_map/ppermute | solution.py:263
  58.3 0.0 collective-permute-start.6
  58.3 1.5 %collective-permute-done.6 = f32[16,4224]{1,0:T(8,128)S(1)} collective-permute-done((f32[16,4224]{1,0:T(8,128)S(1)}, f32[16,4224]{1,0:T(8,128)S(1)}, u32[]{:S(2)}, u32[]{:S(2)}) %collective-permute-start.6) | collective-permute-done | bytes 270368 | tf_op jit(solution)/shard_map/ppermute | solution.py:272
  59.9 0.0 copy-done.3
  59.9 1.0 %reduce-precision_convert_fusion.1 = (bf16[16,4096]{1,0:T(8,128)(2,1)S(1)}, f32[16,4096]{1,0:T(8,128)S(1)}, f32[16,4096]{1,0:T(8,128)}) fusion(f32[16,4096]{1,0:T(8,128)S(1)} %multiply_add_fusion, f32[16,4224]{1,0:T(8,128)S(1)} %get-tuple-element.74, f32[16,4224]{1,0:T(8,128)S(1)} %get-tuple-element.75, f32[16,4096]{1,0:T(8,128)S(1)} %copy-done.3, ...), kind=kLoop, calls=%fused_computation.49 | loop fusion | flops 1507328 | bytes 3293200 | tf_op jit(solution)/shard_map/convert_element_type | solution.py:211
  60.9 0.8 %fusion = f32[48,256]{1,0:T(8,128)S(1)} fusion(s32[4096]{0:T(1024)S(1)} %copy-done.7, bf16[16,4096]{1,0:T(8,128)(2,1)S(1)} %get-tuple-element.83, bf16[16,4096]{1,0:T(8,128)(2,1)S(1)} %get-tuple-element.82, bf16[16,4096]{1,0:T(8,128)(2,1)S(1)} %get-tuple-element.61), kind=kOutput, calls=%fused_computation.1 | convolution fusion | flops 102891520 | bytes 458752 | tf_op jit(solution)/shard_map/dot_general | solution.py:215
  61.8 0.6 multiply_reduce_fusion
  63.1 0.6 divide_bitcast_fusion
  63.7 0.9 %select_add_fusion.1.sw_ref = f32[16,4096]{1,0:T(8,128)} fusion(f32[16,4224]{1,0:T(8,128)S(1)} %get-tuple-element.75, f32[16,4224]{1,0:T(8,128)S(1)} %get-tuple-element.77, f32[16,4224]{1,0:T(8,128)S(1)} %get-tuple-element.79, f32[16,8448]{1,0:T(8,128)S(1)} %collective-permute-done, f32[16,4096]{1,0:T(8,128)S(1)} %copy-done.4, f32[]{:T(128)S(6)} %mul.187, ...), kind=kLoop, calls=%fused_computation.82 | loop fusion | flops 1048576 | bytes 1572880 | tf_op jit(solution)/shard_map/add | solution.py:287
  64.6 10.1 %shard_map.115 = (bf16[128,4096]{1,0:T(8,128)(2,1)}, bf16[128,4096]{1,0:T(8,128)(2,1)}, bf16[128,4096]{1,0:T(8,128)(2,1)}, bf16[128,4096]{1,0:T(8,128)(2,1)}) custom-call(bf16[128,4096]{1,0:T(8,128)(2,1)} %q_ref.11, bf16[128,4096]{1,0:T(8,128)(2,1)} %k_ref.11, bf16[128,4096]{1,0:T(8,128)(2,1)} %v_ref.11, bf16[128,4096]{1,0:T(8,128)(2,1)} %g_ref.11, ...), custom_call_target="tpu_custom_call" | custom-call | tf_op jit(solution)/shard_map/pallas_call | solution.py:194
  (11 shorter events, 0.3 us)
Async XLA Ops:
  2.0 12.6 %copy-start.7 = (s32[4096]{0:T(1024)S(1)}, s32[4096]{0:T(1024)}, u32[]{:S(2)}) copy-start(s32[4096]{0:T(1024)} %param.13) | copy-start | bytes 49156
  13.4 2.0 %copy-start.5 = (f32[16,4096]{1,0:T(8,128)S(1)}, f32[16,4096]{1,0:T(8,128)}, u32[]{:S(2)}) copy-start(f32[16,4096]{1,0:T(8,128)} %get-tuple-element.32) | copy-start | bytes 786436
  13.5 2.0 %copy-start.6 = (f32[16,4096]{1,0:T(8,128)S(1)}, f32[16,4096]{1,0:T(8,128)}, u32[]{:S(2)}) copy-start(f32[16,4096]{1,0:T(8,128)} %get-tuple-element.33) | copy-start | bytes 786436
  13.5 4.1 %copy-start = (f32[16,4096]{1,0:T(8,128)S(1)}, f32[16,4096]{1,0:T(8,128)}, u32[]{:S(2)}) copy-start(f32[16,4096]{1,0:T(8,128)} %get-tuple-element.36.pw_ref) | copy-start | bytes 786436
  13.5 4.1 %copy-start.4 = (f32[16,4096]{1,0:T(8,128)S(1)}, f32[16,4096]{1,0:T(8,128)}, u32[]{:S(2)}) copy-start(f32[16,4096]{1,0:T(8,128)} %get-tuple-element.35) | copy-start | bytes 786436
  15.5 2.1 %collective-permute-start = (f32[16,8448]{1,0:T(8,128)S(1)}, f32[16,8448]{1,0:T(8,128)S(1)}, u32[]{:S(2)}, u32[]{:S(2)}) collective-permute-start(f32[16,8448]{1,0:T(8,128)S(1)} %pad_maximum_fusion), channel_id=1, source_target_pairs={{0,1},{1,0},{2,3},{3,2},{4,5},{5,4},{6,7},{7,6},{8,9},{9,8},{10,11... | collective-permute-start | bytes 1622024 | tf_op jit(solution)/shard_map/ppermute | solution.py:258
  18.8 9.7 %collective-permute-start.1 = (f32[16,4224]{1,0:T(8,128)S(1)}, f32[16,4224]{1,0:T(8,128)S(1)}, u32[]{:S(2)}, u32[]{:S(2)}) collective-permute-start(f32[16,4224]{1,0:T(8,128)S(1)} %fusion.40), channel_id=1, source_target_pairs={{0,2},{1,3},{2,0},{3,1},{4,6},{5,7},{6,4},{7,5},{8,10},{9,11},{10,... | collective-permute-start | bytes 811016 | tf_op jit(solution)/shard_map/ppermute | solution.py:263
  21.7 8.4 %copy-start.1 = (f32[16,4096]{1,0:T(8,128)S(1)}, f32[16,4096]{1,0:T(8,128)}, u32[]{:S(2)}) copy-start(f32[16,4096]{1,0:T(8,128)} %get-tuple-element.36.pw_ref) | copy-start | bytes 786436
  28.5 1.5 %collective-permute-start.2 = (f32[16,4224]{1,0:T(8,128)S(1)}, f32[16,4224]{1,0:T(8,128)S(1)}, u32[]{:S(2)}, u32[]{:S(2)}) collective-permute-start(f32[16,4224]{1,0:T(8,128)S(1)} %collective-permute-done.1), channel_id=1, source_target_pairs={{0,1},{1,0},{2,3},{3,2},{4,5},{5,4},{6,7},{7,6},{8,9},{9,8},{10,11... | collective-permute-start | bytes 811016 | tf_op jit(solution)/shard_map/ppermute | solution.py:272
  31.4 10.2 %copy-start.2 = (f32[16,4096]{1,0:T(8,128)S(1)}, f32[16,4096]{1,0:T(8,128)}, u32[]{:S(2)}) copy-start(f32[16,4096]{1,0:T(8,128)} %get-tuple-element.36.pw_ref) | copy-start | bytes 786436
  31.4 8.6 %collective-permute-start.3 = (f32[16,4224]{1,0:T(8,128)S(1)}, f32[16,4224]{1,0:T(8,128)S(1)}, u32[]{:S(2)}, u32[]{:S(2)}) collective-permute-start(f32[16,4224]{1,0:T(8,128)S(1)} %fusion.38), channel_id=1, source_target_pairs={{0,4},{1,5},{2,6},{3,7},{4,0},{5,1},{6,2},{7,3},{8,12},{9,13},{10,... | collective-permute-start | bytes 811016 | tf_op jit(solution)/shard_map/ppermute | solution.py:263
  40.0 1.5 %collective-permute-start.4 = (f32[16,4224]{1,0:T(8,128)S(1)}, f32[16,4224]{1,0:T(8,128)S(1)}, u32[]{:S(2)}, u32[]{:S(2)}) collective-permute-start(f32[16,4224]{1,0:T(8,128)S(1)} %collective-permute-done.3), channel_id=1, source_target_pairs={{0,1},{1,0},{2,3},{3,2},{4,5},{5,4},{6,7},{7,6},{8,9},{9,8},{10,11... | collective-permute-start | bytes 811016 | tf_op jit(solution)/shard_map/ppermute | solution.py:272
  42.9 15.4 %collective-permute-start.5 = (f32[16,4224]{1,0:T(8,128)S(1)}, f32[16,4224]{1,0:T(8,128)S(1)}, u32[]{:S(2)}, u32[]{:S(2)}) collective-permute-start(f32[16,4224]{1,0:T(8,128)S(1)} %fusion.36), channel_id=1, source_target_pairs={{0,8},{1,9},{2,10},{3,11},{4,12},{5,13},{6,14},{7,15},{8,0},{9,1},... | collective-permute-start | bytes 811016 | tf_op jit(solution)/shard_map/ppermute | solution.py:263
  51.6 8.3 %copy-start.3 = (f32[16,4096]{1,0:T(8,128)S(1)}, f32[16,4096]{1,0:T(8,128)}, u32[]{:S(2)}) copy-start(f32[16,4096]{1,0:T(8,128)} %get-tuple-element.36.pw_ref) | copy-start | bytes 786436
  58.3 1.5 %collective-permute-start.6 = (f32[16,4224]{1,0:T(8,128)S(1)}, f32[16,4224]{1,0:T(8,128)S(1)}, u32[]{:S(2)}, u32[]{:S(2)}) collective-permute-start(f32[16,4224]{1,0:T(8,128)S(1)} %collective-permute-done.5), channel_id=1, source_target_pairs={{0,1},{1,0},{2,3},{3,2},{4,5},{5,4},{6,7},{7,6},{8,9},{9,8},{10,11... | collective-permute-start | bytes 811016 | tf_op jit(solution)/shard_map/ppermute | solution.py:272

commit v18 on v17

--- a/solution.py
+++ b/solution.py
@@ -11,25 +11,32 @@
 LANE = 128
 
 
+def gathered(par, member):
+    f32 = jnp.float32
+    bf16 = jnp.bfloat16
+    hi = par.astype(bf16)
+    rest = par - hi.astype(f32)
+    mid = rest.astype(bf16)
+    lo = (rest - mid.astype(f32)).astype(bf16)
+    dims = (((0,), (0,)), ((), ()))
+
+    def one(piece):
+        return lax.dot_general(piece, member, dims, preferred_element_type=f32)
+
+    return (one(hi) + one(mid)) + one(lo)
+
+
 def carry_kernel(
-    q_ref, k_ref, v_ref, g_ref, grp_ref, par_ref,
+    q_ref, k_ref, v_ref, g_ref, grp_ref, dr_ref, rs_ref,
     xend_ref, head_ref, tot_ref, rate_ref, p_ref, w_ref, mix_ref, up_ref,
 ):
     f32 = jnp.float32
     bf16 = jnp.bfloat16
-    groups = par_ref.shape[1]
-    modes = rate_ref.shape[0]
+    groups = dr_ref.shape[0]
     ids = lax.broadcasted_iota(jnp.int32, (groups, grp_ref.shape[1]), 0)
     member = (ids == grp_ref[...]).astype(bf16)
-    par = par_ref[...]
-    hi = par.astype(bf16)
-    rest = par - hi.astype(f32)
-    mid = rest.astype(bf16)
-    lo = (rest - mid.astype(f32)).astype(bf16)
-    prod = jnp.dot(jnp.concatenate([hi, mid, lo], axis=0), member, preferred_element_type=f32)
-    both = 2 * modes
-    rate = (prod[0:modes] + prod[both : both + modes]) + prod[2 * both : 2 * both + modes]
-    weight = (prod[modes:both] + prod[both + modes : 2 * both]) + prod[2 * both + modes :]
+    rate = gathered(dr_ref[...], member)
+    weight = gathered(rs_ref[...], member)
     rate_ref[...] = rate
     w_ref[...] = weight
     p_ref[...] = jnp.exp(-rate)
@@ -141,21 +148,21 @@
         vg_ref[:, cols] = (mg * k_ref[:, cols].astype(f32)).astype(jnp.bfloat16)
 
 
-def local_carries(query_proj, key_proj, value_proj, out_grad, group_row, params):
+def local_carries(query_proj, key_proj, value_proj, out_grad, group_row, decay_rate, residue):
     rows, width = query_proj.shape
-    modes = params.shape[0] // 2
+    modes = decay_rate.shape[1]
     big = pl.BlockSpec((rows, BLOCK), lambda i: (0, i))
     small = pl.BlockSpec((modes, BLOCK), lambda i: (0, i))
     row = pl.BlockSpec((1, BLOCK), lambda i: (0, i))
-    whole = pl.BlockSpec(params.shape, lambda i: (0, 0))
+    whole = pl.BlockSpec(decay_rate.shape, lambda i: (0, 0))
     return pl.pallas_call(
         carry_kernel,
         grid=(width // BLOCK,),
-        in_specs=[big, big, big, big, row, whole],
+        in_specs=[big, big, big, big, row, whole, whole],
         out_specs=[small] * 6,
         out_shape=[jax.ShapeDtypeStruct((modes, width), jnp.float32)] * 6,
         scratch_shapes=[pltpu.VMEM((rows, BLOCK), jnp.float32)] * 2,
-    )(query_proj, key_proj, value_proj, out_grad, group_row, params)
+    )(query_proj, key_proj, value_proj, out_grad, group_row, decay_rate, residue)
 
 
 def local_scans(query_proj, key_proj, value_proj, out_grad, factor, weight, first, previous):
@@ -223,9 +230,8 @@
         member = (group_of[None, :] == jnp.arange(group_count, dtype=jnp.int32)[:, None]).astype(
             jnp.bfloat16
         )
-        params = jnp.concatenate([decay_rate.T, residue.T], axis=0)
         end_state, head_adjoint, local_total, rate, factor, weight = local_carries(
-            query_proj, key_proj, value_proj, out_grad, group_of.reshape(1, -1), params
+            query_proj, key_proj, value_proj, out_grad, group_of.reshape(1, -1), decay_rate, residue
         )
         width = query_proj.shape[1]
         modes = factor.shape[0]

time: 75 us -> 78.2 us (1.043)
  local copies, waits for them, and re-layouts: 0.04 us -> 2.96 us
  Pallas kernels: 44.9 us -> 46.4 us
  other arithmetic: 6.93 us -> 5.59 us
    unnamed x16 -> x18, local copies, waits for them, and re-layouts: 0.04 us -> 2.96 us
    pallas_call x1, Pallas kernels: 11.5 us -> 13 us  [local_carries(): pl.pallas_call(carry_kernel, grid=(width // BLOCK,), in_specs=[big, big,...]
    concatenate x1 -> x0, other arithmetic: 1.34 us -> none  [on_device(): params = jnp.concatenate([decay_rate.T, residue.T], axis=0)]
  transfers between devices with their start and end apart: 7 -> 7, of which waited for: 7 -> 7; matrix products, arithmetic and copies ran while one was open for 0% -> 0% of each run, Pallas kernels for 31% -> 30%
where the time goes in v18:
time: 78.2 us; the launch traced here: 77.8 us
  Pallas kernels  46.4 us (59%)
  waiting for transfers between devices  8.97 us (11%)
  starting transfers between devices  8.16 us (10%)
  other arithmetic  5.59 us (7%)
  matrix products  4.1 us (5%)
  local copies, waits for them, and re-layouts  2.96 us (4%)
  between operations  1.57 us (2%)
    pallas_call x4, Pallas kernels, local_scans(): pl.pallas_call(local_kernel, grid=(1,), in_specs=specs, out_specs=[big, b...  23.4 us
    pallas_call x1, Pallas kernels, local_carries(): pl.pallas_call(carry_kernel, grid=(width // BLOCK,), in_specs=[big, big,...  13 us
    pallas_call x1, Pallas kernels, corrected(): pl.pallas_call(correct_kernel, grid=(width // BLOCK,), in_specs=[big] * 6...  10.1 us
    ppermute x3, starting transfers between devices, on_device(): got_mine = lax.ppermute(mine, 'ctx', pairs)  7.63 us
    ppermute x3, waiting for transfers between devices, on_device(): lax.ppermute(got_mine, 'ctx', [(i, i ^ 1) for i in range(count)])  4.63 us
    dot_general x5, matrix products, split_dot(): jnp.dot(jnp.concatenate([hi, mid, lo], axis=0), member, preferred_element...  4.1 us
    unnamed x18, local copies, waits for them, and re-layouts  2.96 us
    ppermute x3, waiting for transfers between devices, on_device(): got_mine = lax.ppermute(mine, 'ctx', pairs)  2.78 us
  transfers between devices with their start and end apart: 7, of which 7 were waited for; matrix products, arithmetic and copies ran while one was open for 0% of the time, Pallas kernels for 30%

profile of v18, /device:TPU:0, one launch (start us, length us, event | category | flops | bytes accessed | tf_op | source)
XLA Modules:
  0.0 77.8 jit_solution(16781657687455080182)
XLA Ops:
  0.6 1.5 %copy.18.dr_ref = f32[256,16]{1,0:T(8,128)} copy(f32[256,16]{0,1:T(8,128)} %param.11) | data formatting | bytes 32768 | tf_op args[4]
  2.1 1.5 %copy.19.rs_ref = f32[256,16]{1,0:T(8,128)} copy(f32[256,16]{0,1:T(8,128)} %param.12) | data formatting | bytes 32768 | tf_op args[5]
  3.6 0.0 copy-start.7
  3.6 13.0 %shard_map.110 = (f32[16,4096]{1,0:T(8,128)}, f32[16,4096]{1,0:T(8,128)}, f32[16,4096]{1,0:T(8,128)}, f32[16,4096]{1,0:T(8,128)}, f32[16,4096]{1,0:T(8,128)}, /*index=5*/f32[16,4096]{1,0:T(8,128)}) custom-call(bf16[128,4096]{1,0:T(8,128)(2,1)} %q_ref.11, bf16[128,4096]{1,0:T(8,128)(2,1)} %k_ref.11, bf16[128,4096]{1,0:T(8,128)(2,1)} %v_ref.11, ...), custom_call_target="tpu_custom_call" | custom-call | tf_op jit(solution)/shard_map/pallas_call | solution.py:158
  16.5 0.0 copy-start.5
  16.6 0.0 copy-start.6
  16.6 0.0 copy-start
  16.6 0.0 copy-start.4
  16.6 1.1 %reduce-precision_convert_fusion.9 = (bf16[16,4096]{1,0:T(8,128)(2,1)S(1)}, bf16[16,4096]{1,0:T(8,128)(2,1)S(1)}, bf16[16,4096]{1,0:T(8,128)(2,1)S(1)}) fusion(f32[16,4096]{1,0:T(8,128)} %get-tuple-element.34), kind=kLoop, calls=%fused_computation.65 | loop fusion | flops 458752 | bytes 655360 | tf_op jit(solution)/shard_map/convert_element_type | solution.py:218
  17.7 0.0 copy-done.7
  17.7 0.8 %fusion.4 = f32[48,256]{1,0:T(8,128)S(1)} fusion(s32[4096]{0:T(1024)S(1)} %copy-done.7, bf16[16,4096]{1,0:T(8,128)(2,1)S(1)} %get-tuple-element.91, bf16[16,4096]{1,0:T(8,128)(2,1)S(1)} %get-tuple-element.92, bf16[16,4096]{1,0:T(8,128)(2,1)S(1)} %get-tuple-element.90), kind=kOutput, calls=%fused_computation.5 | convolution fusion | flops 102891520 | bytes 458752 | tf_op jit(solution)/shard_map/dot_general | solution.py:222
  18.5 0.0 copy-done.5
  18.5 0.0 copy-done.6
  18.6 0.5 collective-permute-start
  19.1 1.6 %collective-permute-done = f32[16,8448]{1,0:T(8,128)S(1)} collective-permute-done((f32[16,8448]{1,0:T(8,128)S(1)}, f32[16,8448]{1,0:T(8,128)S(1)}, u32[]{:S(2)}, u32[]{:S(2)}) %collective-permute-start) | collective-permute-done | bytes 540704 | tf_op jit(solution)/shard_map/ppermute | solution.py:264
  20.7 0.0 copy-done
  20.7 0.0 copy-done.4
  20.7 0.1 reduce-precision_convert_fusion.7
  20.9 0.8 %fusion.3 = f32[48,256]{1,0:T(8,128)S(1)} fusion(s32[4096]{0:T(1024)S(1)} %copy-done.7, bf16[16,4096]{1,0:T(8,128)(2,1)S(1)} %get-tuple-element.89, bf16[16,4096]{1,0:T(8,128)(2,1)S(1)} %get-tuple-element.88, bf16[16,4096]{1,0:T(8,128)(2,1)S(1)} %get-tuple-element.69), kind=kOutput, calls=%fused_computation.4 | convolution fusion | flops 102891520 | bytes 458752 | tf_op jit(solution)/shard_map/dot_general | solution.py:222
  21.7 0.1 fusion.40
  21.9 3.0 %collective-permute-start.1 = (f32[16,4224]{1,0:T(8,128)S(1)}, f32[16,4224]{1,0:T(8,128)S(1)}, u32[]{:S(2)}, u32[]{:S(2)}) collective-permute-start(f32[16,4224]{1,0:T(8,128)S(1)} %fusion.40), channel_id=1, source_target_pairs={{0,2},{1,3},{2,0},{3,1},{4,6},{5,7},{6,4},{7,5},{8,10},{9,11},{10,... | collective-permute-start | bytes 811016 | tf_op jit(solution)/shard_map/ppermute | solution.py:269
  24.8 0.0 copy-start.1
  24.8 5.8 %shard_map.111 = (f32[128,4096]{1,0:T(8,128)}, f32[128,4096]{1,0:T(8,128)}) custom-call(bf16[128,4096]{1,0:T(8,128)(2,1)} %q_ref.11, bf16[128,4096]{1,0:T(8,128)(2,1)} %k_ref.11, bf16[128,4096]{1,0:T(8,128)(2,1)} %v_ref.11, bf16[128,4096]{1,0:T(8,128)(2,1)} %g_ref.11, f32[16,4096]{1,0:T(8,128)} %get-tuple-element.36.pw_ref, f32[16,4096]{1,0:T(8,128)} %get-tuple-element.37.rw_ref), custom_call_target="tpu_custom_call" | custom-call | tf_op jit(solution)/shard_map/pallas_call | solution.py:181
  30.7 0.9 %collective-permute-done.1 = f32[16,4224]{1,0:T(8,128)S(1)} collective-permute-done((f32[16,4224]{1,0:T(8,128)S(1)}, f32[16,4224]{1,0:T(8,128)S(1)}, u32[]{:S(2)}, u32[]{:S(2)}) %collective-permute-start.1) | collective-permute-done | bytes 270368 | tf_op jit(solution)/shard_map/ppermute | solution.py:269
  31.6 0.0 collective-permute-start.2
  31.6 1.5 %collective-permute-done.2 = f32[16,4224]{1,0:T(8,128)S(1)} collective-permute-done((f32[16,4224]{1,0:T(8,128)S(1)}, f32[16,4224]{1,0:T(8,128)S(1)}, u32[]{:S(2)}, u32[]{:S(2)}) %collective-permute-start.2) | collective-permute-done | bytes 270368 | tf_op jit(solution)/shard_map/ppermute | solution.py:278
  33.2 0.0 copy-done.1
  33.2 0.1 reduce-precision_convert_fusion.5
  33.3 0.1 reduce-precision_convert_fusion.4
  33.5 0.8 %fusion.2 = f32[48,256]{1,0:T(8,128)S(1)} fusion(s32[4096]{0:T(1024)S(1)} %copy-done.7, bf16[16,4096]{1,0:T(8,128)(2,1)S(1)} %get-tuple-element.87, bf16[16,4096]{1,0:T(8,128)(2,1)S(1)} %get-tuple-element.86, bf16[16,4096]{1,0:T(8,128)(2,1)S(1)} %get-tuple-element.66), kind=kOutput, calls=%fused_computation.3 | convolution fusion | flops 102891520 | bytes 458752 | tf_op jit(solution)/shard_map/dot_general | solution.py:222
  34.3 0.1 fusion.38
  34.5 0.0 copy-start.2
  34.5 1.9 %collective-permute-start.3 = (f32[16,4224]{1,0:T(8,128)S(1)}, f32[16,4224]{1,0:T(8,128)S(1)}, u32[]{:S(2)}, u32[]{:S(2)}) collective-permute-start(f32[16,4224]{1,0:T(8,128)S(1)} %fusion.38), channel_id=1, source_target_pairs={{0,4},{1,5},{2,6},{3,7},{4,0},{5,1},{6,2},{7,3},{8,12},{9,13},{10,... | collective-permute-start | bytes 811016 | tf_op jit(solution)/shard_map/ppermute | solution.py:269
  36.3 5.8 %shard_map.112 = (f32[128,4096]{1,0:T(8,128)}, f32[128,4096]{1,0:T(8,128)}) custom-call(bf16[128,4096]{1,0:T(8,128)(2,1)} %q_ref.11, bf16[128,4096]{1,0:T(8,128)(2,1)} %k_ref.11, bf16[128,4096]{1,0:T(8,128)(2,1)} %v_ref.11, bf16[128,4096]{1,0:T(8,128)(2,1)} %g_ref.11, ...), custom_call_target="tpu_custom_call", output_to_operand_aliasing={{0}: (6, {}), {1}: (7, {})} | custom-call | tf_op jit(solution)/shard_map/pallas_call | solution.py:181
  42.1 1.0 %collective-permute-done.3 = f32[16,4224]{1,0:T(8,128)S(1)} collective-permute-done((f32[16,4224]{1,0:T(8,128)S(1)}, f32[16,4224]{1,0:T(8,128)S(1)}, u32[]{:S(2)}, u32[]{:S(2)}) %collective-permute-start.3) | collective-permute-done | bytes 270368 | tf_op jit(solution)/shard_map/ppermute | solution.py:269
  43.1 0.0 collective-permute-start.4
  43.1 1.5 %collective-permute-done.4 = f32[16,4224]{1,0:T(8,128)S(1)} collective-permute-done((f32[16,4224]{1,0:T(8,128)S(1)}, f32[16,4224]{1,0:T(8,128)S(1)}, u32[]{:S(2)}, u32[]{:S(2)}) %collective-permute-start.4) | collective-permute-done | bytes 270368 | tf_op jit(solution)/shard_map/ppermute | solution.py:278
  44.7 0.0 copy-done.2
  44.7 0.1 reduce-precision_convert_fusion.3
  44.9 0.8 %fusion.1 = f32[48,256]{1,0:T(8,128)S(1)} fusion(s32[4096]{0:T(1024)S(1)} %copy-done.7, bf16[16,4096]{1,0:T(8,128)(2,1)S(1)} %get-tuple-element.85, bf16[16,4096]{1,0:T(8,128)(2,1)S(1)} %get-tuple-element.84, bf16[16,4096]{1,0:T(8,128)(2,1)S(1)} %get-tuple-element.63), kind=kOutput, calls=%fused_computation.2 | convolution fusion | flops 102891520 | bytes 458752 | tf_op jit(solution)/shard_map/dot_general | solution.py:222
  45.7 0.1 multiply_add_fusion
  45.8 0.1 fusion.36
  46.0 2.8 %collective-permute-start.5 = (f32[16,4224]{1,0:T(8,128)S(1)}, f32[16,4224]{1,0:T(8,128)S(1)}, u32[]{:S(2)}, u32[]{:S(2)}) collective-permute-start(f32[16,4224]{1,0:T(8,128)S(1)} %fusion.36), channel_id=1, source_target_pairs={{0,8},{1,9},{2,10},{3,11},{4,12},{5,13},{6,14},{7,15},{8,0},{9,1},... | collective-permute-start | bytes 811016 | tf_op jit(solution)/shard_map/ppermute | solution.py:269
  48.8 5.9 %shard_map.113 = (f32[128,4096]{1,0:T(8,128)}, f32[128,4096]{1,0:T(8,128)}) custom-call(bf16[128,4096]{1,0:T(8,128)(2,1)} %q_ref.11, bf16[128,4096]{1,0:T(8,128)(2,1)} %k_ref.11, bf16[128,4096]{1,0:T(8,128)(2,1)} %v_ref.11, bf16[128,4096]{1,0:T(8,128)(2,1)} %g_ref.11, ...), custom_call_target="tpu_custom_call", output_to_operand_aliasing={{0}: (6, {}), {1}: (7, {})} | custom-call | tf_op jit(solution)/shard_map/pallas_call | solution.py:181
  54.7 0.0 copy-start.3
  54.7 5.8 %shard_map.114 = (f32[128,4096]{1,0:T(8,128)}, f32[128,4096]{1,0:T(8,128)}) custom-call(bf16[128,4096]{1,0:T(8,128)(2,1)} %q_ref.11, bf16[128,4096]{1,0:T(8,128)(2,1)} %k_ref.11, bf16[128,4096]{1,0:T(8,128)(2,1)} %v_ref.11, bf16[128,4096]{1,0:T(8,128)(2,1)} %g_ref.11, ...), custom_call_target="tpu_custom_call", output_to_operand_aliasing={{0}: (6, {}), {1}: (7, {})} | custom-call | tf_op jit(solution)/shard_map/pallas_call | solution.py:181
  60.5 0.9 %collective-permute-done.5 = f32[16,4224]{1,0:T(8,128)S(1)} collective-permute-done((f32[16,4224]{1,0:T(8,128)S(1)}, f32[16,4224]{1,0:T(8,128)S(1)}, u32[]{:S(2)}, u32[]{:S(2)}) %collective-permute-start.5) | collective-permute-done | bytes 270368 | tf_op jit(solution)/shard_map/ppermute | solution.py:269
  61.4 0.0 collective-permute-start.6
  61.4 1.5 %collective-permute-done.6 = f32[16,4224]{1,0:T(8,128)S(1)} collective-permute-done((f32[16,4224]{1,0:T(8,128)S(1)}, f32[16,4224]{1,0:T(8,128)S(1)}, u32[]{:S(2)}, u32[]{:S(2)}) %collective-permute-start.6) | collective-permute-done | bytes 270368 | tf_op jit(solution)/shard_map/ppermute | solution.py:278
  63.0 0.0 copy-done.3
  63.0 1.0 %reduce-precision_convert_fusion.1 = (bf16[16,4096]{1,0:T(8,128)(2,1)S(1)}, f32[16,4096]{1,0:T(8,128)S(1)}, f32[16,4096]{1,0:T(8,128)}) fusion(f32[16,4096]{1,0:T(8,128)S(1)} %multiply_add_fusion, f32[16,4224]{1,0:T(8,128)S(1)} %get-tuple-element.74, f32[16,4224]{1,0:T(8,128)S(1)} %get-tuple-element.75, f32[16,4096]{1,0:T(8,128)S(1)} %copy-done.3, ...), kind=kLoop, calls=%fused_computation.49 | loop fusion | flops 1507328 | bytes 3293200 | tf_op jit(solution)/shard_map/convert_element_type | solution.py:218
  64.0 0.8 %fusion = f32[48,256]{1,0:T(8,128)S(1)} fusion(s32[4096]{0:T(1024)S(1)} %copy-done.7, bf16[16,4096]{1,0:T(8,128)(2,1)S(1)} %get-tuple-element.83, bf16[16,4096]{1,0:T(8,128)(2,1)S(1)} %get-tuple-element.82, bf16[16,4096]{1,0:T(8,128)(2,1)S(1)} %get-tuple-element.61), kind=kOutput, calls=%fused_computation.1 | convolution fusion | flops 102891520 | bytes 458752 | tf_op jit(solution)/shard_map/dot_general | solution.py:222
  64.9 0.6 multiply_reduce_fusion
  66.2 0.6 divide_bitcast_fusion
  66.8 0.9 %select_add_fusion.1.sw_ref = f32[16,4096]{1,0:T(8,128)} fusion(f32[16,4224]{1,0:T(8,128)S(1)} %get-tuple-element.75, f32[16,4224]{1,0:T(8,128)S(1)} %get-tuple-element.77, f32[16,4224]{1,0:T(8,128)S(1)} %get-tuple-element.79, f32[16,8448]{1,0:T(8,128)S(1)} %collective-permute-done, f32[16,4096]{1,0:T(8,128)S(1)} %copy-done.4, f32[]{:T(128)S(6)} %mul.187, ...), kind=kLoop, calls=%fused_computation.82 | loop fusion | flops 1048576 | bytes 1572880 | tf_op jit(solution)/shard_map/add | solution.py:293
  67.7 10.1 %shard_map.115 = (bf16[128,4096]{1,0:T(8,128)(2,1)}, bf16[128,4096]{1,0:T(8,128)(2,1)}, bf16[128,4096]{1,0:T(8,128)(2,1)}, bf16[128,4096]{1,0:T(8,128)(2,1)}) custom-call(bf16[128,4096]{1,0:T(8,128)(2,1)} %q_ref.11, bf16[128,4096]{1,0:T(8,128)(2,1)} %k_ref.11, bf16[128,4096]{1,0:T(8,128)(2,1)} %v_ref.11, bf16[128,4096]{1,0:T(8,128)(2,1)} %g_ref.11, ...), custom_call_target="tpu_custom_call" | custom-call | tf_op jit(solution)/shard_map/pallas_call | solution.py:201
  (11 shorter events, 0.3 us)
Async XLA Ops:
  3.6 14.1 %copy-start.7 = (s32[4096]{0:T(1024)S(1)}, s32[4096]{0:T(1024)}, u32[]{:S(2)}) copy-start(s32[4096]{0:T(1024)} %param.13) | copy-start | bytes 49156
  16.5 2.0 %copy-start.5 = (f32[16,4096]{1,0:T(8,128)S(1)}, f32[16,4096]{1,0:T(8,128)}, u32[]{:S(2)}) copy-start(f32[16,4096]{1,0:T(8,128)} %get-tuple-element.32) | copy-start | bytes 786436
  16.6 2.0 %copy-start.6 = (f32[16,4096]{1,0:T(8,128)S(1)}, f32[16,4096]{1,0:T(8,128)}, u32[]{:S(2)}) copy-start(f32[16,4096]{1,0:T(8,128)} %get-tuple-element.33) | copy-start | bytes 786436
  16.6 4.1 %copy-start = (f32[16,4096]{1,0:T(8,128)S(1)}, f32[16,4096]{1,0:T(8,128)}, u32[]{:S(2)}) copy-start(f32[16,4096]{1,0:T(8,128)} %get-tuple-element.36.pw_ref) | copy-start | bytes 786436
  16.6 4.1 %copy-start.4 = (f32[16,4096]{1,0:T(8,128)S(1)}, f32[16,4096]{1,0:T(8,128)}, u32[]{:S(2)}) copy-start(f32[16,4096]{1,0:T(8,128)} %get-tuple-element.35) | copy-start | bytes 786436
  18.6 2.1 %collective-permute-start = (f32[16,8448]{1,0:T(8,128)S(1)}, f32[16,8448]{1,0:T(8,128)S(1)}, u32[]{:S(2)}, u32[]{:S(2)}) collective-permute-start(f32[16,8448]{1,0:T(8,128)S(1)} %pad_maximum_fusion), channel_id=1, source_target_pairs={{0,1},{1,0},{2,3},{3,2},{4,5},{5,4},{6,7},{7,6},{8,9},{9,8},{10,11... | collective-permute-start | bytes 1622024 | tf_op jit(solution)/shard_map/ppermute | solution.py:264
  21.9 9.7 %collective-permute-start.1 = (f32[16,4224]{1,0:T(8,128)S(1)}, f32[16,4224]{1,0:T(8,128)S(1)}, u32[]{:S(2)}, u32[]{:S(2)}) collective-permute-start(f32[16,4224]{1,0:T(8,128)S(1)} %fusion.40), channel_id=1, source_target_pairs={{0,2},{1,3},{2,0},{3,1},{4,6},{5,7},{6,4},{7,5},{8,10},{9,11},{10,... | collective-permute-start | bytes 811016 | tf_op jit(solution)/shard_map/ppermute | solution.py:269
  24.8 8.4 %copy-start.1 = (f32[16,4096]{1,0:T(8,128)S(1)}, f32[16,4096]{1,0:T(8,128)}, u32[]{:S(2)}) copy-start(f32[16,4096]{1,0:T(8,128)} %get-tuple-element.36.pw_ref) | copy-start | bytes 786436
  31.6 1.5 %collective-permute-start.2 = (f32[16,4224]{1,0:T(8,128)S(1)}, f32[16,4224]{1,0:T(8,128)S(1)}, u32[]{:S(2)}, u32[]{:S(2)}) collective-permute-start(f32[16,4224]{1,0:T(8,128)S(1)} %collective-permute-done.1), channel_id=1, source_target_pairs={{0,1},{1,0},{2,3},{3,2},{4,5},{5,4},{6,7},{7,6},{8,9},{9,8},{10,11... | collective-permute-start | bytes 811016 | tf_op jit(solution)/shard_map/ppermute | solution.py:278
  34.5 10.2 %copy-start.2 = (f32[16,4096]{1,0:T(8,128)S(1)}, f32[16,4096]{1,0:T(8,128)}, u32[]{:S(2)}) copy-start(f32[16,4096]{1,0:T(8,128)} %get-tuple-element.36.pw_ref) | copy-start | bytes 786436
  34.5 8.6 %collective-permute-start.3 = (f32[16,4224]{1,0:T(8,128)S(1)}, f32[16,4224]{1,0:T(8,128)S(1)}, u32[]{:S(2)}, u32[]{:S(2)}) collective-permute-start(f32[16,4224]{1,0:T(8,128)S(1)} %fusion.38), channel_id=1, source_target_pairs={{0,4},{1,5},{2,6},{3,7},{4,0},{5,1},{6,2},{7,3},{8,12},{9,13},{10,... | collective-permute-start | bytes 811016 | tf_op jit(solution)/shard_map/ppermute | solution.py:269
  43.1 1.5 %collective-permute-start.4 = (f32[16,4224]{1,0:T(8,128)S(1)}, f32[16,4224]{1,0:T(8,128)S(1)}, u32[]{:S(2)}, u32[]{:S(2)}) collective-permute-start(f32[16,4224]{1,0:T(8,128)S(1)} %collective-permute-done.3), channel_id=1, source_target_pairs={{0,1},{1,0},{2,3},{3,2},{4,5},{5,4},{6,7},{7,6},{8,9},{9,8},{10,11... | collective-permute-start | bytes 811016 | tf_op jit(solution)/shard_map/ppermute | solution.py:278
  46.0 15.4 %collective-permute-start.5 = (f32[16,4224]{1,0:T(8,128)S(1)}, f32[16,4224]{1,0:T(8,128)S(1)}, u32[]{:S(2)}, u32[]{:S(2)}) collective-permute-start(f32[16,4224]{1,0:T(8,128)S(1)} %fusion.36), channel_id=1, source_target_pairs={{0,8},{1,9},{2,10},{3,11},{4,12},{5,13},{6,14},{7,15},{8,0},{9,1},... | collective-permute-start | bytes 811016 | tf_op jit(solution)/shard_map/ppermute | solution.py:269
  54.7 8.3 %copy-start.3 = (f32[16,4096]{1,0:T(8,128)S(1)}, f32[16,4096]{1,0:T(8,128)}, u32[]{:S(2)}) copy-start(f32[16,4096]{1,0:T(8,128)} %get-tuple-element.36.pw_ref) | copy-start | bytes 786436
  61.4 1.5 %collective-permute-start.6 = (f32[16,4224]{1,0:T(8,128)S(1)}, f32[16,4224]{1,0:T(8,128)S(1)}, u32[]{:S(2)}, u32[]{:S(2)}) collective-permute-start(f32[16,4224]{1,0:T(8,128)S(1)} %collective-permute-done.5), channel_id=1, source_target_pairs={{0,1},{1,0},{2,3},{3,2},{4,5},{5,4},{6,7},{7,6},{8,9},{9,8},{10,11... | collective-permute-start | bytes 811016 | tf_op jit(solution)/shard_map/ppermute | solution.py:278

commit v19 on v17

--- a/solution.py
+++ b/solution.py
@@ -129,7 +129,7 @@
 
     p = p_ref[...]
     r = r_ref[...]
-    lax.fori_loop(0, rows, body, ((r * p) * s_ref[...], (r * p) * b_ref[...]), unroll=8)
+    lax.fori_loop(0, rows, body, ((r * p) * s_ref[...], (r * p) * b_ref[...]), unroll=16)
     for c in range(lanes):
         cols = slice(c * LANE, (c + 1) * LANE)
         band = slice(c * rows, (c + 1) * rows)

time: 75 us -> 74.7 us (level)
  no operation moved by 1% of the time
where the time goes in v19:
time: 74.7 us; the launch traced here: 74.3 us
  Pallas kernels  44.5 us (60%)
  waiting for transfers between devices  8.97 us (12%)
  starting transfers between devices  8.16 us (11%)
  other arithmetic  6.93 us (9%)
  matrix products  4.1 us (5%)
  between operations  1.57 us (2%)
    pallas_call x4, Pallas kernels, local_scans(): pl.pallas_call(local_kernel, grid=(1,), in_specs=specs, out_specs=[big, b...  23.4 us
    pallas_call x1, Pallas kernels, local_carries(): pl.pallas_call(carry_kernel, grid=(width // BLOCK,), in_specs=[big, big,...  11.5 us
    pallas_call x1, Pallas kernels, corrected(): pl.pallas_call(correct_kernel, grid=(width // BLOCK,), in_specs=[big] * 6...  9.71 us
    ppermute x3, starting transfers between devices, on_device(): got_mine = lax.ppermute(mine, 'ctx', pairs)  7.64 us
    ppermute x3, waiting for transfers between devices, on_device(): lax.ppermute(got_mine, 'ctx', [(i, i ^ 1) for i in range(count)])  4.63 us
    dot_general x5, matrix products, split_dot(): jnp.dot(jnp.concatenate([hi, mid, lo], axis=0), member, preferred_element...  4.1 us
    ppermute x3, waiting for transfers between devices, on_device(): got_mine = lax.ppermute(mine, 'ctx', pairs)  2.78 us
    convert_element_type x5, other arithmetic, split_dot(): hi = top.astype(bf16)  2.48 us
  transfers between devices with their start and end apart: 7, of which 7 were waited for; matrix products, arithmetic and copies ran while one was open for 0% of the time, Pallas kernels for 31%

profile of v19, /device:TPU:0, one launch (start us, length us, event | category | flops | bytes accessed | tf_op | source)
XLA Modules:
  0.0 74.3 jit_solution(18284163107148420775)
XLA Ops:
  0.6 1.3 %pad_maximum_fusion.4.par_ref = f32[32,256]{1,0:T(8,128)} fusion(f32[16,256]{1,0:T(8,128)} %bitcast.6, f32[16,256]{1,0:T(8,128)} %bitcast.7), kind=kLoop, calls=%fused_computation.108 | loop fusion | flops 8192 | bytes 65536 | tf_op jit(solution)/shard_map/concatenate | solution.py:226
  2.0 0.0 copy-start.7
  2.0 11.5 %shard_map.110 = (f32[16,4096]{1,0:T(8,128)}, f32[16,4096]{1,0:T(8,128)}, f32[16,4096]{1,0:T(8,128)}, f32[16,4096]{1,0:T(8,128)}, f32[16,4096]{1,0:T(8,128)}, /*index=5*/f32[16,4096]{1,0:T(8,128)}) custom-call(bf16[128,4096]{1,0:T(8,128)(2,1)} %q_ref.11, bf16[128,4096]{1,0:T(8,128)(2,1)} %k_ref.11, bf16[128,4096]{1,0:T(8,128)(2,1)} %v_ref.11, ...), custom_call_target="tpu_custom_call" | custom-call | tf_op jit(solution)/shard_map/pallas_call | solution.py:151
  13.4 0.0 copy-start.5
  13.5 0.0 copy-start.6
  13.5 0.0 copy-start
  13.5 0.0 copy-start.4
  13.5 1.1 %reduce-precision_convert_fusion.9 = (bf16[16,4096]{1,0:T(8,128)(2,1)S(1)}, bf16[16,4096]{1,0:T(8,128)(2,1)S(1)}, bf16[16,4096]{1,0:T(8,128)(2,1)S(1)}) fusion(f32[16,4096]{1,0:T(8,128)} %get-tuple-element.34), kind=kLoop, calls=%fused_computation.65 | loop fusion | flops 458752 | bytes 655360 | tf_op jit(solution)/shard_map/convert_element_type | solution.py:211
  14.6 0.0 copy-done.7
  14.6 0.8 %fusion.4 = f32[48,256]{1,0:T(8,128)S(1)} fusion(s32[4096]{0:T(1024)S(1)} %copy-done.7, bf16[16,4096]{1,0:T(8,128)(2,1)S(1)} %get-tuple-element.91, bf16[16,4096]{1,0:T(8,128)(2,1)S(1)} %get-tuple-element.92, bf16[16,4096]{1,0:T(8,128)(2,1)S(1)} %get-tuple-element.90), kind=kOutput, calls=%fused_computation.5 | convolution fusion | flops 102891520 | bytes 458752 | tf_op jit(solution)/shard_map/dot_general | solution.py:215
  15.4 0.0 copy-done.5
  15.4 0.0 copy-done.6
  15.5 0.5 collective-permute-start
  16.0 1.6 %collective-permute-done = f32[16,8448]{1,0:T(8,128)S(1)} collective-permute-done((f32[16,8448]{1,0:T(8,128)S(1)}, f32[16,8448]{1,0:T(8,128)S(1)}, u32[]{:S(2)}, u32[]{:S(2)}) %collective-permute-start) | collective-permute-done | bytes 540704 | tf_op jit(solution)/shard_map/ppermute | solution.py:258
  17.6 0.0 copy-done
  17.6 0.0 copy-done.4
  17.6 0.1 reduce-precision_convert_fusion.7
  17.8 0.8 %fusion.3 = f32[48,256]{1,0:T(8,128)S(1)} fusion(s32[4096]{0:T(1024)S(1)} %copy-done.7, bf16[16,4096]{1,0:T(8,128)(2,1)S(1)} %get-tuple-element.89, bf16[16,4096]{1,0:T(8,128)(2,1)S(1)} %get-tuple-element.88, bf16[16,4096]{1,0:T(8,128)(2,1)S(1)} %get-tuple-element.69), kind=kOutput, calls=%fused_computation.4 | convolution fusion | flops 102891520 | bytes 458752 | tf_op jit(solution)/shard_map/dot_general | solution.py:215
  18.6 0.1 fusion.40
  18.8 3.0 %collective-permute-start.1 = (f32[16,4224]{1,0:T(8,128)S(1)}, f32[16,4224]{1,0:T(8,128)S(1)}, u32[]{:S(2)}, u32[]{:S(2)}) collective-permute-start(f32[16,4224]{1,0:T(8,128)S(1)} %fusion.40), channel_id=1, source_target_pairs={{0,2},{1,3},{2,0},{3,1},{4,6},{5,7},{6,4},{7,5},{8,10},{9,11},{10,... | collective-permute-start | bytes 811016 | tf_op jit(solution)/shard_map/ppermute | solution.py:263
  21.7 0.0 copy-start.1
  21.7 5.8 %shard_map.111 = (f32[128,4096]{1,0:T(8,128)}, f32[128,4096]{1,0:T(8,128)}) custom-call(bf16[128,4096]{1,0:T(8,128)(2,1)} %q_ref.11, bf16[128,4096]{1,0:T(8,128)(2,1)} %k_ref.11, bf16[128,4096]{1,0:T(8,128)(2,1)} %v_ref.11, bf16[128,4096]{1,0:T(8,128)(2,1)} %g_ref.11, f32[16,4096]{1,0:T(8,128)} %get-tuple-element.36.pw_ref, f32[16,4096]{1,0:T(8,128)} %get-tuple-element.37.rw_ref), custom_call_target="tpu_custom_call" | custom-call | tf_op jit(solution)/shard_map/pallas_call | solution.py:174
  27.6 0.9 %collective-permute-done.1 = f32[16,4224]{1,0:T(8,128)S(1)} collective-permute-done((f32[16,4224]{1,0:T(8,128)S(1)}, f32[16,4224]{1,0:T(8,128)S(1)}, u32[]{:S(2)}, u32[]{:S(2)}) %collective-permute-start.1) | collective-permute-done | bytes 270368 | tf_op jit(solution)/shard_map/ppermute | solution.py:263
  28.5 0.0 collective-permute-start.2
  28.5 1.5 %collective-permute-done.2 = f32[16,4224]{1,0:T(8,128)S(1)} collective-permute-done((f32[16,4224]{1,0:T(8,128)S(1)}, f32[16,4224]{1,0:T(8,128)S(1)}, u32[]{:S(2)}, u32[]{:S(2)}) %collective-permute-start.2) | collective-permute-done | bytes 270368 | tf_op jit(solution)/shard_map/ppermute | solution.py:272
  30.1 0.0 copy-done.1
  30.1 0.1 reduce-precision_convert_fusion.5
  30.2 0.1 reduce-precision_convert_fusion.4
  30.4 0.8 %fusion.2 = f32[48,256]{1,0:T(8,128)S(1)} fusion(s32[4096]{0:T(1024)S(1)} %copy-done.7, bf16[16,4096]{1,0:T(8,128)(2,1)S(1)} %get-tuple-element.87, bf16[16,4096]{1,0:T(8,128)(2,1)S(1)} %get-tuple-element.86, bf16[16,4096]{1,0:T(8,128)(2,1)S(1)} %get-tuple-element.66), kind=kOutput, calls=%fused_computation.3 | convolution fusion | flops 102891520 | bytes 458752 | tf_op jit(solution)/shard_map/dot_general | solution.py:215
  31.2 0.1 fusion.38
  31.4 0.0 copy-start.2
  31.4 1.9 %collective-permute-start.3 = (f32[16,4224]{1,0:T(8,128)S(1)}, f32[16,4224]{1,0:T(8,128)S(1)}, u32[]{:S(2)}, u32[]{:S(2)}) collective-permute-start(f32[16,4224]{1,0:T(8,128)S(1)} %fusion.38), channel_id=1, source_target_pairs={{0,4},{1,5},{2,6},{3,7},{4,0},{5,1},{6,2},{7,3},{8,12},{9,13},{10,... | collective-permute-start | bytes 811016 | tf_op jit(solution)/shard_map/ppermute | solution.py:263
  33.2 5.8 %shard_map.112 = (f32[128,4096]{1,0:T(8,128)}, f32[128,4096]{1,0:T(8,128)}) custom-call(bf16[128,4096]{1,0:T(8,128)(2,1)} %q_ref.11, bf16[128,4096]{1,0:T(8,128)(2,1)} %k_ref.11, bf16[128,4096]{1,0:T(8,128)(2,1)} %v_ref.11, bf16[128,4096]{1,0:T(8,128)(2,1)} %g_ref.11, ...), custom_call_target="tpu_custom_call", output_to_operand_aliasing={{0}: (6, {}), {1}: (7, {})} | custom-call | tf_op jit(solution)/shard_map/pallas_call | solution.py:174
  39.0 1.0 %collective-permute-done.3 = f32[16,4224]{1,0:T(8,128)S(1)} collective-permute-done((f32[16,4224]{1,0:T(8,128)S(1)}, f32[16,4224]{1,0:T(8,128)S(1)}, u32[]{:S(2)}, u32[]{:S(2)}) %collective-permute-start.3) | collective-permute-done | bytes 270368 | tf_op jit(solution)/shard_map/ppermute | solution.py:263
  40.0 0.0 collective-permute-start.4
  40.0 1.5 %collective-permute-done.4 = f32[16,4224]{1,0:T(8,128)S(1)} collective-permute-done((f32[16,4224]{1,0:T(8,128)S(1)}, f32[16,4224]{1,0:T(8,128)S(1)}, u32[]{:S(2)}, u32[]{:S(2)}) %collective-permute-start.4) | collective-permute-done | bytes 270368 | tf_op jit(solution)/shard_map/ppermute | solution.py:272
  41.6 0.0 copy-done.2
  41.6 0.1 reduce-precision_convert_fusion.3
  41.8 0.8 %fusion.1 = f32[48,256]{1,0:T(8,128)S(1)} fusion(s32[4096]{0:T(1024)S(1)} %copy-done.7, bf16[16,4096]{1,0:T(8,128)(2,1)S(1)} %get-tuple-element.85, bf16[16,4096]{1,0:T(8,128)(2,1)S(1)} %get-tuple-element.84, bf16[16,4096]{1,0:T(8,128)(2,1)S(1)} %get-tuple-element.63), kind=kOutput, calls=%fused_computation.2 | convolution fusion | flops 102891520 | bytes 458752 | tf_op jit(solution)/shard_map/dot_general | solution.py:215
  42.6 0.1 multiply_add_fusion
  42.7 0.1 fusion.36
  42.9 2.8 %collective-permute-start.5 = (f32[16,4224]{1,0:T(8,128)S(1)}, f32[16,4224]{1,0:T(8,128)S(1)}, u32[]{:S(2)}, u32[]{:S(2)}) collective-permute-start(f32[16,4224]{1,0:T(8,128)S(1)} %fusion.36), channel_id=1, source_target_pairs={{0,8},{1,9},{2,10},{3,11},{4,12},{5,13},{6,14},{7,15},{8,0},{9,1},... | collective-permute-start | bytes 811016 | tf_op jit(solution)/shard_map/ppermute | solution.py:263
  45.7 5.9 %shard_map.113 = (f32[128,4096]{1,0:T(8,128)}, f32[128,4096]{1,0:T(8,128)}) custom-call(bf16[128,4096]{1,0:T(8,128)(2,1)} %q_ref.11, bf16[128,4096]{1,0:T(8,128)(2,1)} %k_ref.11, bf16[128,4096]{1,0:T(8,128)(2,1)} %v_ref.11, bf16[128,4096]{1,0:T(8,128)(2,1)} %g_ref.11, ...), custom_call_target="tpu_custom_call", output_to_operand_aliasing={{0}: (6, {}), {1}: (7, {})} | custom-call | tf_op jit(solution)/shard_map/pallas_call | solution.py:174
  51.6 0.0 copy-start.3
  51.6 5.8 %shard_map.114 = (f32[128,4096]{1,0:T(8,128)}, f32[128,4096]{1,0:T(8,128)}) custom-call(bf16[128,4096]{1,0:T(8,128)(2,1)} %q_ref.11, bf16[128,4096]{1,0:T(8,128)(2,1)} %k_ref.11, bf16[128,4096]{1,0:T(8,128)(2,1)} %v_ref.11, bf16[128,4096]{1,0:T(8,128)(2,1)} %g_ref.11, ...), custom_call_target="tpu_custom_call", output_to_operand_aliasing={{0}: (6, {}), {1}: (7, {})} | custom-call | tf_op jit(solution)/shard_map/pallas_call | solution.py:174
  57.4 0.9 %collective-permute-done.5 = f32[16,4224]{1,0:T(8,128)S(1)} collective-permute-done((f32[16,4224]{1,0:T(8,128)S(1)}, f32[16,4224]{1,0:T(8,128)S(1)}, u32[]{:S(2)}, u32[]{:S(2)}) %collective-permute-start.5) | collective-permute-done | bytes 270368 | tf_op jit(solution)/shard_map/ppermute | solution.py:263
  58.3 0.0 collective-permute-start.6
  58.3 1.5 %collective-permute-done.6 = f32[16,4224]{1,0:T(8,128)S(1)} collective-permute-done((f32[16,4224]{1,0:T(8,128)S(1)}, f32[16,4224]{1,0:T(8,128)S(1)}, u32[]{:S(2)}, u32[]{:S(2)}) %collective-permute-start.6) | collective-permute-done | bytes 270368 | tf_op jit(solution)/shard_map/ppermute | solution.py:272
  59.9 0.0 copy-done.3
  59.9 1.0 %reduce-precision_convert_fusion.1 = (bf16[16,4096]{1,0:T(8,128)(2,1)S(1)}, f32[16,4096]{1,0:T(8,128)S(1)}, f32[16,4096]{1,0:T(8,128)}) fusion(f32[16,4096]{1,0:T(8,128)S(1)} %multiply_add_fusion, f32[16,4224]{1,0:T(8,128)S(1)} %get-tuple-element.74, f32[16,4224]{1,0:T(8,128)S(1)} %get-tuple-element.75, f32[16,4096]{1,0:T(8,128)S(1)} %copy-done.3, ...), kind=kLoop, calls=%fused_computation.49 | loop fusion | flops 1507328 | bytes 3293200 | tf_op jit(solution)/shard_map/convert_element_type | solution.py:211
  60.9 0.8 %fusion = f32[48,256]{1,0:T(8,128)S(1)} fusion(s32[4096]{0:T(1024)S(1)} %copy-done.7, bf16[16,4096]{1,0:T(8,128)(2,1)S(1)} %get-tuple-element.83, bf16[16,4096]{1,0:T(8,128)(2,1)S(1)} %get-tuple-element.82, bf16[16,4096]{1,0:T(8,128)(2,1)S(1)} %get-tuple-element.61), kind=kOutput, calls=%fused_computation.1 | convolution fusion | flops 102891520 | bytes 458752 | tf_op jit(solution)/shard_map/dot_general | solution.py:215
  61.8 0.6 multiply_reduce_fusion
  63.1 0.6 divide_bitcast_fusion
  63.7 0.9 %select_add_fusion.1.sw_ref = f32[16,4096]{1,0:T(8,128)} fusion(f32[16,4224]{1,0:T(8,128)S(1)} %get-tuple-element.75, f32[16,4224]{1,0:T(8,128)S(1)} %get-tuple-element.77, f32[16,4224]{1,0:T(8,128)S(1)} %get-tuple-element.79, f32[16,8448]{1,0:T(8,128)S(1)} %collective-permute-done, f32[16,4096]{1,0:T(8,128)S(1)} %copy-done.4, f32[]{:T(128)S(6)} %mul.187, ...), kind=kLoop, calls=%fused_computation.82 | loop fusion | flops 1048576 | bytes 1572880 | tf_op jit(solution)/shard_map/add | solution.py:287
  64.6 9.7 %shard_map.115 = (bf16[128,4096]{1,0:T(8,128)(2,1)}, bf16[128,4096]{1,0:T(8,128)(2,1)}, bf16[128,4096]{1,0:T(8,128)(2,1)}, bf16[128,4096]{1,0:T(8,128)(2,1)}) custom-call(bf16[128,4096]{1,0:T(8,128)(2,1)} %q_ref.11, bf16[128,4096]{1,0:T(8,128)(2,1)} %k_ref.11, bf16[128,4096]{1,0:T(8,128)(2,1)} %v_ref.11, bf16[128,4096]{1,0:T(8,128)(2,1)} %g_ref.11, ...), custom_call_target="tpu_custom_call" | custom-call | tf_op jit(solution)/shard_map/pallas_call | solution.py:194
  (11 shorter events, 0.3 us)
Async XLA Ops:
  2.0 12.6 %copy-start.7 = (s32[4096]{0:T(1024)S(1)}, s32[4096]{0:T(1024)}, u32[]{:S(2)}) copy-start(s32[4096]{0:T(1024)} %param.13) | copy-start | bytes 49156
  13.4 2.0 %copy-start.5 = (f32[16,4096]{1,0:T(8,128)S(1)}, f32[16,4096]{1,0:T(8,128)}, u32[]{:S(2)}) copy-start(f32[16,4096]{1,0:T(8,128)} %get-tuple-element.32) | copy-start | bytes 786436
  13.5 2.0 %copy-start.6 = (f32[16,4096]{1,0:T(8,128)S(1)}, f32[16,4096]{1,0:T(8,128)}, u32[]{:S(2)}) copy-start(f32[16,4096]{1,0:T(8,128)} %get-tuple-element.33) | copy-start | bytes 786436
  13.5 4.1 %copy-start = (f32[16,4096]{1,0:T(8,128)S(1)}, f32[16,4096]{1,0:T(8,128)}, u32[]{:S(2)}) copy-start(f32[16,4096]{1,0:T(8,128)} %get-tuple-element.36.pw_ref) | copy-start | bytes 786436
  13.5 4.1 %copy-start.4 = (f32[16,4096]{1,0:T(8,128)S(1)}, f32[16,4096]{1,0:T(8,128)}, u32[]{:S(2)}) copy-start(f32[16,4096]{1,0:T(8,128)} %get-tuple-element.35) | copy-start | bytes 786436
  15.5 2.1 %collective-permute-start = (f32[16,8448]{1,0:T(8,128)S(1)}, f32[16,8448]{1,0:T(8,128)S(1)}, u32[]{:S(2)}, u32[]{:S(2)}) collective-permute-start(f32[16,8448]{1,0:T(8,128)S(1)} %pad_maximum_fusion), channel_id=1, source_target_pairs={{0,1},{1,0},{2,3},{3,2},{4,5},{5,4},{6,7},{7,6},{8,9},{9,8},{10,11... | collective-permute-start | bytes 1622024 | tf_op jit(solution)/shard_map/ppermute | solution.py:258
  18.8 9.7 %collective-permute-start.1 = (f32[16,4224]{1,0:T(8,128)S(1)}, f32[16,4224]{1,0:T(8,128)S(1)}, u32[]{:S(2)}, u32[]{:S(2)}) collective-permute-start(f32[16,4224]{1,0:T(8,128)S(1)} %fusion.40), channel_id=1, source_target_pairs={{0,2},{1,3},{2,0},{3,1},{4,6},{5,7},{6,4},{7,5},{8,10},{9,11},{10,... | collective-permute-start | bytes 811016 | tf_op jit(solution)/shard_map/ppermute | solution.py:263
  21.7 8.4 %copy-start.1 = (f32[16,4096]{1,0:T(8,128)S(1)}, f32[16,4096]{1,0:T(8,128)}, u32[]{:S(2)}) copy-start(f32[16,4096]{1,0:T(8,128)} %get-tuple-element.36.pw_ref) | copy-start | bytes 786436
  28.5 1.5 %collective-permute-start.2 = (f32[16,4224]{1,0:T(8,128)S(1)}, f32[16,4224]{1,0:T(8,128)S(1)}, u32[]{:S(2)}, u32[]{:S(2)}) collective-permute-start(f32[16,4224]{1,0:T(8,128)S(1)} %collective-permute-done.1), channel_id=1, source_target_pairs={{0,1},{1,0},{2,3},{3,2},{4,5},{5,4},{6,7},{7,6},{8,9},{9,8},{10,11... | collective-permute-start | bytes 811016 | tf_op jit(solution)/shard_map/ppermute | solution.py:272
  31.4 10.2 %copy-start.2 = (f32[16,4096]{1,0:T(8,128)S(1)}, f32[16,4096]{1,0:T(8,128)}, u32[]{:S(2)}) copy-start(f32[16,4096]{1,0:T(8,128)} %get-tuple-element.36.pw_ref) | copy-start | bytes 786436
  31.4 8.6 %collective-permute-start.3 = (f32[16,4224]{1,0:T(8,128)S(1)}, f32[16,4224]{1,0:T(8,128)S(1)}, u32[]{:S(2)}, u32[]{:S(2)}) collective-permute-start(f32[16,4224]{1,0:T(8,128)S(1)} %fusion.38), channel_id=1, source_target_pairs={{0,4},{1,5},{2,6},{3,7},{4,0},{5,1},{6,2},{7,3},{8,12},{9,13},{10,... | collective-permute-start | bytes 811016 | tf_op jit(solution)/shard_map/ppermute | solution.py:263
  40.0 1.5 %collective-permute-start.4 = (f32[16,4224]{1,0:T(8,128)S(1)}, f32[16,4224]{1,0:T(8,128)S(1)}, u32[]{:S(2)}, u32[]{:S(2)}) collective-permute-start(f32[16,4224]{1,0:T(8,128)S(1)} %collective-permute-done.3), channel_id=1, source_target_pairs={{0,1},{1,0},{2,3},{3,2},{4,5},{5,4},{6,7},{7,6},{8,9},{9,8},{10,11... | collective-permute-start | bytes 811016 | tf_op jit(solution)/shard_map/ppermute | solution.py:272
  42.9 15.4 %collective-permute-start.5 = (f32[16,4224]{1,0:T(8,128)S(1)}, f32[16,4224]{1,0:T(8,128)S(1)}, u32[]{:S(2)}, u32[]{:S(2)}) collective-permute-start(f32[16,4224]{1,0:T(8,128)S(1)} %fusion.36), channel_id=1, source_target_pairs={{0,8},{1,9},{2,10},{3,11},{4,12},{5,13},{6,14},{7,15},{8,0},{9,1},... | collective-permute-start | bytes 811016 | tf_op jit(solution)/shard_map/ppermute | solution.py:263
  51.6 8.3 %copy-start.3 = (f32[16,4096]{1,0:T(8,128)S(1)}, f32[16,4096]{1,0:T(8,128)}, u32[]{:S(2)}) copy-start(f32[16,4096]{1,0:T(8,128)} %get-tuple-element.36.pw_ref) | copy-start | bytes 786436
  58.3 1.5 %collective-permute-start.6 = (f32[16,4224]{1,0:T(8,128)S(1)}, f32[16,4224]{1,0:T(8,128)S(1)}, u32[]{:S(2)}, u32[]{:S(2)}) collective-permute-start(f32[16,4224]{1,0:T(8,128)S(1)} %collective-permute-done.5), channel_id=1, source_target_pairs={{0,1},{1,0},{2,3},{3,2},{4,5},{5,4},{6,7},{7,6},{8,9},{9,8},{10,11... | collective-permute-start | bytes 811016 | tf_op jit(solution)/shard_map/ppermute | solution.py:272

commit v20 on v17

--- a/solution.py
+++ b/solution.py
@@ -56,7 +56,7 @@
             return x, tot, a
 
         zero = jnp.zeros(p.shape, f32)
-        x, tot, a = lax.fori_loop(0, chunks, body, (zero, zero, zero))
+        x, tot, a = lax.fori_loop(0, chunks, body, (zero, zero, zero), unroll=2)
         xend_ref[:, cols] = x
         head_ref[:, cols] = a
         tot_ref[:, cols] = tot

time: 75 us -> 74.6 us (level)
  no operation moved by 1% of the time
where the time goes in v20:
time: 74.6 us; the launch traced here: 74.3 us
  Pallas kernels  44.5 us (60%)
  waiting for transfers between devices  8.98 us (12%)
  starting transfers between devices  8.16 us (11%)
  other arithmetic  6.93 us (9%)
  matrix products  4.1 us (5%)
  between operations  1.57 us (2%)
    pallas_call x4, Pallas kernels, local_scans(): pl.pallas_call(local_kernel, grid=(1,), in_specs=specs, out_specs=[big, b...  23.4 us
    pallas_call x1, Pallas kernels, local_carries(): pl.pallas_call(carry_kernel, grid=(width // BLOCK,), in_specs=[big, big,...  11.1 us
    pallas_call x1, Pallas kernels, corrected(): pl.pallas_call(correct_kernel, grid=(width // BLOCK,), in_specs=[big] * 6...  10.1 us
    ppermute x3, starting transfers between devices, on_device(): got_mine = lax.ppermute(mine, 'ctx', pairs)  7.64 us
    ppermute x3, waiting for transfers between devices, on_device(): lax.ppermute(got_mine, 'ctx', [(i, i ^ 1) for i in range(count)])  4.63 us
    dot_general x5, matrix products, split_dot(): jnp.dot(jnp.concatenate([hi, mid, lo], axis=0), member, preferred_element...  4.1 us
    ppermute x3, waiting for transfers between devices, on_device(): got_mine = lax.ppermute(mine, 'ctx', pairs)  2.78 us
    convert_element_type x5, other arithmetic, split_dot(): hi = top.astype(bf16)  2.48 us
  transfers between devices with their start and end apart: 7, of which 7 were waited for; matrix products, arithmetic and copies ran while one was open for 0% of the time, Pallas kernels for 31%

profile of v20, /device:TPU:0, one launch (start us, length us, event | category | flops | bytes accessed | tf_op | source)
XLA Modules:
  0.0 74.3 jit_solution(12620972725814555508)
XLA Ops:
  0.6 1.3 %pad_maximum_fusion.4.par_ref = f32[32,256]{1,0:T(8,128)} fusion(f32[16,256]{1,0:T(8,128)} %bitcast.6, f32[16,256]{1,0:T(8,128)} %bitcast.7), kind=kLoop, calls=%fused_computation.108 | loop fusion | flops 8192 | bytes 65536 | tf_op jit(solution)/shard_map/concatenate | solution.py:226
  2.0 0.0 copy-start.7
  2.0 11.1 %shard_map.110 = (f32[16,4096]{1,0:T(8,128)}, f32[16,4096]{1,0:T(8,128)}, f32[16,4096]{1,0:T(8,128)}, f32[16,4096]{1,0:T(8,128)}, f32[16,4096]{1,0:T(8,128)}, /*index=5*/f32[16,4096]{1,0:T(8,128)}) custom-call(bf16[128,4096]{1,0:T(8,128)(2,1)} %q_ref.11, bf16[128,4096]{1,0:T(8,128)(2,1)} %k_ref.11, bf16[128,4096]{1,0:T(8,128)(2,1)} %v_ref.11, ...), custom_call_target="tpu_custom_call" | custom-call | tf_op jit(solution)/shard_map/pallas_call | solution.py:151
  13.0 0.0 copy-start.5
  13.0 0.0 copy-start.6
  13.1 0.0 copy-start
  13.1 0.0 copy-start.4
  13.1 1.1 %reduce-precision_convert_fusion.9 = (bf16[16,4096]{1,0:T(8,128)(2,1)S(1)}, bf16[16,4096]{1,0:T(8,128)(2,1)S(1)}, bf16[16,4096]{1,0:T(8,128)(2,1)S(1)}) fusion(f32[16,4096]{1,0:T(8,128)} %get-tuple-element.34), kind=kLoop, calls=%fused_computation.65 | loop fusion | flops 458752 | bytes 655360 | tf_op jit(solution)/shard_map/convert_element_type | solution.py:211
  14.2 0.0 copy-done.7
  14.2 0.8 %fusion.4 = f32[48,256]{1,0:T(8,128)S(1)} fusion(s32[4096]{0:T(1024)S(1)} %copy-done.7, bf16[16,4096]{1,0:T(8,128)(2,1)S(1)} %get-tuple-element.91, bf16[16,4096]{1,0:T(8,128)(2,1)S(1)} %get-tuple-element.92, bf16[16,4096]{1,0:T(8,128)(2,1)S(1)} %get-tuple-element.90), kind=kOutput, calls=%fused_computation.5 | convolution fusion | flops 102891520 | bytes 458752 | tf_op jit(solution)/shard_map/dot_general | solution.py:215
  15.0 0.0 copy-done.5
  15.0 0.0 copy-done.6
  15.1 0.5 collective-permute-start
  15.6 1.6 %collective-permute-done = f32[16,8448]{1,0:T(8,128)S(1)} collective-permute-done((f32[16,8448]{1,0:T(8,128)S(1)}, f32[16,8448]{1,0:T(8,128)S(1)}, u32[]{:S(2)}, u32[]{:S(2)}) %collective-permute-start) | collective-permute-done | bytes 540704 | tf_op jit(solution)/shard_map/ppermute | solution.py:258
  17.2 0.0 copy-done
  17.2 0.0 copy-done.4
  17.2 0.1 reduce-precision_convert_fusion.7
  17.4 0.8 %fusion.3 = f32[48,256]{1,0:T(8,128)S(1)} fusion(s32[4096]{0:T(1024)S(1)} %copy-done.7, bf16[16,4096]{1,0:T(8,128)(2,1)S(1)} %get-tuple-element.89, bf16[16,4096]{1,0:T(8,128)(2,1)S(1)} %get-tuple-element.88, bf16[16,4096]{1,0:T(8,128)(2,1)S(1)} %get-tuple-element.69), kind=kOutput, calls=%fused_computation.4 | convolution fusion | flops 102891520 | bytes 458752 | tf_op jit(solution)/shard_map/dot_general | solution.py:215
  18.2 0.1 fusion.40
  18.4 3.0 %collective-permute-start.1 = (f32[16,4224]{1,0:T(8,128)S(1)}, f32[16,4224]{1,0:T(8,128)S(1)}, u32[]{:S(2)}, u32[]{:S(2)}) collective-permute-start(f32[16,4224]{1,0:T(8,128)S(1)} %fusion.40), channel_id=1, source_target_pairs={{0,2},{1,3},{2,0},{3,1},{4,6},{5,7},{6,4},{7,5},{8,10},{9,11},{10,... | collective-permute-start | bytes 811016 | tf_op jit(solution)/shard_map/ppermute | solution.py:263
  21.3 0.0 copy-start.1
  21.3 5.8 %shard_map.111 = (f32[128,4096]{1,0:T(8,128)}, f32[128,4096]{1,0:T(8,128)}) custom-call(bf16[128,4096]{1,0:T(8,128)(2,1)} %q_ref.11, bf16[128,4096]{1,0:T(8,128)(2,1)} %k_ref.11, bf16[128,4096]{1,0:T(8,128)(2,1)} %v_ref.11, bf16[128,4096]{1,0:T(8,128)(2,1)} %g_ref.11, f32[16,4096]{1,0:T(8,128)} %get-tuple-element.36.pw_ref, f32[16,4096]{1,0:T(8,128)} %get-tuple-element.37.rw_ref), custom_call_target="tpu_custom_call" | custom-call | tf_op jit(solution)/shard_map/pallas_call | solution.py:174
  27.2 0.9 %collective-permute-done.1 = f32[16,4224]{1,0:T(8,128)S(1)} collective-permute-done((f32[16,4224]{1,0:T(8,128)S(1)}, f32[16,4224]{1,0:T(8,128)S(1)}, u32[]{:S(2)}, u32[]{:S(2)}) %collective-permute-start.1) | collective-permute-done | bytes 270368 | tf_op jit(solution)/shard_map/ppermute | solution.py:263
  28.1 0.0 collective-permute-start.2
  28.1 1.5 %collective-permute-done.2 = f32[16,4224]{1,0:T(8,128)S(1)} collective-permute-done((f32[16,4224]{1,0:T(8,128)S(1)}, f32[16,4224]{1,0:T(8,128)S(1)}, u32[]{:S(2)}, u32[]{:S(2)}) %collective-permute-start.2) | collective-permute-done | bytes 270368 | tf_op jit(solution)/shard_map/ppermute | solution.py:272
  29.7 0.0 copy-done.1
  29.7 0.1 reduce-precision_convert_fusion.5
  29.8 0.1 reduce-precision_convert_fusion.4
  29.9 0.8 %fusion.2 = f32[48,256]{1,0:T(8,128)S(1)} fusion(s32[4096]{0:T(1024)S(1)} %copy-done.7, bf16[16,4096]{1,0:T(8,128)(2,1)S(1)} %get-tuple-element.87, bf16[16,4096]{1,0:T(8,128)(2,1)S(1)} %get-tuple-element.86, bf16[16,4096]{1,0:T(8,128)(2,1)S(1)} %get-tuple-element.66), kind=kOutput, calls=%fused_computation.3 | convolution fusion | flops 102891520 | bytes 458752 | tf_op jit(solution)/shard_map/dot_general | solution.py:215
  30.8 0.1 fusion.38
  30.9 0.0 copy-start.2
  31.0 1.9 %collective-permute-start.3 = (f32[16,4224]{1,0:T(8,128)S(1)}, f32[16,4224]{1,0:T(8,128)S(1)}, u32[]{:S(2)}, u32[]{:S(2)}) collective-permute-start(f32[16,4224]{1,0:T(8,128)S(1)} %fusion.38), channel_id=1, source_target_pairs={{0,4},{1,5},{2,6},{3,7},{4,0},{5,1},{6,2},{7,3},{8,12},{9,13},{10,... | collective-permute-start | bytes 811016 | tf_op jit(solution)/shard_map/ppermute | solution.py:263
  32.8 5.8 %shard_map.112 = (f32[128,4096]{1,0:T(8,128)}, f32[128,4096]{1,0:T(8,128)}) custom-call(bf16[128,4096]{1,0:T(8,128)(2,1)} %q_ref.11, bf16[128,4096]{1,0:T(8,128)(2,1)} %k_ref.11, bf16[128,4096]{1,0:T(8,128)(2,1)} %v_ref.11, bf16[128,4096]{1,0:T(8,128)(2,1)} %g_ref.11, ...), custom_call_target="tpu_custom_call", output_to_operand_aliasing={{0}: (6, {}), {1}: (7, {})} | custom-call | tf_op jit(solution)/shard_map/pallas_call | solution.py:174
  38.6 1.0 %collective-permute-done.3 = f32[16,4224]{1,0:T(8,128)S(1)} collective-permute-done((f32[16,4224]{1,0:T(8,128)S(1)}, f32[16,4224]{1,0:T(8,128)S(1)}, u32[]{:S(2)}, u32[]{:S(2)}) %collective-permute-start.3) | collective-permute-done | bytes 270368 | tf_op jit(solution)/shard_map/ppermute | solution.py:263
  39.6 0.0 collective-permute-start.4
  39.6 1.5 %collective-permute-done.4 = f32[16,4224]{1,0:T(8,128)S(1)} collective-permute-done((f32[16,4224]{1,0:T(8,128)S(1)}, f32[16,4224]{1,0:T(8,128)S(1)}, u32[]{:S(2)}, u32[]{:S(2)}) %collective-permute-start.4) | collective-permute-done | bytes 270368 | tf_op jit(solution)/shard_map/ppermute | solution.py:272
  41.2 0.0 copy-done.2
  41.2 0.1 reduce-precision_convert_fusion.3
  41.4 0.8 %fusion.1 = f32[48,256]{1,0:T(8,128)S(1)} fusion(s32[4096]{0:T(1024)S(1)} %copy-done.7, bf16[16,4096]{1,0:T(8,128)(2,1)S(1)} %get-tuple-element.85, bf16[16,4096]{1,0:T(8,128)(2,1)S(1)} %get-tuple-element.84, bf16[16,4096]{1,0:T(8,128)(2,1)S(1)} %get-tuple-element.63), kind=kOutput, calls=%fused_computation.2 | convolution fusion | flops 102891520 | bytes 458752 | tf_op jit(solution)/shard_map/dot_general | solution.py:215
  42.2 0.1 multiply_add_fusion
  42.3 0.1 fusion.36
  42.5 2.8 %collective-permute-start.5 = (f32[16,4224]{1,0:T(8,128)S(1)}, f32[16,4224]{1,0:T(8,128)S(1)}, u32[]{:S(2)}, u32[]{:S(2)}) collective-permute-start(f32[16,4224]{1,0:T(8,128)S(1)} %fusion.36), channel_id=1, source_target_pairs={{0,8},{1,9},{2,10},{3,11},{4,12},{5,13},{6,14},{7,15},{8,0},{9,1},... | collective-permute-start | bytes 811016 | tf_op jit(solution)/shard_map/ppermute | solution.py:263
  45.3 5.9 %shard_map.113 = (f32[128,4096]{1,0:T(8,128)}, f32[128,4096]{1,0:T(8,128)}) custom-call(bf16[128,4096]{1,0:T(8,128)(2,1)} %q_ref.11, bf16[128,4096]{1,0:T(8,128)(2,1)} %k_ref.11, bf16[128,4096]{1,0:T(8,128)(2,1)} %v_ref.11, bf16[128,4096]{1,0:T(8,128)(2,1)} %g_ref.11, ...), custom_call_target="tpu_custom_call", output_to_operand_aliasing={{0}: (6, {}), {1}: (7, {})} | custom-call | tf_op jit(solution)/shard_map/pallas_call | solution.py:174
  51.1 0.0 copy-start.3
  51.2 5.8 %shard_map.114 = (f32[128,4096]{1,0:T(8,128)}, f32[128,4096]{1,0:T(8,128)}) custom-call(bf16[128,4096]{1,0:T(8,128)(2,1)} %q_ref.11, bf16[128,4096]{1,0:T(8,128)(2,1)} %k_ref.11, bf16[128,4096]{1,0:T(8,128)(2,1)} %v_ref.11, bf16[128,4096]{1,0:T(8,128)(2,1)} %g_ref.11, ...), custom_call_target="tpu_custom_call", output_to_operand_aliasing={{0}: (6, {}), {1}: (7, {})} | custom-call | tf_op jit(solution)/shard_map/pallas_call | solution.py:174
  57.0 0.9 %collective-permute-done.5 = f32[16,4224]{1,0:T(8,128)S(1)} collective-permute-done((f32[16,4224]{1,0:T(8,128)S(1)}, f32[16,4224]{1,0:T(8,128)S(1)}, u32[]{:S(2)}, u32[]{:S(2)}) %collective-permute-start.5) | collective-permute-done | bytes 270368 | tf_op jit(solution)/shard_map/ppermute | solution.py:263
  57.9 0.0 collective-permute-start.6
  57.9 1.5 %collective-permute-done.6 = f32[16,4224]{1,0:T(8,128)S(1)} collective-permute-done((f32[16,4224]{1,0:T(8,128)S(1)}, f32[16,4224]{1,0:T(8,128)S(1)}, u32[]{:S(2)}, u32[]{:S(2)}) %collective-permute-start.6) | collective-permute-done | bytes 270368 | tf_op jit(solution)/shard_map/ppermute | solution.py:272
  59.5 0.0 copy-done.3
  59.5 1.0 %reduce-precision_convert_fusion.1 = (bf16[16,4096]{1,0:T(8,128)(2,1)S(1)}, f32[16,4096]{1,0:T(8,128)S(1)}, f32[16,4096]{1,0:T(8,128)}) fusion(f32[16,4096]{1,0:T(8,128)S(1)} %multiply_add_fusion, f32[16,4224]{1,0:T(8,128)S(1)} %get-tuple-element.74, f32[16,4224]{1,0:T(8,128)S(1)} %get-tuple-element.75, f32[16,4096]{1,0:T(8,128)S(1)} %copy-done.3, ...), kind=kLoop, calls=%fused_computation.49 | loop fusion | flops 1507328 | bytes 3293200 | tf_op jit(solution)/shard_map/convert_element_type | solution.py:211
  60.5 0.8 %fusion = f32[48,256]{1,0:T(8,128)S(1)} fusion(s32[4096]{0:T(1024)S(1)} %copy-done.7, bf16[16,4096]{1,0:T(8,128)(2,1)S(1)} %get-tuple-element.83, bf16[16,4096]{1,0:T(8,128)(2,1)S(1)} %get-tuple-element.82, bf16[16,4096]{1,0:T(8,128)(2,1)S(1)} %get-tuple-element.61), kind=kOutput, calls=%fused_computation.1 | convolution fusion | flops 102891520 | bytes 458752 | tf_op jit(solution)/shard_map/dot_general | solution.py:215
  61.3 0.6 multiply_reduce_fusion
  62.7 0.6 divide_bitcast_fusion
  63.3 0.9 %select_add_fusion.1.sw_ref = f32[16,4096]{1,0:T(8,128)} fusion(f32[16,4224]{1,0:T(8,128)S(1)} %get-tuple-element.75, f32[16,4224]{1,0:T(8,128)S(1)} %get-tuple-element.77, f32[16,4224]{1,0:T(8,128)S(1)} %get-tuple-element.79, f32[16,8448]{1,0:T(8,128)S(1)} %collective-permute-done, f32[16,4096]{1,0:T(8,128)S(1)} %copy-done.4, f32[]{:T(128)S(6)} %mul.187, ...), kind=kLoop, calls=%fused_computation.82 | loop fusion | flops 1048576 | bytes 1572880 | tf_op jit(solution)/shard_map/add | solution.py:287
  64.2 10.1 %shard_map.115 = (bf16[128,4096]{1,0:T(8,128)(2,1)}, bf16[128,4096]{1,0:T(8,128)(2,1)}, bf16[128,4096]{1,0:T(8,128)(2,1)}, bf16[128,4096]{1,0:T(8,128)(2,1)}) custom-call(bf16[128,4096]{1,0:T(8,128)(2,1)} %q_ref.11, bf16[128,4096]{1,0:T(8,128)(2,1)} %k_ref.11, bf16[128,4096]{1,0:T(8,128)(2,1)} %v_ref.11, bf16[128,4096]{1,0:T(8,128)(2,1)} %g_ref.11, ...), custom_call_target="tpu_custom_call" | custom-call | tf_op jit(solution)/shard_map/pallas_call | solution.py:194
  (11 shorter events, 0.3 us)
Async XLA Ops:
  2.0 12.2 %copy-start.7 = (s32[4096]{0:T(1024)S(1)}, s32[4096]{0:T(1024)}, u32[]{:S(2)}) copy-start(s32[4096]{0:T(1024)} %param.13) | copy-start | bytes 49156
  13.0 2.0 %copy-start.5 = (f32[16,4096]{1,0:T(8,128)S(1)}, f32[16,4096]{1,0:T(8,128)}, u32[]{:S(2)}) copy-start(f32[16,4096]{1,0:T(8,128)} %get-tuple-element.32) | copy-start | bytes 786436
  13.0 2.0 %copy-start.6 = (f32[16,4096]{1,0:T(8,128)S(1)}, f32[16,4096]{1,0:T(8,128)}, u32[]{:S(2)}) copy-start(f32[16,4096]{1,0:T(8,128)} %get-tuple-element.33) | copy-start | bytes 786436
  13.1 4.1 %copy-start = (f32[16,4096]{1,0:T(8,128)S(1)}, f32[16,4096]{1,0:T(8,128)}, u32[]{:S(2)}) copy-start(f32[16,4096]{1,0:T(8,128)} %get-tuple-element.36.pw_ref) | copy-start | bytes 786436
  13.1 4.1 %copy-start.4 = (f32[16,4096]{1,0:T(8,128)S(1)}, f32[16,4096]{1,0:T(8,128)}, u32[]{:S(2)}) copy-start(f32[16,4096]{1,0:T(8,128)} %get-tuple-element.35) | copy-start | bytes 786436
  15.1 2.1 %collective-permute-start = (f32[16,8448]{1,0:T(8,128)S(1)}, f32[16,8448]{1,0:T(8,128)S(1)}, u32[]{:S(2)}, u32[]{:S(2)}) collective-permute-start(f32[16,8448]{1,0:T(8,128)S(1)} %pad_maximum_fusion), channel_id=1, source_target_pairs={{0,1},{1,0},{2,3},{3,2},{4,5},{5,4},{6,7},{7,6},{8,9},{9,8},{10,11... | collective-permute-start | bytes 1622024 | tf_op jit(solution)/shard_map/ppermute | solution.py:258
  18.4 9.7 %collective-permute-start.1 = (f32[16,4224]{1,0:T(8,128)S(1)}, f32[16,4224]{1,0:T(8,128)S(1)}, u32[]{:S(2)}, u32[]{:S(2)}) collective-permute-start(f32[16,4224]{1,0:T(8,128)S(1)} %fusion.40), channel_id=1, source_target_pairs={{0,2},{1,3},{2,0},{3,1},{4,6},{5,7},{6,4},{7,5},{8,10},{9,11},{10,... | collective-permute-start | bytes 811016 | tf_op jit(solution)/shard_map/ppermute | solution.py:263
  21.3 8.4 %copy-start.1 = (f32[16,4096]{1,0:T(8,128)S(1)}, f32[16,4096]{1,0:T(8,128)}, u32[]{:S(2)}) copy-start(f32[16,4096]{1,0:T(8,128)} %get-tuple-element.36.pw_ref) | copy-start | bytes 786436
  28.1 1.5 %collective-permute-start.2 = (f32[16,4224]{1,0:T(8,128)S(1)}, f32[16,4224]{1,0:T(8,128)S(1)}, u32[]{:S(2)}, u32[]{:S(2)}) collective-permute-start(f32[16,4224]{1,0:T(8,128)S(1)} %collective-permute-done.1), channel_id=1, source_target_pairs={{0,1},{1,0},{2,3},{3,2},{4,5},{5,4},{6,7},{7,6},{8,9},{9,8},{10,11... | collective-permute-start | bytes 811016 | tf_op jit(solution)/shard_map/ppermute | solution.py:272
  30.9 10.2 %copy-start.2 = (f32[16,4096]{1,0:T(8,128)S(1)}, f32[16,4096]{1,0:T(8,128)}, u32[]{:S(2)}) copy-start(f32[16,4096]{1,0:T(8,128)} %get-tuple-element.36.pw_ref) | copy-start | bytes 786436
  31.0 8.6 %collective-permute-start.3 = (f32[16,4224]{1,0:T(8,128)S(1)}, f32[16,4224]{1,0:T(8,128)S(1)}, u32[]{:S(2)}, u32[]{:S(2)}) collective-permute-start(f32[16,4224]{1,0:T(8,128)S(1)} %fusion.38), channel_id=1, source_target_pairs={{0,4},{1,5},{2,6},{3,7},{4,0},{5,1},{6,2},{7,3},{8,12},{9,13},{10,... | collective-permute-start | bytes 811016 | tf_op jit(solution)/shard_map/ppermute | solution.py:263
  39.6 1.5 %collective-permute-start.4 = (f32[16,4224]{1,0:T(8,128)S(1)}, f32[16,4224]{1,0:T(8,128)S(1)}, u32[]{:S(2)}, u32[]{:S(2)}) collective-permute-start(f32[16,4224]{1,0:T(8,128)S(1)} %collective-permute-done.3), channel_id=1, source_target_pairs={{0,1},{1,0},{2,3},{3,2},{4,5},{5,4},{6,7},{7,6},{8,9},{9,8},{10,11... | collective-permute-start | bytes 811016 | tf_op jit(solution)/shard_map/ppermute | solution.py:272
  42.5 15.4 %collective-permute-start.5 = (f32[16,4224]{1,0:T(8,128)S(1)}, f32[16,4224]{1,0:T(8,128)S(1)}, u32[]{:S(2)}, u32[]{:S(2)}) collective-permute-start(f32[16,4224]{1,0:T(8,128)S(1)} %fusion.36), channel_id=1, source_target_pairs={{0,8},{1,9},{2,10},{3,11},{4,12},{5,13},{6,14},{7,15},{8,0},{9,1},... | collective-permute-start | bytes 811016 | tf_op jit(solution)/shard_map/ppermute | solution.py:263
  51.1 8.3 %copy-start.3 = (f32[16,4096]{1,0:T(8,128)S(1)}, f32[16,4096]{1,0:T(8,128)}, u32[]{:S(2)}) copy-start(f32[16,4096]{1,0:T(8,128)} %get-tuple-element.36.pw_ref) | copy-start | bytes 786436
  57.9 1.5 %collective-permute-start.6 = (f32[16,4224]{1,0:T(8,128)S(1)}, f32[16,4224]{1,0:T(8,128)S(1)}, u32[]{:S(2)}, u32[]{:S(2)}) collective-permute-start(f32[16,4224]{1,0:T(8,128)S(1)} %collective-permute-done.5), channel_id=1, source_target_pairs={{0,1},{1,0},{2,3},{3,2},{4,5},{5,4},{6,7},{7,6},{8,9},{9,8},{10,11... | collective-permute-start | bytes 811016 | tf_op jit(solution)/shard_map/ppermute | solution.py:272
